TPU v7x, 128 devices: a whole 4x4x4 slice. The times are simulated.
128 devices in a mesh: req: 16 (over y, x), head: 8 (over z, core).
Axes of the slice: x: 4, y: 4, z: 4, core: 2. Of those that a mesh axis runs over, the one named last changes fastest.
Arguments:
- hidden_in: bfloat16 [4864, 3072], P('req', 'head'), may hold values from -6 to 6
- dec_query: bfloat16 [768, 3072], P('req', 'head'), may hold values from -5.5 to 5.5
- dec_key: bfloat16 [768, 3072], P('req', 'head'), may hold values from -6 to 6
- dec_value: bfloat16 [768, 3072], P('req', 'head'), may hold values from -6 to 6
- pre_query: bfloat16 [4096, 3072], P('req', 'head'), may hold values from -5.5 to 5.5
- pre_key: bfloat16 [4096, 3072], P('req', 'head'), may hold values from -6 to 6
- pre_value: bfloat16 [4096, 3072], P('req', 'head'), may hold values from -6 to 6
- cache_key: bfloat16 [32, 2048, 3072], P('req', None, 'head'), may hold values from -5.5 to 5.5
- cache_value: bfloat16 [32, 2048, 3072], P('req', None, 'head'), may hold values from -6 to 6
- group_of: int32 [768, 1], replicated, may hold values from 0 to 31; in each aligned block of 768 rows (0 to 767, 768 to 1535, ...) at most 48 rows name the same one
- cache_length: int32 [32], P('req'), may hold values from 256 to 2048, as said below
- stretch_start: int32 [16], P('req'), may hold values from 256 to 2048, as said below
- row_owner: int32 [4864, 1], P('req'), may hold values from 0 to 15; in each aligned block of 304 rows (0 to 303, 304 to 607, ...) at most 40 rows name the same one
- out_weight: bfloat16 [3072, 3072], P('head'), may hold values from -0.109375 to 0.109375
- norm_gain: float32 [3072], replicated, may hold values from 0.1 to 1.9
- gate_weight: bfloat16 [3072, 4096], P(None, 'head'), may hold values from -0.109375 to 0.109375
- up_weight: bfloat16 [3072, 4096], P(None, 'head'), may hold values from -0.109375 to 0.109375
- down_weight: bfloat16 [4096, 3072], P('head'), may hold values from -0.09375 to 0.09375
Outputs:
- layer_out: bfloat16 [10240, 3072], P(('req', 'head'))
Inputs may be any that keep to these rules, and one draw needn't show every extreme that they name: `group_of`: at most 48 requests share a cache group, exactly 48 in some group; every group has a request. `cache_length`: some group has all 2048 rows valid. `stretch_start`: some stretch follows all 2048 cached rows. `row_owner`: among the 304 rows of one index of req at most 40 share an owner, exactly 40 on some index.
All inputs are finite; a program needn't handle non-finite values.
Results may differ from a plain program's by a relative error of at most 0.02.
Values may be sent and summed in bfloat16 or wider, within the bound.
No kernel may reach another device: no remote copies, remote signals or barrier semaphores. Data moves between devices by JAX's collectives and lax.ppermute only.
A program may use at most 128 MiB of HBM per device.

v0:
```python
import math

import jax
import jax.numpy as jnp
from jax import lax
from jax.sharding import PartitionSpec as P

HD = 96
CAP = 48


eps_norm = 1e-05


def head_split(matrix):
    return matrix.reshape(matrix.shape[0], matrix.shape[1] // HD, HD)


def softmax_rows(scores, allowed):
    masked = jnp.where(allowed, scores, -jnp.inf)
    highest = jnp.max(masked, axis=-1, keepdims=True)
    raised = jnp.exp(masked - highest)
    return (raised / jnp.sum(raised, axis=-1, keepdims=True)).astype(jnp.bfloat16)


def rank_within(onehot, axis):
    return jnp.sum((jnp.cumsum(onehot, axis=axis) - 1) * onehot, axis=-1)


def pair_then_z_scatter(x):
    rows, cols = x.shape
    n = lax.axis_size("head")
    ring = n // 2
    width = cols // n
    h = lax.axis_index("head")
    zc = h // 2
    on_first = h % 2 == 0
    even = jnp.concatenate([x[:, (2 * z) * width : (2 * z + 1) * width] for z in range(ring)], 1)
    odd = jnp.concatenate([x[:, (2 * z + 1) * width : (2 * z + 2) * width] for z in range(ring)], 1)
    mine = jnp.where(on_first, even, odd)
    other = jnp.where(on_first, odd, even)
    got = lax.ppermute(other, "head", [(i, i ^ 1) for i in range(n)])
    pair_sum = (mine.astype(jnp.float32) + got.astype(jnp.float32)).astype(jnp.bfloat16)
    acc = lax.dynamic_slice_in_dim(pair_sum, zc * width, width, 1).astype(jnp.float32)
    for d in range(1, ring):
        perm = [(i, ((i // 2 + d) % ring) * 2 + i % 2) for i in range(n)]
        piece = lax.dynamic_slice_in_dim(pair_sum, ((zc + d) % ring) * width, width, 1)
        acc = acc + lax.ppermute(piece, "head", perm).astype(jnp.float32)
    return acc


def z_then_pair_gather(y):
    rows, width = y.shape
    n = lax.axis_size("head")
    ring = n // 2
    h = lax.axis_index("head")
    zc = h // 2
    on_first = h % 2 == 0
    parts = [y]
    for d in range(1, ring):
        perm = [(i, ((i // 2 + d) % ring) * 2 + i % 2) for i in range(n)]
        parts.append(lax.ppermute(y, "head", perm))
    stacked = jnp.stack(parts, 0)
    in_order = jnp.concatenate(
        [lax.dynamic_index_in_dim(stacked, (zc - zz) % ring, 0, keepdims=False) for zz in range(ring)], 1
    )
    got = lax.ppermute(in_order, "head", [(i, i ^ 1) for i in range(n)])
    pieces = []
    for z in range(ring):
        mine_z = in_order[:, z * width : (z + 1) * width]
        got_z = got[:, z * width : (z + 1) * width]
        pieces.append(jnp.where(on_first, mine_z, got_z))
        pieces.append(jnp.where(on_first, got_z, mine_z))
    return jnp.concatenate(pieces, 1)


def on_device(
    hidden_in,
    dec_query,
    dec_key,
    dec_value,
    pre_query,
    pre_key,
    pre_value,
    cache_key,
    cache_value,
    group_of,
    cache_length,
    stretch_start,
    row_owner,
    out_weight,
    norm_gain,
    gate_weight,
    up_weight,
    down_weight,
):
    factor = 1.0 / math.sqrt(HD)
    width_here = dec_query.shape[1]
    req_count = lax.axis_size("req")
    head_count = lax.axis_size("head")
    me = lax.axis_index("req")
    groups_here = cache_key.shape[0]
    length_cache = cache_key.shape[1]
    per_home = dec_query.shape[0]
    members = group_of[:, 0]
    total_reqs = members.shape[0]

    holder_of = members // groups_here
    holder_hot = (holder_of[:, None] == jnp.arange(req_count, dtype=jnp.int32)[None, :]).astype(jnp.int32)
    rank_all = rank_within(holder_hot.reshape(req_count, per_home, req_count), 1).reshape(total_reqs)
    slot_of = (jnp.arange(total_reqs, dtype=jnp.int32) // per_home) * per_home + rank_all

    my_holder = lax.dynamic_slice_in_dim(holder_of, me * per_home, per_home)
    my_rank = lax.dynamic_slice_in_dim(rank_all, me * per_home, per_home)
    my_slot = my_holder * per_home + my_rank
    packer = (
        my_slot[None, :] == jnp.arange(req_count * per_home, dtype=jnp.int32)[:, None]
    ).astype(jnp.bfloat16)
    stacked_in = jnp.concatenate([dec_query, dec_key, dec_value], axis=1)
    outgoing_q = jnp.dot(packer, stacked_in, preferred_element_type=jnp.float32).astype(jnp.bfloat16)
    arrived_q = lax.all_to_all(outgoing_q, "req", split_axis=0, concat_axis=0, tiled=True)

    first_group = me * groups_here
    wanted = first_group + jnp.arange(groups_here, dtype=jnp.int32)
    belongs = (members[None, :] == wanted[:, None]).astype(jnp.int32)
    ranking = jnp.cumsum(belongs, axis=1) - 1
    places = jnp.arange(CAP, dtype=jnp.int32)
    chosen = ((belongs[:, None, :] == 1) & (ranking[:, None, :] == places[None, :, None])).reshape(
        groups_here * CAP, total_reqs
    )
    chosen_slot = jnp.sum(jnp.where(chosen, slot_of[None, :], 0), axis=1)
    chosen_any = jnp.any(chosen, axis=1)
    chooser = chosen_any[:, None] & (
        chosen_slot[:, None] == jnp.arange(req_count * per_home, dtype=jnp.int32)[None, :]
    )
    picked = jnp.dot(
        chooser.astype(jnp.bfloat16), arrived_q, preferred_element_type=jnp.float32
    ).astype(jnp.bfloat16)
    positions = jnp.arange(length_cache)
    results = []
    for group_pos in range(groups_here):
        rows_block = picked[group_pos * CAP : (group_pos + 1) * CAP]
        picked_q = head_split(rows_block[:, :width_here])
        picked_k = head_split(rows_block[:, width_here : 2 * width_here])
        picked_v = head_split(rows_block[:, 2 * width_here :])
        cache_scores = (
            jnp.einsum(
                "qhd,khd->hqk",
                picked_q,
                head_split(cache_key[group_pos]),
                preferred_element_type=jnp.float32,
            )
            * factor
        )
        own_scores = (
            jnp.sum(picked_q.astype(jnp.float32) * picked_k.astype(jnp.float32), axis=-1).T * factor
        )
        scores = jnp.concatenate([cache_scores, own_scores[:, :, None]], axis=-1)
        allowed = jnp.concatenate([positions < cache_length[group_pos], jnp.ones((1,), bool)])[
            None, None, :
        ]
        weights = softmax_rows(scores, allowed)
        blended = jnp.einsum(
            "hqk,khd->qhd",
            weights[:, :, :length_cache],
            head_split(cache_value[group_pos]),
            preferred_element_type=jnp.float32,
        )
        blended = blended + weights[:, :, length_cache].astype(jnp.float32).T[
            :, :, None
        ] * picked_v.astype(jnp.float32)
        results.append(blended.reshape(CAP, width_here))
    stacked = jnp.concatenate(results, axis=0).astype(jnp.bfloat16)
    going_back = jnp.dot(
        chooser.astype(jnp.bfloat16).T, stacked, preferred_element_type=jnp.float32
    ).astype(jnp.bfloat16)
    came_back = lax.all_to_all(going_back, "req", split_axis=0, concat_axis=0, tiled=True)
    dec_out = jnp.dot(packer.T, came_back, preferred_element_type=jnp.float32).astype(jnp.bfloat16)

    stretch_len = pre_query.shape[0]
    key_rows = jnp.concatenate([cache_key[0], pre_key], axis=0)
    value_rows = jnp.concatenate([cache_value[0], pre_value], axis=0)
    columns = jnp.arange(length_cache + stretch_len)
    row_numbers = jnp.arange(stretch_len)
    allowed_pre = jnp.where(
        columns[None, :] < length_cache,
        columns[None, :] < stretch_start[0],
        columns[None, :] - length_cache <= row_numbers[:, None],
    )
    pre_scores = (
        jnp.einsum(
            "qhd,khd->hqk",
            head_split(pre_query),
            head_split(key_rows),
            preferred_element_type=jnp.float32,
        )
        * factor
    )
    pre_weights = softmax_rows(pre_scores, allowed_pre[None])
    pre_mixed = jnp.einsum(
        "hqk,khd->qhd", pre_weights, head_split(value_rows), preferred_element_type=jnp.float32
    )
    pre_out = pre_mixed.reshape(stretch_len, width_here).astype(jnp.bfloat16)
    attn_rows = jnp.concatenate([dec_out, pre_out], axis=0)
    projected = jnp.dot(attn_rows, out_weight, preferred_element_type=jnp.float32)
    head_me = lax.axis_index("head")
    col_start = head_me * width_here
    own_cols = lax.dynamic_slice_in_dim(projected, col_start, width_here, 1) + hidden_in.astype(
        jnp.float32
    )
    contribution = lax.dynamic_update_slice_in_dim(projected, own_cols, col_start, 1)
    own_residual = pair_then_z_scatter(contribution.astype(jnp.bfloat16))
    residual = z_then_pair_gather(own_residual.astype(jnp.bfloat16))

    residual_wide = residual.astype(jnp.float32)
    squares = jnp.mean(jnp.square(residual_wide), axis=-1, keepdims=True)
    normed = (residual_wide * lax.rsqrt(squares + eps_norm) * norm_gain).astype(jnp.bfloat16)
    gate_act = jnp.dot(normed, gate_weight, preferred_element_type=jnp.float32)
    up_act = jnp.dot(normed, up_weight, preferred_element_type=jnp.float32)
    hidden = (jax.nn.silu(gate_act) * up_act).astype(jnp.bfloat16)
    down_part = jnp.dot(hidden, down_weight, preferred_element_type=jnp.float32).astype(jnp.bfloat16)
    down_cols = pair_then_z_scatter(down_part)
    own_wide = own_residual.astype(jnp.bfloat16).astype(jnp.float32)
    out_cols = (own_wide + down_cols).astype(jnp.bfloat16)

    row_count = residual.shape[0]
    slot_rows = 8 * ((2 * row_count + 8 * req_count - 1) // (8 * req_count))
    owners = row_owner[:, 0]
    onehot_owner = (owners[:, None] == jnp.arange(req_count, dtype=jnp.int32)[None, :]).astype(
        jnp.int32
    )
    before = rank_within(onehot_owner, 0)
    target = owners * slot_rows + before
    placing = (
        target[None, :] == jnp.arange(req_count * slot_rows, dtype=jnp.int32)[:, None]
    ).astype(jnp.bfloat16)
    outgoing = jnp.dot(placing, out_cols, preferred_element_type=jnp.float32).astype(jnp.bfloat16)
    arrived = lax.all_to_all(outgoing, "req", split_axis=0, concat_axis=0, tiled=True)
    return lax.all_to_all(arrived, "head", split_axis=0, concat_axis=1, tiled=True)


def solution(mesh):
    placed = (
        P("req", "head"),
        P("req", "head"),
        P("req", "head"),
        P("req", "head"),
        P("req", "head"),
        P("req", "head"),
        P("req", "head"),
        P("req", None, "head"),
        P("req", None, "head"),
        P(),
        P("req"),
        P("req"),
        P("req", None),
        P("head", None),
        P(),
        P(None, "head"),
        P(None, "head"),
        P("head", None),
    )
    return jax.shard_map(
        on_device, mesh=mesh, in_specs=placed, out_specs=P(("req", "head"), None), check_vma=False
    )
```

profile of v0, /device:TPU:1, one launch (start us, length us, event | category | flops | bytes accessed | tf_op | source)
XLA Modules:
  0.0 198.8 jit_solution(3617092464703296111)
XLA Ops:
  2.4 2.6 %convolution_convert_fusion.1 = bf16[768,1152]{1,0:T(8,128)(2,1)} fusion(s32[48]{0:T(128)S(1)} %dynamic-slice_add_fusion, bf16[48,384]{1,0:T(8,128)(2,1)} %param.21, bf16[48,384]{1,0:T(8,128)(2,1)} %param.20, bf16[48,384]{1,0:T(8,128)(2,1)} %param.19), kind=kOutput, calls=%fused_computation.21 | convolution fusion | flops 86188032 | bytes 1880256 | tf_op jit(solution)/shard_map/dot_general | solution.py:120
  5.0 7.6 %all-to-all-start = ((bf16[16,48,1152]{2,1,0:T(8,128)(2,1)}), bf16[16,48,1152]{2,1,0:T(8,128)(2,1)}, u32[]{:S(2)}, u32[]{:S(2)}) async-start(bf16[16,48,1152]{2,1,0:T(8,128)(2,1)} %bitcast.100), calls=%async_computation | async-start | bytes 3538944 | tf_op jit(solution)/shard_map/all_to_all | solution.py:121
  14.4 3.9 %fusion.120 = (bf16[1,2048,384]{2,1,0:T(8,128)(2,1)}, bf16[1,2048,384]{2,1,0:T(8,128)(2,1)}) fusion(bf16[2,2048,384]{2,1,0:T(8,128)(2,1)} %param.25), kind=kLoop, calls=%fused_computation.206 | loop fusion | bytes 6291456 | tf_op jit(solution)/shard_map/slice | solution.py:150
  18.2 2.7 %copy.124 = bf16[1,2048,384]{1,2,0:T(8,128)(2,1)} copy(bf16[1,2048,384]{2,1,0:T(8,128)(2,1)} %get-tuple-element.8) | data formatting | bytes 3145728 | tf_op jit(solution)/shard_map/slice | solution.py:150
  20.9 4.0 %fusion.121 = (bf16[1,2048,384]{2,1,0:T(8,128)(2,1)}, bf16[1,2048,384]{2,1,0:T(8,128)(2,1)}) fusion(bf16[2,2048,384]{2,1,0:T(8,128)(2,1)} %param.26), kind=kLoop, calls=%fused_computation.207 | loop fusion | bytes 6291456 | tf_op jit(solution)/shard_map/slice | solution.py:166
  24.8 2.6 %copy.128 = bf16[1,2048,384]{1,2,0:T(8,128)(2,1)} copy(bf16[1,2048,384]{2,1,0:T(8,128)(2,1)} %get-tuple-element.10) | data formatting | bytes 3145728 | tf_op jit(solution)/shard_map/slice | solution.py:166
  27.4 2.6 %copy.131 = bf16[1,2048,384]{1,2,0:T(8,128)(2,1)} copy(bf16[1,2048,384]{2,1,0:T(8,128)(2,1)} %get-tuple-element.7) | data formatting | bytes 3145728 | tf_op jit(solution)/shard_map/slice | solution.py:150
  30.1 2.7 %copy.135 = bf16[1,2048,384]{1,2,0:T(8,128)(2,1)} copy(bf16[1,2048,384]{2,1,0:T(8,128)(2,1)} %get-tuple-element.9) | data formatting | bytes 3145728 | tf_op jit(solution)/shard_map/slice | solution.py:166
  39.4 2.7 %fusion.15 = pred[256,2304]{0,1:T(8,128)(4,1)} fusion(s32[2304]{0:T(1024)S(1)} %iota_add_fusion, pred[2304]{0:T(1024)(128)(4,1)S(1)} %get-tuple-element.51, pred[2304]{0:T(1024)(128)(4,1)S(1)} %get-tuple-element.52), kind=kLoop, calls=%fused_computation.25 | loop fusion | flops 1179648 | bytes 603648 | tf_op jit(solution)/shard_map/jit(_where)/select_n | solution.py:185
  42.1 2.0 convolution_convert_fusion.2
  51.2 2.3 %fusion.31 = bf16[48,4,96]{2,0,1:T(8,128)(2,1)S(1)} fusion(bf16[2048,4,96]{0,2,1:T(8,128)(2,1)} %bitcast.105, bf16[4,48,2049]{2,1,0:T(8,128)(2,1)} %copy-done.3, f32[48,4,96]{2,1,0:T(4,128)S(1)} %reshape.286, f32[48,4]{0,1:T(4,128)S(1)} %bitcast.124), kind=kOutput, calls=%fused_computation.51 | convolution fusion | flops 75552768 | bytes 2470656 | tf_op jit(solution)/shard_map/hqk,khd->qhd/dot_general | solution.py:163
  58.1 2.3 %fusion.32 = bf16[48,4,96]{2,0,1:T(8,128)(2,1)S(1)} fusion(bf16[2048,4,96]{0,2,1:T(8,128)(2,1)} %bitcast.107, bf16[4,48,2049]{2,1,0:T(8,128)(2,1)} %copy-done.2, f32[48,4,96]{2,1,0:T(4,128)S(1)} %reshape.288, f32[48,4]{0,1:T(4,128)S(1)} %bitcast.123), kind=kOutput, calls=%fused_computation.52 | convolution fusion | flops 75552768 | bytes 2470656 | tf_op jit(solution)/shard_map/hqk,khd->qhd/dot_general | solution.py:163
  61.8 6.7 %all-to-all-start.1 = ((bf16[16,48,384]{2,1,0:T(8,128)(2,1)}), bf16[16,48,384]{2,1,0:T(8,128)(2,1)}, u32[]{:S(2)}, u32[]{:S(2)}) async-start(bf16[16,48,384]{2,1,0:T(8,128)(2,1)} %bitcast.108), calls=%async_computation.1 | async-start | bytes 1179648 | tf_op jit(solution)/shard_map/all_to_all | solution.py:177
  68.5 5.0 %fusion.126 = f32[4,256]{1,0:T(4,128)S(1)} fusion(pred[256,2304]{0,1:T(8,128)(4,1)} %fusion.15, bf16[256,4,96]{0,2,1:T(8,128)(2,1)} %bitcast.115, bf16[256,4,96]{0,2,1:T(8,128)(2,1)S(1)} %bitcast.113, bf16[2048,4,96]{0,2,1:T(8,128)(2,1)} %bitcast.102), kind=kOutput, calls=%fused_computation.212 | convolution fusion | flops 465963264 | bytes 2560000 | tf_op jit(solution)/shard_map/sub | solution.py:22
  73.5 7.7 %fusion.26 = bf16[4,96,256]{2,1,0:T(8,128)(2,1)} fusion(f32[4,256]{1,0:T(4,128)S(1)} %fusion.126, bf16[256,4,96]{0,2,1:T(8,128)(2,1)} %bitcast.117, bf16[2048,4,96]{0,2,1:T(8,128)(2,1)} %bitcast.106, pred[256,2304]{0,1:T(8,128)(4,1)} %fusion.15, bf16[256,4,96]{0,2,1:T(8,128)(2,1)} %bitcast.116, bf16[256,4,96]{0,2,1:T(8,128)(2,1)S(1)} %bitcast.114, ...), kind=kOutput, calls=%fused_computation.46 | convolution fusion | flops 924945664 | bytes 4526080 | tf_op jit(solution)/shard_map/hqk,khd->qhd/dot_general | solution.py:200
  82.6 3.1 %fusion.56 = f32[304,3072]{1,0:T(8,128)S(1)} fusion(bf16[384,3072]{1,0:T(8,128)(2,1)} %param.31, bf16[256,384]{0,1:T(8,128)(2,1)} %bitcast.118, bf16[48,384]{0,1:T(8,128)(2,1)S(1)} %copy.142), kind=kOutput, calls=%fused_computation.85 | convolution fusion | flops 717692928 | bytes 6328320 | tf_op jit(solution)/shard_map/dot_general | solution.py:205
  89.8 2.5 %collective-permute-done = bf16[304,1536]{1,0:T(8,128)(2,1)} collective-permute-done((bf16[304,1536]{1,0:T(8,128)(2,1)}, bf16[304,1536]{1,0:T(8,128)(2,1)}, u32[]{:S(2)}, u32[]{:S(2)}) %collective-permute-start) | collective-permute-done | bytes 933920 | tf_op jit(solution)/shard_map/ppermute | solution.py:42
  92.2 2.0 add_convert_fusion.1
  97.7 3.3 %collective-permute-start.2 = (bf16[304,384]{1,0:T(8,128)(2,1)}, bf16[304,384]{1,0:T(8,128)(2,1)}, u32[]{:S(2)}, u32[]{:S(2)}) collective-permute-start(bf16[304,384]{1,0:T(8,128)(2,1)} %get-tuple-element.36), channel_id=1, source_target_pairs={{0,4},{1,5},{2,6},{3,7},{4,0},{5,1},{6,2},{7,3},{8,12},{9,13},{10,... | collective-permute-start | bytes 700424 | tf_op jit(solution)/shard_map/ppermute | solution.py:48
  101.7 4.0 %collective-permute-done.1 = bf16[304,384]{1,0:T(8,128)(2,1)S(1)} collective-permute-done((bf16[304,384]{1,0:T(8,128)(2,1)}, bf16[304,384]{1,0:T(8,128)(2,1)S(1)}, u32[]{:S(2)}, u32[]{:S(2)}) %collective-permute-start.1) | collective-permute-done | bytes 233504 | tf_op jit(solution)/shard_map/ppermute | solution.py:48
  105.7 6.0 %collective-permute-done.2 = bf16[304,384]{1,0:T(8,128)(2,1)} collective-permute-done((bf16[304,384]{1,0:T(8,128)(2,1)}, bf16[304,384]{1,0:T(8,128)(2,1)}, u32[]{:S(2)}, u32[]{:S(2)}) %collective-permute-start.2) | collective-permute-done | bytes 233504 | tf_op jit(solution)/shard_map/ppermute | solution.py:48
  114.3 2.6 %collective-permute-start.5 = (bf16[304,384]{1,0:T(8,128)(2,1)S(1)}, bf16[304,384]{1,0:T(8,128)(2,1)}, u32[]{:S(2)}, u32[]{:S(2)}) collective-permute-start(bf16[304,384]{1,0:T(8,128)(2,1)S(1)} %add_convert_fusion.3), channel_id=1, source_target_pairs={{0,4},{1,5},{2,6},{3,7},{4,0},{5,1},{6,2},{7,3},{8,12},{9,13},{10,... | collective-permute-start | bytes 700424 | tf_op jit(solution)/shard_map/ppermute | solution.py:62
  117.0 3.5 %collective-permute-done.4 = bf16[304,384]{1,0:T(8,128)(2,1)} collective-permute-done((bf16[304,384]{1,0:T(8,128)(2,1)S(1)}, bf16[304,384]{1,0:T(8,128)(2,1)}, u32[]{:S(2)}, u32[]{:S(2)}) %collective-permute-start.4) | collective-permute-done | bytes 233504 | tf_op jit(solution)/shard_map/ppermute | solution.py:62
  120.5 6.8 %collective-permute-done.5 = bf16[304,384]{1,0:T(8,128)(2,1)} collective-permute-done((bf16[304,384]{1,0:T(8,128)(2,1)S(1)}, bf16[304,384]{1,0:T(8,128)(2,1)}, u32[]{:S(2)}, u32[]{:S(2)}) %collective-permute-start.5) | collective-permute-done | bytes 233504 | tf_op jit(solution)/shard_map/ppermute | solution.py:62
  130.3 2.1 %collective-permute-done.7 = bf16[304,1536]{1,0:T(8,128)(2,1)S(1)} collective-permute-done((bf16[304,1536]{1,0:T(8,128)(2,1)S(1)}, bf16[304,1536]{1,0:T(8,128)(2,1)S(1)}, u32[]{:S(2)}, u32[]{:S(2)}) %collective-permute-start.7) | collective-permute-done | bytes 933920 | tf_op jit(solution)/shard_map/ppermute | solution.py:67
  135.4 2.0 %fusion.51 = f32[304,512]{1,0:T(8,128)} fusion(bf16[3072,512]{1,0:T(8,128)(2,1)S(1)} %copy-done.35, bf16[304,3072]{1,0:T(8,128)(2,1)S(1)} %select_dynamic-update-slice_fusion, f32[3072]{0:T(1024)S(1)} %copy-done.36, f32[304]{0:T(512)S(1)} %add_rsqrt_fusion), kind=kOutput, calls=%fused_computation.76 | convolution fusion | flops 960036864 | bytes 5649600 | tf_op jit(solution)/shard_map/dot_general | solution.py:218
  137.4 6.1 %convolution_convert_fusion = bf16[304,3072]{1,0:T(8,128)(2,1)} fusion(bf16[512,3072]{1,0:T(8,128)(2,1)S(1)} %copy-done, bf16[3072,512]{1,0:T(8,128)(2,1)} %param.34, f32[304,512]{1,0:T(8,128)} %fusion.51, bf16[304,3072]{1,0:T(8,128)(2,1)} %copy-done.4, f32[3072]{0:T(1024)S(1)} %copy-done.36, f32[304]{0:T(512)S(1)} %add_rsqrt_fusion), kind=kOutput, calls=%fused_computation.15 | convolution fusion | flops 1918205952 | bytes 10663104 | tf_op jit(solution)/shard_map/dot_general | solution.py:221
  150.1 2.0 add_convert_fusion
  155.3 5.3 %collective-permute-done.10 = bf16[304,384]{1,0:T(8,128)(2,1)S(1)} collective-permute-done((bf16[304,384]{1,0:T(8,128)(2,1)S(1)}, bf16[304,384]{1,0:T(8,128)(2,1)S(1)}, u32[]{:S(2)}, u32[]{:S(2)}) %collective-permute-start.10) | collective-permute-done | bytes 233504 | tf_op jit(solution)/shard_map/ppermute | solution.py:48
  160.6 4.6 %collective-permute-done.11 = bf16[304,384]{1,0:T(8,128)(2,1)S(1)} collective-permute-done((bf16[304,384]{1,0:T(8,128)(2,1)S(1)}, bf16[304,384]{1,0:T(8,128)(2,1)S(1)}, u32[]{:S(2)}, u32[]{:S(2)}) %collective-permute-start.11) | collective-permute-done | bytes 233504 | tf_op jit(solution)/shard_map/ppermute | solution.py:48
  166.9 16.9 %all_to_all.52 = bf16[16,40,384]{2,1,0:T(8,128)(2,1)S(1)} all-to-all(bf16[16,40,384]{2,1,0:T(8,128)(2,1)S(1)} %bitcast.112), channel_id=1, replica_groups=mesh['req'=16,'head'=8] {'req'}, dimensions={0} | all-to-all | bytes 983040 | tf_op jit(solution)/shard_map/all_to_all | solution.py:238
  183.8 14.1 %all_to_all.53 = bf16[8,80,384]{2,1,0:T(8,128)(2,1)S(1)} all-to-all(bf16[8,80,384]{2,1,0:T(8,128)(2,1)S(1)} %bitcast.109), channel_id=1, replica_groups=mesh['req'=16,'head'=8] {'head'}, dimensions={0} | all-to-all | bytes 983040 | tf_op jit(solution)/shard_map/all_to_all | solution.py:239
  (180 shorter events, 53.4 us)
Async XLA Ops:
  0.0 137.4 %copy-start = (bf16[512,3072]{1,0:T(8,128)(2,1)S(1)}, bf16[512,3072]{1,0:T(8,128)(2,1)}, u32[]{:S(2)}) copy-start(bf16[512,3072]{1,0:T(8,128)(2,1)} %param.35) | copy-start | bytes 9437188
  2.4 2.6 %copy-start.26 = (s32[48]{0:T(128)}, s32[48]{0:T(128)S(1)}, u32[]{:S(2)}) copy-start(s32[48]{0:T(128)S(1)} %dynamic-slice_add_fusion) | copy-start | bytes 580
  5.0 37.1 %all-to-all-start = ((bf16[16,48,1152]{2,1,0:T(8,128)(2,1)}), bf16[16,48,1152]{2,1,0:T(8,128)(2,1)}, u32[]{:S(2)}, u32[]{:S(2)}) async-start(bf16[16,48,1152]{2,1,0:T(8,128)(2,1)} %bitcast.100), calls=%async_computation | async-start | bytes 3538944 | tf_op jit(solution)/shard_map/all_to_all | solution.py:121
  14.3 27.8 %copy-start.30 = (s32[96]{0:T(128)}, s32[96]{0:T(128)S(1)}, u32[]{:S(2)}) copy-start(s32[96]{0:T(128)S(1)} %eq.178) | copy-start | bytes 1156
  14.4 27.7 %copy-start.32 = (pred[96]{0:T(512)(128)(4,1)}, pred[96]{0:T(512)(128)(4,1)S(1)}, u32[]{:S(2)}) copy-start(pred[96]{0:T(512)(128)(4,1)S(1)} %and.89) | copy-start | bytes 292
  30.1 3.4 %copy-start.23 = (bf16[256,384]{1,0:T(8,128)(2,1)S(1)}, bf16[256,384]{1,0:T(8,128)(2,1)}, u32[]{:S(2)}) copy-start(bf16[256,384]{1,0:T(8,128)(2,1)} %param.23) | copy-start | bytes 589828
  30.1 4.2 %copy-start.24 = (bf16[256,384]{1,0:T(8,128)(2,1)S(1)}, bf16[256,384]{1,0:T(8,128)(2,1)}, u32[]{:S(2)}) copy-start(bf16[256,384]{1,0:T(8,128)(2,1)} %param.22) | copy-start | bytes 589828
  30.1 6.8 %copy-start.29 = (s32[2]{0:T(128)S(1)}, s32[2]{0:T(128)}, u32[]{:S(2)}) copy-start(s32[2]{0:T(128)} %param.28) | copy-start | bytes 28
  53.8 2.5 %copy-start.28 = (pred[2049]{0:T(1024)(128)(4,1)S(1)}, pred[2049]{0:T(1024)(128)(4,1)}, u32[]{:S(2)}) copy-start(pred[2049]{0:T(1024)(128)(4,1)} %get-tuple-element.53) | copy-start | bytes 6151
  57.8 2.7 %copy-start.31 = (s32[96]{0:T(128)S(1)}, s32[96]{0:T(128)}, u32[]{:S(2)}) copy-start(s32[96]{0:T(128)} %copy-done.30) | copy-start | bytes 1156
  57.8 2.7 %copy-start.33 = (pred[96]{0:T(512)(128)(4,1)S(1)}, pred[96]{0:T(512)(128)(4,1)}, u32[]{:S(2)}) copy-start(pred[96]{0:T(512)(128)(4,1)} %copy-done.32) | copy-start | bytes 292
  58.0 10.4 %copy-start.25 = (bf16[256,384]{0,1:T(8,128)(2,1)S(1)}, bf16[256,384]{0,1:T(8,128)(2,1)}, u32[]{:S(2)}) copy-start(bf16[256,384]{0,1:T(8,128)(2,1)} %copy.139) | copy-start | bytes 589828
  61.8 19.3 %all-to-all-start.1 = ((bf16[16,48,384]{2,1,0:T(8,128)(2,1)}), bf16[16,48,384]{2,1,0:T(8,128)(2,1)}, u32[]{:S(2)}, u32[]{:S(2)}) async-start(bf16[16,48,384]{2,1,0:T(8,128)(2,1)} %bitcast.108), calls=%async_computation.1 | async-start | bytes 1179648 | tf_op jit(solution)/shard_map/all_to_all | solution.py:177
  73.5 7.7 %copy-start.27 = (s32[48]{0:T(128)S(1)}, s32[48]{0:T(128)}, u32[]{:S(2)}) copy-start(s32[48]{0:T(128)} %copy-done.26) | copy-start | bytes 580
  82.6 3.1 %copy-start.21 = (bf16[304,384]{1,0:T(8,128)(2,1)S(1)}, bf16[304,384]{1,0:T(8,128)(2,1)}, u32[]{:S(2)}) copy-start(bf16[304,384]{1,0:T(8,128)(2,1)} %param.18) | copy-start | bytes 700420
  88.2 4.1 %collective-permute-start = (bf16[304,1536]{1,0:T(8,128)(2,1)}, bf16[304,1536]{1,0:T(8,128)(2,1)}, u32[]{:S(2)}, u32[]{:S(2)}) collective-permute-start(bf16[304,1536]{1,0:T(8,128)(2,1)} %broadcast_select_fusion.1), channel_id=1, source_target_pairs={{0,1},{1,0},{2,3},{3,2},{4,5},{5,4},{6,7},{7,6},{8,9},{9,8},{10,11... | collective-permute-start | bytes 2801672 | tf_op jit(solution)/shard_map/ppermute | solution.py:42
  96.0 9.7 %collective-permute-start.1 = (bf16[304,384]{1,0:T(8,128)(2,1)}, bf16[304,384]{1,0:T(8,128)(2,1)S(1)}, u32[]{:S(2)}, u32[]{:S(2)}) collective-permute-start(bf16[304,384]{1,0:T(8,128)(2,1)} %get-tuple-element.34), channel_id=1, source_target_pairs={{0,2},{1,3},{2,4},{3,5},{4,6},{5,7},{6,0},{7,1},{8,10},{9,11},{10,... | collective-permute-start | bytes 700424 | tf_op jit(solution)/shard_map/ppermute | solution.py:48
  97.7 14.0 %collective-permute-start.2 = (bf16[304,384]{1,0:T(8,128)(2,1)}, bf16[304,384]{1,0:T(8,128)(2,1)}, u32[]{:S(2)}, u32[]{:S(2)}) collective-permute-start(bf16[304,384]{1,0:T(8,128)(2,1)} %get-tuple-element.36), channel_id=1, source_target_pairs={{0,4},{1,5},{2,6},{3,7},{4,0},{5,1},{6,2},{7,3},{8,12},{9,13},{10,... | collective-permute-start | bytes 700424 | tf_op jit(solution)/shard_map/ppermute | solution.py:48
  101.0 10.7 %collective-permute-start.3 = (bf16[304,384]{1,0:T(8,128)(2,1)}, bf16[304,384]{1,0:T(8,128)(2,1)}, u32[]{:S(2)}, u32[]{:S(2)}) collective-permute-start(bf16[304,384]{1,0:T(8,128)(2,1)} %get-tuple-element.35), channel_id=1, source_target_pairs={{0,6},{1,7},{2,0},{3,1},{4,2},{5,3},{6,4},{7,5},{8,14},{9,15},{10,... | collective-permute-start | bytes 700424 | tf_op jit(solution)/shard_map/ppermute | solution.py:48
  105.7 6.0 %copy-start.22 = (bf16[304,384]{1,0:T(8,128)(2,1)}, bf16[304,384]{1,0:T(8,128)(2,1)S(1)}, u32[]{:S(2)}) copy-start(bf16[304,384]{1,0:T(8,128)(2,1)S(1)} %collective-permute-done.1) | copy-start | bytes 700420
  113.1 15.6 %copy-start.19 = (bf16[304,384]{1,0:T(8,128)(2,1)}, bf16[304,384]{1,0:T(8,128)(2,1)S(1)}, u32[]{:S(2)}) copy-start(bf16[304,384]{1,0:T(8,128)(2,1)S(1)} %add_convert_fusion.3) | copy-start | bytes 700420
  113.1 7.4 %collective-permute-start.4 = (bf16[304,384]{1,0:T(8,128)(2,1)S(1)}, bf16[304,384]{1,0:T(8,128)(2,1)}, u32[]{:S(2)}, u32[]{:S(2)}) collective-permute-start(bf16[304,384]{1,0:T(8,128)(2,1)S(1)} %add_convert_fusion.3), channel_id=1, source_target_pairs={{0,2},{1,3},{2,4},{3,5},{4,6},{5,7},{6,0},{7,1},{8,10},{9,11},{10,... | collective-permute-start | bytes 700424 | tf_op jit(solution)/shard_map/ppermute | solution.py:62
  114.3 13.0 %collective-permute-start.5 = (bf16[304,384]{1,0:T(8,128)(2,1)S(1)}, bf16[304,384]{1,0:T(8,128)(2,1)}, u32[]{:S(2)}, u32[]{:S(2)}) collective-permute-start(bf16[304,384]{1,0:T(8,128)(2,1)S(1)} %add_convert_fusion.3), channel_id=1, source_target_pairs={{0,4},{1,5},{2,6},{3,7},{4,0},{5,1},{6,2},{7,3},{8,12},{9,13},{10,... | collective-permute-start | bytes 700424 | tf_op jit(solution)/shard_map/ppermute | solution.py:62
  116.9 10.4 %collective-permute-start.6 = (bf16[304,384]{1,0:T(8,128)(2,1)S(1)}, bf16[304,384]{1,0:T(8,128)(2,1)}, u32[]{:S(2)}, u32[]{:S(2)}) collective-permute-start(bf16[304,384]{1,0:T(8,128)(2,1)S(1)} %add_convert_fusion.3), channel_id=1, source_target_pairs={{0,6},{1,7},{2,0},{3,1},{4,2},{5,3},{6,4},{7,5},{8,14},{9,15},{10,... | collective-permute-start | bytes 700424 | tf_op jit(solution)/shard_map/ppermute | solution.py:62
  128.8 3.6 %collective-permute-start.7 = (bf16[304,1536]{1,0:T(8,128)(2,1)S(1)}, bf16[304,1536]{1,0:T(8,128)(2,1)S(1)}, u32[]{:S(2)}, u32[]{:S(2)}) collective-permute-start(bf16[304,1536]{1,0:T(8,128)(2,1)S(1)} %pad_maximum_fusion.3), channel_id=1, source_target_pairs={{0,1},{1,0},{2,3},{3,2},{4,5},{5,4},{6,7},{7,6},{8,9},{9,8},{10,11... | collective-permute-start | bytes 2801672 | tf_op jit(solution)/shard_map/ppermute | solution.py:67
  132.8 2.6 %copy-start.35 = (bf16[3072,512]{1,0:T(8,128)(2,1)S(1)}, bf16[3072,512]{1,0:T(8,128)(2,1)}, u32[]{:S(2)}) copy-start(bf16[3072,512]{1,0:T(8,128)(2,1)} %param.33) | copy-start | bytes 9437188
  132.8 2.6 %copy-start.36 = (f32[3072]{0:T(1024)S(1)}, f32[3072]{0:T(1024)}, u32[]{:S(2)}) copy-start(f32[3072]{0:T(1024)} %param.32) | copy-start | bytes 36868
  147.1 2.9 %collective-permute-start.8 = (bf16[304,1536]{1,0:T(8,128)(2,1)}, bf16[304,1536]{1,0:T(8,128)(2,1)}, u32[]{:S(2)}, u32[]{:S(2)}) collective-permute-start(bf16[304,1536]{1,0:T(8,128)(2,1)} %broadcast_select_fusion), channel_id=1, source_target_pairs={{0,1},{1,0},{2,3},{3,2},{4,5},{5,4},{6,7},{7,6},{8,9},{9,8},{10,11... | collective-permute-start | bytes 2801672 | tf_op jit(solution)/shard_map/ppermute | solution.py:42
  148.8 17.5 %copy-start.20 = (bf16[304,384]{1,0:T(8,128)(2,1)S(1)}, bf16[304,384]{1,0:T(8,128)(2,1)}, u32[]{:S(2)}) copy-start(bf16[304,384]{1,0:T(8,128)(2,1)} %copy-done.19) | copy-start | bytes 700420
  152.1 8.5 %collective-permute-start.10 = (bf16[304,384]{1,0:T(8,128)(2,1)S(1)}, bf16[304,384]{1,0:T(8,128)(2,1)S(1)}, u32[]{:S(2)}, u32[]{:S(2)}) collective-permute-start(bf16[304,384]{1,0:T(8,128)(2,1)S(1)} %get-tuple-element.29), channel_id=1, source_target_pairs={{0,4},{1,5},{2,6},{3,7},{4,0},{5,1},{6,2},{7,3},{8,12},{9,13},{10,... | collective-permute-start | bytes 700424 | tf_op jit(solution)/shard_map/ppermute | solution.py:48
  153.5 11.7 %collective-permute-start.11 = (bf16[304,384]{1,0:T(8,128)(2,1)S(1)}, bf16[304,384]{1,0:T(8,128)(2,1)S(1)}, u32[]{:S(2)}, u32[]{:S(2)}) collective-permute-start(bf16[304,384]{1,0:T(8,128)(2,1)S(1)} %get-tuple-element.28), channel_id=1, source_target_pairs={{0,6},{1,7},{2,0},{3,1},{4,2},{5,3},{6,4},{7,5},{8,14},{9,15},{10,... | collective-permute-start | bytes 700424 | tf_op jit(solution)/shard_map/ppermute | solution.py:48
  155.3 11.1 %collective-permute-start.9 = (bf16[304,384]{1,0:T(8,128)(2,1)S(1)}, bf16[304,384]{1,0:T(8,128)(2,1)S(1)}, u32[]{:S(2)}, u32[]{:S(2)}) collective-permute-start(bf16[304,384]{1,0:T(8,128)(2,1)S(1)} %get-tuple-element.27), channel_id=1, source_target_pairs={{0,2},{1,3},{2,4},{3,5},{4,6},{5,7},{6,0},{7,1},{8,10},{9,11},{10,... | collective-permute-start | bytes 700424 | tf_op jit(solution)/shard_map/ppermute | solution.py:48
  (19 other events, 29.9 us)
where the time goes:
time: 200 us; the launch traced here: 199 us
  matrix products  39.7 us (20%)
  waiting for transfers between devices  37.1 us (19%)
  local copies, waits for them, and re-layouts  36.5 us (18%)
  blocking collectives  31.1 us (16%)
  starting transfers between devices  30.4 us (15%)
  other arithmetic  22.6 us (11%)
    ppermute x6, waiting for transfers between devices, pair_then_z_scatter(): acc = acc + lax.ppermute(piece, 'head', perm).astype(jnp.float32)  21 us
    all_to_all x1, blocking collectives, on_device(): lax.all_to_all(outgoing, 'req', split_axis=0, concat_axis=0, tiled=True)  16.9 us
    all_to_all x1, blocking collectives, on_device(): lax.all_to_all(arrived, 'head', split_axis=0, concat_axis=1, tiled=True)  14.1 us
    ppermute x3, waiting for transfers between devices, z_then_pair_gather(): parts.append(lax.ppermute(y, 'head', perm))  10.3 us
    unnamed x78, local copies, waits for them, and re-layouts  9.28 us
    slice x3, local copies, waits for them, and re-layouts, on_device(): cache_value[group_pos]  9.26 us
    slice x3, local copies, waits for them, and re-layouts, on_device(): cache_key[group_pos]  9.16 us
    ppermute x6, starting transfers between devices, pair_then_z_scatter(): acc = acc + lax.ppermute(piece, 'head', perm).astype(jnp.float32)  8.82 us
  transfers between devices with their start and end apart: 14, of which 10 were waited for; matrix products, arithmetic and copies ran while one was open for 21% of the time, Pallas kernels for 0%

commit v1 on v0

--- a/solution.py
+++ b/solution.py
@@ -10,17 +10,6 @@
 
 
 eps_norm = 1e-05
-
-
-def head_split(matrix):
-    return matrix.reshape(matrix.shape[0], matrix.shape[1] // HD, HD)
-
-
-def softmax_rows(scores, allowed):
-    masked = jnp.where(allowed, scores, -jnp.inf)
-    highest = jnp.max(masked, axis=-1, keepdims=True)
-    raised = jnp.exp(masked - highest)
-    return (raised / jnp.sum(raised, axis=-1, keepdims=True)).astype(jnp.bfloat16)
 
 
 def rank_within(onehot, axis):
@@ -136,40 +125,40 @@
     picked = jnp.dot(
         chooser.astype(jnp.bfloat16), arrived_q, preferred_element_type=jnp.float32
     ).astype(jnp.bfloat16)
+    heads_here = width_here // HD
+    head_mask = (jnp.arange(width_here) // HD)[None, :] == jnp.arange(heads_here)[:, None]
     positions = jnp.arange(length_cache)
     results = []
     for group_pos in range(groups_here):
         rows_block = picked[group_pos * CAP : (group_pos + 1) * CAP]
-        picked_q = head_split(rows_block[:, :width_here])
-        picked_k = head_split(rows_block[:, width_here : 2 * width_here])
-        picked_v = head_split(rows_block[:, 2 * width_here :])
-        cache_scores = (
-            jnp.einsum(
-                "qhd,khd->hqk",
-                picked_q,
-                head_split(cache_key[group_pos]),
-                preferred_element_type=jnp.float32,
-            )
+        q_rows = rows_block[:, :width_here]
+        k_own = rows_block[:, width_here : 2 * width_here]
+        v_own = rows_block[:, 2 * width_here :]
+        q_stack = jnp.where(head_mask[:, None, :], q_rows[None], 0).reshape(heads_here * CAP, width_here)
+        cache_scores = lax.dot_general(
+            q_stack, cache_key[group_pos], (((1,), (1,)), ((), ())), preferred_element_type=jnp.float32
+        ) * factor
+        own_prod = q_rows.astype(jnp.float32) * k_own.astype(jnp.float32)
+        own_scores = (
+            jnp.sum(jnp.where(head_mask[:, None, :], own_prod[None], 0.0), axis=-1).reshape(heads_here * CAP, 1)
             * factor
         )
-        own_scores = (
-            jnp.sum(picked_q.astype(jnp.float32) * picked_k.astype(jnp.float32), axis=-1).T * factor
+        valid = (positions < cache_length[group_pos])[None, :]
+        cache_scores = jnp.where(valid, cache_scores, -jnp.inf)
+        highest = jnp.maximum(jnp.max(cache_scores, axis=-1, keepdims=True), own_scores)
+        raised = jnp.exp(cache_scores - highest)
+        raised_own = jnp.exp(own_scores - highest)
+        total = jnp.sum(raised, axis=-1, keepdims=True) + raised_own
+        weights = (raised / total).astype(jnp.bfloat16)
+        weight_own = (raised_own / total).astype(jnp.bfloat16).astype(jnp.float32)
+        mixed = jnp.dot(weights, cache_value[group_pos], preferred_element_type=jnp.float32)
+        mixed = mixed + weight_own * v_own.astype(jnp.float32)[None].repeat(heads_here, 0).reshape(
+            heads_here * CAP, width_here
         )
-        scores = jnp.concatenate([cache_scores, own_scores[:, :, None]], axis=-1)
-        allowed = jnp.concatenate([positions < cache_length[group_pos], jnp.ones((1,), bool)])[
-            None, None, :
-        ]
-        weights = softmax_rows(scores, allowed)
-        blended = jnp.einsum(
-            "hqk,khd->qhd",
-            weights[:, :, :length_cache],
-            head_split(cache_value[group_pos]),
-            preferred_element_type=jnp.float32,
+        blended = jnp.sum(
+            jnp.where(head_mask[:, None, :], mixed.reshape(heads_here, CAP, width_here), 0.0), axis=0
         )
-        blended = blended + weights[:, :, length_cache].astype(jnp.float32).T[
-            :, :, None
-        ] * picked_v.astype(jnp.float32)
-        results.append(blended.reshape(CAP, width_here))
+        results.append(blended)
     stacked = jnp.concatenate(results, axis=0).astype(jnp.bfloat16)
     going_back = jnp.dot(
         chooser.astype(jnp.bfloat16).T, stacked, preferred_element_type=jnp.float32
@@ -178,29 +167,28 @@
     dec_out = jnp.dot(packer.T, came_back, preferred_element_type=jnp.float32).astype(jnp.bfloat16)
 
     stretch_len = pre_query.shape[0]
-    key_rows = jnp.concatenate([cache_key[0], pre_key], axis=0)
-    value_rows = jnp.concatenate([cache_value[0], pre_value], axis=0)
-    columns = jnp.arange(length_cache + stretch_len)
     row_numbers = jnp.arange(stretch_len)
-    allowed_pre = jnp.where(
-        columns[None, :] < length_cache,
-        columns[None, :] < stretch_start[0],
-        columns[None, :] - length_cache <= row_numbers[:, None],
-    )
-    pre_scores = (
-        jnp.einsum(
-            "qhd,khd->hqk",
-            head_split(pre_query),
-            head_split(key_rows),
-            preferred_element_type=jnp.float32,
-        )
-        * factor
-    )
-    pre_weights = softmax_rows(pre_scores, allowed_pre[None])
-    pre_mixed = jnp.einsum(
-        "hqk,khd->qhd", pre_weights, head_split(value_rows), preferred_element_type=jnp.float32
-    )
-    pre_out = pre_mixed.reshape(stretch_len, width_here).astype(jnp.bfloat16)
+    pre_stack = jnp.where(head_mask[:, None, :], pre_query[None], 0).reshape(heads_here * stretch_len, width_here)
+    dims = (((1,), (1,)), ((), ()))
+    cache_part = lax.dot_general(pre_stack, cache_key[0], dims, preferred_element_type=jnp.float32) * factor
+    self_part = lax.dot_general(pre_stack, pre_key, dims, preferred_element_type=jnp.float32) * factor
+    cache_part = jnp.where((positions < stretch_start[0])[None, :], cache_part, -jnp.inf)
+    causal = (row_numbers[None, :] <= row_numbers[:, None])[None]
+    self_part = jnp.where(causal, self_part.reshape(heads_here, stretch_len, stretch_len), -jnp.inf).reshape(
+        heads_here * stretch_len, stretch_len
+    )
+    highest = jnp.maximum(
+        jnp.max(cache_part, axis=-1, keepdims=True), jnp.max(self_part, axis=-1, keepdims=True)
+    )
+    raised_cache = jnp.exp(cache_part - highest)
+    raised_self = jnp.exp(self_part - highest)
+    total = jnp.sum(raised_cache, axis=-1, keepdims=True) + jnp.sum(raised_self, axis=-1, keepdims=True)
+    pre_mixed = jnp.dot(
+        (raised_cache / total).astype(jnp.bfloat16), cache_value[0], preferred_element_type=jnp.float32
+    ) + jnp.dot((raised_self / total).astype(jnp.bfloat16), pre_value, preferred_element_type=jnp.float32)
+    pre_out = jnp.sum(
+        jnp.where(head_mask[:, None, :], pre_mixed.reshape(heads_here, stretch_len, width_here), 0.0), axis=0
+    ).astype(jnp.bfloat16)
     attn_rows = jnp.concatenate([dec_out, pre_out], axis=0)
     projected = jnp.dot(attn_rows, out_weight, preferred_element_type=jnp.float32)
     head_me = lax.axis_index("head")

time: 200 us -> 184 us (0.920)
  local copies, waits for them, and re-layouts: 36.5 us -> 12.3 us
  waiting for transfers between devices: 37.1 us -> 54.8 us
  starting transfers between devices: 30.4 us -> 23.6 us
  blocking collectives: 31.1 us -> 28.6 us
    slice x8 -> x2, local copies, waits for them, and re-layouts: 19.3 us -> 0.8 us  [the longest x1 0.58 us: on_device(): valid = (positions < cache_length[group_pos])[None, :]]
    all_to_all x1, waiting for transfers between devices: 0.01 us -> 9.53 us  [on_device(): lax.all_to_all(outgoing_q, 'req', split_axis=0, concat_axis=0, tiled=True)]
    dot_general x5 -> x8, matrix products: 15.9 us -> 22.4 us  [the longest x1 7.48 us: on_device(): jnp.dot((raised_cache / total).astype(jnp.bfloat16), cache_value[0], pref...]
    sub x1 -> x0, matrix products: 4.98 us -> none  [softmax_rows(): raised = jnp.exp(masked - highest)]
    ppermute x6, waiting for transfers between devices: 21 us -> 25.8 us  [pair_then_z_scatter(): acc = acc + lax.ppermute(piece, 'head', perm).astype(jnp.float32)]
    reduce_sum x2 -> x8, other arithmetic: 0.25 us -> 3.5 us  [the longest x1 2.22 us: on_device(): jnp.sum(raised_cache, axis=-1, keepdims=True)]
    ppermute x6, starting transfers between devices: 8.82 us -> 5.99 us  [pair_then_z_scatter(): acc = acc + lax.ppermute(piece, 'head', perm).astype(jnp.float32)]
    unnamed x78 -> x66, local copies, waits for them, and re-layouts: 9.28 us -> 6.58 us
  transfers between devices with their start and end apart: 14 -> 14, of which waited for: 10 -> 13; matrix products, arithmetic and copies ran while one was open for 21% -> 14% of each run, Pallas kernels for 0% -> 0%
where the time goes in v1:
time: 184 us
  waiting for transfers between devices  54.8 us (30%)
  matrix products  41.1 us (22%)
  blocking collectives  28.6 us (16%)
  starting transfers between devices  23.6 us (13%)
  other arithmetic  21.9 us (12%)
  local copies, waits for them, and re-layouts  12.3 us (7%)
    ppermute x6, waiting for transfers between devices, pair_then_z_scatter(): acc = acc + lax.ppermute(piece, 'head', perm).astype(jnp.float32)  25.8 us
    all_to_all x1, blocking collectives, on_device(): lax.all_to_all(outgoing, 'req', split_axis=0, concat_axis=0, tiled=True)  15.3 us
    all_to_all x1, blocking collectives, on_device(): lax.all_to_all(arrived, 'head', split_axis=0, concat_axis=1, tiled=True)  13.2 us
    ppermute x3, waiting for transfers between devices, z_then_pair_gather(): parts.append(lax.ppermute(y, 'head', perm))  12.9 us
    all_to_all x1, waiting for transfers between devices, on_device(): lax.all_to_all(outgoing_q, 'req', split_axis=0, concat_axis=0, tiled=True)  9.53 us
    all_to_all x1, starting transfers between devices, on_device(): lax.all_to_all(outgoing_q, 'req', split_axis=0, concat_axis=0, tiled=True)  7.62 us
    dot_general x1, matrix products, on_device(): jnp.dot((raised_cache / total).astype(jnp.bfloat16), cache_value[0], pref...  7.48 us
    unnamed x66, local copies, waits for them, and re-layouts  6.58 us
  transfers between devices with their start and end apart: 14, of which 13 were waited for; matrix products, arithmetic and copies ran while one was open for 14% of the time, Pallas kernels for 0%

profile of v1, /device:TPU:1, one launch (start us, length us, event | category | flops | bytes accessed | tf_op | source)
XLA Modules:
  0.0 183.6 jit_solution(4124171484084239980)
XLA Ops:
  2.4 2.6 %convolution_convert_fusion.1 = bf16[768,1152]{1,0:T(8,128)(2,1)} fusion(s32[48]{0:T(128)S(1)} %dynamic-slice_add_fusion, bf16[48,384]{1,0:T(8,128)(2,1)} %param.21, bf16[48,384]{1,0:T(8,128)(2,1)} %param.20, bf16[48,384]{1,0:T(8,128)(2,1)} %param.19), kind=kOutput, calls=%fused_computation.12 | convolution fusion | flops 86188032 | bytes 1880256 | tf_op jit(solution)/shard_map/dot_general | solution.py:109
  5.0 7.6 %all-to-all-start = ((bf16[16,48,1152]{2,1,0:T(8,128)(2,1)}), bf16[16,48,1152]{2,1,0:T(8,128)(2,1)}, u32[]{:S(2)}, u32[]{:S(2)}) async-start(bf16[16,48,1152]{2,1,0:T(8,128)(2,1)} %bitcast.97), calls=%async_computation | async-start | bytes 3538944 | tf_op jit(solution)/shard_map/all_to_all | solution.py:110
  17.2 2.4 %fusion.109 = (f32[1024]{0:T(1024)S(1)}, f32[1024,256]{0,1:T(8,128)}) fusion(pred[1024,256]{0,1:T(8,128)(4,1)S(1)} %bitcast.109, bf16[1024,384]{1,0:T(8,128)(2,1)S(1)} %bitcast.104, bf16[256,384]{1,0:T(8,128)(2,1)} %param.23), kind=kOutput, calls=%fused_computation.219 | convolution fusion | flops 202112000 | bytes 2297856 | tf_op jit(solution)/shard_map/dot_general | solution.py:174
  19.7 4.3 %fusion = (f32[1024]{0:T(1024)S(1)}, f32[1024,2048]{1,0:T(8,128)S(1)}) fusion(pred[2048]{0:T(1024)(128)(4,1)S(1)} %iota_compare_fusion.12, bf16[1024,384]{1,0:T(8,128)(2,1)} %bitcast.105, bf16[2,2048,384]{2,1,0:T(8,128)(2,1)} %param.25), kind=kOutput, calls=%fused_computation.3 | convolution fusion | flops 1616903168 | bytes 10754048 | tf_op jit(solution)/shard_map/dot_general | solution.py:173
  24.2 2.2 %fusion.1 = f32[1024]{0:T(1024)S(1)} fusion(f32[1024,2048]{1,0:T(8,128)S(1)} %get-tuple-element.50, f32[1024]{0:T(1024)S(1)} %max.38, pred[2048]{0:T(1024)(128)(4,1)S(1)} %iota_compare_fusion.12), kind=kLoop, calls=%fused_computation.4 | loop fusion | flops 8387584 | bytes 8398848 | tf_op jit(solution)/shard_map/reduce_sum | solution.py:185
  29.1 9.5 %all-to-all-done = bf16[16,48,1152]{2,1,0:T(8,128)(2,1)} async-done(((bf16[16,48,1152]{2,1,0:T(8,128)(2,1)}), bf16[16,48,1152]{2,1,0:T(8,128)(2,1)}, u32[]{:S(2)}, u32[]{:S(2)}) %all-to-all-start) | async-done | bytes 1769504 | tf_op jit(solution)/shard_map/all_to_all | solution.py:110
  38.7 2.0 %convolution_convert_fusion.2 = bf16[96,1152]{1,0:T(8,128)(2,1)S(1)} fusion(bf16[768,1152]{1,0:T(8,128)(2,1)} %bitcast.3, s32[96]{0:T(128)S(1)} %eq.237, pred[96]{0:T(512)(128)(4,1)S(1)} %and.111), kind=kOutput, calls=%fused_computation.17 | convolution fusion | flops 170127360 | bytes 1991136 | tf_op jit(solution)/shard_map/dot_general | solution.py:125
  41.6 2.4 %fusion.111 = (f32[192]{0:T(256)S(1)}, f32[192,2048]{1,0:T(8,128)S(1)}) fusion(bf16[192,384]{1,0:T(8,128)(2,1)S(1)} %bitcast.111, bf16[2,2048,384]{2,1,0:T(8,128)(2,1)} %param.25, pred[2048]{0:T(1024)(128)(4,1)S(1)} %iota_compare_fusion.14), kind=kOutput, calls=%fused_computation.221 | convolution fusion | flops 303169344 | bytes 3296000 | tf_op jit(solution)/shard_map/dot_general | solution.py:138
  45.4 2.4 %fusion.110 = (f32[192]{0:T(256)S(1)}, f32[192,2048]{1,0:T(8,128)S(1)}) fusion(bf16[192,384]{1,0:T(8,128)(2,1)S(1)} %bitcast.110, bf16[2,2048,384]{2,1,0:T(8,128)(2,1)} %param.25, pred[2048]{0:T(1024)(128)(4,1)S(1)} %iota_compare_fusion.13), kind=kOutput, calls=%fused_computation.220 | convolution fusion | flops 303169344 | bytes 3296000 | tf_op jit(solution)/shard_map/dot_general | solution.py:138
  50.3 4.5 %all-to-all-start.1 = ((bf16[16,48,384]{2,1,0:T(8,128)(2,1)}), bf16[16,48,384]{2,1,0:T(8,128)(2,1)}, u32[]{:S(2)}, u32[]{:S(2)}) async-start(bf16[16,48,384]{2,1,0:T(8,128)(2,1)} %bitcast.98), calls=%async_computation.1 | async-start | bytes 1179648 | tf_op jit(solution)/shard_map/all_to_all | solution.py:166
  54.8 7.5 %fusion.2 = f32[1024,384]{1,0:T(8,128)} fusion(f32[1024,2048]{1,0:T(8,128)} %copy-done.1, f32[1024]{0:T(1024)S(1)} %add.225, f32[1024]{0:T(1024)S(1)} %max.38, pred[2048]{0:T(1024)(128)(4,1)S(1)} %iota_compare_fusion.12, bf16[2,2048,384]{2,1,0:T(8,128)(2,1)} %param.26), kind=kOutput, calls=%fused_computation.7 | convolution fusion | flops 1621098496 | bytes 11544576 | tf_op jit(solution)/shard_map/dot_general | solution.py:186
  62.3 2.2 %convolution_add_fusion = f32[1024,384]{1,0:T(8,128)S(1)} fusion(f32[1024,384]{1,0:T(8,128)} %fusion.2, bf16[256,384]{1,0:T(8,128)(2,1)S(1)} %copy-done.30, f32[1024,256]{0,1:T(8,128)} %get-tuple-element.52, f32[1024]{0:T(1024)S(1)} %add.225, f32[1024]{0:T(1024)S(1)} %max.38), kind=kOutput, calls=%fused_computation.36 | convolution fusion | flops 202506240 | bytes 4399104 | tf_op jit(solution)/shard_map/dot_general | solution.py:188
  66.7 2.8 %fusion.58 = f32[304,3072]{1,0:T(8,128)S(1)} fusion(bf16[384,3072]{1,0:T(8,128)(2,1)} %param.31, bf16[256,384]{1,0:T(8,128)(2,1)S(1)} %select_reduce_fusion, bf16[48,384]{1,0:T(8,128)(2,1)S(1)} %convolution_convert_fusion.5), kind=kOutput, calls=%fused_computation.100 | convolution fusion | flops 717692928 | bytes 6328320 | tf_op jit(solution)/shard_map/dot_general | solution.py:193
  72.1 2.7 %collective-permute-start = (bf16[304,1536]{1,0:T(8,128)(2,1)}, bf16[304,1536]{1,0:T(8,128)(2,1)}, u32[]{:S(2)}, u32[]{:S(2)}) collective-permute-start(bf16[304,1536]{1,0:T(8,128)(2,1)} %broadcast_select_fusion.1), channel_id=1, source_target_pairs={{0,1},{1,0},{2,3},{3,2},{4,5},{5,4},{6,7},{7,6},{8,9},{9,8},{10,11... | collective-permute-start | bytes 2801672 | tf_op jit(solution)/shard_map/ppermute | solution.py:31
  74.7 2.5 %collective-permute-done = bf16[304,1536]{1,0:T(8,128)(2,1)} collective-permute-done((bf16[304,1536]{1,0:T(8,128)(2,1)}, bf16[304,1536]{1,0:T(8,128)(2,1)}, u32[]{:S(2)}, u32[]{:S(2)}) %collective-permute-start) | collective-permute-done | bytes 933920 | tf_op jit(solution)/shard_map/ppermute | solution.py:31
  77.2 2.0 %add_convert_fusion.1 = bf16[304,1536]{1,0:T(8,128)(2,1)S(1)} fusion(bf16[304,1536]{1,0:T(8,128)(2,1)} %collective-permute-done, pred[]{:T(512)S(6)} %eq.217, bf16[304,384]{1,0:T(8,128)(2,1)} %copy-done.4, bf16[304,384]{1,0:T(8,128)(2,1)} %copy-done.5, bf16[304,384]{1,0:T(8,128)(2,1)} %copy-done.6, bf16[304,384]{1,0:T(8,128)(2,1)} %copy-done.7, ...), kind=kLoop, calls=%fused_computation.19 | loop fusion | flops 9805824 | bytes 3735553 | tf_op jit(solution)/shard_map/convert_element_type | solution.py:32
  81.0 3.8 %collective-permute-start.3 = (bf16[304,384]{1,0:T(8,128)(2,1)}, bf16[304,384]{1,0:T(8,128)(2,1)S(1)}, u32[]{:S(2)}, u32[]{:S(2)}) collective-permute-start(bf16[304,384]{1,0:T(8,128)(2,1)} %get-tuple-element.33), channel_id=1, source_target_pairs={{0,6},{1,7},{2,0},{3,1},{4,2},{5,3},{6,4},{7,5},{8,14},{9,15},{10,... | collective-permute-start | bytes 700424 | tf_op jit(solution)/shard_map/ppermute | solution.py:37
  85.5 9.3 %collective-permute-done.3 = bf16[304,384]{1,0:T(8,128)(2,1)S(1)} collective-permute-done((bf16[304,384]{1,0:T(8,128)(2,1)}, bf16[304,384]{1,0:T(8,128)(2,1)S(1)}, u32[]{:S(2)}, u32[]{:S(2)}) %collective-permute-start.3) | collective-permute-done | bytes 233504 | tf_op jit(solution)/shard_map/ppermute | solution.py:37
  95.5 3.2 %collective-permute-done.1 = bf16[304,384]{1,0:T(8,128)(2,1)} collective-permute-done((bf16[304,384]{1,0:T(8,128)(2,1)}, bf16[304,384]{1,0:T(8,128)(2,1)}, u32[]{:S(2)}, u32[]{:S(2)}) %collective-permute-start.1) | collective-permute-done | bytes 233504 | tf_op jit(solution)/shard_map/ppermute | solution.py:37
  98.6 1.4 add_convert_fusion.3
  101.6 5.1 %collective-permute-done.6 = bf16[304,384]{1,0:T(8,128)(2,1)} collective-permute-done((bf16[304,384]{1,0:T(8,128)(2,1)S(1)}, bf16[304,384]{1,0:T(8,128)(2,1)}, u32[]{:S(2)}, u32[]{:S(2)}) %collective-permute-start.6) | collective-permute-done | bytes 233504 | tf_op jit(solution)/shard_map/ppermute | solution.py:51
  107.6 6.9 %collective-permute-done.4 = bf16[304,384]{1,0:T(8,128)(2,1)} collective-permute-done((bf16[304,384]{1,0:T(8,128)(2,1)S(1)}, bf16[304,384]{1,0:T(8,128)(2,1)}, u32[]{:S(2)}, u32[]{:S(2)}) %collective-permute-start.4) | collective-permute-done | bytes 233504 | tf_op jit(solution)/shard_map/ppermute | solution.py:51
  116.8 2.1 %collective-permute-done.7 = bf16[304,1536]{1,0:T(8,128)(2,1)S(1)} collective-permute-done((bf16[304,1536]{1,0:T(8,128)(2,1)S(1)}, bf16[304,1536]{1,0:T(8,128)(2,1)S(1)}, u32[]{:S(2)}, u32[]{:S(2)}) %collective-permute-start.7) | collective-permute-done | bytes 933920 | tf_op jit(solution)/shard_map/ppermute | solution.py:56
  121.9 2.0 %fusion.46 = f32[304,512]{1,0:T(8,128)} fusion(bf16[3072,512]{1,0:T(8,128)(2,1)S(1)} %copy-done.29, bf16[304,3072]{1,0:T(8,128)(2,1)S(1)} %select_dynamic-update-slice_fusion, f32[3072]{0:T(1024)S(1)} %copy-done.31, f32[304]{0:T(512)S(1)} %add_rsqrt_fusion), kind=kOutput, calls=%fused_computation.76 | convolution fusion | flops 960036864 | bytes 5649600 | tf_op jit(solution)/shard_map/dot_general | solution.py:206
  123.9 6.1 %convolution_convert_fusion = bf16[304,3072]{1,0:T(8,128)(2,1)} fusion(bf16[512,3072]{1,0:T(8,128)(2,1)S(1)} %copy-done, bf16[3072,512]{1,0:T(8,128)(2,1)} %param.34, f32[304,512]{1,0:T(8,128)} %fusion.46, bf16[304,3072]{1,0:T(8,128)(2,1)} %copy-done.3, f32[3072]{0:T(1024)S(1)} %copy-done.31, f32[304]{0:T(512)S(1)} %add_rsqrt_fusion), kind=kOutput, calls=%fused_computation.8 | convolution fusion | flops 1918205952 | bytes 10663104 | tf_op jit(solution)/shard_map/dot_general | solution.py:209
  130.0 1.8 fusion.104
  136.6 2.0 %add_convert_fusion = bf16[304,1536]{1,0:T(8,128)(2,1)S(1)} fusion(bf16[304,1536]{1,0:T(8,128)(2,1)} %collective-permute-done.8, pred[]{:T(512)S(6)} %eq.217, bf16[304,384]{1,0:T(8,128)(2,1)} %copy-done.11, bf16[304,384]{1,0:T(8,128)(2,1)} %copy-done.12, bf16[304,384]{1,0:T(8,128)(2,1)} %copy-done.13, bf16[304,384]{1,0:T(8,128)(2,1)} %copy-done.14, ...), kind=kLoop, calls=%fused_computation.18 | loop fusion | flops 9805824 | bytes 3735553 | tf_op jit(solution)/shard_map/convert_element_type | solution.py:32
  140.2 5.4 %collective-permute-done.11 = bf16[304,384]{1,0:T(8,128)(2,1)S(1)} collective-permute-done((bf16[304,384]{1,0:T(8,128)(2,1)S(1)}, bf16[304,384]{1,0:T(8,128)(2,1)S(1)}, u32[]{:S(2)}, u32[]{:S(2)}) %collective-permute-start.11) | collective-permute-done | bytes 233504 | tf_op jit(solution)/shard_map/ppermute | solution.py:37
  145.6 2.0 %collective-permute-done.10 = bf16[304,384]{1,0:T(8,128)(2,1)S(1)} collective-permute-done((bf16[304,384]{1,0:T(8,128)(2,1)S(1)}, bf16[304,384]{1,0:T(8,128)(2,1)S(1)}, u32[]{:S(2)}, u32[]{:S(2)}) %collective-permute-start.10) | collective-permute-done | bytes 233504 | tf_op jit(solution)/shard_map/ppermute | solution.py:37
  147.6 6.0 %collective-permute-done.9 = bf16[304,384]{1,0:T(8,128)(2,1)S(1)} collective-permute-done((bf16[304,384]{1,0:T(8,128)(2,1)S(1)}, bf16[304,384]{1,0:T(8,128)(2,1)S(1)}, u32[]{:S(2)}, u32[]{:S(2)}) %collective-permute-start.9) | collective-permute-done | bytes 233504 | tf_op jit(solution)/shard_map/ppermute | solution.py:37
  154.2 15.3 %all_to_all.52 = bf16[16,40,384]{2,1,0:T(8,128)(2,1)S(1)} all-to-all(bf16[16,40,384]{2,1,0:T(8,128)(2,1)S(1)} %bitcast.106), channel_id=1, replica_groups=mesh['req'=16,'head'=8] {'req'}, dimensions={0} | all-to-all | bytes 983040 | tf_op jit(solution)/shard_map/all_to_all | solution.py:226
  169.5 13.2 %all_to_all.53 = bf16[8,80,384]{2,1,0:T(8,128)(2,1)S(1)} all-to-all(bf16[8,80,384]{2,1,0:T(8,128)(2,1)S(1)} %bitcast.99), channel_id=1, replica_groups=mesh['req'=16,'head'=8] {'head'}, dimensions={0} | all-to-all | bytes 983040 | tf_op jit(solution)/shard_map/all_to_all | solution.py:227
  (165 shorter events, 37.3 us)
Async XLA Ops:
  0.0 123.9 %copy-start = (bf16[512,3072]{1,0:T(8,128)(2,1)S(1)}, bf16[512,3072]{1,0:T(8,128)(2,1)}, u32[]{:S(2)}) copy-start(bf16[512,3072]{1,0:T(8,128)(2,1)} %param.35) | copy-start | bytes 9437188
  5.0 33.7 %all-to-all-start = ((bf16[16,48,1152]{2,1,0:T(8,128)(2,1)}), bf16[16,48,1152]{2,1,0:T(8,128)(2,1)}, u32[]{:S(2)}, u32[]{:S(2)}) async-start(bf16[16,48,1152]{2,1,0:T(8,128)(2,1)} %bitcast.97), calls=%async_computation | async-start | bytes 3538944 | tf_op jit(solution)/shard_map/all_to_all | solution.py:110
  19.7 4.3 %copy-start.18 = (f32[1024,256]{0,1:T(8,128)S(1)}, f32[1024,256]{0,1:T(8,128)}, u32[]{:S(2)}) copy-start(f32[1024,256]{0,1:T(8,128)} %get-tuple-element.52) | copy-start | bytes 3145732
  24.0 3.2 %copy-start.1 = (f32[1024,2048]{1,0:T(8,128)}, f32[1024,2048]{1,0:T(8,128)S(1)}, u32[]{:S(2)}) copy-start(f32[1024,2048]{1,0:T(8,128)S(1)} %get-tuple-element.50) | copy-start | bytes 25165828
  24.2 3.0 %copy-start.25 = (s32[2]{0:T(128)S(1)}, s32[2]{0:T(128)}, u32[]{:S(2)}) copy-start(s32[2]{0:T(128)} %param.28) | copy-start | bytes 28
  41.6 2.9 %copy-start.27 = (bf16[2,2048,384]{2,1,0:T(8,128)(2,1)S(1)}, bf16[2,2048,384]{2,1,0:T(8,128)(2,1)}, u32[]{:S(2)}) copy-start(bf16[2,2048,384]{2,1,0:T(8,128)(2,1)} %param.26) | copy-start | bytes 9437188
  45.4 2.9 %copy-start.28 = (bf16[2,2048,384]{2,1,0:T(8,128)(2,1)S(1)}, bf16[2,2048,384]{2,1,0:T(8,128)(2,1)}, u32[]{:S(2)}) copy-start(bf16[2,2048,384]{2,1,0:T(8,128)(2,1)} %param.26) | copy-start | bytes 9437188
  50.3 15.1 %all-to-all-start.1 = ((bf16[16,48,384]{2,1,0:T(8,128)(2,1)}), bf16[16,48,384]{2,1,0:T(8,128)(2,1)}, u32[]{:S(2)}, u32[]{:S(2)}) async-start(bf16[16,48,384]{2,1,0:T(8,128)(2,1)} %bitcast.98), calls=%async_computation.1 | async-start | bytes 1179648 | tf_op jit(solution)/shard_map/all_to_all | solution.py:166
  54.8 7.5 %copy-start.30 = (bf16[256,384]{1,0:T(8,128)(2,1)S(1)}, bf16[256,384]{1,0:T(8,128)(2,1)}, u32[]{:S(2)}) copy-start(bf16[256,384]{1,0:T(8,128)(2,1)} %param.24) | copy-start | bytes 589828
  66.7 2.9 %copy-start.22 = (bf16[304,384]{1,0:T(8,128)(2,1)S(1)}, bf16[304,384]{1,0:T(8,128)(2,1)}, u32[]{:S(2)}) copy-start(bf16[304,384]{1,0:T(8,128)(2,1)} %param.18) | copy-start | bytes 700420
  70.2 1.9 %copy-start.5 = (bf16[304,384]{1,0:T(8,128)(2,1)}, bf16[304,384]{1,0:T(8,128)(2,1)S(1)}, u32[]{:S(2)}) copy-start(bf16[304,384]{1,0:T(8,128)(2,1)S(1)} %get-tuple-element.19) | copy-start | bytes 700420
  70.2 1.9 %copy-start.6 = (bf16[304,384]{1,0:T(8,128)(2,1)}, bf16[304,384]{1,0:T(8,128)(2,1)S(1)}, u32[]{:S(2)}) copy-start(bf16[304,384]{1,0:T(8,128)(2,1)S(1)} %get-tuple-element.20) | copy-start | bytes 700420
  72.1 5.2 %collective-permute-start = (bf16[304,1536]{1,0:T(8,128)(2,1)}, bf16[304,1536]{1,0:T(8,128)(2,1)}, u32[]{:S(2)}, u32[]{:S(2)}) collective-permute-start(bf16[304,1536]{1,0:T(8,128)(2,1)} %broadcast_select_fusion.1), channel_id=1, source_target_pairs={{0,1},{1,0},{2,3},{3,2},{4,5},{5,4},{6,7},{7,6},{8,9},{9,8},{10,11... | collective-permute-start | bytes 2801672 | tf_op jit(solution)/shard_map/ppermute | solution.py:31
  81.0 13.8 %collective-permute-start.3 = (bf16[304,384]{1,0:T(8,128)(2,1)}, bf16[304,384]{1,0:T(8,128)(2,1)S(1)}, u32[]{:S(2)}, u32[]{:S(2)}) collective-permute-start(bf16[304,384]{1,0:T(8,128)(2,1)} %get-tuple-element.33), channel_id=1, source_target_pairs={{0,6},{1,7},{2,0},{3,1},{4,2},{5,3},{6,4},{7,5},{8,14},{9,15},{10,... | collective-permute-start | bytes 700424 | tf_op jit(solution)/shard_map/ppermute | solution.py:37
  84.8 10.0 %collective-permute-start.2 = (bf16[304,384]{1,0:T(8,128)(2,1)}, bf16[304,384]{1,0:T(8,128)(2,1)}, u32[]{:S(2)}, u32[]{:S(2)}) collective-permute-start(bf16[304,384]{1,0:T(8,128)(2,1)} %get-tuple-element.34), channel_id=1, source_target_pairs={{0,4},{1,5},{2,6},{3,7},{4,0},{5,1},{6,2},{7,3},{8,12},{9,13},{10,... | collective-permute-start | bytes 700424 | tf_op jit(solution)/shard_map/ppermute | solution.py:37
  84.8 13.9 %collective-permute-start.1 = (bf16[304,384]{1,0:T(8,128)(2,1)}, bf16[304,384]{1,0:T(8,128)(2,1)}, u32[]{:S(2)}, u32[]{:S(2)}) collective-permute-start(bf16[304,384]{1,0:T(8,128)(2,1)} %get-tuple-element.32), channel_id=1, source_target_pairs={{0,2},{1,3},{2,4},{3,5},{4,6},{5,7},{6,0},{7,1},{8,10},{9,11},{10,... | collective-permute-start | bytes 700424 | tf_op jit(solution)/shard_map/ppermute | solution.py:37
  100.0 15.9 %copy-start.19 = (bf16[304,384]{1,0:T(8,128)(2,1)}, bf16[304,384]{1,0:T(8,128)(2,1)S(1)}, u32[]{:S(2)}) copy-start(bf16[304,384]{1,0:T(8,128)(2,1)S(1)} %add_convert_fusion.3) | copy-start | bytes 700420
  100.0 6.6 %collective-permute-start.6 = (bf16[304,384]{1,0:T(8,128)(2,1)S(1)}, bf16[304,384]{1,0:T(8,128)(2,1)}, u32[]{:S(2)}, u32[]{:S(2)}) collective-permute-start(bf16[304,384]{1,0:T(8,128)(2,1)S(1)} %add_convert_fusion.3), channel_id=1, source_target_pairs={{0,6},{1,7},{2,0},{3,1},{4,2},{5,3},{6,4},{7,5},{8,14},{9,15},{10,... | collective-permute-start | bytes 700424 | tf_op jit(solution)/shard_map/ppermute | solution.py:51
  100.3 7.4 %collective-permute-start.5 = (bf16[304,384]{1,0:T(8,128)(2,1)S(1)}, bf16[304,384]{1,0:T(8,128)(2,1)}, u32[]{:S(2)}, u32[]{:S(2)}) collective-permute-start(bf16[304,384]{1,0:T(8,128)(2,1)S(1)} %add_convert_fusion.3), channel_id=1, source_target_pairs={{0,4},{1,5},{2,6},{3,7},{4,0},{5,1},{6,2},{7,3},{8,12},{9,13},{10,... | collective-permute-start | bytes 700424 | tf_op jit(solution)/shard_map/ppermute | solution.py:51
  100.8 13.7 %collective-permute-start.4 = (bf16[304,384]{1,0:T(8,128)(2,1)S(1)}, bf16[304,384]{1,0:T(8,128)(2,1)}, u32[]{:S(2)}, u32[]{:S(2)}) collective-permute-start(bf16[304,384]{1,0:T(8,128)(2,1)S(1)} %add_convert_fusion.3), channel_id=1, source_target_pairs={{0,2},{1,3},{2,4},{3,5},{4,6},{5,7},{6,0},{7,1},{8,10},{9,11},{10,... | collective-permute-start | bytes 700424 | tf_op jit(solution)/shard_map/ppermute | solution.py:51
  116.0 2.9 %collective-permute-start.7 = (bf16[304,1536]{1,0:T(8,128)(2,1)S(1)}, bf16[304,1536]{1,0:T(8,128)(2,1)S(1)}, u32[]{:S(2)}, u32[]{:S(2)}) collective-permute-start(bf16[304,1536]{1,0:T(8,128)(2,1)S(1)} %pad_maximum_fusion.3), channel_id=1, source_target_pairs={{0,1},{1,0},{2,3},{3,2},{4,5},{5,4},{6,7},{7,6},{8,9},{9,8},{10,11... | collective-permute-start | bytes 2801672 | tf_op jit(solution)/shard_map/ppermute | solution.py:56
  119.4 2.6 %copy-start.29 = (bf16[3072,512]{1,0:T(8,128)(2,1)S(1)}, bf16[3072,512]{1,0:T(8,128)(2,1)}, u32[]{:S(2)}) copy-start(bf16[3072,512]{1,0:T(8,128)(2,1)} %param.33) | copy-start | bytes 9437188
  119.4 2.6 %copy-start.31 = (f32[3072]{0:T(1024)S(1)}, f32[3072]{0:T(1024)}, u32[]{:S(2)}) copy-start(f32[3072]{0:T(1024)} %param.32) | copy-start | bytes 36868
  131.8 1.9 %copy-start.12 = (bf16[304,384]{1,0:T(8,128)(2,1)}, bf16[304,384]{1,0:T(8,128)(2,1)S(1)}, u32[]{:S(2)}) copy-start(bf16[304,384]{1,0:T(8,128)(2,1)S(1)} %get-tuple-element.11) | copy-start | bytes 700420
  131.8 1.9 %copy-start.13 = (bf16[304,384]{1,0:T(8,128)(2,1)}, bf16[304,384]{1,0:T(8,128)(2,1)S(1)}, u32[]{:S(2)}) copy-start(bf16[304,384]{1,0:T(8,128)(2,1)S(1)} %get-tuple-element.12) | copy-start | bytes 700420
  131.8 1.9 %copy-start.14 = (bf16[304,384]{1,0:T(8,128)(2,1)}, bf16[304,384]{1,0:T(8,128)(2,1)S(1)}, u32[]{:S(2)}) copy-start(bf16[304,384]{1,0:T(8,128)(2,1)S(1)} %get-tuple-element.13) | copy-start | bytes 700420
  131.8 2.3 %copy-start.26 = (s32[304,1]{0,1:T(1,128)S(1)}, s32[304,1]{0,1:T(1,128)}, u32[]{:S(2)}) copy-start(s32[304,1]{0,1:T(1,128)} %param.30) | copy-start | bytes 3652
  133.7 2.9 %collective-permute-start.8 = (bf16[304,1536]{1,0:T(8,128)(2,1)}, bf16[304,1536]{1,0:T(8,128)(2,1)}, u32[]{:S(2)}, u32[]{:S(2)}) collective-permute-start(bf16[304,1536]{1,0:T(8,128)(2,1)} %broadcast_select_fusion), channel_id=1, source_target_pairs={{0,1},{1,0},{2,3},{3,2},{4,5},{5,4},{6,7},{7,6},{8,9},{9,8},{10,11... | collective-permute-start | bytes 2801672 | tf_op jit(solution)/shard_map/ppermute | solution.py:31
  135.4 18.2 %copy-start.20 = (bf16[304,384]{1,0:T(8,128)(2,1)S(1)}, bf16[304,384]{1,0:T(8,128)(2,1)}, u32[]{:S(2)}) copy-start(bf16[304,384]{1,0:T(8,128)(2,1)} %copy-done.19) | copy-start | bytes 700420
  138.7 6.9 %collective-permute-start.11 = (bf16[304,384]{1,0:T(8,128)(2,1)S(1)}, bf16[304,384]{1,0:T(8,128)(2,1)S(1)}, u32[]{:S(2)}, u32[]{:S(2)}) collective-permute-start(bf16[304,384]{1,0:T(8,128)(2,1)S(1)} %get-tuple-element.26), channel_id=1, source_target_pairs={{0,6},{1,7},{2,0},{3,1},{4,2},{5,3},{6,4},{7,5},{8,14},{9,15},{10,... | collective-permute-start | bytes 700424 | tf_op jit(solution)/shard_map/ppermute | solution.py:37
  139.5 8.1 %collective-permute-start.10 = (bf16[304,384]{1,0:T(8,128)(2,1)S(1)}, bf16[304,384]{1,0:T(8,128)(2,1)S(1)}, u32[]{:S(2)}, u32[]{:S(2)}) collective-permute-start(bf16[304,384]{1,0:T(8,128)(2,1)S(1)} %get-tuple-element.27), channel_id=1, source_target_pairs={{0,4},{1,5},{2,6},{3,7},{4,0},{5,1},{6,2},{7,3},{8,12},{9,13},{10,... | collective-permute-start | bytes 700424 | tf_op jit(solution)/shard_map/ppermute | solution.py:37
  139.6 14.0 %collective-permute-start.9 = (bf16[304,384]{1,0:T(8,128)(2,1)S(1)}, bf16[304,384]{1,0:T(8,128)(2,1)S(1)}, u32[]{:S(2)}, u32[]{:S(2)}) collective-permute-start(bf16[304,384]{1,0:T(8,128)(2,1)S(1)} %get-tuple-element.25), channel_id=1, source_target_pairs={{0,2},{1,3},{2,4},{3,5},{4,6},{5,7},{6,0},{7,1},{8,10},{9,11},{10,... | collective-permute-start | bytes 700424 | tf_op jit(solution)/shard_map/ppermute | solution.py:37
  (14 other events, 19.0 us)

commit v2 on v1

--- a/solution.py
+++ b/solution.py
@@ -189,29 +189,32 @@
     pre_out = jnp.sum(
         jnp.where(head_mask[:, None, :], pre_mixed.reshape(heads_here, stretch_len, width_here), 0.0), axis=0
     ).astype(jnp.bfloat16)
-    attn_rows = jnp.concatenate([dec_out, pre_out], axis=0)
-    projected = jnp.dot(attn_rows, out_weight, preferred_element_type=jnp.float32)
     head_me = lax.axis_index("head")
     col_start = head_me * width_here
-    own_cols = lax.dynamic_slice_in_dim(projected, col_start, width_here, 1) + hidden_in.astype(
-        jnp.float32
-    )
-    contribution = lax.dynamic_update_slice_in_dim(projected, own_cols, col_start, 1)
-    own_residual = pair_then_z_scatter(contribution.astype(jnp.bfloat16))
-    residual = z_then_pair_gather(own_residual.astype(jnp.bfloat16))
-
-    residual_wide = residual.astype(jnp.float32)
-    squares = jnp.mean(jnp.square(residual_wide), axis=-1, keepdims=True)
-    normed = (residual_wide * lax.rsqrt(squares + eps_norm) * norm_gain).astype(jnp.bfloat16)
-    gate_act = jnp.dot(normed, gate_weight, preferred_element_type=jnp.float32)
-    up_act = jnp.dot(normed, up_weight, preferred_element_type=jnp.float32)
-    hidden = (jax.nn.silu(gate_act) * up_act).astype(jnp.bfloat16)
-    down_part = jnp.dot(hidden, down_weight, preferred_element_type=jnp.float32).astype(jnp.bfloat16)
-    down_cols = pair_then_z_scatter(down_part)
-    own_wide = own_residual.astype(jnp.bfloat16).astype(jnp.float32)
-    out_cols = (own_wide + down_cols).astype(jnp.bfloat16)
-
-    row_count = residual.shape[0]
+
+    def feed_forward(attn_chunk, hidden_chunk):
+        projected = jnp.dot(attn_chunk, out_weight, preferred_element_type=jnp.float32)
+        own_cols = lax.dynamic_slice_in_dim(projected, col_start, width_here, 1) + hidden_chunk.astype(
+            jnp.float32
+        )
+        contribution = lax.dynamic_update_slice_in_dim(projected, own_cols, col_start, 1)
+        own_residual = pair_then_z_scatter(contribution.astype(jnp.bfloat16)).astype(jnp.bfloat16)
+        residual = z_then_pair_gather(own_residual)
+        residual_wide = residual.astype(jnp.float32)
+        squares = jnp.mean(jnp.square(residual_wide), axis=-1, keepdims=True)
+        normed = (residual_wide * lax.rsqrt(squares + eps_norm) * norm_gain).astype(jnp.bfloat16)
+        gate_act = jnp.dot(normed, gate_weight, preferred_element_type=jnp.float32)
+        up_act = jnp.dot(normed, up_weight, preferred_element_type=jnp.float32)
+        hidden = (jax.nn.silu(gate_act) * up_act).astype(jnp.bfloat16)
+        down_part = jnp.dot(hidden, down_weight, preferred_element_type=jnp.float32).astype(jnp.bfloat16)
+        down_cols = pair_then_z_scatter(down_part)
+        return (own_residual.astype(jnp.float32) + down_cols).astype(jnp.bfloat16)
+
+    pre_cols = feed_forward(pre_out, hidden_in[per_home:])
+    dec_cols = feed_forward(dec_out, hidden_in[:per_home])
+    out_cols = jnp.concatenate([dec_cols, pre_cols], axis=0)
+
+    row_count = hidden_in.shape[0]
     slot_rows = 8 * ((2 * row_count + 8 * req_count - 1) // (8 * req_count))
     owners = row_owner[:, 0]
     onehot_owner = (owners[:, None] == jnp.arange(req_count, dtype=jnp.int32)[None, :]).astype(

time: 184 us -> 217 us (1.18)
  other arithmetic: 21.9 us -> 52.2 us
  waiting for transfers between devices: 54.8 us -> 35.4 us
  starting transfers between devices: 23.6 us -> 37.8 us
  local copies, waits for them, and re-layouts: 12.3 us -> 18.9 us
    all_to_all x1, waiting for transfers between devices: 9.53 us -> 0.01 us  [on_device(): lax.all_to_all(outgoing_q, 'req', split_axis=0, concat_axis=0, tiled=True)]
    dot_general x4 -> x6, matrix products: 12.3 us -> 21.7 us  [the longest x2 9.5 us: feed_forward(): jnp.dot(hidden, down_weight, preferred_element_type=jnp.float32)]
    unnamed x10 -> x17, other arithmetic: 1.54 us -> 9.92 us
    ppermute x6 -> x12, starting transfers between devices: 5.99 us -> 12.1 us  [pair_then_z_scatter(): acc = acc + lax.ppermute(piece, 'head', perm).astype(jnp.float32)]
    dot_general x1, matrix products: 7.48 us -> 2.44 us  [on_device(): jnp.dot((raised_cache / total).astype(jnp.bfloat16), cache_value[0], pref...]
    another operation x6, other arithmetic: 1.74 us -> 6.51 us
    ppermute x3 -> x6, starting transfers between devices: 1.54 us -> 6.03 us  [z_then_pair_gather(): parts.append(lax.ppermute(y, 'head', perm))]
    ppermute x6 -> x12, waiting for transfers between devices: 25.8 us -> 21.5 us  [pair_then_z_scatter(): acc = acc + lax.ppermute(piece, 'head', perm).astype(jnp.float32)]
  transfers between devices with their start and end apart: 14 -> 26, of which waited for: 13 -> 12; matrix products, arithmetic and copies ran while one was open for 14% -> 36% of each run, Pallas kernels for 0% -> 0%
where the time goes in v2:
time: 217 us; the launch traced here: 215 us
  other arithmetic  52.2 us (24%)
  matrix products  41.5 us (19%)
  starting transfers between devices  37.8 us (17%)
  waiting for transfers between devices  35.4 us (16%)
  blocking collectives  27.5 us (13%)
  local copies, waits for them, and re-layouts  18.9 us (9%)
    ppermute x12, waiting for transfers between devices, pair_then_z_scatter(): acc = acc + lax.ppermute(piece, 'head', perm).astype(jnp.float32)  21.5 us
    all_to_all x1, blocking collectives, on_device(): lax.all_to_all(outgoing, 'req', split_axis=0, concat_axis=0, tiled=True)  14 us
    all_to_all x1, blocking collectives, on_device(): lax.all_to_all(arrived, 'head', split_axis=0, concat_axis=1, tiled=True)  13.5 us
    ppermute x12, starting transfers between devices, pair_then_z_scatter(): acc = acc + lax.ppermute(piece, 'head', perm).astype(jnp.float32)  12.1 us
    ppermute x6, waiting for transfers between devices, z_then_pair_gather(): parts.append(lax.ppermute(y, 'head', perm))  11.6 us
    unnamed x17, other arithmetic  9.92 us
    dot_general x2, matrix products, feed_forward(): jnp.dot(hidden, down_weight, preferred_element_type=jnp.float32)  9.5 us
    dot_general x2, matrix products, feed_forward(): jnp.dot(attn_chunk, out_weight, preferred_element_type=jnp.float32)  7.75 us
  transfers between devices with their start and end apart: 26, of which 12 were waited for; matrix products, arithmetic and copies ran while one was open for 36% of the time, Pallas kernels for 0%

profile of v2, /device:TPU:1, one launch (start us, length us, event | category | flops | bytes accessed | tf_op | source)
XLA Modules:
  0.0 215.2 jit_solution(14622587487360420466)
XLA Ops:
  2.3 4.0 %fusion = (f32[1024]{0:T(1024)S(1)}, f32[1024,2048]{1,0:T(8,128)S(1)}) fusion(pred[2048]{0:T(1024)(128)(4,1)S(1)} %iota_compare_fusion.13, bf16[1024,384]{1,0:T(8,128)(2,1)S(1)} %bitcast.121, bf16[2,2048,384]{2,1,0:T(8,128)(2,1)} %param.25), kind=kOutput, calls=%fused_computation.3 | convolution fusion | flops 1616903168 | bytes 10754048 | tf_op jit(solution)/shard_map/dot_general | solution.py:173
  6.8 2.2 %fusion.1 = f32[1024]{0:T(1024)S(1)} fusion(f32[1024,2048]{1,0:T(8,128)S(1)} %get-tuple-element.80, f32[1024]{0:T(1024)S(1)} %max.38, pred[2048]{0:T(1024)(128)(4,1)S(1)} %iota_compare_fusion.13), kind=kLoop, calls=%fused_computation.4 | loop fusion | flops 8387584 | bytes 8398848 | tf_op jit(solution)/shard_map/reduce_sum | solution.py:185
  9.2 2.4 %fusion.2 = f32[1024,384]{1,0:T(8,128)S(1)} fusion(f32[1024,2048]{1,0:T(8,128)S(1)} %get-tuple-element.80, f32[1024]{0:T(1024)S(1)} %add.336, f32[1024]{0:T(1024)S(1)} %max.38, pred[2048]{0:T(1024)(128)(4,1)S(1)} %iota_compare_fusion.13, bf16[2,2048,384]{2,1,0:T(8,128)(2,1)S(1)} %copy-done.52), kind=kOutput, calls=%fused_computation.5 | convolution fusion | flops 1621098496 | bytes 11544576 | tf_op jit(solution)/shard_map/dot_general | solution.py:186
  12.3 4.3 %fusion.130 = f32[256,3072]{1,0:T(8,128)} fusion(bf16[256,384]{1,0:T(8,128)(2,1)S(1)} %select_reduce_fusion, bf16[384,3072]{1,0:T(8,128)(2,1)} %param.31), kind=kOutput, calls=%fused_computation.272 | convolution fusion | flops 603979776 | bytes 5701632 | tf_op jit(solution)/shard_map/dot_general | solution.py:196
  16.6 1.9 add_dynamic-update-slice_fusion
  18.5 2.1 convert_element_type.290
  25.9 2.5 %fusion.126 = s32[16,48]{0,1:T(8,128)} fusion(s32[16,48]{0,1:T(8,128)} %copy.35), kind=kOutput, calls=%fused_computation.268 | output fusion | flops 650496 | bytes 6144 | tf_op jit(solution)/shard_map/jit(cumsum)/reduce_window_sum | solution.py:16
  32.0 2.6 %convolution_convert_fusion.2 = bf16[768,1152]{1,0:T(8,128)(2,1)} fusion(s32[48]{0:T(128)S(1)} %dynamic-slice_add_fusion, bf16[48,384]{1,0:T(8,128)(2,1)} %param.21, bf16[48,384]{1,0:T(8,128)(2,1)} %param.20, bf16[48,384]{1,0:T(8,128)(2,1)} %param.19), kind=kOutput, calls=%fused_computation.10 | convolution fusion | flops 86188032 | bytes 1880256 | tf_op jit(solution)/shard_map/dot_general | solution.py:109
  34.6 6.9 %all-to-all-start = ((bf16[16,48,1152]{2,1,0:T(8,128)(2,1)}), bf16[16,48,1152]{2,1,0:T(8,128)(2,1)}, u32[]{:S(2)}, u32[]{:S(2)}) async-start(bf16[16,48,1152]{2,1,0:T(8,128)(2,1)} %bitcast.114), calls=%async_computation | async-start | bytes 3538944 | tf_op jit(solution)/shard_map/all_to_all | solution.py:110
  43.0 2.6 %reduce-window.14 = s32[16,3,128]{2,0,1:T(8,128)} reduce-window(s32[16,3,128]{2,0,1:T(8,128)} %copy_bitcast_fusion, s32[]{:T(128)} %constant.197.clone.1), window={size=1x1x128 pad=0_0x0_0x127_0}, to_apply=%region_0.1 | reduce-window | flops 780288 | bytes 49156 | tf_op jit(solution)/shard_map/reduce-window
  60.2 1.8 add_convert_fusion.1
  62.0 3.8 %collective-permute-start.15 = (bf16[256,384]{1,0:T(8,128)(2,1)S(1)}, bf16[256,384]{1,0:T(8,128)(2,1)S(1)}, u32[]{:S(2)}, u32[]{:S(2)}) collective-permute-start(bf16[256,384]{1,0:T(8,128)(2,1)S(1)} %get-tuple-element.33), channel_id=1, source_target_pairs={{0,6},{1,7},{2,0},{3,1},{4,2},{5,3},{6,4},{7,5},{8,14},{9,15},{10,... | collective-permute-start | bytes 589832 | tf_op jit(solution)/shard_map/ppermute | solution.py:37
  66.6 7.4 %collective-permute-done.15 = bf16[256,384]{1,0:T(8,128)(2,1)S(1)} collective-permute-done((bf16[256,384]{1,0:T(8,128)(2,1)S(1)}, bf16[256,384]{1,0:T(8,128)(2,1)S(1)}, u32[]{:S(2)}, u32[]{:S(2)}) %collective-permute-start.15) | collective-permute-done | bytes 196640 | tf_op jit(solution)/shard_map/ppermute | solution.py:37
  74.0 3.8 %collective-permute-done.13 = bf16[256,384]{1,0:T(8,128)(2,1)S(1)} collective-permute-done((bf16[256,384]{1,0:T(8,128)(2,1)S(1)}, bf16[256,384]{1,0:T(8,128)(2,1)S(1)}, u32[]{:S(2)}, u32[]{:S(2)}) %collective-permute-start.13) | collective-permute-done | bytes 196640 | tf_op jit(solution)/shard_map/ppermute | solution.py:37
  81.3 2.4 %collective-permute-done.18 = bf16[256,384]{1,0:T(8,128)(2,1)S(1)} collective-permute-done((bf16[256,384]{1,0:T(8,128)(2,1)S(1)}, bf16[256,384]{1,0:T(8,128)(2,1)S(1)}, u32[]{:S(2)}, u32[]{:S(2)}) %collective-permute-start.18) | collective-permute-done | bytes 196640 | tf_op jit(solution)/shard_map/ppermute | solution.py:51
  84.5 6.2 %collective-permute-done.16 = bf16[256,384]{1,0:T(8,128)(2,1)S(1)} collective-permute-done((bf16[256,384]{1,0:T(8,128)(2,1)S(1)}, bf16[256,384]{1,0:T(8,128)(2,1)S(1)}, u32[]{:S(2)}, u32[]{:S(2)}) %collective-permute-start.16) | collective-permute-done | bytes 196640 | tf_op jit(solution)/shard_map/ppermute | solution.py:51
  93.0 2.0 convolution_convert_fusion.3
  99.2 2.4 %fusion.128 = (f32[192]{0:T(256)S(1)}, f32[192,2048]{1,0:T(8,128)S(1)}) fusion(bf16[192,384]{1,0:T(8,128)(2,1)S(1)} %bitcast.132, bf16[2,2048,384]{2,1,0:T(8,128)(2,1)} %param.25, pred[2048]{0:T(1024)(128)(4,1)} %iota_compare_fusion.15), kind=kOutput, calls=%fused_computation.270 | convolution fusion | flops 303169344 | bytes 3296000 | tf_op jit(solution)/shard_map/dot_general | solution.py:138
  105.5 2.4 %fusion.127 = (f32[192]{0:T(256)S(1)}, f32[192,2048]{1,0:T(8,128)S(1)}) fusion(bf16[192,384]{1,0:T(8,128)(2,1)} %bitcast.131, bf16[2,2048,384]{2,1,0:T(8,128)(2,1)} %param.25, pred[2048]{0:T(1024)(128)(4,1)} %iota_compare_fusion.14), kind=kOutput, calls=%fused_computation.269 | convolution fusion | flops 303169344 | bytes 3296000 | tf_op jit(solution)/shard_map/dot_general | solution.py:138
  110.9 6.5 %all-to-all-start.1 = ((bf16[16,48,384]{2,1,0:T(8,128)(2,1)}), bf16[16,48,384]{2,1,0:T(8,128)(2,1)}, u32[]{:S(2)}, u32[]{:S(2)}) async-start(bf16[16,48,384]{2,1,0:T(8,128)(2,1)} %bitcast.115), calls=%async_computation.1 | async-start | bytes 1179648 | tf_op jit(solution)/shard_map/all_to_all | solution.py:166
  127.2 2.0 all-to-all-done.1
  129.2 3.5 %fusion.34 = f32[48,3072]{1,0:T(8,128)} fusion(bf16[384,3072]{1,0:T(8,128)(2,1)} %param.31, bf16[768,384]{1,0:T(8,128)(2,1)} %bitcast.16, s32[48]{0:T(128)S(1)} %copy-done.44), kind=kOutput, calls=%fused_computation.55 | convolution fusion | flops 141613056 | bytes 3539136 | tf_op jit(solution)/shard_map/dot_general | solution.py:196
  137.0 3.7 %fusion.54 = f32[256,512]{1,0:T(8,128)} fusion(bf16[3072,512]{1,0:T(8,128)(2,1)} %param.33, bf16[256,3072]{1,0:T(8,128)(2,1)S(1)} %copy-done.6, f32[3072]{0:T(1024)S(1)} %copy-done.38, f32[256]{0:T(256)S(1)} %add_rsqrt_fusion), kind=kOutput, calls=%fused_computation.88 | convolution fusion | flops 808452096 | bytes 5256192 | tf_op jit(solution)/shard_map/dot_general | solution.py:206
  142.4 5.6 %convolution_convert_fusion = bf16[256,3072]{1,0:T(8,128)(2,1)} fusion(bf16[512,3072]{1,0:T(8,128)(2,1)S(1)} %copy-done, bf16[3072,512]{1,0:T(8,128)(2,1)} %param.34, f32[256,512]{1,0:T(8,128)} %fusion.54, bf16[256,3072]{1,0:T(8,128)(2,1)} %copy-done.5, f32[3072]{0:T(1024)S(1)} %copy-done.38, f32[256]{0:T(256)S(1)} %add_rsqrt_fusion), kind=kOutput, calls=%fused_computation.8 | convolution fusion | flops 1615331328 | bytes 9974784 | tf_op jit(solution)/shard_map/dot_general | solution.py:209
  148.0 2.5 %collective-permute-start.6 = (bf16[48,384]{1,0:T(8,128)(2,1)S(1)}, bf16[48,384]{1,0:T(8,128)(2,1)S(1)}, u32[]{:S(2)}, u32[]{:S(2)}) collective-permute-start(bf16[48,384]{1,0:T(8,128)(2,1)S(1)} %add_convert_fusion.7), channel_id=1, source_target_pairs={{0,6},{1,7},{2,0},{3,1},{4,2},{5,3},{6,4},{7,5},{8,14},{9,15},{10,... | collective-permute-start | bytes 110600 | tf_op jit(solution)/shard_map/ppermute | solution.py:51
  156.5 2.1 collective-permute-start.7
  161.6 3.9 %convolution_convert_fusion.1 = bf16[48,3072]{1,0:T(8,128)(2,1)} fusion(bf16[512,3072]{1,0:T(8,128)(2,1)S(1)} %copy-done, bf16[3072,512]{1,0:T(8,128)(2,1)} %param.34, f32[48,512]{1,0:T(8,128)S(1)} %fusion.88, bf16[48,3072]{1,0:T(8,128)(2,1)S(1)} %select_dynamic-update-slice_fusion.8, f32[3072]{0:T(1024)S(1)} %copy-done.38, f32[48]{0:T(128)} %copy-done.46), kind=kOutput, calls=%fused_computation.9 | convolution fusion | flops 302874624 | bytes 6992064 | tf_op jit(solution)/shard_map/dot_general | solution.py:209
  171.4 2.5 %collective-permute-start.23 = (bf16[256,384]{1,0:T(8,128)(2,1)S(1)}, bf16[256,384]{1,0:T(8,128)(2,1)S(1)}, u32[]{:S(2)}, u32[]{:S(2)}) collective-permute-start(bf16[256,384]{1,0:T(8,128)(2,1)S(1)} %get-tuple-element.26), channel_id=1, source_target_pairs={{0,6},{1,7},{2,0},{3,1},{4,2},{5,3},{6,4},{7,5},{8,14},{9,15},{10,... | collective-permute-start | bytes 589832 | tf_op jit(solution)/shard_map/ppermute | solution.py:37
  177.4 3.1 %collective-permute-done.22 = bf16[256,384]{1,0:T(8,128)(2,1)S(1)} collective-permute-done((bf16[256,384]{1,0:T(8,128)(2,1)S(1)}, bf16[256,384]{1,0:T(8,128)(2,1)S(1)}, u32[]{:S(2)}, u32[]{:S(2)}) %collective-permute-start.22) | collective-permute-done | bytes 196640 | tf_op jit(solution)/shard_map/ppermute | solution.py:37
  180.4 5.9 %collective-permute-done.21 = bf16[256,384]{1,0:T(8,128)(2,1)S(1)} collective-permute-done((bf16[256,384]{1,0:T(8,128)(2,1)S(1)}, bf16[256,384]{1,0:T(8,128)(2,1)S(1)}, u32[]{:S(2)}, u32[]{:S(2)}) %collective-permute-start.21) | collective-permute-done | bytes 196640 | tf_op jit(solution)/shard_map/ppermute | solution.py:37
  186.9 14.0 %all_to_all.52 = bf16[16,40,384]{2,1,0:T(8,128)(2,1)S(1)} all-to-all(bf16[16,40,384]{2,1,0:T(8,128)(2,1)S(1)} %bitcast.123), channel_id=1, replica_groups=mesh['req'=16,'head'=8] {'req'}, dimensions={0} | all-to-all | bytes 983040 | tf_op jit(solution)/shard_map/all_to_all | solution.py:229
  200.8 13.5 %all_to_all.53 = bf16[8,80,384]{2,1,0:T(8,128)(2,1)S(1)} all-to-all(bf16[8,80,384]{2,1,0:T(8,128)(2,1)S(1)} %bitcast.116), channel_id=1, replica_groups=mesh['req'=16,'head'=8] {'head'}, dimensions={0} | all-to-all | bytes 983040 | tf_op jit(solution)/shard_map/all_to_all | solution.py:230
  (267 shorter events, 80.9 us)
Async XLA Ops:
  0.0 142.4 %copy-start = (bf16[512,3072]{1,0:T(8,128)(2,1)S(1)}, bf16[512,3072]{1,0:T(8,128)(2,1)}, u32[]{:S(2)}) copy-start(bf16[512,3072]{1,0:T(8,128)(2,1)} %param.35) | copy-start | bytes 9437188
  22.5 37.7 %collective-permute-start.12 = (bf16[256,1536]{1,0:T(8,128)(2,1)}, bf16[256,1536]{1,0:T(8,128)(2,1)}, u32[]{:S(2)}, u32[]{:S(2)}) collective-permute-start(bf16[256,1536]{1,0:T(8,128)(2,1)} %broadcast_select_fusion.2), channel_id=1, source_target_pairs={{0,1},{1,0},{2,3},{3,2},{4,5},{5,4},{6,7},{7,6},{8,9},{9,8},{10,11... | collective-permute-start | bytes 2359304 | tf_op jit(solution)/shard_map/ppermute | solution.py:31
  34.6 58.4 %all-to-all-start = ((bf16[16,48,1152]{2,1,0:T(8,128)(2,1)}), bf16[16,48,1152]{2,1,0:T(8,128)(2,1)}, u32[]{:S(2)}, u32[]{:S(2)}) async-start(bf16[16,48,1152]{2,1,0:T(8,128)(2,1)} %bitcast.114), calls=%async_computation | async-start | bytes 3538944 | tf_op jit(solution)/shard_map/all_to_all | solution.py:110
  57.6 35.4 %copy-start.50 = (pred[96]{0:T(512)(128)(4,1)}, pred[96]{0:T(512)(128)(4,1)S(1)}, u32[]{:S(2)}) copy-start(pred[96]{0:T(512)(128)(4,1)S(1)} %and.127) | copy-start | bytes 292
  61.9 18.7 %copy-start.40 = (s32[304]{0:T(512)S(1)}, s32[304]{0:T(512)}, u32[]{:S(2)}) copy-start(s32[304]{0:T(512)} %copy-done.39) | copy-start | bytes 3652
  62.0 12.0 %collective-permute-start.15 = (bf16[256,384]{1,0:T(8,128)(2,1)S(1)}, bf16[256,384]{1,0:T(8,128)(2,1)S(1)}, u32[]{:S(2)}, u32[]{:S(2)}) collective-permute-start(bf16[256,384]{1,0:T(8,128)(2,1)S(1)} %get-tuple-element.33), channel_id=1, source_target_pairs={{0,6},{1,7},{2,0},{3,1},{4,2},{5,3},{6,4},{7,5},{8,14},{9,15},{10,... | collective-permute-start | bytes 589832 | tf_op jit(solution)/shard_map/ppermute | solution.py:37
  65.9 8.2 %collective-permute-start.14 = (bf16[256,384]{1,0:T(8,128)(2,1)S(1)}, bf16[256,384]{1,0:T(8,128)(2,1)S(1)}, u32[]{:S(2)}, u32[]{:S(2)}) collective-permute-start(bf16[256,384]{1,0:T(8,128)(2,1)S(1)} %get-tuple-element.34), channel_id=1, source_target_pairs={{0,4},{1,5},{2,6},{3,7},{4,0},{5,1},{6,2},{7,3},{8,12},{9,13},{10,... | collective-permute-start | bytes 589832 | tf_op jit(solution)/shard_map/ppermute | solution.py:37
  65.9 12.0 %collective-permute-start.13 = (bf16[256,384]{1,0:T(8,128)(2,1)S(1)}, bf16[256,384]{1,0:T(8,128)(2,1)S(1)}, u32[]{:S(2)}, u32[]{:S(2)}) collective-permute-start(bf16[256,384]{1,0:T(8,128)(2,1)S(1)} %get-tuple-element.32), channel_id=1, source_target_pairs={{0,2},{1,3},{2,4},{3,5},{4,6},{5,7},{6,0},{7,1},{8,10},{9,11},{10,... | collective-permute-start | bytes 589832 | tf_op jit(solution)/shard_map/ppermute | solution.py:37
  77.9 13.0 %copy-start.7 = (bf16[256,384]{1,0:T(8,128)(2,1)}, bf16[256,384]{1,0:T(8,128)(2,1)S(1)}, u32[]{:S(2)}) copy-start(bf16[256,384]{1,0:T(8,128)(2,1)S(1)} %add_convert_fusion.3) | copy-start | bytes 589828
  77.9 5.7 %collective-permute-start.18 = (bf16[256,384]{1,0:T(8,128)(2,1)S(1)}, bf16[256,384]{1,0:T(8,128)(2,1)S(1)}, u32[]{:S(2)}, u32[]{:S(2)}) collective-permute-start(bf16[256,384]{1,0:T(8,128)(2,1)S(1)} %add_convert_fusion.3), channel_id=1, source_target_pairs={{0,6},{1,7},{2,0},{3,1},{4,2},{5,3},{6,4},{7,5},{8,14},{9,15},{10,... | collective-permute-start | bytes 589832 | tf_op jit(solution)/shard_map/ppermute | solution.py:51
  78.0 6.5 %collective-permute-start.17 = (bf16[256,384]{1,0:T(8,128)(2,1)S(1)}, bf16[256,384]{1,0:T(8,128)(2,1)S(1)}, u32[]{:S(2)}, u32[]{:S(2)}) collective-permute-start(bf16[256,384]{1,0:T(8,128)(2,1)S(1)} %add_convert_fusion.3), channel_id=1, source_target_pairs={{0,4},{1,5},{2,6},{3,7},{4,0},{5,1},{6,2},{7,3},{8,12},{9,13},{10,... | collective-permute-start | bytes 589832 | tf_op jit(solution)/shard_map/ppermute | solution.py:51
  78.7 12.0 %collective-permute-start.16 = (bf16[256,384]{1,0:T(8,128)(2,1)S(1)}, bf16[256,384]{1,0:T(8,128)(2,1)S(1)}, u32[]{:S(2)}, u32[]{:S(2)}) collective-permute-start(bf16[256,384]{1,0:T(8,128)(2,1)S(1)} %add_convert_fusion.3), channel_id=1, source_target_pairs={{0,2},{1,3},{2,4},{3,5},{4,6},{5,7},{6,0},{7,1},{8,10},{9,11},{10,... | collective-permute-start | bytes 589832 | tf_op jit(solution)/shard_map/ppermute | solution.py:51
  92.5 24.9 %collective-permute-start.19 = (bf16[256,1536]{1,0:T(8,128)(2,1)}, bf16[256,1536]{1,0:T(8,128)(2,1)}, u32[]{:S(2)}, u32[]{:S(2)}) collective-permute-start(bf16[256,1536]{1,0:T(8,128)(2,1)} %pad_maximum_fusion.3), channel_id=1, source_target_pairs={{0,1},{1,0},{2,3},{3,2},{4,5},{5,4},{6,7},{7,6},{8,9},{9,8},{10,11... | collective-permute-start | bytes 2359304 | tf_op jit(solution)/shard_map/ppermute | solution.py:56
  110.9 18.3 %all-to-all-start.1 = ((bf16[16,48,384]{2,1,0:T(8,128)(2,1)}), bf16[16,48,384]{2,1,0:T(8,128)(2,1)}, u32[]{:S(2)}, u32[]{:S(2)}) async-start(bf16[16,48,384]{2,1,0:T(8,128)(2,1)} %bitcast.115), calls=%async_computation.1 | async-start | bytes 1179648 | tf_op jit(solution)/shard_map/all_to_all | solution.py:166
  135.5 5.3 %collective-permute-start = (bf16[48,1536]{1,0:T(8,128)(2,1)S(1)}, bf16[48,1536]{1,0:T(8,128)(2,1)S(1)}, u32[]{:S(2)}, u32[]{:S(2)}) collective-permute-start(bf16[48,1536]{1,0:T(8,128)(2,1)S(1)} %broadcast_select_fusion.6), channel_id=1, source_target_pairs={{0,1},{1,0},{2,3},{3,2},{4,5},{5,4},{6,7},{7,6},{8,9},{9,8},{10,11... | collective-permute-start | bytes 442376 | tf_op jit(solution)/shard_map/ppermute | solution.py:31
  140.9 7.1 %collective-permute-start.3 = (bf16[48,384]{1,0:T(8,128)(2,1)S(1)}, bf16[48,384]{1,0:T(8,128)(2,1)S(1)}, u32[]{:S(2)}, u32[]{:S(2)}) collective-permute-start(bf16[48,384]{1,0:T(8,128)(2,1)S(1)} %get-tuple-element.65), channel_id=1, source_target_pairs={{0,6},{1,7},{2,0},{3,1},{4,2},{5,3},{6,4},{7,5},{8,14},{9,15},{10,... | collective-permute-start | bytes 110600 | tf_op jit(solution)/shard_map/ppermute | solution.py:37
  141.7 6.3 %collective-permute-start.2 = (bf16[48,384]{1,0:T(8,128)(2,1)S(1)}, bf16[48,384]{1,0:T(8,128)(2,1)S(1)}, u32[]{:S(2)}, u32[]{:S(2)}) collective-permute-start(bf16[48,384]{1,0:T(8,128)(2,1)S(1)} %get-tuple-element.66), channel_id=1, source_target_pairs={{0,4},{1,5},{2,6},{3,7},{4,0},{5,1},{6,2},{7,3},{8,12},{9,13},{10,... | collective-permute-start | bytes 110600 | tf_op jit(solution)/shard_map/ppermute | solution.py:37
  141.8 6.2 %collective-permute-start.1 = (bf16[48,384]{1,0:T(8,128)(2,1)S(1)}, bf16[48,384]{1,0:T(8,128)(2,1)S(1)}, u32[]{:S(2)}, u32[]{:S(2)}) collective-permute-start(bf16[48,384]{1,0:T(8,128)(2,1)S(1)} %get-tuple-element.64), channel_id=1, source_target_pairs={{0,2},{1,3},{2,4},{3,5},{4,6},{5,7},{6,0},{7,1},{8,10},{9,11},{10,... | collective-permute-start | bytes 110600 | tf_op jit(solution)/shard_map/ppermute | solution.py:37
  148.0 8.4 %copy-start.31 = (bf16[48,384]{1,0:T(8,128)(2,1)}, bf16[48,384]{1,0:T(8,128)(2,1)S(1)}, u32[]{:S(2)}) copy-start(bf16[48,384]{1,0:T(8,128)(2,1)S(1)} %add_convert_fusion.7) | copy-start | bytes 110596
  148.0 6.2 %collective-permute-start.6 = (bf16[48,384]{1,0:T(8,128)(2,1)S(1)}, bf16[48,384]{1,0:T(8,128)(2,1)S(1)}, u32[]{:S(2)}, u32[]{:S(2)}) collective-permute-start(bf16[48,384]{1,0:T(8,128)(2,1)S(1)} %add_convert_fusion.7), channel_id=1, source_target_pairs={{0,6},{1,7},{2,0},{3,1},{4,2},{5,3},{6,4},{7,5},{8,14},{9,15},{10,... | collective-permute-start | bytes 110600 | tf_op jit(solution)/shard_map/ppermute | solution.py:51
  150.5 4.3 %collective-permute-start.5 = (bf16[48,384]{1,0:T(8,128)(2,1)S(1)}, bf16[48,384]{1,0:T(8,128)(2,1)S(1)}, u32[]{:S(2)}, u32[]{:S(2)}) collective-permute-start(bf16[48,384]{1,0:T(8,128)(2,1)S(1)} %add_convert_fusion.7), channel_id=1, source_target_pairs={{0,4},{1,5},{2,6},{3,7},{4,0},{5,1},{6,2},{7,3},{8,12},{9,13},{10,... | collective-permute-start | bytes 110600 | tf_op jit(solution)/shard_map/ppermute | solution.py:51
  151.8 4.6 %collective-permute-start.4 = (bf16[48,384]{1,0:T(8,128)(2,1)S(1)}, bf16[48,384]{1,0:T(8,128)(2,1)S(1)}, u32[]{:S(2)}, u32[]{:S(2)}) collective-permute-start(bf16[48,384]{1,0:T(8,128)(2,1)S(1)} %add_convert_fusion.7), channel_id=1, source_target_pairs={{0,2},{1,3},{2,4},{3,5},{4,6},{5,7},{6,0},{7,1},{8,10},{9,11},{10,... | collective-permute-start | bytes 110600 | tf_op jit(solution)/shard_map/ppermute | solution.py:51
  156.5 3.4 %collective-permute-start.7 = (bf16[48,1536]{1,0:T(8,128)(2,1)S(1)}, bf16[48,1536]{1,0:T(8,128)(2,1)S(1)}, u32[]{:S(2)}, u32[]{:S(2)}) collective-permute-start(bf16[48,1536]{1,0:T(8,128)(2,1)S(1)} %pad_maximum_fusion.9), channel_id=1, source_target_pairs={{0,1},{1,0},{2,3},{3,2},{4,5},{5,4},{6,7},{7,6},{8,9},{9,8},{10,11... | collective-permute-start | bytes 442376 | tf_op jit(solution)/shard_map/ppermute | solution.py:56
  159.8 10.1 %collective-permute-start.20 = (bf16[256,1536]{1,0:T(8,128)(2,1)}, bf16[256,1536]{1,0:T(8,128)(2,1)}, u32[]{:S(2)}, u32[]{:S(2)}) collective-permute-start(bf16[256,1536]{1,0:T(8,128)(2,1)} %broadcast_select_fusion.1), channel_id=1, source_target_pairs={{0,1},{1,0},{2,3},{3,2},{4,5},{5,4},{6,7},{7,6},{8,9},{9,8},{10,11... | collective-permute-start | bytes 2359304 | tf_op jit(solution)/shard_map/ppermute | solution.py:31
  166.7 1.6 collective-permute-start.8
  168.3 6.9 %collective-permute-start.11 = (bf16[48,384]{1,0:T(8,128)(2,1)S(1)}, bf16[48,384]{1,0:T(8,128)(2,1)S(1)}, u32[]{:S(2)}, u32[]{:S(2)}) collective-permute-start(bf16[48,384]{1,0:T(8,128)(2,1)S(1)} %get-tuple-element.58), channel_id=1, source_target_pairs={{0,6},{1,7},{2,0},{3,1},{4,2},{5,3},{6,4},{7,5},{8,14},{9,15},{10,... | collective-permute-start | bytes 110600 | tf_op jit(solution)/shard_map/ppermute | solution.py:37
  168.5 7.5 %collective-permute-start.10 = (bf16[48,384]{1,0:T(8,128)(2,1)S(1)}, bf16[48,384]{1,0:T(8,128)(2,1)S(1)}, u32[]{:S(2)}, u32[]{:S(2)}) collective-permute-start(bf16[48,384]{1,0:T(8,128)(2,1)S(1)} %get-tuple-element.59), channel_id=1, source_target_pairs={{0,4},{1,5},{2,6},{3,7},{4,0},{5,1},{6,2},{7,3},{8,12},{9,13},{10,... | collective-permute-start | bytes 110600 | tf_op jit(solution)/shard_map/ppermute | solution.py:37
  169.6 16.7 %copy-start.8 = (bf16[256,384]{1,0:T(8,128)(2,1)S(1)}, bf16[256,384]{1,0:T(8,128)(2,1)}, u32[]{:S(2)}) copy-start(bf16[256,384]{1,0:T(8,128)(2,1)} %copy-done.7) | copy-start | bytes 589828
  169.6 6.3 %collective-permute-start.9 = (bf16[48,384]{1,0:T(8,128)(2,1)S(1)}, bf16[48,384]{1,0:T(8,128)(2,1)S(1)}, u32[]{:S(2)}, u32[]{:S(2)}) collective-permute-start(bf16[48,384]{1,0:T(8,128)(2,1)S(1)} %get-tuple-element.57), channel_id=1, source_target_pairs={{0,2},{1,3},{2,4},{3,5},{4,6},{5,7},{6,0},{7,1},{8,10},{9,11},{10,... | collective-permute-start | bytes 110600 | tf_op jit(solution)/shard_map/ppermute | solution.py:37
  171.4 5.9 %collective-permute-start.23 = (bf16[256,384]{1,0:T(8,128)(2,1)S(1)}, bf16[256,384]{1,0:T(8,128)(2,1)S(1)}, u32[]{:S(2)}, u32[]{:S(2)}) collective-permute-start(bf16[256,384]{1,0:T(8,128)(2,1)S(1)} %get-tuple-element.26), channel_id=1, source_target_pairs={{0,6},{1,7},{2,0},{3,1},{4,2},{5,3},{6,4},{7,5},{8,14},{9,15},{10,... | collective-permute-start | bytes 589832 | tf_op jit(solution)/shard_map/ppermute | solution.py:37
  174.0 6.5 %collective-permute-start.22 = (bf16[256,384]{1,0:T(8,128)(2,1)S(1)}, bf16[256,384]{1,0:T(8,128)(2,1)S(1)}, u32[]{:S(2)}, u32[]{:S(2)}) collective-permute-start(bf16[256,384]{1,0:T(8,128)(2,1)S(1)} %get-tuple-element.27), channel_id=1, source_target_pairs={{0,4},{1,5},{2,6},{3,7},{4,0},{5,1},{6,2},{7,3},{8,12},{9,13},{10,... | collective-permute-start | bytes 589832 | tf_op jit(solution)/shard_map/ppermute | solution.py:37
  175.2 11.1 %collective-permute-start.21 = (bf16[256,384]{1,0:T(8,128)(2,1)S(1)}, bf16[256,384]{1,0:T(8,128)(2,1)S(1)}, u32[]{:S(2)}, u32[]{:S(2)}) collective-permute-start(bf16[256,384]{1,0:T(8,128)(2,1)S(1)} %get-tuple-element.25), channel_id=1, source_target_pairs={{0,2},{1,3},{2,4},{3,5},{4,6},{5,7},{6,0},{7,1},{8,10},{9,11},{10,... | collective-permute-start | bytes 589832 | tf_op jit(solution)/shard_map/ppermute | solution.py:37
  (51 other events, 173.0 us)

commit v3 on v2

--- a/solution.py
+++ b/solution.py
@@ -107,6 +107,9 @@
     ).astype(jnp.bfloat16)
     stacked_in = jnp.concatenate([dec_query, dec_key, dec_value], axis=1)
     outgoing_q = jnp.dot(packer, stacked_in, preferred_element_type=jnp.float32).astype(jnp.bfloat16)
+    outgoing_q, pre_query, pre_key, pre_value = lax.optimization_barrier(
+        (outgoing_q, pre_query, pre_key, pre_value)
+    )
     arrived_q = lax.all_to_all(outgoing_q, "req", split_axis=0, concat_axis=0, tiled=True)
 
     first_group = me * groups_here

time: 217 us -> 204 us (0.940)
  waiting for transfers between devices: 35.4 us -> 25.5 us
  other arithmetic: 52.2 us -> 43.9 us
  starting transfers between devices: 37.8 us -> 45.7 us
  matrix products: 41.5 us -> 38.4 us
    ppermute x12, waiting for transfers between devices: 21.5 us -> 16.2 us  [pair_then_z_scatter(): acc = acc + lax.ppermute(piece, 'head', perm).astype(jnp.float32)]
    ppermute x6, waiting for transfers between devices: 11.6 us -> 6.96 us  [z_then_pair_gather(): parts.append(lax.ppermute(y, 'head', perm))]
    ppermute x12, starting transfers between devices: 12.1 us -> 16.4 us  [pair_then_z_scatter(): acc = acc + lax.ppermute(piece, 'head', perm).astype(jnp.float32)]
    all_to_all x1, blocking collectives: 13.5 us -> 16.7 us  [on_device(): lax.all_to_all(arrived, 'head', split_axis=0, concat_axis=1, tiled=True)]
    unnamed x116 -> x110, local copies, waits for them, and re-layouts: 6.39 us -> 5.8 us
  transfers between devices with their start and end apart: 26 -> 26, of which waited for: 12 -> 9; matrix products, arithmetic and copies ran while one was open for 36% -> 40% of each run, Pallas kernels for 0% -> 0%
where the time goes in v3:
time: 204 us; the launch traced here: 202 us
  starting transfers between devices  45.7 us (22%)
  other arithmetic  43.9 us (22%)
  matrix products  38.4 us (19%)
  blocking collectives  29.4 us (14%)
  waiting for transfers between devices  25.5 us (12%)
  local copies, waits for them, and re-layouts  17.5 us (9%)
    all_to_all x1, blocking collectives, on_device(): lax.all_to_all(arrived, 'head', split_axis=0, concat_axis=1, tiled=True)  16.7 us
    ppermute x12, starting transfers between devices, pair_then_z_scatter(): acc = acc + lax.ppermute(piece, 'head', perm).astype(jnp.float32)  16.4 us
    ppermute x12, waiting for transfers between devices, pair_then_z_scatter(): acc = acc + lax.ppermute(piece, 'head', perm).astype(jnp.float32)  16.2 us
    all_to_all x1, blocking collectives, on_device(): lax.all_to_all(outgoing, 'req', split_axis=0, concat_axis=0, tiled=True)  12.7 us
    unnamed x17, other arithmetic  9.58 us
    dot_general x2, matrix products, feed_forward(): jnp.dot(hidden, down_weight, preferred_element_type=jnp.float32)  9.5 us
    all_to_all x1, starting transfers between devices, on_device(): lax.all_to_all(outgoing_q, 'req', split_axis=0, concat_axis=0, tiled=True)  7.75 us
    ppermute x6, starting transfers between devices, z_then_pair_gather(): parts.append(lax.ppermute(y, 'head', perm))  7.6 us
  transfers between devices with their start and end apart: 26, of which 9 were waited for; matrix products, arithmetic and copies ran while one was open for 40% of the time, Pallas kernels for 0%

profile of v3, /device:TPU:1, one launch (start us, length us, event | category | flops | bytes accessed | tf_op | source)
XLA Modules:
  0.0 202.1 jit_solution(14680529077778355248)
XLA Ops:
  3.0 2.6 %convolution_convert_fusion.2 = bf16[768,1152]{1,0:T(8,128)(2,1)} fusion(s32[48]{0:T(128)S(1)} %dynamic-slice_add_fusion, bf16[48,384]{1,0:T(8,128)(2,1)} %param.21, bf16[48,384]{1,0:T(8,128)(2,1)} %param.20, bf16[48,384]{1,0:T(8,128)(2,1)} %param.19), kind=kOutput, calls=%fused_computation.10 | convolution fusion | flops 86188032 | bytes 1880256 | tf_op jit(solution)/shard_map/dot_general | solution.py:109
  5.6 7.8 %all-to-all-start = ((bf16[16,48,1152]{2,1,0:T(8,128)(2,1)}), bf16[16,48,1152]{2,1,0:T(8,128)(2,1)}, u32[]{:S(2)}, u32[]{:S(2)}) async-start(bf16[16,48,1152]{2,1,0:T(8,128)(2,1)} %bitcast.114), calls=%async_computation | async-start | bytes 3538944 | tf_op jit(solution)/shard_map/all_to_all | solution.py:113
  16.4 2.5 %fusion = (f32[1024]{0:T(1024)S(1)}, f32[1024,2048]{1,0:T(8,128)S(1)}) fusion(pred[2048]{0:T(1024)(128)(4,1)S(1)} %iota_compare_fusion.13, bf16[1024,384]{1,0:T(8,128)(2,1)S(1)} %bitcast.122, bf16[2,2048,384]{2,1,0:T(8,128)(2,1)S(1)} %copy-done.48), kind=kOutput, calls=%fused_computation.3 | convolution fusion | flops 1616903168 | bytes 10754048 | tf_op jit(solution)/shard_map/dot_general | solution.py:176
  19.1 2.2 %fusion.1 = f32[1024]{0:T(1024)S(1)} fusion(f32[1024,2048]{1,0:T(8,128)S(1)} %get-tuple-element.88, f32[1024]{0:T(1024)S(1)} %max.38, pred[2048]{0:T(1024)(128)(4,1)S(1)} %iota_compare_fusion.13), kind=kLoop, calls=%fused_computation.4 | loop fusion | flops 8387584 | bytes 8398848 | tf_op jit(solution)/shard_map/reduce_sum | solution.py:188
  21.4 2.4 %fusion.2 = f32[1024,384]{1,0:T(8,128)S(1)} fusion(f32[1024,2048]{1,0:T(8,128)S(1)} %get-tuple-element.88, f32[1024]{0:T(1024)S(1)} %add.336, f32[1024]{0:T(1024)S(1)} %max.38, pred[2048]{0:T(1024)(128)(4,1)S(1)} %iota_compare_fusion.13, bf16[2,2048,384]{2,1,0:T(8,128)(2,1)S(1)} %copy-done.49), kind=kOutput, calls=%fused_computation.5 | convolution fusion | flops 1621098496 | bytes 11544576 | tf_op jit(solution)/shard_map/dot_general | solution.py:189
  24.5 2.7 %fusion.130 = f32[256,3072]{1,0:T(8,128)S(1)} fusion(bf16[256,384]{1,0:T(8,128)(2,1)S(1)} %select_reduce_fusion, bf16[384,3072]{1,0:T(8,128)(2,1)} %param.31), kind=kOutput, calls=%fused_computation.272 | convolution fusion | flops 603979776 | bytes 5701632 | tf_op jit(solution)/shard_map/dot_general | solution.py:199
  41.5 2.6 %reduce-window.14 = s32[16,3,128]{2,0,1:T(8,128)} reduce-window(s32[16,3,128]{2,0,1:T(8,128)} %copy_bitcast_fusion, s32[]{:T(128)} %constant.197.clone.1), window={size=1x1x128 pad=0_0x0_0x127_0}, to_apply=%region_0.1 | reduce-window | flops 780288 | bytes 49156 | tf_op jit(solution)/shard_map/reduce-window
  47.7 1.8 add_convert_fusion.1
  49.5 1.7 collective-permute-start.13
  51.2 3.3 %collective-permute-start.14 = (bf16[256,384]{1,0:T(8,128)(2,1)S(1)}, bf16[256,384]{1,0:T(8,128)(2,1)S(1)}, u32[]{:S(2)}, u32[]{:S(2)}) collective-permute-start(bf16[256,384]{1,0:T(8,128)(2,1)S(1)} %get-tuple-element.42), channel_id=1, source_target_pairs={{0,4},{1,5},{2,6},{3,7},{4,0},{5,1},{6,2},{7,3},{8,12},{9,13},{10,... | collective-permute-start | bytes 589832 | tf_op jit(solution)/shard_map/ppermute | solution.py:37
  55.3 3.1 %collective-permute-done.13 = bf16[256,384]{1,0:T(8,128)(2,1)S(1)} collective-permute-done((bf16[256,384]{1,0:T(8,128)(2,1)S(1)}, bf16[256,384]{1,0:T(8,128)(2,1)S(1)}, u32[]{:S(2)}, u32[]{:S(2)}) %collective-permute-start.13) | collective-permute-done | bytes 196640 | tf_op jit(solution)/shard_map/ppermute | solution.py:37
  58.5 5.1 %collective-permute-done.14 = bf16[256,384]{1,0:T(8,128)(2,1)S(1)} collective-permute-done((bf16[256,384]{1,0:T(8,128)(2,1)S(1)}, bf16[256,384]{1,0:T(8,128)(2,1)S(1)}, u32[]{:S(2)}, u32[]{:S(2)}) %collective-permute-start.14) | collective-permute-done | bytes 196640 | tf_op jit(solution)/shard_map/ppermute | solution.py:37
  64.9 2.4 %collective-permute-start.17 = (bf16[256,384]{1,0:T(8,128)(2,1)S(1)}, bf16[256,384]{1,0:T(8,128)(2,1)S(1)}, u32[]{:S(2)}, u32[]{:S(2)}) collective-permute-start(bf16[256,384]{1,0:T(8,128)(2,1)S(1)} %add_convert_fusion.3), channel_id=1, source_target_pairs={{0,4},{1,5},{2,6},{3,7},{4,0},{5,1},{6,2},{7,3},{8,12},{9,13},{10,... | collective-permute-start | bytes 589832 | tf_op jit(solution)/shard_map/ppermute | solution.py:51
  70.4 5.7 %collective-permute-done.17 = bf16[256,384]{1,0:T(8,128)(2,1)S(1)} collective-permute-done((bf16[256,384]{1,0:T(8,128)(2,1)S(1)}, bf16[256,384]{1,0:T(8,128)(2,1)S(1)}, u32[]{:S(2)}, u32[]{:S(2)}) %collective-permute-start.17) | collective-permute-done | bytes 196640 | tf_op jit(solution)/shard_map/ppermute | solution.py:51
  79.3 2.0 convolution_convert_fusion.3
  85.6 2.4 %fusion.128 = (f32[192]{0:T(256)S(1)}, f32[192,2048]{1,0:T(8,128)S(1)}) fusion(bf16[192,384]{1,0:T(8,128)(2,1)S(1)} %bitcast.132, bf16[2,2048,384]{2,1,0:T(8,128)(2,1)} %param.25, pred[2048]{0:T(1024)(128)(4,1)} %iota_compare_fusion.15), kind=kOutput, calls=%fused_computation.270 | convolution fusion | flops 303169344 | bytes 3296000 | tf_op jit(solution)/shard_map/dot_general | solution.py:141
  91.9 2.4 %fusion.127 = (f32[192]{0:T(256)S(1)}, f32[192,2048]{1,0:T(8,128)S(1)}) fusion(bf16[192,384]{1,0:T(8,128)(2,1)} %bitcast.131, bf16[2,2048,384]{2,1,0:T(8,128)(2,1)} %param.25, pred[2048]{0:T(1024)(128)(4,1)} %iota_compare_fusion.14), kind=kOutput, calls=%fused_computation.269 | convolution fusion | flops 303169344 | bytes 3296000 | tf_op jit(solution)/shard_map/dot_general | solution.py:141
  97.3 6.9 %all-to-all-start.1 = ((bf16[16,48,384]{2,1,0:T(8,128)(2,1)}), bf16[16,48,384]{2,1,0:T(8,128)(2,1)}, u32[]{:S(2)}, u32[]{:S(2)}) async-start(bf16[16,48,384]{2,1,0:T(8,128)(2,1)} %bitcast.115), calls=%async_computation.1 | async-start | bytes 1179648 | tf_op jit(solution)/shard_map/all_to_all | solution.py:169
  114.0 2.0 %all-to-all-done.1 = bf16[16,48,384]{2,1,0:T(8,128)(2,1)} async-done(((bf16[16,48,384]{2,1,0:T(8,128)(2,1)}), bf16[16,48,384]{2,1,0:T(8,128)(2,1)}, u32[]{:S(2)}, u32[]{:S(2)}) %all-to-all-start.1) | async-done | bytes 589856 | tf_op jit(solution)/shard_map/all_to_all | solution.py:169
  116.1 3.4 %fusion.34 = f32[48,3072]{1,0:T(8,128)} fusion(bf16[384,3072]{1,0:T(8,128)(2,1)} %param.31, bf16[768,384]{1,0:T(8,128)(2,1)} %bitcast.16, s32[48]{0:T(128)S(1)} %copy-done.42), kind=kOutput, calls=%fused_computation.55 | convolution fusion | flops 141613056 | bytes 3539136 | tf_op jit(solution)/shard_map/dot_general | solution.py:199
  123.9 3.7 %fusion.54 = f32[256,512]{1,0:T(8,128)} fusion(bf16[3072,512]{1,0:T(8,128)(2,1)} %param.33, bf16[256,3072]{1,0:T(8,128)(2,1)S(1)} %copy-done.6, f32[3072]{0:T(1024)S(1)} %copy-done.40, f32[256]{0:T(256)S(1)} %add_rsqrt_fusion), kind=kOutput, calls=%fused_computation.88 | convolution fusion | flops 808452096 | bytes 5256192 | tf_op jit(solution)/shard_map/dot_general | solution.py:209
  128.5 2.5 %collective-permute-start.2 = (bf16[48,384]{1,0:T(8,128)(2,1)S(1)}, bf16[48,384]{1,0:T(8,128)(2,1)S(1)}, u32[]{:S(2)}, u32[]{:S(2)}) collective-permute-start(bf16[48,384]{1,0:T(8,128)(2,1)S(1)} %get-tuple-element.74), channel_id=1, source_target_pairs={{0,4},{1,5},{2,6},{3,7},{4,0},{5,1},{6,2},{7,3},{8,12},{9,13},{10,... | collective-permute-start | bytes 110600 | tf_op jit(solution)/shard_map/ppermute | solution.py:37
  131.2 5.6 %convolution_convert_fusion = bf16[256,3072]{1,0:T(8,128)(2,1)} fusion(bf16[512,3072]{1,0:T(8,128)(2,1)S(1)} %copy-done, bf16[3072,512]{1,0:T(8,128)(2,1)} %param.34, f32[256,512]{1,0:T(8,128)} %fusion.54, bf16[256,3072]{1,0:T(8,128)(2,1)} %copy-done.5, f32[3072]{0:T(1024)S(1)} %copy-done.40, f32[256]{0:T(256)S(1)} %add_rsqrt_fusion), kind=kOutput, calls=%fused_computation.8 | convolution fusion | flops 1615331328 | bytes 9974784 | tf_op jit(solution)/shard_map/dot_general | solution.py:212
  138.6 2.0 %collective-permute-start.6 = (bf16[48,384]{1,0:T(8,128)(2,1)S(1)}, bf16[48,384]{1,0:T(8,128)(2,1)S(1)}, u32[]{:S(2)}, u32[]{:S(2)}) collective-permute-start(bf16[48,384]{1,0:T(8,128)(2,1)S(1)} %add_convert_fusion.7), channel_id=1, source_target_pairs={{0,6},{1,7},{2,0},{3,1},{4,2},{5,3},{6,4},{7,5},{8,14},{9,15},{10,... | collective-permute-start | bytes 110600 | tf_op jit(solution)/shard_map/ppermute | solution.py:51
  142.7 2.3 %collective-permute-start.7 = (bf16[48,1536]{1,0:T(8,128)(2,1)S(1)}, bf16[48,1536]{1,0:T(8,128)(2,1)S(1)}, u32[]{:S(2)}, u32[]{:S(2)}) collective-permute-start(bf16[48,1536]{1,0:T(8,128)(2,1)S(1)} %pad_maximum_fusion.9), channel_id=1, source_target_pairs={{0,1},{1,0},{2,3},{3,2},{4,5},{5,4},{6,7},{7,6},{8,9},{9,8},{10,11... | collective-permute-start | bytes 442376 | tf_op jit(solution)/shard_map/ppermute | solution.py:56
  147.8 3.9 %convolution_convert_fusion.1 = bf16[48,3072]{1,0:T(8,128)(2,1)} fusion(bf16[512,3072]{1,0:T(8,128)(2,1)S(1)} %copy-done, bf16[3072,512]{1,0:T(8,128)(2,1)} %param.34, f32[48,512]{1,0:T(8,128)S(1)} %fusion.88, bf16[48,3072]{1,0:T(8,128)(2,1)S(1)} %select_dynamic-update-slice_fusion.8, f32[3072]{0:T(1024)S(1)} %copy-done.40, f32[48]{0:T(128)} %copy-done.43), kind=kOutput, calls=%fused_computation.9 | convolution fusion | flops 302874624 | bytes 6992064 | tf_op jit(solution)/shard_map/dot_general | solution.py:212
  154.6 1.8 collective-permute-start.10
  160.8 2.6 %collective-permute-start.22 = (bf16[256,384]{1,0:T(8,128)(2,1)S(1)}, bf16[256,384]{1,0:T(8,128)(2,1)S(1)}, u32[]{:S(2)}, u32[]{:S(2)}) collective-permute-start(bf16[256,384]{1,0:T(8,128)(2,1)S(1)} %get-tuple-element.35), channel_id=1, source_target_pairs={{0,4},{1,5},{2,6},{3,7},{4,0},{5,1},{6,2},{7,3},{8,12},{9,13},{10,... | collective-permute-start | bytes 589832 | tf_op jit(solution)/shard_map/ppermute | solution.py:37
  163.4 2.7 %collective-permute-done.21 = bf16[256,384]{1,0:T(8,128)(2,1)S(1)} collective-permute-done((bf16[256,384]{1,0:T(8,128)(2,1)S(1)}, bf16[256,384]{1,0:T(8,128)(2,1)S(1)}, u32[]{:S(2)}, u32[]{:S(2)}) %collective-permute-start.21) | collective-permute-done | bytes 196640 | tf_op jit(solution)/shard_map/ppermute | solution.py:37
  166.1 5.2 %collective-permute-done.22 = bf16[256,384]{1,0:T(8,128)(2,1)S(1)} collective-permute-done((bf16[256,384]{1,0:T(8,128)(2,1)S(1)}, bf16[256,384]{1,0:T(8,128)(2,1)S(1)}, u32[]{:S(2)}, u32[]{:S(2)}) %collective-permute-start.22) | collective-permute-done | bytes 196640 | tf_op jit(solution)/shard_map/ppermute | solution.py:37
  171.9 12.7 %all_to_all.52 = bf16[16,40,384]{2,1,0:T(8,128)(2,1)S(1)} all-to-all(bf16[16,40,384]{2,1,0:T(8,128)(2,1)S(1)} %bitcast.123), channel_id=1, replica_groups=mesh['req'=16,'head'=8] {'req'}, dimensions={0} | all-to-all | bytes 983040 | tf_op jit(solution)/shard_map/all_to_all | solution.py:232
  184.6 16.7 %all_to_all.53 = bf16[8,80,384]{2,1,0:T(8,128)(2,1)S(1)} all-to-all(bf16[8,80,384]{2,1,0:T(8,128)(2,1)S(1)} %bitcast.116), channel_id=1, replica_groups=mesh['req'=16,'head'=8] {'head'}, dimensions={0} | all-to-all | bytes 983040 | tf_op jit(solution)/shard_map/all_to_all | solution.py:233
  (261 shorter events, 73.6 us)
Async XLA Ops:
  0.0 131.2 %copy-start = (bf16[512,3072]{1,0:T(8,128)(2,1)S(1)}, bf16[512,3072]{1,0:T(8,128)(2,1)}, u32[]{:S(2)}) copy-start(bf16[512,3072]{1,0:T(8,128)(2,1)} %param.35) | copy-start | bytes 9437188
  5.6 8.9 %copy-start.38 = (bf16[256,384]{1,0:T(8,128)(2,1)S(1)}, bf16[256,384]{1,0:T(8,128)(2,1)}, u32[]{:S(2)}) copy-start(bf16[256,384]{1,0:T(8,128)(2,1)} %param.22) | copy-start | bytes 589828
  5.6 73.7 %all-to-all-start = ((bf16[16,48,1152]{2,1,0:T(8,128)(2,1)}), bf16[16,48,1152]{2,1,0:T(8,128)(2,1)}, u32[]{:S(2)}, u32[]{:S(2)}) async-start(bf16[16,48,1152]{2,1,0:T(8,128)(2,1)} %bitcast.114), calls=%async_computation | async-start | bytes 3538944 | tf_op jit(solution)/shard_map/all_to_all | solution.py:113
  29.5 18.2 %collective-permute-start.12 = (bf16[256,1536]{1,0:T(8,128)(2,1)}, bf16[256,1536]{1,0:T(8,128)(2,1)}, u32[]{:S(2)}, u32[]{:S(2)}) collective-permute-start(bf16[256,1536]{1,0:T(8,128)(2,1)} %broadcast_select_fusion.2), channel_id=1, source_target_pairs={{0,1},{1,0},{2,3},{3,2},{4,5},{5,4},{6,7},{7,6},{8,9},{9,8},{10,11... | collective-permute-start | bytes 2359304 | tf_op jit(solution)/shard_map/ppermute | solution.py:31
  47.7 7.6 %copy-start.37 = (s32[16,3,128]{2,0,1:T(8,128)S(1)}, s32[16,3,128]{2,0,1:T(8,128)}, u32[]{:S(2)}) copy-start(s32[16,3,128]{2,0,1:T(8,128)} %reduce-window.14) | copy-start | bytes 73732
  49.5 8.9 %collective-permute-start.13 = (bf16[256,384]{1,0:T(8,128)(2,1)S(1)}, bf16[256,384]{1,0:T(8,128)(2,1)S(1)}, u32[]{:S(2)}, u32[]{:S(2)}) collective-permute-start(bf16[256,384]{1,0:T(8,128)(2,1)S(1)} %get-tuple-element.40), channel_id=1, source_target_pairs={{0,2},{1,3},{2,4},{3,5},{4,6},{5,7},{6,0},{7,1},{8,10},{9,11},{10,... | collective-permute-start | bytes 589832 | tf_op jit(solution)/shard_map/ppermute | solution.py:37
  51.2 12.3 %collective-permute-start.14 = (bf16[256,384]{1,0:T(8,128)(2,1)S(1)}, bf16[256,384]{1,0:T(8,128)(2,1)S(1)}, u32[]{:S(2)}, u32[]{:S(2)}) collective-permute-start(bf16[256,384]{1,0:T(8,128)(2,1)S(1)} %get-tuple-element.42), channel_id=1, source_target_pairs={{0,4},{1,5},{2,6},{3,7},{4,0},{5,1},{6,2},{7,3},{8,12},{9,13},{10,... | collective-permute-start | bytes 589832 | tf_op jit(solution)/shard_map/ppermute | solution.py:37
  54.5 9.0 %collective-permute-start.15 = (bf16[256,384]{1,0:T(8,128)(2,1)S(1)}, bf16[256,384]{1,0:T(8,128)(2,1)S(1)}, u32[]{:S(2)}, u32[]{:S(2)}) collective-permute-start(bf16[256,384]{1,0:T(8,128)(2,1)S(1)} %get-tuple-element.41), channel_id=1, source_target_pairs={{0,6},{1,7},{2,0},{3,1},{4,2},{5,3},{6,4},{7,5},{8,14},{9,15},{10,... | collective-permute-start | bytes 589832 | tf_op jit(solution)/shard_map/ppermute | solution.py:37
  63.7 12.6 %copy-start.7 = (bf16[256,384]{1,0:T(8,128)(2,1)}, bf16[256,384]{1,0:T(8,128)(2,1)S(1)}, u32[]{:S(2)}) copy-start(bf16[256,384]{1,0:T(8,128)(2,1)S(1)} %add_convert_fusion.3) | copy-start | bytes 589828
  63.7 6.7 %collective-permute-start.16 = (bf16[256,384]{1,0:T(8,128)(2,1)S(1)}, bf16[256,384]{1,0:T(8,128)(2,1)S(1)}, u32[]{:S(2)}, u32[]{:S(2)}) collective-permute-start(bf16[256,384]{1,0:T(8,128)(2,1)S(1)} %add_convert_fusion.3), channel_id=1, source_target_pairs={{0,2},{1,3},{2,4},{3,5},{4,6},{5,7},{6,0},{7,1},{8,10},{9,11},{10,... | collective-permute-start | bytes 589832 | tf_op jit(solution)/shard_map/ppermute | solution.py:51
  64.9 11.2 %collective-permute-start.17 = (bf16[256,384]{1,0:T(8,128)(2,1)S(1)}, bf16[256,384]{1,0:T(8,128)(2,1)S(1)}, u32[]{:S(2)}, u32[]{:S(2)}) collective-permute-start(bf16[256,384]{1,0:T(8,128)(2,1)S(1)} %add_convert_fusion.3), channel_id=1, source_target_pairs={{0,4},{1,5},{2,6},{3,7},{4,0},{5,1},{6,2},{7,3},{8,12},{9,13},{10,... | collective-permute-start | bytes 589832 | tf_op jit(solution)/shard_map/ppermute | solution.py:51
  67.4 8.7 %collective-permute-start.18 = (bf16[256,384]{1,0:T(8,128)(2,1)S(1)}, bf16[256,384]{1,0:T(8,128)(2,1)S(1)}, u32[]{:S(2)}, u32[]{:S(2)}) collective-permute-start(bf16[256,384]{1,0:T(8,128)(2,1)S(1)} %add_convert_fusion.3), channel_id=1, source_target_pairs={{0,6},{1,7},{2,0},{3,1},{4,2},{5,3},{6,4},{7,5},{8,14},{9,15},{10,... | collective-permute-start | bytes 589832 | tf_op jit(solution)/shard_map/ppermute | solution.py:51
  78.0 26.3 %collective-permute-start.19 = (bf16[256,1536]{1,0:T(8,128)(2,1)}, bf16[256,1536]{1,0:T(8,128)(2,1)}, u32[]{:S(2)}, u32[]{:S(2)}) collective-permute-start(bf16[256,1536]{1,0:T(8,128)(2,1)} %pad_maximum_fusion.3), channel_id=1, source_target_pairs={{0,1},{1,0},{2,3},{3,2},{4,5},{5,4},{6,7},{7,6},{8,9},{9,8},{10,11... | collective-permute-start | bytes 2359304 | tf_op jit(solution)/shard_map/ppermute | solution.py:56
  97.3 18.7 %all-to-all-start.1 = ((bf16[16,48,384]{2,1,0:T(8,128)(2,1)}), bf16[16,48,384]{2,1,0:T(8,128)(2,1)}, u32[]{:S(2)}, u32[]{:S(2)}) async-start(bf16[16,48,384]{2,1,0:T(8,128)(2,1)} %bitcast.115), calls=%async_computation.1 | async-start | bytes 1179648 | tf_op jit(solution)/shard_map/all_to_all | solution.py:169
  109.4 6.6 %copy-start.42 = (s32[48]{0:T(128)S(1)}, s32[48]{0:T(128)}, u32[]{:S(2)}) copy-start(s32[48]{0:T(128)} %copy-done.41) | copy-start | bytes 580
  122.4 5.3 %collective-permute-start = (bf16[48,1536]{1,0:T(8,128)(2,1)S(1)}, bf16[48,1536]{1,0:T(8,128)(2,1)S(1)}, u32[]{:S(2)}, u32[]{:S(2)}) collective-permute-start(bf16[48,1536]{1,0:T(8,128)(2,1)S(1)} %broadcast_select_fusion.6), channel_id=1, source_target_pairs={{0,1},{1,0},{2,3},{3,2},{4,5},{5,4},{6,7},{7,6},{8,9},{9,8},{10,11... | collective-permute-start | bytes 442376 | tf_op jit(solution)/shard_map/ppermute | solution.py:31
  127.7 9.1 %collective-permute-start.1 = (bf16[48,384]{1,0:T(8,128)(2,1)S(1)}, bf16[48,384]{1,0:T(8,128)(2,1)S(1)}, u32[]{:S(2)}, u32[]{:S(2)}) collective-permute-start(bf16[48,384]{1,0:T(8,128)(2,1)S(1)} %get-tuple-element.72), channel_id=1, source_target_pairs={{0,2},{1,3},{2,4},{3,5},{4,6},{5,7},{6,0},{7,1},{8,10},{9,11},{10,... | collective-permute-start | bytes 110600 | tf_op jit(solution)/shard_map/ppermute | solution.py:37
  128.5 8.3 %collective-permute-start.2 = (bf16[48,384]{1,0:T(8,128)(2,1)S(1)}, bf16[48,384]{1,0:T(8,128)(2,1)S(1)}, u32[]{:S(2)}, u32[]{:S(2)}) collective-permute-start(bf16[48,384]{1,0:T(8,128)(2,1)S(1)} %get-tuple-element.74), channel_id=1, source_target_pairs={{0,4},{1,5},{2,6},{3,7},{4,0},{5,1},{6,2},{7,3},{8,12},{9,13},{10,... | collective-permute-start | bytes 110600 | tf_op jit(solution)/shard_map/ppermute | solution.py:37
  131.0 5.8 %collective-permute-start.3 = (bf16[48,384]{1,0:T(8,128)(2,1)S(1)}, bf16[48,384]{1,0:T(8,128)(2,1)S(1)}, u32[]{:S(2)}, u32[]{:S(2)}) collective-permute-start(bf16[48,384]{1,0:T(8,128)(2,1)S(1)} %get-tuple-element.73), channel_id=1, source_target_pairs={{0,6},{1,7},{2,0},{3,1},{4,2},{5,3},{6,4},{7,5},{8,14},{9,15},{10,... | collective-permute-start | bytes 110600 | tf_op jit(solution)/shard_map/ppermute | solution.py:37
  136.9 5.5 %collective-permute-start.4 = (bf16[48,384]{1,0:T(8,128)(2,1)S(1)}, bf16[48,384]{1,0:T(8,128)(2,1)S(1)}, u32[]{:S(2)}, u32[]{:S(2)}) collective-permute-start(bf16[48,384]{1,0:T(8,128)(2,1)S(1)} %add_convert_fusion.7), channel_id=1, source_target_pairs={{0,2},{1,3},{2,4},{3,5},{4,6},{5,7},{6,0},{7,1},{8,10},{9,11},{10,... | collective-permute-start | bytes 110600 | tf_op jit(solution)/shard_map/ppermute | solution.py:51
  138.2 4.4 %collective-permute-start.5 = (bf16[48,384]{1,0:T(8,128)(2,1)S(1)}, bf16[48,384]{1,0:T(8,128)(2,1)S(1)}, u32[]{:S(2)}, u32[]{:S(2)}) collective-permute-start(bf16[48,384]{1,0:T(8,128)(2,1)S(1)} %add_convert_fusion.7), channel_id=1, source_target_pairs={{0,4},{1,5},{2,6},{3,7},{4,0},{5,1},{6,2},{7,3},{8,12},{9,13},{10,... | collective-permute-start | bytes 110600 | tf_op jit(solution)/shard_map/ppermute | solution.py:51
  138.6 4.0 %collective-permute-start.6 = (bf16[48,384]{1,0:T(8,128)(2,1)S(1)}, bf16[48,384]{1,0:T(8,128)(2,1)S(1)}, u32[]{:S(2)}, u32[]{:S(2)}) collective-permute-start(bf16[48,384]{1,0:T(8,128)(2,1)S(1)} %add_convert_fusion.7), channel_id=1, source_target_pairs={{0,6},{1,7},{2,0},{3,1},{4,2},{5,3},{6,4},{7,5},{8,14},{9,15},{10,... | collective-permute-start | bytes 110600 | tf_op jit(solution)/shard_map/ppermute | solution.py:51
  142.7 3.5 %collective-permute-start.7 = (bf16[48,1536]{1,0:T(8,128)(2,1)S(1)}, bf16[48,1536]{1,0:T(8,128)(2,1)S(1)}, u32[]{:S(2)}, u32[]{:S(2)}) collective-permute-start(bf16[48,1536]{1,0:T(8,128)(2,1)S(1)} %pad_maximum_fusion.9), channel_id=1, source_target_pairs={{0,1},{1,0},{2,3},{3,2},{4,5},{5,4},{6,7},{7,6},{8,9},{9,8},{10,11... | collective-permute-start | bytes 442376 | tf_op jit(solution)/shard_map/ppermute | solution.py:56
  146.1 11.8 %collective-permute-start.20 = (bf16[256,1536]{1,0:T(8,128)(2,1)}, bf16[256,1536]{1,0:T(8,128)(2,1)}, u32[]{:S(2)}, u32[]{:S(2)}) collective-permute-start(bf16[256,1536]{1,0:T(8,128)(2,1)} %broadcast_select_fusion.1), channel_id=1, source_target_pairs={{0,1},{1,0},{2,3},{3,2},{4,5},{5,4},{6,7},{7,6},{8,9},{9,8},{10,11... | collective-permute-start | bytes 2359304 | tf_op jit(solution)/shard_map/ppermute | solution.py:31
  152.9 1.6 collective-permute-start.8
  154.6 8.7 %collective-permute-start.10 = (bf16[48,384]{1,0:T(8,128)(2,1)S(1)}, bf16[48,384]{1,0:T(8,128)(2,1)S(1)}, u32[]{:S(2)}, u32[]{:S(2)}) collective-permute-start(bf16[48,384]{1,0:T(8,128)(2,1)S(1)} %get-tuple-element.67), channel_id=1, source_target_pairs={{0,4},{1,5},{2,6},{3,7},{4,0},{5,1},{6,2},{7,3},{8,12},{9,13},{10,... | collective-permute-start | bytes 110600 | tf_op jit(solution)/shard_map/ppermute | solution.py:37
  156.4 6.9 %collective-permute-start.11 = (bf16[48,384]{1,0:T(8,128)(2,1)S(1)}, bf16[48,384]{1,0:T(8,128)(2,1)S(1)}, u32[]{:S(2)}, u32[]{:S(2)}) collective-permute-start(bf16[48,384]{1,0:T(8,128)(2,1)S(1)} %get-tuple-element.66), channel_id=1, source_target_pairs={{0,6},{1,7},{2,0},{3,1},{4,2},{5,3},{6,4},{7,5},{8,14},{9,15},{10,... | collective-permute-start | bytes 110600 | tf_op jit(solution)/shard_map/ppermute | solution.py:37
  157.8 13.5 %copy-start.8 = (bf16[256,384]{1,0:T(8,128)(2,1)S(1)}, bf16[256,384]{1,0:T(8,128)(2,1)}, u32[]{:S(2)}) copy-start(bf16[256,384]{1,0:T(8,128)(2,1)} %copy-done.7) | copy-start | bytes 589828
  157.8 5.5 %collective-permute-start.9 = (bf16[48,384]{1,0:T(8,128)(2,1)S(1)}, bf16[48,384]{1,0:T(8,128)(2,1)S(1)}, u32[]{:S(2)}, u32[]{:S(2)}) collective-permute-start(bf16[48,384]{1,0:T(8,128)(2,1)S(1)} %get-tuple-element.65), channel_id=1, source_target_pairs={{0,2},{1,3},{2,4},{3,5},{4,6},{5,7},{6,0},{7,1},{8,10},{9,11},{10,... | collective-permute-start | bytes 110600 | tf_op jit(solution)/shard_map/ppermute | solution.py:37
  159.5 6.7 %collective-permute-start.21 = (bf16[256,384]{1,0:T(8,128)(2,1)S(1)}, bf16[256,384]{1,0:T(8,128)(2,1)S(1)}, u32[]{:S(2)}, u32[]{:S(2)}) collective-permute-start(bf16[256,384]{1,0:T(8,128)(2,1)S(1)} %get-tuple-element.33), channel_id=1, source_target_pairs={{0,2},{1,3},{2,4},{3,5},{4,6},{5,7},{6,0},{7,1},{8,10},{9,11},{10,... | collective-permute-start | bytes 589832 | tf_op jit(solution)/shard_map/ppermute | solution.py:37
  160.8 10.6 %collective-permute-start.22 = (bf16[256,384]{1,0:T(8,128)(2,1)S(1)}, bf16[256,384]{1,0:T(8,128)(2,1)S(1)}, u32[]{:S(2)}, u32[]{:S(2)}) collective-permute-start(bf16[256,384]{1,0:T(8,128)(2,1)S(1)} %get-tuple-element.35), channel_id=1, source_target_pairs={{0,4},{1,5},{2,6},{3,7},{4,0},{5,1},{6,2},{7,3},{8,12},{9,13},{10,... | collective-permute-start | bytes 589832 | tf_op jit(solution)/shard_map/ppermute | solution.py:37
  163.3 8.0 %collective-permute-start.23 = (bf16[256,384]{1,0:T(8,128)(2,1)S(1)}, bf16[256,384]{1,0:T(8,128)(2,1)S(1)}, u32[]{:S(2)}, u32[]{:S(2)}) collective-permute-start(bf16[256,384]{1,0:T(8,128)(2,1)S(1)} %get-tuple-element.34), channel_id=1, source_target_pairs={{0,6},{1,7},{2,0},{3,1},{4,2},{5,3},{6,4},{7,5},{8,14},{9,15},{10,... | collective-permute-start | bytes 589832 | tf_op jit(solution)/shard_map/ppermute | solution.py:37
  (48 other events, 148.8 us)

commit v4 on v1

--- a/solution.py
+++ b/solution.py
@@ -105,8 +105,7 @@
     packer = (
         my_slot[None, :] == jnp.arange(req_count * per_home, dtype=jnp.int32)[:, None]
     ).astype(jnp.bfloat16)
-    stacked_in = jnp.concatenate([dec_query, dec_key, dec_value], axis=1)
-    outgoing_q = jnp.dot(packer, stacked_in, preferred_element_type=jnp.float32).astype(jnp.bfloat16)
+    outgoing_q = jnp.dot(packer, dec_query, preferred_element_type=jnp.float32).astype(jnp.bfloat16)
     arrived_q = lax.all_to_all(outgoing_q, "req", split_axis=0, concat_axis=0, tiled=True)
 
     first_group = me * groups_here
@@ -129,42 +128,51 @@
     head_mask = (jnp.arange(width_here) // HD)[None, :] == jnp.arange(heads_here)[:, None]
     positions = jnp.arange(length_cache)
     results = []
+    pad_cols = 128
     for group_pos in range(groups_here):
-        rows_block = picked[group_pos * CAP : (group_pos + 1) * CAP]
-        q_rows = rows_block[:, :width_here]
-        k_own = rows_block[:, width_here : 2 * width_here]
-        v_own = rows_block[:, 2 * width_here :]
+        q_rows = picked[group_pos * CAP : (group_pos + 1) * CAP]
         q_stack = jnp.where(head_mask[:, None, :], q_rows[None], 0).reshape(heads_here * CAP, width_here)
         cache_scores = lax.dot_general(
             q_stack, cache_key[group_pos], (((1,), (1,)), ((), ())), preferred_element_type=jnp.float32
         ) * factor
-        own_prod = q_rows.astype(jnp.float32) * k_own.astype(jnp.float32)
-        own_scores = (
-            jnp.sum(jnp.where(head_mask[:, None, :], own_prod[None], 0.0), axis=-1).reshape(heads_here * CAP, 1)
-            * factor
-        )
         valid = (positions < cache_length[group_pos])[None, :]
         cache_scores = jnp.where(valid, cache_scores, -jnp.inf)
-        highest = jnp.maximum(jnp.max(cache_scores, axis=-1, keepdims=True), own_scores)
+        highest = jnp.max(cache_scores, axis=-1, keepdims=True)
         raised = jnp.exp(cache_scores - highest)
-        raised_own = jnp.exp(own_scores - highest)
-        total = jnp.sum(raised, axis=-1, keepdims=True) + raised_own
+        total = jnp.sum(raised, axis=-1, keepdims=True)
         weights = (raised / total).astype(jnp.bfloat16)
-        weight_own = (raised_own / total).astype(jnp.bfloat16).astype(jnp.float32)
         mixed = jnp.dot(weights, cache_value[group_pos], preferred_element_type=jnp.float32)
-        mixed = mixed + weight_own * v_own.astype(jnp.float32)[None].repeat(heads_here, 0).reshape(
-            heads_here * CAP, width_here
-        )
         blended = jnp.sum(
             jnp.where(head_mask[:, None, :], mixed.reshape(heads_here, CAP, width_here), 0.0), axis=0
         )
-        results.append(blended)
-    stacked = jnp.concatenate(results, axis=0).astype(jnp.bfloat16)
+        spread = (highest + jnp.log(total)).reshape(heads_here, CAP).T
+        spread_hi = spread.astype(jnp.bfloat16)
+        spread_lo = (spread - spread_hi.astype(jnp.float32)).astype(jnp.bfloat16)
+        tail = jnp.zeros((CAP, pad_cols - 2 * heads_here), jnp.bfloat16)
+        results.append(
+            jnp.concatenate([blended.astype(jnp.bfloat16), spread_hi, spread_lo, tail], axis=1)
+        )
+    stacked = jnp.concatenate(results, axis=0)
     going_back = jnp.dot(
         chooser.astype(jnp.bfloat16).T, stacked, preferred_element_type=jnp.float32
     ).astype(jnp.bfloat16)
     came_back = lax.all_to_all(going_back, "req", split_axis=0, concat_axis=0, tiled=True)
-    dec_out = jnp.dot(packer.T, came_back, preferred_element_type=jnp.float32).astype(jnp.bfloat16)
+    dec_back = jnp.dot(packer.T, came_back, preferred_element_type=jnp.float32)
+    cache_mix = dec_back[:, :width_here]
+    cache_spread = (
+        dec_back[:, width_here : width_here + heads_here]
+        + dec_back[:, width_here + heads_here : width_here + 2 * heads_here]
+    )
+    own_prod = dec_query.astype(jnp.float32) * dec_key.astype(jnp.float32)
+    own_scores = jnp.sum(jnp.where(head_mask[:, None, :], own_prod[None], 0.0), axis=-1).T * factor
+    top = jnp.maximum(cache_spread, own_scores)
+    part_cache = jnp.exp(cache_spread - top)
+    part_own = jnp.exp(own_scores - top)
+    share_own = part_own / (part_cache + part_own)
+    share_cols = jnp.sum(jnp.where(head_mask[:, None, :], share_own.T[:, :, None], 0.0), axis=0)
+    dec_out = (
+        (1.0 - share_cols) * cache_mix + share_cols * dec_value.astype(jnp.float32)
+    ).astype(jnp.bfloat16)
 
     stretch_len = pre_query.shape[0]
     row_numbers = jnp.arange(stretch_len)

time: 184 us -> 183 us (level)
  blocking collectives: 28.6 us -> 26.3 us
  matrix products: 41.1 us -> 39.2 us
    all_to_all x1, waiting for transfers between devices: 9.53 us -> 0.01 us  [on_device(): lax.all_to_all(outgoing_q, 'req', split_axis=0, concat_axis=0, tiled=True)]
    all_to_all x1, waiting for transfers between devices: 0.76 us -> 10.2 us  [on_device(): lax.all_to_all(going_back, 'req', split_axis=0, concat_axis=0, tiled=True)]
    dot_general x2, matrix products: 1.3 us -> 4.48 us  [on_device(): jnp.dot(weights, cache_value[group_pos], preferred_element_type=jnp.float32)]
    convert_element_type x0 -> x5, other arithmetic: none -> 2.56 us  [the longest x2 2.53 us: on_device(): weights = (raised / total).astype(jnp.bfloat16)]
    all_to_all x1, blocking collectives: 15.3 us -> 13.1 us  [on_device(): lax.all_to_all(outgoing, 'req', split_axis=0, concat_axis=0, tiled=True)]
    all_to_all x1, starting transfers between devices: 4.47 us -> 6.67 us  [on_device(): lax.all_to_all(going_back, 'req', split_axis=0, concat_axis=0, tiled=True)]
    dot_general x1, matrix products: 2.4 us -> 0.49 us  [on_device(): lax.dot_general(pre_stack, pre_key, dims, preferred_element_type=jnp.floa...]
    unnamed x66 -> x70, local copies, waits for them, and re-layouts: 6.58 us -> 6.45 us
  transfers between devices with their start and end apart: 14 -> 14, of which waited for: 13 -> 12; matrix products, arithmetic and copies ran while one was open for 14% -> 12% of each run, Pallas kernels for 0% -> 0%
where the time goes in v4:
time: 183 us
  waiting for transfers between devices  54.7 us (30%)
  matrix products  39.2 us (21%)
  blocking collectives  26.3 us (14%)
  starting transfers between devices  25.4 us (14%)
  other arithmetic  22.6 us (12%)
  local copies, waits for them, and re-layouts  12.8 us (7%)
    ppermute x6, waiting for transfers between devices, pair_then_z_scatter(): acc = acc + lax.ppermute(piece, 'head', perm).astype(jnp.float32)  25.8 us
    all_to_all x1, blocking collectives, on_device(): lax.all_to_all(arrived, 'head', split_axis=0, concat_axis=1, tiled=True)  13.2 us
    all_to_all x1, blocking collectives, on_device(): lax.all_to_all(outgoing, 'req', split_axis=0, concat_axis=0, tiled=True)  13.1 us
    ppermute x3, waiting for transfers between devices, z_then_pair_gather(): parts.append(lax.ppermute(y, 'head', perm))  12.9 us
    all_to_all x1, waiting for transfers between devices, on_device(): lax.all_to_all(going_back, 'req', split_axis=0, concat_axis=0, tiled=True)  10.2 us
    all_to_all x1, starting transfers between devices, on_device(): lax.all_to_all(outgoing_q, 'req', split_axis=0, concat_axis=0, tiled=True)  7.62 us
    dot_general x1, matrix products, on_device(): jnp.dot((raised_cache / total).astype(jnp.bfloat16), cache_value[0], pref...  7.44 us
    all_to_all x1, starting transfers between devices, on_device(): lax.all_to_all(going_back, 'req', split_axis=0, concat_axis=0, tiled=True)  6.67 us
  transfers between devices with their start and end apart: 14, of which 12 were waited for; matrix products, arithmetic and copies ran while one was open for 12% of the time, Pallas kernels for 0%

profile of v4, /device:TPU:1, one launch (start us, length us, event | category | flops | bytes accessed | tf_op | source)
XLA Modules:
  0.0 182.6 jit_solution(7409916737679432933)
XLA Ops:
  2.4 1.9 %convolution_convert_fusion.2 = bf16[768,384]{1,0:T(8,128)(2,1)} fusion(bf16[48,384]{1,0:T(8,128)(2,1)} %param.19, s32[48]{0:T(128)S(1)} %dynamic-slice_add_fusion), kind=kOutput, calls=%fused_computation.44 | convolution fusion | flops 28643328 | bytes 626880 | tf_op jit(solution)/shard_map/dot_general | solution.py:108
  4.3 7.6 %all-to-all-start = ((bf16[16,48,384]{2,1,0:T(8,128)(2,1)}), bf16[16,48,384]{2,1,0:T(8,128)(2,1)}, u32[]{:S(2)}, u32[]{:S(2)}) async-start(bf16[16,48,384]{2,1,0:T(8,128)(2,1)} %bitcast.120), calls=%async_computation | async-start | bytes 1179648 | tf_op jit(solution)/shard_map/all_to_all | solution.py:109
  13.1 4.0 %fusion = (f32[1024]{0:T(1024)S(1)}, f32[1024,2048]{1,0:T(8,128)S(1)}) fusion(pred[2048]{0:T(1024)(128)(4,1)S(1)} %iota_compare_fusion.12, bf16[1024,384]{1,0:T(8,128)(2,1)S(1)} %bitcast.127, bf16[2,2048,384]{2,1,0:T(8,128)(2,1)} %param.25), kind=kOutput, calls=%fused_computation.3 | convolution fusion | flops 1616903168 | bytes 10754048 | tf_op jit(solution)/shard_map/dot_general | solution.py:181
  17.6 2.2 %fusion.1 = f32[1024]{0:T(1024)S(1)} fusion(f32[1024,2048]{1,0:T(8,128)S(1)} %get-tuple-element.50, f32[1024]{0:T(1024)S(1)} %max.12, pred[2048]{0:T(1024)(128)(4,1)S(1)} %iota_compare_fusion.12), kind=kLoop, calls=%fused_computation.4 | loop fusion | flops 8387584 | bytes 8398848 | tf_op jit(solution)/shard_map/reduce_sum | solution.py:193
  22.1 7.4 %fusion.2 = f32[1024,384]{1,0:T(8,128)} fusion(f32[1024,2048]{1,0:T(8,128)} %copy-done.1, f32[1024]{0:T(1024)S(1)} %add.227, f32[1024]{0:T(1024)S(1)} %max.12, pred[2048]{0:T(1024)(128)(4,1)S(1)} %iota_compare_fusion.12, bf16[2,2048,384]{2,1,0:T(8,128)(2,1)} %param.26), kind=kOutput, calls=%fused_computation.7 | convolution fusion | flops 1621098496 | bytes 11544576 | tf_op jit(solution)/shard_map/dot_general | solution.py:194
  33.5 2.2 %fusion.122 = (f32[192]{0:T(256)S(1)}, f32[192,2048]{1,0:T(8,128)S(1)}) fusion(bf16[192,384]{1,0:T(8,128)(2,1)S(1)} %bitcast.134, bf16[2,2048,384]{2,1,0:T(8,128)(2,1)} %param.25, pred[2048]{0:T(1024)(128)(4,1)S(1)} %iota_compare_fusion.13), kind=kOutput, calls=%fused_computation.224 | convolution fusion | flops 303169344 | bytes 3296000 | tf_op jit(solution)/shard_map/dot_general | solution.py:135
  40.7 2.2 %fusion.33 = bf16[48,384]{1,0:T(8,128)(2,1)S(1)} fusion(bf16[4,48,2048]{2,1,0:T(8,128)(2,1)} %bitcast.129, bf16[2,2048,384]{2,1,0:T(8,128)(2,1)} %param.26, pred[4,384]{1,0:T(4,128)(4,1)S(1)} %iota_compare_fusion.15), kind=kOutput, calls=%fused_computation.50 | convolution fusion | flops 302118912 | bytes 2397696 | tf_op jit(solution)/shard_map/dot_general | solution.py:144
  43.2 2.2 %fusion.36 = bf16[48,384]{1,0:T(8,128)(2,1)S(1)} fusion(bf16[4,48,2048]{2,1,0:T(8,128)(2,1)} %bitcast.130, bf16[2,2048,384]{2,1,0:T(8,128)(2,1)} %param.26, pred[4,384]{1,0:T(4,128)(4,1)S(1)} %iota_compare_fusion.15), kind=kOutput, calls=%fused_computation.51 | convolution fusion | flops 302118912 | bytes 2397696 | tf_op jit(solution)/shard_map/dot_general | solution.py:144
  46.9 6.7 %all-to-all-start.1 = ((bf16[16,48,512]{2,1,0:T(8,128)(2,1)}), bf16[16,48,512]{2,1,0:T(8,128)(2,1)}, u32[]{:S(2)}, u32[]{:S(2)}) async-start(bf16[16,48,512]{2,1,0:T(8,128)(2,1)} %bitcast.126), calls=%async_computation.1 | async-start | bytes 1572864 | tf_op jit(solution)/shard_map/all_to_all | solution.py:159
  53.7 2.3 %convolution_add_fusion = f32[1024,384]{1,0:T(8,128)S(1)} fusion(f32[1024,384]{1,0:T(8,128)} %fusion.2, bf16[256,384]{1,0:T(8,128)(2,1)} %param.24, f32[1024,256]{0,1:T(8,128)} %copy-done.18, f32[1024]{0:T(1024)S(1)} %add.227, f32[1024]{0:T(1024)S(1)} %max.12), kind=kOutput, calls=%fused_computation.34 | convolution fusion | flops 202506240 | bytes 4399104 | tf_op jit(solution)/shard_map/dot_general | solution.py:196
  56.2 10.2 %all-to-all-done.1 = bf16[16,48,512]{2,1,0:T(8,128)(2,1)} async-done(((bf16[16,48,512]{2,1,0:T(8,128)(2,1)}), bf16[16,48,512]{2,1,0:T(8,128)(2,1)}, u32[]{:S(2)}, u32[]{:S(2)}) %all-to-all-start.1) | async-done | bytes 786464 | tf_op jit(solution)/shard_map/all_to_all | solution.py:159
  66.5 1.4 fusion.53
  68.3 2.8 %fusion.61 = f32[304,3072]{1,0:T(8,128)S(1)} fusion(bf16[384,3072]{1,0:T(8,128)(2,1)} %param.31, bf16[256,384]{1,0:T(8,128)(2,1)S(1)} %select_reduce_fusion, bf16[48,384]{1,0:T(8,128)(2,1)S(1)} %fusion.89), kind=kOutput, calls=%fused_computation.94 | convolution fusion | flops 717692928 | bytes 6328320 | tf_op jit(solution)/shard_map/dot_general | solution.py:201
  73.6 2.6 %collective-permute-start = (bf16[304,1536]{1,0:T(8,128)(2,1)}, bf16[304,1536]{1,0:T(8,128)(2,1)}, u32[]{:S(2)}, u32[]{:S(2)}) collective-permute-start(bf16[304,1536]{1,0:T(8,128)(2,1)} %broadcast_select_fusion.1), channel_id=1, source_target_pairs={{0,1},{1,0},{2,3},{3,2},{4,5},{5,4},{6,7},{7,6},{8,9},{9,8},{10,11... | collective-permute-start | bytes 2801672 | tf_op jit(solution)/shard_map/ppermute | solution.py:31
  76.2 2.5 %collective-permute-done = bf16[304,1536]{1,0:T(8,128)(2,1)} collective-permute-done((bf16[304,1536]{1,0:T(8,128)(2,1)}, bf16[304,1536]{1,0:T(8,128)(2,1)}, u32[]{:S(2)}, u32[]{:S(2)}) %collective-permute-start) | collective-permute-done | bytes 933920 | tf_op jit(solution)/shard_map/ppermute | solution.py:31
  78.6 2.0 %add_convert_fusion.1 = bf16[304,1536]{1,0:T(8,128)(2,1)S(1)} fusion(bf16[304,1536]{1,0:T(8,128)(2,1)} %collective-permute-done, pred[]{:T(512)S(6)} %eq.217, bf16[304,384]{1,0:T(8,128)(2,1)} %copy-done.4, bf16[304,384]{1,0:T(8,128)(2,1)} %copy-done.5, bf16[304,384]{1,0:T(8,128)(2,1)} %copy-done.6, bf16[304,384]{1,0:T(8,128)(2,1)} %copy-done.7, ...), kind=kLoop, calls=%fused_computation.17 | loop fusion | flops 9805824 | bytes 3735553 | tf_op jit(solution)/shard_map/convert_element_type | solution.py:32
  82.4 3.8 %collective-permute-start.3 = (bf16[304,384]{1,0:T(8,128)(2,1)}, bf16[304,384]{1,0:T(8,128)(2,1)S(1)}, u32[]{:S(2)}, u32[]{:S(2)}) collective-permute-start(bf16[304,384]{1,0:T(8,128)(2,1)} %get-tuple-element.35), channel_id=1, source_target_pairs={{0,6},{1,7},{2,0},{3,1},{4,2},{5,3},{6,4},{7,5},{8,14},{9,15},{10,... | collective-permute-start | bytes 700424 | tf_op jit(solution)/shard_map/ppermute | solution.py:37
  86.9 9.3 %collective-permute-done.3 = bf16[304,384]{1,0:T(8,128)(2,1)S(1)} collective-permute-done((bf16[304,384]{1,0:T(8,128)(2,1)}, bf16[304,384]{1,0:T(8,128)(2,1)S(1)}, u32[]{:S(2)}, u32[]{:S(2)}) %collective-permute-start.3) | collective-permute-done | bytes 233504 | tf_op jit(solution)/shard_map/ppermute | solution.py:37
  96.9 3.2 %collective-permute-done.1 = bf16[304,384]{1,0:T(8,128)(2,1)} collective-permute-done((bf16[304,384]{1,0:T(8,128)(2,1)}, bf16[304,384]{1,0:T(8,128)(2,1)}, u32[]{:S(2)}, u32[]{:S(2)}) %collective-permute-start.1) | collective-permute-done | bytes 233504 | tf_op jit(solution)/shard_map/ppermute | solution.py:37
  100.0 1.4 add_convert_fusion.3
  103.0 5.1 %collective-permute-done.6 = bf16[304,384]{1,0:T(8,128)(2,1)} collective-permute-done((bf16[304,384]{1,0:T(8,128)(2,1)S(1)}, bf16[304,384]{1,0:T(8,128)(2,1)}, u32[]{:S(2)}, u32[]{:S(2)}) %collective-permute-start.6) | collective-permute-done | bytes 233504 | tf_op jit(solution)/shard_map/ppermute | solution.py:51
  109.0 6.9 %collective-permute-done.4 = bf16[304,384]{1,0:T(8,128)(2,1)} collective-permute-done((bf16[304,384]{1,0:T(8,128)(2,1)S(1)}, bf16[304,384]{1,0:T(8,128)(2,1)}, u32[]{:S(2)}, u32[]{:S(2)}) %collective-permute-start.4) | collective-permute-done | bytes 233504 | tf_op jit(solution)/shard_map/ppermute | solution.py:51
  118.0 2.1 %collective-permute-done.7 = bf16[304,1536]{1,0:T(8,128)(2,1)S(1)} collective-permute-done((bf16[304,1536]{1,0:T(8,128)(2,1)S(1)}, bf16[304,1536]{1,0:T(8,128)(2,1)S(1)}, u32[]{:S(2)}, u32[]{:S(2)}) %collective-permute-start.7) | collective-permute-done | bytes 933920 | tf_op jit(solution)/shard_map/ppermute | solution.py:56
  123.1 2.0 %fusion.48 = f32[304,512]{1,0:T(8,128)} fusion(bf16[3072,512]{1,0:T(8,128)(2,1)S(1)} %copy-done.30, bf16[304,3072]{1,0:T(8,128)(2,1)S(1)} %select_dynamic-update-slice_fusion, f32[3072]{0:T(1024)S(1)} %copy-done.32, f32[304]{0:T(512)S(1)} %add_rsqrt_fusion), kind=kOutput, calls=%fused_computation.73 | convolution fusion | flops 960036864 | bytes 5649600 | tf_op jit(solution)/shard_map/dot_general | solution.py:214
  125.1 6.1 %convolution_convert_fusion = bf16[304,3072]{1,0:T(8,128)(2,1)} fusion(bf16[512,3072]{1,0:T(8,128)(2,1)S(1)} %copy-done, bf16[3072,512]{1,0:T(8,128)(2,1)} %param.34, f32[304,512]{1,0:T(8,128)} %fusion.48, bf16[304,3072]{1,0:T(8,128)(2,1)} %copy-done.3, f32[3072]{0:T(1024)S(1)} %copy-done.32, f32[304]{0:T(512)S(1)} %add_rsqrt_fusion), kind=kOutput, calls=%fused_computation.8 | convolution fusion | flops 1918205952 | bytes 10663104 | tf_op jit(solution)/shard_map/dot_general | solution.py:217
  131.2 1.8 fusion.116
  137.8 2.0 %add_convert_fusion = bf16[304,1536]{1,0:T(8,128)(2,1)S(1)} fusion(bf16[304,1536]{1,0:T(8,128)(2,1)} %collective-permute-done.8, pred[]{:T(512)S(6)} %eq.217, bf16[304,384]{1,0:T(8,128)(2,1)} %copy-done.11, bf16[304,384]{1,0:T(8,128)(2,1)} %copy-done.12, bf16[304,384]{1,0:T(8,128)(2,1)} %copy-done.13, bf16[304,384]{1,0:T(8,128)(2,1)} %copy-done.14, ...), kind=kLoop, calls=%fused_computation.16 | loop fusion | flops 9805824 | bytes 3735553 | tf_op jit(solution)/shard_map/convert_element_type | solution.py:32
  141.4 5.4 %collective-permute-done.11 = bf16[304,384]{1,0:T(8,128)(2,1)S(1)} collective-permute-done((bf16[304,384]{1,0:T(8,128)(2,1)S(1)}, bf16[304,384]{1,0:T(8,128)(2,1)S(1)}, u32[]{:S(2)}, u32[]{:S(2)}) %collective-permute-start.11) | collective-permute-done | bytes 233504 | tf_op jit(solution)/shard_map/ppermute | solution.py:37
  146.8 2.0 %collective-permute-done.10 = bf16[304,384]{1,0:T(8,128)(2,1)S(1)} collective-permute-done((bf16[304,384]{1,0:T(8,128)(2,1)S(1)}, bf16[304,384]{1,0:T(8,128)(2,1)S(1)}, u32[]{:S(2)}, u32[]{:S(2)}) %collective-permute-start.10) | collective-permute-done | bytes 233504 | tf_op jit(solution)/shard_map/ppermute | solution.py:37
  148.8 6.0 %collective-permute-done.9 = bf16[304,384]{1,0:T(8,128)(2,1)S(1)} collective-permute-done((bf16[304,384]{1,0:T(8,128)(2,1)S(1)}, bf16[304,384]{1,0:T(8,128)(2,1)S(1)}, u32[]{:S(2)}, u32[]{:S(2)}) %collective-permute-start.9) | collective-permute-done | bytes 233504 | tf_op jit(solution)/shard_map/ppermute | solution.py:37
  155.4 13.1 %all_to_all.52 = bf16[16,40,384]{2,1,0:T(8,128)(2,1)S(1)} all-to-all(bf16[16,40,384]{2,1,0:T(8,128)(2,1)S(1)} %bitcast.131), channel_id=1, replica_groups=mesh['req'=16,'head'=8] {'req'}, dimensions={0} | all-to-all | bytes 983040 | tf_op jit(solution)/shard_map/all_to_all | solution.py:234
  168.5 13.2 %all_to_all.53 = bf16[8,80,384]{2,1,0:T(8,128)(2,1)S(1)} all-to-all(bf16[8,80,384]{2,1,0:T(8,128)(2,1)S(1)} %bitcast.121), channel_id=1, replica_groups=mesh['req'=16,'head'=8] {'head'}, dimensions={0} | all-to-all | bytes 983040 | tf_op jit(solution)/shard_map/all_to_all | solution.py:235
  (174 shorter events, 37.7 us)
Async XLA Ops:
  0.0 125.1 %copy-start = (bf16[512,3072]{1,0:T(8,128)(2,1)S(1)}, bf16[512,3072]{1,0:T(8,128)(2,1)}, u32[]{:S(2)}) copy-start(bf16[512,3072]{1,0:T(8,128)(2,1)} %param.35) | copy-start | bytes 9437188
  0.0 13.0 %copy-start.23 = (bf16[256,384]{1,0:T(8,128)(2,1)S(1)}, bf16[256,384]{1,0:T(8,128)(2,1)}, u32[]{:S(2)}) copy-start(bf16[256,384]{1,0:T(8,128)(2,1)} %param.22) | copy-start | bytes 589828
  4.3 27.8 %all-to-all-start = ((bf16[16,48,384]{2,1,0:T(8,128)(2,1)}), bf16[16,48,384]{2,1,0:T(8,128)(2,1)}, u32[]{:S(2)}, u32[]{:S(2)}) async-start(bf16[16,48,384]{2,1,0:T(8,128)(2,1)} %bitcast.120), calls=%async_computation | async-start | bytes 1179648 | tf_op jit(solution)/shard_map/all_to_all | solution.py:109
  13.1 4.0 %copy-start.31 = (bf16[256,384]{1,0:T(8,128)(2,1)S(1)}, bf16[256,384]{1,0:T(8,128)(2,1)}, u32[]{:S(2)}) copy-start(bf16[256,384]{1,0:T(8,128)(2,1)} %param.23) | copy-start | bytes 589828
  17.1 3.2 %copy-start.1 = (f32[1024,2048]{1,0:T(8,128)}, f32[1024,2048]{1,0:T(8,128)S(1)}, u32[]{:S(2)}) copy-start(f32[1024,2048]{1,0:T(8,128)S(1)} %get-tuple-element.50) | copy-start | bytes 25165828
  17.6 3.1 %copy-start.18 = (f32[1024,256]{0,1:T(8,128)}, f32[1024,256]{0,1:T(8,128)S(1)}, u32[]{:S(2)}) copy-start(f32[1024,256]{0,1:T(8,128)S(1)} %get-tuple-element.52) | copy-start | bytes 3145732
  22.1 7.9 %copy-start.27 = (s32[2]{0:T(128)S(1)}, s32[2]{0:T(128)}, u32[]{:S(2)}) copy-start(s32[2]{0:T(128)} %param.28) | copy-start | bytes 28
  35.7 2.2 %copy-start.29 = (bf16[2,2048,384]{2,1,0:T(8,128)(2,1)S(1)}, bf16[2,2048,384]{2,1,0:T(8,128)(2,1)}, u32[]{:S(2)}) copy-start(bf16[2,2048,384]{2,1,0:T(8,128)(2,1)} %param.25) | copy-start | bytes 9437188
  45.5 8.1 %copy-start.24 = (bf16[48,384]{1,0:T(8,128)(2,1)S(1)}, bf16[48,384]{1,0:T(8,128)(2,1)}, u32[]{:S(2)}) copy-start(bf16[48,384]{1,0:T(8,128)(2,1)} %param.19) | copy-start | bytes 110596
  45.5 8.1 %copy-start.26 = (bf16[48,384]{1,0:T(8,128)(2,1)S(1)}, bf16[48,384]{1,0:T(8,128)(2,1)}, u32[]{:S(2)}) copy-start(bf16[48,384]{1,0:T(8,128)(2,1)} %param.20) | copy-start | bytes 110596
  46.9 19.5 %all-to-all-start.1 = ((bf16[16,48,512]{2,1,0:T(8,128)(2,1)}), bf16[16,48,512]{2,1,0:T(8,128)(2,1)}, u32[]{:S(2)}, u32[]{:S(2)}) async-start(bf16[16,48,512]{2,1,0:T(8,128)(2,1)} %bitcast.126), calls=%async_computation.1 | async-start | bytes 1572864 | tf_op jit(solution)/shard_map/all_to_all | solution.py:159
  56.1 12.1 %copy-start.25 = (bf16[48,384]{1,0:T(8,128)(2,1)S(1)}, bf16[48,384]{1,0:T(8,128)(2,1)}, u32[]{:S(2)}) copy-start(bf16[48,384]{1,0:T(8,128)(2,1)} %param.21) | copy-start | bytes 110596
  68.3 2.9 %copy-start.21 = (bf16[304,384]{1,0:T(8,128)(2,1)S(1)}, bf16[304,384]{1,0:T(8,128)(2,1)}, u32[]{:S(2)}) copy-start(bf16[304,384]{1,0:T(8,128)(2,1)} %param.18) | copy-start | bytes 700420
  71.7 1.9 %copy-start.5 = (bf16[304,384]{1,0:T(8,128)(2,1)}, bf16[304,384]{1,0:T(8,128)(2,1)S(1)}, u32[]{:S(2)}) copy-start(bf16[304,384]{1,0:T(8,128)(2,1)S(1)} %get-tuple-element.21) | copy-start | bytes 700420
  73.6 5.0 %collective-permute-start = (bf16[304,1536]{1,0:T(8,128)(2,1)}, bf16[304,1536]{1,0:T(8,128)(2,1)}, u32[]{:S(2)}, u32[]{:S(2)}) collective-permute-start(bf16[304,1536]{1,0:T(8,128)(2,1)} %broadcast_select_fusion.1), channel_id=1, source_target_pairs={{0,1},{1,0},{2,3},{3,2},{4,5},{5,4},{6,7},{7,6},{8,9},{9,8},{10,11... | collective-permute-start | bytes 2801672 | tf_op jit(solution)/shard_map/ppermute | solution.py:31
  82.4 13.7 %collective-permute-start.3 = (bf16[304,384]{1,0:T(8,128)(2,1)}, bf16[304,384]{1,0:T(8,128)(2,1)S(1)}, u32[]{:S(2)}, u32[]{:S(2)}) collective-permute-start(bf16[304,384]{1,0:T(8,128)(2,1)} %get-tuple-element.35), channel_id=1, source_target_pairs={{0,6},{1,7},{2,0},{3,1},{4,2},{5,3},{6,4},{7,5},{8,14},{9,15},{10,... | collective-permute-start | bytes 700424 | tf_op jit(solution)/shard_map/ppermute | solution.py:37
  86.2 10.0 %collective-permute-start.2 = (bf16[304,384]{1,0:T(8,128)(2,1)}, bf16[304,384]{1,0:T(8,128)(2,1)}, u32[]{:S(2)}, u32[]{:S(2)}) collective-permute-start(bf16[304,384]{1,0:T(8,128)(2,1)} %get-tuple-element.36), channel_id=1, source_target_pairs={{0,4},{1,5},{2,6},{3,7},{4,0},{5,1},{6,2},{7,3},{8,12},{9,13},{10,... | collective-permute-start | bytes 700424 | tf_op jit(solution)/shard_map/ppermute | solution.py:37
  86.2 13.9 %collective-permute-start.1 = (bf16[304,384]{1,0:T(8,128)(2,1)}, bf16[304,384]{1,0:T(8,128)(2,1)}, u32[]{:S(2)}, u32[]{:S(2)}) collective-permute-start(bf16[304,384]{1,0:T(8,128)(2,1)} %get-tuple-element.34), channel_id=1, source_target_pairs={{0,2},{1,3},{2,4},{3,5},{4,6},{5,7},{6,0},{7,1},{8,10},{9,11},{10,... | collective-permute-start | bytes 700424 | tf_op jit(solution)/shard_map/ppermute | solution.py:37
  101.4 15.9 %copy-start.19 = (bf16[304,384]{1,0:T(8,128)(2,1)}, bf16[304,384]{1,0:T(8,128)(2,1)S(1)}, u32[]{:S(2)}) copy-start(bf16[304,384]{1,0:T(8,128)(2,1)S(1)} %add_convert_fusion.3) | copy-start | bytes 700420
  101.4 6.6 %collective-permute-start.6 = (bf16[304,384]{1,0:T(8,128)(2,1)S(1)}, bf16[304,384]{1,0:T(8,128)(2,1)}, u32[]{:S(2)}, u32[]{:S(2)}) collective-permute-start(bf16[304,384]{1,0:T(8,128)(2,1)S(1)} %add_convert_fusion.3), channel_id=1, source_target_pairs={{0,6},{1,7},{2,0},{3,1},{4,2},{5,3},{6,4},{7,5},{8,14},{9,15},{10,... | collective-permute-start | bytes 700424 | tf_op jit(solution)/shard_map/ppermute | solution.py:51
  101.7 7.4 %collective-permute-start.5 = (bf16[304,384]{1,0:T(8,128)(2,1)S(1)}, bf16[304,384]{1,0:T(8,128)(2,1)}, u32[]{:S(2)}, u32[]{:S(2)}) collective-permute-start(bf16[304,384]{1,0:T(8,128)(2,1)S(1)} %add_convert_fusion.3), channel_id=1, source_target_pairs={{0,4},{1,5},{2,6},{3,7},{4,0},{5,1},{6,2},{7,3},{8,12},{9,13},{10,... | collective-permute-start | bytes 700424 | tf_op jit(solution)/shard_map/ppermute | solution.py:51
  102.2 13.7 %collective-permute-start.4 = (bf16[304,384]{1,0:T(8,128)(2,1)S(1)}, bf16[304,384]{1,0:T(8,128)(2,1)}, u32[]{:S(2)}, u32[]{:S(2)}) collective-permute-start(bf16[304,384]{1,0:T(8,128)(2,1)S(1)} %add_convert_fusion.3), channel_id=1, source_target_pairs={{0,2},{1,3},{2,4},{3,5},{4,6},{5,7},{6,0},{7,1},{8,10},{9,11},{10,... | collective-permute-start | bytes 700424 | tf_op jit(solution)/shard_map/ppermute | solution.py:51
  117.4 2.7 %collective-permute-start.7 = (bf16[304,1536]{1,0:T(8,128)(2,1)S(1)}, bf16[304,1536]{1,0:T(8,128)(2,1)S(1)}, u32[]{:S(2)}, u32[]{:S(2)}) collective-permute-start(bf16[304,1536]{1,0:T(8,128)(2,1)S(1)} %pad_maximum_fusion.3), channel_id=1, source_target_pairs={{0,1},{1,0},{2,3},{3,2},{4,5},{5,4},{6,7},{7,6},{8,9},{9,8},{10,11... | collective-permute-start | bytes 2801672 | tf_op jit(solution)/shard_map/ppermute | solution.py:56
  120.5 2.6 %copy-start.30 = (bf16[3072,512]{1,0:T(8,128)(2,1)S(1)}, bf16[3072,512]{1,0:T(8,128)(2,1)}, u32[]{:S(2)}) copy-start(bf16[3072,512]{1,0:T(8,128)(2,1)} %param.33) | copy-start | bytes 9437188
  120.6 2.6 %copy-start.32 = (f32[3072]{0:T(1024)S(1)}, f32[3072]{0:T(1024)}, u32[]{:S(2)}) copy-start(f32[3072]{0:T(1024)} %param.32) | copy-start | bytes 36868
  133.0 1.9 %copy-start.12 = (bf16[304,384]{1,0:T(8,128)(2,1)}, bf16[304,384]{1,0:T(8,128)(2,1)S(1)}, u32[]{:S(2)}) copy-start(bf16[304,384]{1,0:T(8,128)(2,1)S(1)} %get-tuple-element.13) | copy-start | bytes 700420
  133.0 2.3 %copy-start.28 = (s32[304,1]{0,1:T(1,128)S(1)}, s32[304,1]{0,1:T(1,128)}, u32[]{:S(2)}) copy-start(s32[304,1]{0,1:T(1,128)} %param.30) | copy-start | bytes 3652
  134.9 2.9 %collective-permute-start.8 = (bf16[304,1536]{1,0:T(8,128)(2,1)}, bf16[304,1536]{1,0:T(8,128)(2,1)}, u32[]{:S(2)}, u32[]{:S(2)}) collective-permute-start(bf16[304,1536]{1,0:T(8,128)(2,1)} %broadcast_select_fusion), channel_id=1, source_target_pairs={{0,1},{1,0},{2,3},{3,2},{4,5},{5,4},{6,7},{7,6},{8,9},{9,8},{10,11... | collective-permute-start | bytes 2801672 | tf_op jit(solution)/shard_map/ppermute | solution.py:31
  136.6 18.2 %copy-start.20 = (bf16[304,384]{1,0:T(8,128)(2,1)S(1)}, bf16[304,384]{1,0:T(8,128)(2,1)}, u32[]{:S(2)}) copy-start(bf16[304,384]{1,0:T(8,128)(2,1)} %copy-done.19) | copy-start | bytes 700420
  139.9 6.9 %collective-permute-start.11 = (bf16[304,384]{1,0:T(8,128)(2,1)S(1)}, bf16[304,384]{1,0:T(8,128)(2,1)S(1)}, u32[]{:S(2)}, u32[]{:S(2)}) collective-permute-start(bf16[304,384]{1,0:T(8,128)(2,1)S(1)} %get-tuple-element.28), channel_id=1, source_target_pairs={{0,6},{1,7},{2,0},{3,1},{4,2},{5,3},{6,4},{7,5},{8,14},{9,15},{10,... | collective-permute-start | bytes 700424 | tf_op jit(solution)/shard_map/ppermute | solution.py:37
  140.7 8.1 %collective-permute-start.10 = (bf16[304,384]{1,0:T(8,128)(2,1)S(1)}, bf16[304,384]{1,0:T(8,128)(2,1)S(1)}, u32[]{:S(2)}, u32[]{:S(2)}) collective-permute-start(bf16[304,384]{1,0:T(8,128)(2,1)S(1)} %get-tuple-element.29), channel_id=1, source_target_pairs={{0,4},{1,5},{2,6},{3,7},{4,0},{5,1},{6,2},{7,3},{8,12},{9,13},{10,... | collective-permute-start | bytes 700424 | tf_op jit(solution)/shard_map/ppermute | solution.py:37
  140.8 14.0 %collective-permute-start.9 = (bf16[304,384]{1,0:T(8,128)(2,1)S(1)}, bf16[304,384]{1,0:T(8,128)(2,1)S(1)}, u32[]{:S(2)}, u32[]{:S(2)}) collective-permute-start(bf16[304,384]{1,0:T(8,128)(2,1)S(1)} %get-tuple-element.27), channel_id=1, source_target_pairs={{0,2},{1,3},{2,4},{3,5},{4,6},{5,7},{6,0},{7,1},{8,10},{9,11},{10,... | collective-permute-start | bytes 700424 | tf_op jit(solution)/shard_map/ppermute | solution.py:37
  (15 other events, 22.8 us)

commit v5 on v4

--- a/solution.py
+++ b/solution.py
@@ -197,29 +197,39 @@
     pre_out = jnp.sum(
         jnp.where(head_mask[:, None, :], pre_mixed.reshape(heads_here, stretch_len, width_here), 0.0), axis=0
     ).astype(jnp.bfloat16)
+    dec_out, pre_out = lax.optimization_barrier((dec_out, pre_out))
     attn_rows = jnp.concatenate([dec_out, pre_out], axis=0)
-    projected = jnp.dot(attn_rows, out_weight, preferred_element_type=jnp.float32)
     head_me = lax.axis_index("head")
     col_start = head_me * width_here
-    own_cols = lax.dynamic_slice_in_dim(projected, col_start, width_here, 1) + hidden_in.astype(
-        jnp.float32
-    )
-    contribution = lax.dynamic_update_slice_in_dim(projected, own_cols, col_start, 1)
-    own_residual = pair_then_z_scatter(contribution.astype(jnp.bfloat16))
-    residual = z_then_pair_gather(own_residual.astype(jnp.bfloat16))
-
-    residual_wide = residual.astype(jnp.float32)
-    squares = jnp.mean(jnp.square(residual_wide), axis=-1, keepdims=True)
-    normed = (residual_wide * lax.rsqrt(squares + eps_norm) * norm_gain).astype(jnp.bfloat16)
-    gate_act = jnp.dot(normed, gate_weight, preferred_element_type=jnp.float32)
-    up_act = jnp.dot(normed, up_weight, preferred_element_type=jnp.float32)
-    hidden = (jax.nn.silu(gate_act) * up_act).astype(jnp.bfloat16)
-    down_part = jnp.dot(hidden, down_weight, preferred_element_type=jnp.float32).astype(jnp.bfloat16)
-    down_cols = pair_then_z_scatter(down_part)
-    own_wide = own_residual.astype(jnp.bfloat16).astype(jnp.float32)
-    out_cols = (own_wide + down_cols).astype(jnp.bfloat16)
-
-    row_count = residual.shape[0]
+
+    def feed_forward(attn_chunk, hidden_chunk):
+        projected = jnp.dot(attn_chunk, out_weight, preferred_element_type=jnp.float32)
+        own_cols = lax.dynamic_slice_in_dim(projected, col_start, width_here, 1) + hidden_chunk.astype(
+            jnp.float32
+        )
+        contribution = lax.dynamic_update_slice_in_dim(projected, own_cols, col_start, 1)
+        own_residual = pair_then_z_scatter(contribution.astype(jnp.bfloat16)).astype(jnp.bfloat16)
+        residual = z_then_pair_gather(own_residual)
+        residual_wide = residual.astype(jnp.float32)
+        squares = jnp.mean(jnp.square(residual_wide), axis=-1, keepdims=True)
+        normed = (residual_wide * lax.rsqrt(squares + eps_norm) * norm_gain).astype(jnp.bfloat16)
+        gate_act = jnp.dot(normed, gate_weight, preferred_element_type=jnp.float32)
+        up_act = jnp.dot(normed, up_weight, preferred_element_type=jnp.float32)
+        hidden = (jax.nn.silu(gate_act) * up_act).astype(jnp.bfloat16)
+        down_part = jnp.dot(hidden, down_weight, preferred_element_type=jnp.float32).astype(jnp.bfloat16)
+        down_cols = pair_then_z_scatter(down_part)
+        return (own_residual.astype(jnp.float32) + down_cols).astype(jnp.bfloat16)
+
+    row_count = hidden_in.shape[0]
+    half = row_count // 2
+    out_cols = jnp.concatenate(
+        [
+            feed_forward(attn_rows[:half], hidden_in[:half]),
+            feed_forward(attn_rows[half:], hidden_in[half:]),
+        ],
+        axis=0,
+    )
+
     slot_rows = 8 * ((2 * row_count + 8 * req_count - 1) // (8 * req_count))
     owners = row_owner[:, 0]
     onehot_owner = (owners[:, None] == jnp.arange(req_count, dtype=jnp.int32)[None, :]).astype(

time: 183 us -> 173 us (0.945)
  waiting for transfers between devices: 54.7 us -> 20.7 us
  starting transfers between devices: 25.4 us -> 47.6 us
    ppermute x6 -> x12, waiting for transfers between devices: 25.8 us -> 7.1 us  [pair_then_z_scatter(): acc = acc + lax.ppermute(piece, 'head', perm).astype(jnp.float32)]
    ppermute x3 -> x6, waiting for transfers between devices: 12.9 us -> 2.16 us  [z_then_pair_gather(): parts.append(lax.ppermute(y, 'head', perm))]
    ppermute x6 -> x12, starting transfers between devices: 6 us -> 16.7 us  [pair_then_z_scatter(): acc = acc + lax.ppermute(piece, 'head', perm).astype(jnp.float32)]
    ppermute x3 -> x6, starting transfers between devices: 1.54 us -> 8.05 us  [z_then_pair_gather(): parts.append(lax.ppermute(y, 'head', perm))]
    unnamed x10 -> x17, other arithmetic: 1.54 us -> 7.9 us
    ppermute x1 -> x2, starting transfers between devices: 0.57 us -> 4.81 us  [z_then_pair_gather(): got = lax.ppermute(in_order, 'head', [(i, i ^ 1) for i in range(n)])]
    dot_general x2, matrix products: 4.48 us -> 1.15 us  [on_device(): jnp.dot(weights, cache_value[group_pos], preferred_element_type=jnp.float32)]
    dot_general x3 -> x6, matrix products: 10.9 us -> 14.1 us  [the longest x2 8.89 us: feed_forward(): jnp.dot(hidden, down_weight, preferred_element_type=jnp.float32)]
  transfers between devices with their start and end apart: 14 -> 26, of which waited for: 12 -> 11; matrix products, arithmetic and copies ran while one was open for 12% -> 29% of each run, Pallas kernels for 0% -> 0%
where the time goes in v5:
time: 173 us; the launch traced here: 172 us
  starting transfers between devices  47.6 us (28%)
  matrix products  39 us (23%)
  blocking collectives  27.6 us (16%)
  other arithmetic  23.4 us (14%)
  waiting for transfers between devices  20.7 us (12%)
  local copies, waits for them, and re-layouts  11.7 us (7%)
  between operations  1.77 us (1%)
    ppermute x12, starting transfers between devices, pair_then_z_scatter(): acc = acc + lax.ppermute(piece, 'head', perm).astype(jnp.float32)  16.7 us
    all_to_all x1, blocking collectives, on_device(): lax.all_to_all(arrived, 'head', split_axis=0, concat_axis=1, tiled=True)  15.7 us
    all_to_all x1, blocking collectives, on_device(): lax.all_to_all(outgoing, 'req', split_axis=0, concat_axis=0, tiled=True)  11.9 us
    all_to_all x1, waiting for transfers between devices, on_device(): lax.all_to_all(going_back, 'req', split_axis=0, concat_axis=0, tiled=True)  10.4 us
    dot_general x2, matrix products, feed_forward(): jnp.dot(hidden, down_weight, preferred_element_type=jnp.float32)  8.89 us
    ppermute x6, starting transfers between devices, z_then_pair_gather(): parts.append(lax.ppermute(y, 'head', perm))  8.05 us
    unnamed x17, other arithmetic  7.9 us
    all_to_all x1, starting transfers between devices, on_device(): lax.all_to_all(outgoing_q, 'req', split_axis=0, concat_axis=0, tiled=True)  7.62 us
  transfers between devices with their start and end apart: 26, of which 11 were waited for; matrix products, arithmetic and copies ran while one was open for 29% of the time, Pallas kernels for 0%

profile of v5, /device:TPU:1, one launch (start us, length us, event | category | flops | bytes accessed | tf_op | source)
XLA Modules:
  0.0 171.8 jit_solution(17130769494660819772)
XLA Ops:
  2.4 1.9 %convolution_convert_fusion.3 = bf16[768,384]{1,0:T(8,128)(2,1)} fusion(bf16[48,384]{1,0:T(8,128)(2,1)} %param.19, s32[48]{0:T(128)S(1)} %dynamic-slice_add_fusion), kind=kOutput, calls=%fused_computation.48 | convolution fusion | flops 28643328 | bytes 626880 | tf_op jit(solution)/shard_map/dot_general | solution.py:108
  4.3 7.6 %all-to-all-start = ((bf16[16,48,384]{2,1,0:T(8,128)(2,1)}), bf16[16,48,384]{2,1,0:T(8,128)(2,1)}, u32[]{:S(2)}, u32[]{:S(2)}) async-start(bf16[16,48,384]{2,1,0:T(8,128)(2,1)} %bitcast.136), calls=%async_computation | async-start | bytes 1179648 | tf_op jit(solution)/shard_map/all_to_all | solution.py:109
  16.3 4.0 %fusion = (f32[1024]{0:T(1024)S(1)}, f32[1024,2048]{1,0:T(8,128)S(1)}) fusion(pred[2048]{0:T(1024)(128)(4,1)S(1)} %iota_compare_fusion.12, bf16[1024,384]{1,0:T(8,128)(2,1)S(1)} %bitcast.144, bf16[2,2048,384]{2,1,0:T(8,128)(2,1)} %param.25), kind=kOutput, calls=%fused_computation.3 | convolution fusion | flops 1616903168 | bytes 10754048 | tf_op jit(solution)/shard_map/dot_general | solution.py:181
  20.8 2.2 %fusion.1 = f32[1024]{0:T(1024)S(1)} fusion(f32[1024,2048]{1,0:T(8,128)S(1)} %get-tuple-element.82, f32[1024]{0:T(1024)S(1)} %max.12, pred[2048]{0:T(1024)(128)(4,1)S(1)} %iota_compare_fusion.12), kind=kLoop, calls=%fused_computation.4 | loop fusion | flops 8387584 | bytes 8398848 | tf_op jit(solution)/shard_map/reduce_sum | solution.py:193
  25.3 7.4 %fusion.2 = f32[1024,384]{1,0:T(8,128)} fusion(f32[1024,2048]{1,0:T(8,128)} %copy-done.2, f32[1024]{0:T(1024)S(1)} %add.298, f32[1024]{0:T(1024)S(1)} %max.12, pred[2048]{0:T(1024)(128)(4,1)S(1)} %iota_compare_fusion.12, bf16[2,2048,384]{2,1,0:T(8,128)(2,1)} %param.26), kind=kOutput, calls=%fused_computation.5 | convolution fusion | flops 1621098496 | bytes 11544576 | tf_op jit(solution)/shard_map/dot_general | solution.py:194
  34.9 2.2 %fusion.142 = (f32[192]{0:T(256)S(1)}, f32[192,2048]{1,0:T(8,128)S(1)}) fusion(bf16[192,384]{1,0:T(8,128)(2,1)S(1)} %bitcast.151, bf16[2,2048,384]{2,1,0:T(8,128)(2,1)} %param.25, pred[2048]{0:T(1024)(128)(4,1)S(1)} %iota_compare_fusion.14), kind=kOutput, calls=%fused_computation.278 | convolution fusion | flops 303169344 | bytes 3296000 | tf_op jit(solution)/shard_map/dot_general | solution.py:135
  43.6 1.4 convolution_convert_fusion.2
  44.9 6.7 %all-to-all-start.1 = ((bf16[16,48,512]{2,1,0:T(8,128)(2,1)}), bf16[16,48,512]{2,1,0:T(8,128)(2,1)}, u32[]{:S(2)}, u32[]{:S(2)}) async-start(bf16[16,48,512]{2,1,0:T(8,128)(2,1)} %bitcast.143), calls=%async_computation.1 | async-start | bytes 1572864 | tf_op jit(solution)/shard_map/all_to_all | solution.py:159
  51.6 2.3 %convolution_add_fusion = f32[1024,384]{1,0:T(8,128)S(1)} fusion(f32[1024,384]{1,0:T(8,128)} %fusion.2, bf16[256,384]{1,0:T(8,128)(2,1)} %param.24, f32[1024,256]{0,1:T(8,128)} %copy-done.27, f32[1024]{0:T(1024)S(1)} %add.298, f32[1024]{0:T(1024)S(1)} %max.12), kind=kOutput, calls=%fused_computation.38 | convolution fusion | flops 202506240 | bytes 4399104 | tf_op jit(solution)/shard_map/dot_general | solution.py:196
  54.1 10.4 %all-to-all-done.1 = bf16[16,48,512]{2,1,0:T(8,128)(2,1)} async-done(((bf16[16,48,512]{2,1,0:T(8,128)(2,1)}), bf16[16,48,512]{2,1,0:T(8,128)(2,1)}, u32[]{:S(2)}, u32[]{:S(2)}) %all-to-all-start.1) | async-done | bytes 786464 | tf_op jit(solution)/shard_map/all_to_all | solution.py:159
  64.5 1.4 fusion.48
  66.3 2.5 %fusion.87 = f32[152,3072]{1,0:T(8,128)S(1)} fusion(bf16[384,3072]{1,0:T(8,128)(2,1)} %param.31, bf16[256,384]{1,0:T(8,128)(2,1)S(1)} %select_reduce_fusion), kind=kOutput, calls=%fused_computation.149 | convolution fusion | flops 358612992 | bytes 4343808 | tf_op jit(solution)/shard_map/dot_general | solution.py:206
  70.2 2.6 %collective-permute-start = (bf16[152,1536]{1,0:T(8,128)(2,1)S(1)}, bf16[152,1536]{1,0:T(8,128)(2,1)S(1)}, u32[]{:S(2)}, u32[]{:S(2)}) collective-permute-start(bf16[152,1536]{1,0:T(8,128)(2,1)S(1)} %broadcast_select_fusion.4), channel_id=1, source_target_pairs={{0,1},{1,0},{2,3},{3,2},{4,5},{5,4},{6,7},{7,6},{8,9},{9,8},{10,11... | collective-permute-start | bytes 1400840 | tf_op jit(solution)/shard_map/ppermute | solution.py:31
  74.4 1.7 collective-permute-start.1
  76.1 3.3 %collective-permute-start.2 = (bf16[152,384]{1,0:T(8,128)(2,1)S(1)}, bf16[152,384]{1,0:T(8,128)(2,1)S(1)}, u32[]{:S(2)}, u32[]{:S(2)}) collective-permute-start(bf16[152,384]{1,0:T(8,128)(2,1)S(1)} %get-tuple-element.56), channel_id=1, source_target_pairs={{0,4},{1,5},{2,6},{3,7},{4,0},{5,1},{6,2},{7,3},{8,12},{9,13},{10,... | collective-permute-start | bytes 350216 | tf_op jit(solution)/shard_map/ppermute | solution.py:37
  81.7 2.0 %collective-permute-start.15 = (bf16[152,384]{1,0:T(8,128)(2,1)S(1)}, bf16[152,384]{1,0:T(8,128)(2,1)S(1)}, u32[]{:S(2)}, u32[]{:S(2)}) collective-permute-start(bf16[152,384]{1,0:T(8,128)(2,1)S(1)} %get-tuple-element.65), channel_id=1, source_target_pairs={{0,6},{1,7},{2,0},{3,1},{4,2},{5,3},{6,4},{7,5},{8,14},{9,15},{10,... | collective-permute-start | bytes 350216 | tf_op jit(solution)/shard_map/ppermute | solution.py:37
  84.9 1.6 collective-permute-start.4
  86.5 1.9 %collective-permute-start.5 = (bf16[152,384]{1,0:T(8,128)(2,1)S(1)}, bf16[152,384]{1,0:T(8,128)(2,1)S(1)}, u32[]{:S(2)}, u32[]{:S(2)}) collective-permute-start(bf16[152,384]{1,0:T(8,128)(2,1)S(1)} %add_convert_fusion.7), channel_id=1, source_target_pairs={{0,4},{1,5},{2,6},{3,7},{4,0},{5,1},{6,2},{7,3},{8,12},{9,13},{10,... | collective-permute-start | bytes 350216 | tf_op jit(solution)/shard_map/ppermute | solution.py:51
  90.0 1.5 collective-permute-start.16
  91.4 1.9 %collective-permute-start.17 = (bf16[152,384]{1,0:T(8,128)(2,1)S(1)}, bf16[152,384]{1,0:T(8,128)(2,1)S(1)}, u32[]{:S(2)}, u32[]{:S(2)}) collective-permute-start(bf16[152,384]{1,0:T(8,128)(2,1)S(1)} %add_convert_fusion.5), channel_id=1, source_target_pairs={{0,4},{1,5},{2,6},{3,7},{4,0},{5,1},{6,2},{7,3},{8,12},{9,13},{10,... | collective-permute-start | bytes 350216 | tf_op jit(solution)/shard_map/ppermute | solution.py:51
  95.1 2.4 %collective-permute-start.7 = (bf16[152,1536]{1,0:T(8,128)(2,1)S(1)}, bf16[152,1536]{1,0:T(8,128)(2,1)S(1)}, u32[]{:S(2)}, u32[]{:S(2)}) collective-permute-start(bf16[152,1536]{1,0:T(8,128)(2,1)S(1)} %pad_maximum_fusion.3), channel_id=1, source_target_pairs={{0,1},{1,0},{2,3},{3,2},{4,5},{5,4},{6,7},{7,6},{8,9},{9,8},{10,11... | collective-permute-start | bytes 1400840 | tf_op jit(solution)/shard_map/ppermute | solution.py:56
  99.7 2.4 %collective-permute-start.19 = (bf16[152,1536]{1,0:T(8,128)(2,1)}, bf16[152,1536]{1,0:T(8,128)(2,1)}, u32[]{:S(2)}, u32[]{:S(2)}) collective-permute-start(bf16[152,1536]{1,0:T(8,128)(2,1)} %pad_maximum_fusion.9), channel_id=1, source_target_pairs={{0,1},{1,0},{2,3},{3,2},{4,5},{5,4},{6,7},{7,6},{8,9},{9,8},{10,11... | collective-permute-start | bytes 1400840 | tf_op jit(solution)/shard_map/ppermute | solution.py:56
  103.4 1.4 fusion.71
  104.9 4.4 %convolution_convert_fusion.1 = bf16[152,3072]{1,0:T(8,128)(2,1)} fusion(bf16[512,3072]{1,0:T(8,128)(2,1)S(1)} %copy-done, bf16[3072,512]{1,0:T(8,128)(2,1)} %param.34, f32[152,512]{1,0:T(8,128)} %fusion.71, bf16[152,3072]{1,0:T(8,128)(2,1)} %copy-done.5, f32[3072]{0:T(1024)S(1)} %copy-done.40, f32[152]{0:T(256)S(1)} %add_rsqrt_fusion.1), kind=kOutput, calls=%fused_computation.7 | convolution fusion | flops 959102976 | bytes 8483424 | tf_op jit(solution)/shard_map/dot_general | solution.py:219
  109.3 1.4 fusion.133
  122.0 4.4 %convolution_convert_fusion = bf16[152,3072]{1,0:T(8,128)(2,1)} fusion(bf16[512,3072]{1,0:T(8,128)(2,1)S(1)} %copy-done, bf16[3072,512]{1,0:T(8,128)(2,1)} %param.34, f32[152,512]{1,0:T(8,128)S(1)} %fusion.67, bf16[152,3072]{1,0:T(8,128)(2,1)} %copy-done.6, f32[152]{0:T(256)S(1)} %add_rsqrt_fusion, f32[3072]{0:T(1024)S(1)} %copy-done.40), kind=kOutput, calls=%fused_computation.6 | convolution fusion | flops 959102976 | bytes 8483424 | tf_op jit(solution)/shard_map/dot_general | solution.py:219
  126.5 1.4 fusion.135
  129.7 2.0 %collective-permute-start.10 = (bf16[152,384]{1,0:T(8,128)(2,1)S(1)}, bf16[152,384]{1,0:T(8,128)(2,1)S(1)}, u32[]{:S(2)}, u32[]{:S(2)}) collective-permute-start(bf16[152,384]{1,0:T(8,128)(2,1)S(1)} %get-tuple-element.49), channel_id=1, source_target_pairs={{0,4},{1,5},{2,6},{3,7},{4,0},{5,1},{6,2},{7,3},{8,12},{9,13},{10,... | collective-permute-start | bytes 350216 | tf_op jit(solution)/shard_map/ppermute | solution.py:37
  134.0 3.2 %collective-permute-start.22 = (bf16[152,384]{1,0:T(8,128)(2,1)S(1)}, bf16[152,384]{1,0:T(8,128)(2,1)S(1)}, u32[]{:S(2)}, u32[]{:S(2)}) collective-permute-start(bf16[152,384]{1,0:T(8,128)(2,1)S(1)} %get-tuple-element.59), channel_id=1, source_target_pairs={{0,4},{1,5},{2,6},{3,7},{4,0},{5,1},{6,2},{7,3},{8,12},{9,13},{10,... | collective-permute-start | bytes 350216 | tf_op jit(solution)/shard_map/ppermute | solution.py:37
  138.5 3.0 %collective-permute-done.21 = bf16[152,384]{1,0:T(8,128)(2,1)S(1)} collective-permute-done((bf16[152,384]{1,0:T(8,128)(2,1)S(1)}, bf16[152,384]{1,0:T(8,128)(2,1)S(1)}, u32[]{:S(2)}, u32[]{:S(2)}) %collective-permute-start.21) | collective-permute-done | bytes 116768 | tf_op jit(solution)/shard_map/ppermute | solution.py:37
  143.3 11.9 %all_to_all.52 = bf16[16,40,384]{2,1,0:T(8,128)(2,1)S(1)} all-to-all(bf16[16,40,384]{2,1,0:T(8,128)(2,1)S(1)} %bitcast.148), channel_id=1, replica_groups=mesh['req'=16,'head'=8] {'req'}, dimensions={0} | all-to-all | bytes 983040 | tf_op jit(solution)/shard_map/all_to_all | solution.py:244
  155.2 15.7 %all_to_all.53 = bf16[8,80,384]{2,1,0:T(8,128)(2,1)S(1)} all-to-all(bf16[8,80,384]{2,1,0:T(8,128)(2,1)S(1)} %bitcast.137), channel_id=1, replica_groups=mesh['req'=16,'head'=8] {'head'}, dimensions={0} | all-to-all | bytes 983040 | tf_op jit(solution)/shard_map/all_to_all | solution.py:245
  (242 shorter events, 49.7 us)
Async XLA Ops:
  0.0 104.9 %copy-start = (bf16[512,3072]{1,0:T(8,128)(2,1)S(1)}, bf16[512,3072]{1,0:T(8,128)(2,1)}, u32[]{:S(2)}) copy-start(bf16[512,3072]{1,0:T(8,128)(2,1)} %param.35) | copy-start | bytes 9437188
  0.0 13.9 %copy-start.33 = (s32[2]{0:T(128)S(1)}, s32[2]{0:T(128)}, u32[]{:S(2)}) copy-start(s32[2]{0:T(128)} %param.28) | copy-start | bytes 28
  0.0 16.1 %copy-start.29 = (bf16[256,384]{1,0:T(8,128)(2,1)S(1)}, bf16[256,384]{1,0:T(8,128)(2,1)}, u32[]{:S(2)}) copy-start(bf16[256,384]{1,0:T(8,128)(2,1)} %param.22) | copy-start | bytes 589828
  4.3 29.2 %all-to-all-start = ((bf16[16,48,384]{2,1,0:T(8,128)(2,1)}), bf16[16,48,384]{2,1,0:T(8,128)(2,1)}, u32[]{:S(2)}, u32[]{:S(2)}) async-start(bf16[16,48,384]{2,1,0:T(8,128)(2,1)} %bitcast.136), calls=%async_computation | async-start | bytes 1179648 | tf_op jit(solution)/shard_map/all_to_all | solution.py:109
  44.9 19.5 %all-to-all-start.1 = ((bf16[16,48,512]{2,1,0:T(8,128)(2,1)}), bf16[16,48,512]{2,1,0:T(8,128)(2,1)}, u32[]{:S(2)}, u32[]{:S(2)}) async-start(bf16[16,48,512]{2,1,0:T(8,128)(2,1)} %bitcast.143), calls=%async_computation.1 | async-start | bytes 1572864 | tf_op jit(solution)/shard_map/all_to_all | solution.py:159
  54.0 12.3 %copy-start.31 = (bf16[48,384]{1,0:T(8,128)(2,1)S(1)}, bf16[48,384]{1,0:T(8,128)(2,1)}, u32[]{:S(2)}) copy-start(bf16[48,384]{1,0:T(8,128)(2,1)} %param.21) | copy-start | bytes 110596
  70.2 4.0 %collective-permute-start = (bf16[152,1536]{1,0:T(8,128)(2,1)S(1)}, bf16[152,1536]{1,0:T(8,128)(2,1)S(1)}, u32[]{:S(2)}, u32[]{:S(2)}) collective-permute-start(bf16[152,1536]{1,0:T(8,128)(2,1)S(1)} %broadcast_select_fusion.4), channel_id=1, source_target_pairs={{0,1},{1,0},{2,3},{3,2},{4,5},{5,4},{6,7},{7,6},{8,9},{9,8},{10,11... | collective-permute-start | bytes 1400840 | tf_op jit(solution)/shard_map/ppermute | solution.py:31
  73.1 7.1 %collective-permute-start.12 = (bf16[152,1536]{1,0:T(8,128)(2,1)S(1)}, bf16[152,1536]{1,0:T(8,128)(2,1)S(1)}, u32[]{:S(2)}, u32[]{:S(2)}) collective-permute-start(bf16[152,1536]{1,0:T(8,128)(2,1)S(1)} %broadcast_select_fusion.2), channel_id=1, source_target_pairs={{0,1},{1,0},{2,3},{3,2},{4,5},{5,4},{6,7},{7,6},{8,9},{9,8},{10,11... | collective-permute-start | bytes 1400840 | tf_op jit(solution)/shard_map/ppermute | solution.py:31
  74.4 7.2 %collective-permute-start.1 = (bf16[152,384]{1,0:T(8,128)(2,1)S(1)}, bf16[152,384]{1,0:T(8,128)(2,1)S(1)}, u32[]{:S(2)}, u32[]{:S(2)}) collective-permute-start(bf16[152,384]{1,0:T(8,128)(2,1)S(1)} %get-tuple-element.54), channel_id=1, source_target_pairs={{0,2},{1,3},{2,4},{3,5},{4,6},{5,7},{6,0},{7,1},{8,10},{9,11},{10,... | collective-permute-start | bytes 350216 | tf_op jit(solution)/shard_map/ppermute | solution.py:37
  76.1 8.7 %collective-permute-start.2 = (bf16[152,384]{1,0:T(8,128)(2,1)S(1)}, bf16[152,384]{1,0:T(8,128)(2,1)S(1)}, u32[]{:S(2)}, u32[]{:S(2)}) collective-permute-start(bf16[152,384]{1,0:T(8,128)(2,1)S(1)} %get-tuple-element.56), channel_id=1, source_target_pairs={{0,4},{1,5},{2,6},{3,7},{4,0},{5,1},{6,2},{7,3},{8,12},{9,13},{10,... | collective-permute-start | bytes 350216 | tf_op jit(solution)/shard_map/ppermute | solution.py:37
  79.5 5.4 %collective-permute-start.3 = (bf16[152,384]{1,0:T(8,128)(2,1)S(1)}, bf16[152,384]{1,0:T(8,128)(2,1)S(1)}, u32[]{:S(2)}, u32[]{:S(2)}) collective-permute-start(bf16[152,384]{1,0:T(8,128)(2,1)S(1)} %get-tuple-element.55), channel_id=1, source_target_pairs={{0,6},{1,7},{2,0},{3,1},{4,2},{5,3},{6,4},{7,5},{8,14},{9,15},{10,... | collective-permute-start | bytes 350216 | tf_op jit(solution)/shard_map/ppermute | solution.py:37
  80.4 8.0 %collective-permute-start.13 = (bf16[152,384]{1,0:T(8,128)(2,1)S(1)}, bf16[152,384]{1,0:T(8,128)(2,1)S(1)}, u32[]{:S(2)}, u32[]{:S(2)}) collective-permute-start(bf16[152,384]{1,0:T(8,128)(2,1)S(1)} %get-tuple-element.64), channel_id=1, source_target_pairs={{0,2},{1,3},{2,4},{3,5},{4,6},{5,7},{6,0},{7,1},{8,10},{9,11},{10,... | collective-permute-start | bytes 350216 | tf_op jit(solution)/shard_map/ppermute | solution.py:37
  81.2 8.6 %collective-permute-start.14 = (bf16[152,384]{1,0:T(8,128)(2,1)S(1)}, bf16[152,384]{1,0:T(8,128)(2,1)S(1)}, u32[]{:S(2)}, u32[]{:S(2)}) collective-permute-start(bf16[152,384]{1,0:T(8,128)(2,1)S(1)} %get-tuple-element.66), channel_id=1, source_target_pairs={{0,4},{1,5},{2,6},{3,7},{4,0},{5,1},{6,2},{7,3},{8,12},{9,13},{10,... | collective-permute-start | bytes 350216 | tf_op jit(solution)/shard_map/ppermute | solution.py:37
  81.7 8.2 %collective-permute-start.15 = (bf16[152,384]{1,0:T(8,128)(2,1)S(1)}, bf16[152,384]{1,0:T(8,128)(2,1)S(1)}, u32[]{:S(2)}, u32[]{:S(2)}) collective-permute-start(bf16[152,384]{1,0:T(8,128)(2,1)S(1)} %get-tuple-element.65), channel_id=1, source_target_pairs={{0,6},{1,7},{2,0},{3,1},{4,2},{5,3},{6,4},{7,5},{8,14},{9,15},{10,... | collective-permute-start | bytes 350216 | tf_op jit(solution)/shard_map/ppermute | solution.py:37
  84.9 10.1 %copy-start.23 = (bf16[152,384]{1,0:T(8,128)(2,1)}, bf16[152,384]{1,0:T(8,128)(2,1)S(1)}, u32[]{:S(2)}) copy-start(bf16[152,384]{1,0:T(8,128)(2,1)S(1)} %add_convert_fusion.7) | copy-start | bytes 350212
  84.9 8.4 %collective-permute-start.4 = (bf16[152,384]{1,0:T(8,128)(2,1)S(1)}, bf16[152,384]{1,0:T(8,128)(2,1)S(1)}, u32[]{:S(2)}, u32[]{:S(2)}) collective-permute-start(bf16[152,384]{1,0:T(8,128)(2,1)S(1)} %add_convert_fusion.7), channel_id=1, source_target_pairs={{0,2},{1,3},{2,4},{3,5},{4,6},{5,7},{6,0},{7,1},{8,10},{9,11},{10,... | collective-permute-start | bytes 350216 | tf_op jit(solution)/shard_map/ppermute | solution.py:51
  86.5 8.3 %collective-permute-start.5 = (bf16[152,384]{1,0:T(8,128)(2,1)S(1)}, bf16[152,384]{1,0:T(8,128)(2,1)S(1)}, u32[]{:S(2)}, u32[]{:S(2)}) collective-permute-start(bf16[152,384]{1,0:T(8,128)(2,1)S(1)} %add_convert_fusion.7), channel_id=1, source_target_pairs={{0,4},{1,5},{2,6},{3,7},{4,0},{5,1},{6,2},{7,3},{8,12},{9,13},{10,... | collective-permute-start | bytes 350216 | tf_op jit(solution)/shard_map/ppermute | solution.py:51
  88.4 6.4 %collective-permute-start.6 = (bf16[152,384]{1,0:T(8,128)(2,1)S(1)}, bf16[152,384]{1,0:T(8,128)(2,1)S(1)}, u32[]{:S(2)}, u32[]{:S(2)}) collective-permute-start(bf16[152,384]{1,0:T(8,128)(2,1)S(1)} %add_convert_fusion.7), channel_id=1, source_target_pairs={{0,6},{1,7},{2,0},{3,1},{4,2},{5,3},{6,4},{7,5},{8,14},{9,15},{10,... | collective-permute-start | bytes 350216 | tf_op jit(solution)/shard_map/ppermute | solution.py:51
  90.0 7.9 %collective-permute-start.16 = (bf16[152,384]{1,0:T(8,128)(2,1)S(1)}, bf16[152,384]{1,0:T(8,128)(2,1)S(1)}, u32[]{:S(2)}, u32[]{:S(2)}) collective-permute-start(bf16[152,384]{1,0:T(8,128)(2,1)S(1)} %add_convert_fusion.5), channel_id=1, source_target_pairs={{0,2},{1,3},{2,4},{3,5},{4,6},{5,7},{6,0},{7,1},{8,10},{9,11},{10,... | collective-permute-start | bytes 350216 | tf_op jit(solution)/shard_map/ppermute | solution.py:51
  91.4 7.3 %collective-permute-start.17 = (bf16[152,384]{1,0:T(8,128)(2,1)S(1)}, bf16[152,384]{1,0:T(8,128)(2,1)S(1)}, u32[]{:S(2)}, u32[]{:S(2)}) collective-permute-start(bf16[152,384]{1,0:T(8,128)(2,1)S(1)} %add_convert_fusion.5), channel_id=1, source_target_pairs={{0,4},{1,5},{2,6},{3,7},{4,0},{5,1},{6,2},{7,3},{8,12},{9,13},{10,... | collective-permute-start | bytes 350216 | tf_op jit(solution)/shard_map/ppermute | solution.py:51
  93.3 5.4 %collective-permute-start.18 = (bf16[152,384]{1,0:T(8,128)(2,1)S(1)}, bf16[152,384]{1,0:T(8,128)(2,1)S(1)}, u32[]{:S(2)}, u32[]{:S(2)}) collective-permute-start(bf16[152,384]{1,0:T(8,128)(2,1)S(1)} %add_convert_fusion.5), channel_id=1, source_target_pairs={{0,6},{1,7},{2,0},{3,1},{4,2},{5,3},{6,4},{7,5},{8,14},{9,15},{10,... | collective-permute-start | bytes 350216 | tf_op jit(solution)/shard_map/ppermute | solution.py:51
  95.1 7.0 %collective-permute-start.7 = (bf16[152,1536]{1,0:T(8,128)(2,1)S(1)}, bf16[152,1536]{1,0:T(8,128)(2,1)S(1)}, u32[]{:S(2)}, u32[]{:S(2)}) collective-permute-start(bf16[152,1536]{1,0:T(8,128)(2,1)S(1)} %pad_maximum_fusion.3), channel_id=1, source_target_pairs={{0,1},{1,0},{2,3},{3,2},{4,5},{5,4},{6,7},{7,6},{8,9},{9,8},{10,11... | collective-permute-start | bytes 1400840 | tf_op jit(solution)/shard_map/ppermute | solution.py:56
  99.7 13.1 %collective-permute-start.19 = (bf16[152,1536]{1,0:T(8,128)(2,1)}, bf16[152,1536]{1,0:T(8,128)(2,1)}, u32[]{:S(2)}, u32[]{:S(2)}) collective-permute-start(bf16[152,1536]{1,0:T(8,128)(2,1)} %pad_maximum_fusion.9), channel_id=1, source_target_pairs={{0,1},{1,0},{2,3},{3,2},{4,5},{5,4},{6,7},{7,6},{8,9},{9,8},{10,11... | collective-permute-start | bytes 1400840 | tf_op jit(solution)/shard_map/ppermute | solution.py:56
  111.8 16.5 %collective-permute-start.8 = (bf16[152,1536]{1,0:T(8,128)(2,1)}, bf16[152,1536]{1,0:T(8,128)(2,1)}, u32[]{:S(2)}, u32[]{:S(2)}) collective-permute-start(bf16[152,1536]{1,0:T(8,128)(2,1)} %broadcast_select_fusion.3), channel_id=1, source_target_pairs={{0,1},{1,0},{2,3},{3,2},{4,5},{5,4},{6,7},{7,6},{8,9},{9,8},{10,11... | collective-permute-start | bytes 1400840 | tf_op jit(solution)/shard_map/ppermute | solution.py:31
  128.1 5.1 %collective-permute-start.20 = (bf16[152,1536]{1,0:T(8,128)(2,1)S(1)}, bf16[152,1536]{1,0:T(8,128)(2,1)S(1)}, u32[]{:S(2)}, u32[]{:S(2)}) collective-permute-start(bf16[152,1536]{1,0:T(8,128)(2,1)S(1)} %broadcast_select_fusion.1), channel_id=1, source_target_pairs={{0,1},{1,0},{2,3},{3,2},{4,5},{5,4},{6,7},{7,6},{8,9},{9,8},{10,11... | collective-permute-start | bytes 1400840 | tf_op jit(solution)/shard_map/ppermute | solution.py:31
  129.6 13.2 %copy-start.26 = (bf16[152,384]{1,0:T(8,128)(2,1)S(1)}, bf16[152,384]{1,0:T(8,128)(2,1)}, u32[]{:S(2)}) copy-start(bf16[152,384]{1,0:T(8,128)(2,1)} %copy-done.25) | copy-start | bytes 350212
  129.7 7.6 %collective-permute-start.10 = (bf16[152,384]{1,0:T(8,128)(2,1)S(1)}, bf16[152,384]{1,0:T(8,128)(2,1)S(1)}, u32[]{:S(2)}, u32[]{:S(2)}) collective-permute-start(bf16[152,384]{1,0:T(8,128)(2,1)S(1)} %get-tuple-element.49), channel_id=1, source_target_pairs={{0,4},{1,5},{2,6},{3,7},{4,0},{5,1},{6,2},{7,3},{8,12},{9,13},{10,... | collective-permute-start | bytes 350216 | tf_op jit(solution)/shard_map/ppermute | solution.py:37
  131.7 6.0 %collective-permute-start.11 = (bf16[152,384]{1,0:T(8,128)(2,1)S(1)}, bf16[152,384]{1,0:T(8,128)(2,1)S(1)}, u32[]{:S(2)}, u32[]{:S(2)}) collective-permute-start(bf16[152,384]{1,0:T(8,128)(2,1)S(1)} %get-tuple-element.48), channel_id=1, source_target_pairs={{0,6},{1,7},{2,0},{3,1},{4,2},{5,3},{6,4},{7,5},{8,14},{9,15},{10,... | collective-permute-start | bytes 350216 | tf_op jit(solution)/shard_map/ppermute | solution.py:37
  133.1 5.3 %collective-permute-start.9 = (bf16[152,384]{1,0:T(8,128)(2,1)S(1)}, bf16[152,384]{1,0:T(8,128)(2,1)S(1)}, u32[]{:S(2)}, u32[]{:S(2)}) collective-permute-start(bf16[152,384]{1,0:T(8,128)(2,1)S(1)} %get-tuple-element.47), channel_id=1, source_target_pairs={{0,2},{1,3},{2,4},{3,5},{4,6},{5,7},{6,0},{7,1},{8,10},{9,11},{10,... | collective-permute-start | bytes 350216 | tf_op jit(solution)/shard_map/ppermute | solution.py:37
  133.4 8.1 %collective-permute-start.21 = (bf16[152,384]{1,0:T(8,128)(2,1)S(1)}, bf16[152,384]{1,0:T(8,128)(2,1)S(1)}, u32[]{:S(2)}, u32[]{:S(2)}) collective-permute-start(bf16[152,384]{1,0:T(8,128)(2,1)S(1)} %get-tuple-element.57), channel_id=1, source_target_pairs={{0,2},{1,3},{2,4},{3,5},{4,6},{5,7},{6,0},{7,1},{8,10},{9,11},{10,... | collective-permute-start | bytes 350216 | tf_op jit(solution)/shard_map/ppermute | solution.py:37
  134.0 8.8 %collective-permute-start.22 = (bf16[152,384]{1,0:T(8,128)(2,1)S(1)}, bf16[152,384]{1,0:T(8,128)(2,1)S(1)}, u32[]{:S(2)}, u32[]{:S(2)}) collective-permute-start(bf16[152,384]{1,0:T(8,128)(2,1)S(1)} %get-tuple-element.59), channel_id=1, source_target_pairs={{0,4},{1,5},{2,6},{3,7},{4,0},{5,1},{6,2},{7,3},{8,12},{9,13},{10,... | collective-permute-start | bytes 350216 | tf_op jit(solution)/shard_map/ppermute | solution.py:37
  137.3 5.5 %collective-permute-start.23 = (bf16[152,384]{1,0:T(8,128)(2,1)S(1)}, bf16[152,384]{1,0:T(8,128)(2,1)S(1)}, u32[]{:S(2)}, u32[]{:S(2)}) collective-permute-start(bf16[152,384]{1,0:T(8,128)(2,1)S(1)} %get-tuple-element.58), channel_id=1, source_target_pairs={{0,6},{1,7},{2,0},{3,1},{4,2},{5,3},{6,4},{7,5},{8,14},{9,15},{10,... | collective-permute-start | bytes 350216 | tf_op jit(solution)/shard_map/ppermute | solution.py:37
  (35 other events, 111.2 us)

commit v6 on v5

--- a/solution.py
+++ b/solution.py
@@ -197,18 +197,22 @@
     pre_out = jnp.sum(
         jnp.where(head_mask[:, None, :], pre_mixed.reshape(heads_here, stretch_len, width_here), 0.0), axis=0
     ).astype(jnp.bfloat16)
-    dec_out, pre_out = lax.optimization_barrier((dec_out, pre_out))
-    attn_rows = jnp.concatenate([dec_out, pre_out], axis=0)
     head_me = lax.axis_index("head")
     col_start = head_me * width_here
 
-    def feed_forward(attn_chunk, hidden_chunk):
+    def project(attn_chunk, hidden_chunk):
         projected = jnp.dot(attn_chunk, out_weight, preferred_element_type=jnp.float32)
         own_cols = lax.dynamic_slice_in_dim(projected, col_start, width_here, 1) + hidden_chunk.astype(
             jnp.float32
         )
-        contribution = lax.dynamic_update_slice_in_dim(projected, own_cols, col_start, 1)
-        own_residual = pair_then_z_scatter(contribution.astype(jnp.bfloat16)).astype(jnp.bfloat16)
+        return lax.dynamic_update_slice_in_dim(projected, own_cols, col_start, 1).astype(jnp.bfloat16)
+
+    pre_contribution = project(pre_out, hidden_in[per_home:])
+    dec_out, pre_contribution = lax.optimization_barrier((dec_out, pre_contribution))
+    contribution_rows = jnp.concatenate([project(dec_out, hidden_in[:per_home]), pre_contribution], axis=0)
+
+    def feed_forward(contribution):
+        own_residual = pair_then_z_scatter(contribution).astype(jnp.bfloat16)
         residual = z_then_pair_gather(own_residual)
         residual_wide = residual.astype(jnp.float32)
         squares = jnp.mean(jnp.square(residual_wide), axis=-1, keepdims=True)
@@ -224,8 +228,8 @@
     half = row_count // 2
     out_cols = jnp.concatenate(
         [
-            feed_forward(attn_rows[:half], hidden_in[:half]),
-            feed_forward(attn_rows[half:], hidden_in[half:]),
+            feed_forward(contribution_rows[:half]),
+            feed_forward(contribution_rows[half:]),
         ],
         axis=0,
     )

time: 173 us -> 173 us (level)
  other arithmetic: 23.4 us -> 29.2 us
  matrix products: 39 us -> 35.7 us
    dot_general x1, matrix products: 7.43 us -> 2.42 us  [on_device(): jnp.dot((raised_cache / total).astype(jnp.bfloat16), cache_value[0], pref...]
    dot_general x2, matrix products: 3.13 us -> 6.67 us  [project(): jnp.dot(attn_chunk, out_weight, preferred_element_type=jnp.float32)]
    convert_element_type x4, other arithmetic: 0.37 us -> 3.46 us  [the longest x2 3.32 us: project(): lax.dynamic_update_slice_in_dim(projected, own_cols, col_start, 1)]
    dynamic_update_slice x1 -> x2, other arithmetic: 0.1 us -> 2.57 us  [project(): lax.dynamic_update_slice_in_dim(projected, own_cols, col_start, 1)]
    dot_general x1, matrix products: 2.33 us -> 0.49 us  [on_device(): jnp.dot((raised_self / total).astype(jnp.bfloat16), pre_value, preferred_...]
  transfers between devices with their start and end apart: 26 -> 26, of which waited for: 11 -> 11; matrix products, arithmetic and copies ran while one was open for 29% -> 30% of each run, Pallas kernels for 0% -> 0%
where the time goes in v6:
time: 173 us; the launch traced here: 172 us
  starting transfers between devices  47.7 us (28%)
  matrix products  35.7 us (21%)
  other arithmetic  29.2 us (17%)
  blocking collectives  27.6 us (16%)
  waiting for transfers between devices  19.6 us (11%)
  local copies, waits for them, and re-layouts  10.6 us (6%)
    ppermute x12, starting transfers between devices, pair_then_z_scatter(): acc = acc + lax.ppermute(piece, 'head', perm).astype(jnp.float32)  16.7 us
    all_to_all x1, blocking collectives, on_device(): lax.all_to_all(arrived, 'head', split_axis=0, concat_axis=1, tiled=True)  15.8 us
    all_to_all x1, blocking collectives, on_device(): lax.all_to_all(outgoing, 'req', split_axis=0, concat_axis=0, tiled=True)  11.8 us
    all_to_all x1, waiting for transfers between devices, on_device(): lax.all_to_all(going_back, 'req', split_axis=0, concat_axis=0, tiled=True)  9.18 us
    dot_general x2, matrix products, feed_forward(): jnp.dot(hidden, down_weight, preferred_element_type=jnp.float32)  8.89 us
    ppermute x6, starting transfers between devices, z_then_pair_gather(): parts.append(lax.ppermute(y, 'head', perm))  8.05 us
    unnamed x17, other arithmetic  7.9 us
    all_to_all x1, starting transfers between devices, on_device(): lax.all_to_all(outgoing_q, 'req', split_axis=0, concat_axis=0, tiled=True)  7.62 us
  transfers between devices with their start and end apart: 26, of which 11 were waited for; matrix products, arithmetic and copies ran while one was open for 30% of the time, Pallas kernels for 0%

profile of v6, /device:TPU:1, one launch (start us, length us, event | category | flops | bytes accessed | tf_op | source)
XLA Modules:
  0.0 172.1 jit_solution(14245080794123619024)
XLA Ops:
  2.4 1.9 %convolution_convert_fusion.3 = bf16[768,384]{1,0:T(8,128)(2,1)} fusion(bf16[48,384]{1,0:T(8,128)(2,1)} %param.19, s32[48]{0:T(128)S(1)} %dynamic-slice_add_fusion), kind=kOutput, calls=%fused_computation.52 | convolution fusion | flops 28643328 | bytes 626880 | tf_op jit(solution)/shard_map/dot_general | solution.py:108
  4.3 7.6 %all-to-all-start = ((bf16[16,48,384]{2,1,0:T(8,128)(2,1)}), bf16[16,48,384]{2,1,0:T(8,128)(2,1)}, u32[]{:S(2)}, u32[]{:S(2)}) async-start(bf16[16,48,384]{2,1,0:T(8,128)(2,1)} %bitcast.138), calls=%async_computation | async-start | bytes 1179648 | tf_op jit(solution)/shard_map/all_to_all | solution.py:109
  16.6 4.0 %fusion = (f32[1024]{0:T(1024)S(1)}, f32[1024,2048]{1,0:T(8,128)S(1)}) fusion(pred[2048]{0:T(1024)(128)(4,1)S(1)} %iota_compare_fusion.18, bf16[1024,384]{1,0:T(8,128)(2,1)S(1)} %bitcast.146, bf16[2,2048,384]{2,1,0:T(8,128)(2,1)} %param.25), kind=kOutput, calls=%fused_computation.3 | convolution fusion | flops 1616903168 | bytes 10754048 | tf_op jit(solution)/shard_map/dot_general | solution.py:181
  21.2 2.2 %fusion.1 = f32[1024]{0:T(1024)S(1)} fusion(f32[1024,2048]{1,0:T(8,128)S(1)} %get-tuple-element.78, f32[1024]{0:T(1024)S(1)} %max.12, pred[2048]{0:T(1024)(128)(4,1)S(1)} %iota_compare_fusion.18), kind=kLoop, calls=%fused_computation.4 | loop fusion | flops 8387584 | bytes 8398848 | tf_op jit(solution)/shard_map/reduce_sum | solution.py:193
  23.6 2.4 %fusion.2 = f32[1024,384]{1,0:T(8,128)S(1)} fusion(f32[1024,2048]{1,0:T(8,128)S(1)} %get-tuple-element.78, f32[1024]{0:T(1024)S(1)} %add.298, f32[1024]{0:T(1024)S(1)} %max.12, pred[2048]{0:T(1024)(128)(4,1)S(1)} %iota_compare_fusion.18, bf16[2,2048,384]{2,1,0:T(8,128)(2,1)S(1)} %copy-done.34), kind=kOutput, calls=%fused_computation.5 | convolution fusion | flops 1621098496 | bytes 11544576 | tf_op jit(solution)/shard_map/dot_general | solution.py:194
  28.0 4.4 %fusion.170 = f32[256,3072]{1,0:T(8,128)} fusion(bf16[256,384]{1,0:T(8,128)(2,1)S(1)} %select_reduce_fusion, bf16[384,3072]{1,0:T(8,128)(2,1)} %param.31), kind=kOutput, calls=%fused_computation.311 | convolution fusion | flops 603979776 | bytes 5701632 | tf_op jit(solution)/shard_map/dot_general | solution.py:204
  32.4 1.8 %add_dynamic-update-slice_fusion = f32[256,3072]{1,0:T(8,128)} fusion(f32[256,3072]{1,0:T(8,128)} %fusion.170, s32[]{:T(128)S(6)} %select_n.378, bf16[304,384]{1,0:T(8,128)(2,1)S(1)} %copy-done.26), kind=kLoop, calls=%fused_computation.123 | loop fusion | flops 196608 | bytes 983044 | tf_op jit(solution)/shard_map/dynamic_update_slice | solution.py:208
  35.6 2.2 %fusion.167 = (f32[192]{0:T(256)S(1)}, f32[192,2048]{1,0:T(8,128)S(1)}) fusion(bf16[192,384]{1,0:T(8,128)(2,1)S(1)} %bitcast.153, bf16[2,2048,384]{2,1,0:T(8,128)(2,1)} %param.25, pred[2048]{0:T(1024)(128)(4,1)S(1)} %iota_compare_fusion.20), kind=kOutput, calls=%fused_computation.308 | convolution fusion | flops 303169344 | bytes 3296000 | tf_op jit(solution)/shard_map/dot_general | solution.py:135
  45.6 6.7 %all-to-all-start.1 = ((bf16[16,48,512]{2,1,0:T(8,128)(2,1)}), bf16[16,48,512]{2,1,0:T(8,128)(2,1)}, u32[]{:S(2)}, u32[]{:S(2)}) async-start(bf16[16,48,512]{2,1,0:T(8,128)(2,1)} %bitcast.145), calls=%async_computation.1 | async-start | bytes 1572864 | tf_op jit(solution)/shard_map/all_to_all | solution.py:159
  52.5 3.3 %convert_element_type.250 = bf16[256,3072]{1,0:T(8,128)(2,1)} convert(f32[256,3072]{1,0:T(8,128)} %add_dynamic-update-slice_fusion) | non-fusion elementwise | flops 786432 | bytes 4718592 | tf_op jit(solution)/shard_map/convert_element_type | solution.py:208
  55.9 9.2 %all-to-all-done.1 = bf16[16,48,512]{2,1,0:T(8,128)(2,1)} async-done(((bf16[16,48,512]{2,1,0:T(8,128)(2,1)}), bf16[16,48,512]{2,1,0:T(8,128)(2,1)}, u32[]{:S(2)}, u32[]{:S(2)}) %all-to-all-start.1) | async-done | bytes 786464 | tf_op jit(solution)/shard_map/all_to_all | solution.py:159
  65.1 1.4 fusion.74
  66.9 2.3 %fusion.169 = f32[48,3072]{1,0:T(8,128)S(1)} fusion(bf16[48,384]{1,0:T(8,128)(2,1)S(1)} %fusion.129, bf16[384,3072]{1,0:T(8,128)(2,1)} %param.31), kind=kOutput, calls=%fused_computation.310 | convolution fusion | flops 113246208 | bytes 2985984 | tf_op jit(solution)/shard_map/dot_general | solution.py:204
  70.4 2.6 %collective-permute-start = (bf16[152,1536]{1,0:T(8,128)(2,1)S(1)}, bf16[152,1536]{1,0:T(8,128)(2,1)S(1)}, u32[]{:S(2)}, u32[]{:S(2)}) collective-permute-start(bf16[152,1536]{1,0:T(8,128)(2,1)S(1)} %get-tuple-element.11), channel_id=1, source_target_pairs={{0,1},{1,0},{2,3},{3,2},{4,5},{5,4},{6,7},{7,6},{8,9},{9,8},{10,11... | collective-permute-start | bytes 1400840 | tf_op jit(solution)/shard_map/ppermute | solution.py:31
  74.7 1.8 %collective-permute-start.1 = (bf16[152,384]{1,0:T(8,128)(2,1)S(1)}, bf16[152,384]{1,0:T(8,128)(2,1)S(1)}, u32[]{:S(2)}, u32[]{:S(2)}) collective-permute-start(bf16[152,384]{1,0:T(8,128)(2,1)S(1)} %get-tuple-element.52), channel_id=1, source_target_pairs={{0,2},{1,3},{2,4},{3,5},{4,6},{5,7},{6,0},{7,1},{8,10},{9,11},{10,... | collective-permute-start | bytes 350216 | tf_op jit(solution)/shard_map/ppermute | solution.py:37
  76.4 3.3 %collective-permute-start.2 = (bf16[152,384]{1,0:T(8,128)(2,1)S(1)}, bf16[152,384]{1,0:T(8,128)(2,1)S(1)}, u32[]{:S(2)}, u32[]{:S(2)}) collective-permute-start(bf16[152,384]{1,0:T(8,128)(2,1)S(1)} %get-tuple-element.54), channel_id=1, source_target_pairs={{0,4},{1,5},{2,6},{3,7},{4,0},{5,1},{6,2},{7,3},{8,12},{9,13},{10,... | collective-permute-start | bytes 350216 | tf_op jit(solution)/shard_map/ppermute | solution.py:37
  82.0 2.0 %collective-permute-start.15 = (bf16[152,384]{1,0:T(8,128)(2,1)S(1)}, bf16[152,384]{1,0:T(8,128)(2,1)S(1)}, u32[]{:S(2)}, u32[]{:S(2)}) collective-permute-start(bf16[152,384]{1,0:T(8,128)(2,1)S(1)} %get-tuple-element.63), channel_id=1, source_target_pairs={{0,6},{1,7},{2,0},{3,1},{4,2},{5,3},{6,4},{7,5},{8,14},{9,15},{10,... | collective-permute-start | bytes 350216 | tf_op jit(solution)/shard_map/ppermute | solution.py:37
  85.2 1.6 collective-permute-start.4
  86.8 1.9 %collective-permute-start.5 = (bf16[152,384]{1,0:T(8,128)(2,1)S(1)}, bf16[152,384]{1,0:T(8,128)(2,1)S(1)}, u32[]{:S(2)}, u32[]{:S(2)}) collective-permute-start(bf16[152,384]{1,0:T(8,128)(2,1)S(1)} %add_convert_fusion.7), channel_id=1, source_target_pairs={{0,4},{1,5},{2,6},{3,7},{4,0},{5,1},{6,2},{7,3},{8,12},{9,13},{10,... | collective-permute-start | bytes 350216 | tf_op jit(solution)/shard_map/ppermute | solution.py:51
  90.2 1.5 collective-permute-start.16
  91.7 1.9 %collective-permute-start.17 = (bf16[152,384]{1,0:T(8,128)(2,1)S(1)}, bf16[152,384]{1,0:T(8,128)(2,1)S(1)}, u32[]{:S(2)}, u32[]{:S(2)}) collective-permute-start(bf16[152,384]{1,0:T(8,128)(2,1)S(1)} %add_convert_fusion.5), channel_id=1, source_target_pairs={{0,4},{1,5},{2,6},{3,7},{4,0},{5,1},{6,2},{7,3},{8,12},{9,13},{10,... | collective-permute-start | bytes 350216 | tf_op jit(solution)/shard_map/ppermute | solution.py:51
  95.3 2.4 %collective-permute-start.7 = (bf16[152,1536]{1,0:T(8,128)(2,1)S(1)}, bf16[152,1536]{1,0:T(8,128)(2,1)S(1)}, u32[]{:S(2)}, u32[]{:S(2)}) collective-permute-start(bf16[152,1536]{1,0:T(8,128)(2,1)S(1)} %pad_maximum_fusion.1), channel_id=1, source_target_pairs={{0,1},{1,0},{2,3},{3,2},{4,5},{5,4},{6,7},{7,6},{8,9},{9,8},{10,11... | collective-permute-start | bytes 1400840 | tf_op jit(solution)/shard_map/ppermute | solution.py:56
  100.0 2.4 %collective-permute-start.19 = (bf16[152,1536]{1,0:T(8,128)(2,1)}, bf16[152,1536]{1,0:T(8,128)(2,1)}, u32[]{:S(2)}, u32[]{:S(2)}) collective-permute-start(bf16[152,1536]{1,0:T(8,128)(2,1)} %pad_maximum_fusion.7), channel_id=1, source_target_pairs={{0,1},{1,0},{2,3},{3,2},{4,5},{5,4},{6,7},{7,6},{8,9},{9,8},{10,11... | collective-permute-start | bytes 1400840 | tf_op jit(solution)/shard_map/ppermute | solution.py:56
  103.7 1.4 fusion.97
  105.2 4.4 %convolution_convert_fusion.1 = bf16[152,3072]{1,0:T(8,128)(2,1)} fusion(bf16[512,3072]{1,0:T(8,128)(2,1)S(1)} %copy-done, bf16[3072,512]{1,0:T(8,128)(2,1)} %param.34, f32[152,512]{1,0:T(8,128)} %fusion.97, bf16[152,3072]{1,0:T(8,128)(2,1)} %copy-done.4, f32[3072]{0:T(1024)S(1)} %copy-done.40, f32[152]{0:T(256)S(1)} %add_rsqrt_fusion.1), kind=kOutput, calls=%fused_computation.7 | convolution fusion | flops 959102976 | bytes 8483424 | tf_op jit(solution)/shard_map/dot_general | solution.py:223
  122.3 4.4 %convolution_convert_fusion = bf16[152,3072]{1,0:T(8,128)(2,1)} fusion(bf16[512,3072]{1,0:T(8,128)(2,1)S(1)} %copy-done, bf16[3072,512]{1,0:T(8,128)(2,1)} %param.34, f32[152,512]{1,0:T(8,128)S(1)} %fusion.93, bf16[152,3072]{1,0:T(8,128)(2,1)} %copy-done.5, f32[152]{0:T(256)S(1)} %add_rsqrt_fusion, f32[3072]{0:T(1024)S(1)} %copy-done.40), kind=kOutput, calls=%fused_computation.6 | convolution fusion | flops 959102976 | bytes 8483424 | tf_op jit(solution)/shard_map/dot_general | solution.py:223
  126.8 1.4 fusion.161
  129.9 2.0 %collective-permute-start.10 = (bf16[152,384]{1,0:T(8,128)(2,1)S(1)}, bf16[152,384]{1,0:T(8,128)(2,1)S(1)}, u32[]{:S(2)}, u32[]{:S(2)}) collective-permute-start(bf16[152,384]{1,0:T(8,128)(2,1)S(1)} %get-tuple-element.47), channel_id=1, source_target_pairs={{0,4},{1,5},{2,6},{3,7},{4,0},{5,1},{6,2},{7,3},{8,12},{9,13},{10,... | collective-permute-start | bytes 350216 | tf_op jit(solution)/shard_map/ppermute | solution.py:37
  134.3 3.2 %collective-permute-start.22 = (bf16[152,384]{1,0:T(8,128)(2,1)S(1)}, bf16[152,384]{1,0:T(8,128)(2,1)S(1)}, u32[]{:S(2)}, u32[]{:S(2)}) collective-permute-start(bf16[152,384]{1,0:T(8,128)(2,1)S(1)} %get-tuple-element.57), channel_id=1, source_target_pairs={{0,4},{1,5},{2,6},{3,7},{4,0},{5,1},{6,2},{7,3},{8,12},{9,13},{10,... | collective-permute-start | bytes 350216 | tf_op jit(solution)/shard_map/ppermute | solution.py:37
  138.8 3.0 %collective-permute-done.21 = bf16[152,384]{1,0:T(8,128)(2,1)S(1)} collective-permute-done((bf16[152,384]{1,0:T(8,128)(2,1)S(1)}, bf16[152,384]{1,0:T(8,128)(2,1)S(1)}, u32[]{:S(2)}, u32[]{:S(2)}) %collective-permute-start.21) | collective-permute-done | bytes 116768 | tf_op jit(solution)/shard_map/ppermute | solution.py:37
  143.6 11.8 %all_to_all.52 = bf16[16,40,384]{2,1,0:T(8,128)(2,1)S(1)} all-to-all(bf16[16,40,384]{2,1,0:T(8,128)(2,1)S(1)} %bitcast.150), channel_id=1, replica_groups=mesh['req'=16,'head'=8] {'req'}, dimensions={0} | all-to-all | bytes 983040 | tf_op jit(solution)/shard_map/all_to_all | solution.py:248
  155.4 15.8 %all_to_all.53 = bf16[8,80,384]{2,1,0:T(8,128)(2,1)S(1)} all-to-all(bf16[8,80,384]{2,1,0:T(8,128)(2,1)S(1)} %bitcast.139), channel_id=1, replica_groups=mesh['req'=16,'head'=8] {'head'}, dimensions={0} | all-to-all | bytes 983040 | tf_op jit(solution)/shard_map/all_to_all | solution.py:249
  (243 shorter events, 52.0 us)
Async XLA Ops:
  0.0 105.2 %copy-start = (bf16[512,3072]{1,0:T(8,128)(2,1)S(1)}, bf16[512,3072]{1,0:T(8,128)(2,1)}, u32[]{:S(2)}) copy-start(bf16[512,3072]{1,0:T(8,128)(2,1)} %param.35) | copy-start | bytes 9437188
  0.0 13.7 %copy-start.31 = (s32[2]{0:T(128)S(1)}, s32[2]{0:T(128)}, u32[]{:S(2)}) copy-start(s32[2]{0:T(128)} %param.28) | copy-start | bytes 28
  0.0 16.5 %copy-start.27 = (bf16[256,384]{1,0:T(8,128)(2,1)S(1)}, bf16[256,384]{1,0:T(8,128)(2,1)}, u32[]{:S(2)}) copy-start(bf16[256,384]{1,0:T(8,128)(2,1)} %param.22) | copy-start | bytes 589828
  4.3 29.9 %all-to-all-start = ((bf16[16,48,384]{2,1,0:T(8,128)(2,1)}), bf16[16,48,384]{2,1,0:T(8,128)(2,1)}, u32[]{:S(2)}, u32[]{:S(2)}) async-start(bf16[16,48,384]{2,1,0:T(8,128)(2,1)} %bitcast.138), calls=%async_computation | async-start | bytes 1179648 | tf_op jit(solution)/shard_map/all_to_all | solution.py:109
  45.6 19.5 %all-to-all-start.1 = ((bf16[16,48,512]{2,1,0:T(8,128)(2,1)}), bf16[16,48,512]{2,1,0:T(8,128)(2,1)}, u32[]{:S(2)}, u32[]{:S(2)}) async-start(bf16[16,48,512]{2,1,0:T(8,128)(2,1)} %bitcast.145), calls=%async_computation.1 | async-start | bytes 1572864 | tf_op jit(solution)/shard_map/all_to_all | solution.py:159
  52.5 14.4 %copy-start.29 = (bf16[48,384]{1,0:T(8,128)(2,1)S(1)}, bf16[48,384]{1,0:T(8,128)(2,1)}, u32[]{:S(2)}) copy-start(bf16[48,384]{1,0:T(8,128)(2,1)} %param.21) | copy-start | bytes 110596
  70.4 4.0 %collective-permute-start = (bf16[152,1536]{1,0:T(8,128)(2,1)S(1)}, bf16[152,1536]{1,0:T(8,128)(2,1)S(1)}, u32[]{:S(2)}, u32[]{:S(2)}) collective-permute-start(bf16[152,1536]{1,0:T(8,128)(2,1)S(1)} %get-tuple-element.11), channel_id=1, source_target_pairs={{0,1},{1,0},{2,3},{3,2},{4,5},{5,4},{6,7},{7,6},{8,9},{9,8},{10,11... | collective-permute-start | bytes 1400840 | tf_op jit(solution)/shard_map/ppermute | solution.py:31
  73.2 7.3 %collective-permute-start.12 = (bf16[152,1536]{1,0:T(8,128)(2,1)S(1)}, bf16[152,1536]{1,0:T(8,128)(2,1)S(1)}, u32[]{:S(2)}, u32[]{:S(2)}) collective-permute-start(bf16[152,1536]{1,0:T(8,128)(2,1)S(1)} %broadcast_select_fusion.2), channel_id=1, source_target_pairs={{0,1},{1,0},{2,3},{3,2},{4,5},{5,4},{6,7},{7,6},{8,9},{9,8},{10,11... | collective-permute-start | bytes 1400840 | tf_op jit(solution)/shard_map/ppermute | solution.py:31
  74.7 7.3 %collective-permute-start.1 = (bf16[152,384]{1,0:T(8,128)(2,1)S(1)}, bf16[152,384]{1,0:T(8,128)(2,1)S(1)}, u32[]{:S(2)}, u32[]{:S(2)}) collective-permute-start(bf16[152,384]{1,0:T(8,128)(2,1)S(1)} %get-tuple-element.52), channel_id=1, source_target_pairs={{0,2},{1,3},{2,4},{3,5},{4,6},{5,7},{6,0},{7,1},{8,10},{9,11},{10,... | collective-permute-start | bytes 350216 | tf_op jit(solution)/shard_map/ppermute | solution.py:37
  76.4 8.7 %collective-permute-start.2 = (bf16[152,384]{1,0:T(8,128)(2,1)S(1)}, bf16[152,384]{1,0:T(8,128)(2,1)S(1)}, u32[]{:S(2)}, u32[]{:S(2)}) collective-permute-start(bf16[152,384]{1,0:T(8,128)(2,1)S(1)} %get-tuple-element.54), channel_id=1, source_target_pairs={{0,4},{1,5},{2,6},{3,7},{4,0},{5,1},{6,2},{7,3},{8,12},{9,13},{10,... | collective-permute-start | bytes 350216 | tf_op jit(solution)/shard_map/ppermute | solution.py:37
  79.7 5.4 %collective-permute-start.3 = (bf16[152,384]{1,0:T(8,128)(2,1)S(1)}, bf16[152,384]{1,0:T(8,128)(2,1)S(1)}, u32[]{:S(2)}, u32[]{:S(2)}) collective-permute-start(bf16[152,384]{1,0:T(8,128)(2,1)S(1)} %get-tuple-element.53), channel_id=1, source_target_pairs={{0,6},{1,7},{2,0},{3,1},{4,2},{5,3},{6,4},{7,5},{8,14},{9,15},{10,... | collective-permute-start | bytes 350216 | tf_op jit(solution)/shard_map/ppermute | solution.py:37
  80.7 8.0 %collective-permute-start.13 = (bf16[152,384]{1,0:T(8,128)(2,1)S(1)}, bf16[152,384]{1,0:T(8,128)(2,1)S(1)}, u32[]{:S(2)}, u32[]{:S(2)}) collective-permute-start(bf16[152,384]{1,0:T(8,128)(2,1)S(1)} %get-tuple-element.62), channel_id=1, source_target_pairs={{0,2},{1,3},{2,4},{3,5},{4,6},{5,7},{6,0},{7,1},{8,10},{9,11},{10,... | collective-permute-start | bytes 350216 | tf_op jit(solution)/shard_map/ppermute | solution.py:37
  81.5 8.6 %collective-permute-start.14 = (bf16[152,384]{1,0:T(8,128)(2,1)S(1)}, bf16[152,384]{1,0:T(8,128)(2,1)S(1)}, u32[]{:S(2)}, u32[]{:S(2)}) collective-permute-start(bf16[152,384]{1,0:T(8,128)(2,1)S(1)} %get-tuple-element.64), channel_id=1, source_target_pairs={{0,4},{1,5},{2,6},{3,7},{4,0},{5,1},{6,2},{7,3},{8,12},{9,13},{10,... | collective-permute-start | bytes 350216 | tf_op jit(solution)/shard_map/ppermute | solution.py:37
  82.0 8.2 %collective-permute-start.15 = (bf16[152,384]{1,0:T(8,128)(2,1)S(1)}, bf16[152,384]{1,0:T(8,128)(2,1)S(1)}, u32[]{:S(2)}, u32[]{:S(2)}) collective-permute-start(bf16[152,384]{1,0:T(8,128)(2,1)S(1)} %get-tuple-element.63), channel_id=1, source_target_pairs={{0,6},{1,7},{2,0},{3,1},{4,2},{5,3},{6,4},{7,5},{8,14},{9,15},{10,... | collective-permute-start | bytes 350216 | tf_op jit(solution)/shard_map/ppermute | solution.py:37
  85.2 10.1 %copy-start.22 = (bf16[152,384]{1,0:T(8,128)(2,1)}, bf16[152,384]{1,0:T(8,128)(2,1)S(1)}, u32[]{:S(2)}) copy-start(bf16[152,384]{1,0:T(8,128)(2,1)S(1)} %add_convert_fusion.7) | copy-start | bytes 350212
  85.2 8.4 %collective-permute-start.4 = (bf16[152,384]{1,0:T(8,128)(2,1)S(1)}, bf16[152,384]{1,0:T(8,128)(2,1)S(1)}, u32[]{:S(2)}, u32[]{:S(2)}) collective-permute-start(bf16[152,384]{1,0:T(8,128)(2,1)S(1)} %add_convert_fusion.7), channel_id=1, source_target_pairs={{0,2},{1,3},{2,4},{3,5},{4,6},{5,7},{6,0},{7,1},{8,10},{9,11},{10,... | collective-permute-start | bytes 350216 | tf_op jit(solution)/shard_map/ppermute | solution.py:51
  86.8 8.3 %collective-permute-start.5 = (bf16[152,384]{1,0:T(8,128)(2,1)S(1)}, bf16[152,384]{1,0:T(8,128)(2,1)S(1)}, u32[]{:S(2)}, u32[]{:S(2)}) collective-permute-start(bf16[152,384]{1,0:T(8,128)(2,1)S(1)} %add_convert_fusion.7), channel_id=1, source_target_pairs={{0,4},{1,5},{2,6},{3,7},{4,0},{5,1},{6,2},{7,3},{8,12},{9,13},{10,... | collective-permute-start | bytes 350216 | tf_op jit(solution)/shard_map/ppermute | solution.py:51
  88.7 6.4 %collective-permute-start.6 = (bf16[152,384]{1,0:T(8,128)(2,1)S(1)}, bf16[152,384]{1,0:T(8,128)(2,1)S(1)}, u32[]{:S(2)}, u32[]{:S(2)}) collective-permute-start(bf16[152,384]{1,0:T(8,128)(2,1)S(1)} %add_convert_fusion.7), channel_id=1, source_target_pairs={{0,6},{1,7},{2,0},{3,1},{4,2},{5,3},{6,4},{7,5},{8,14},{9,15},{10,... | collective-permute-start | bytes 350216 | tf_op jit(solution)/shard_map/ppermute | solution.py:51
  90.2 7.9 %collective-permute-start.16 = (bf16[152,384]{1,0:T(8,128)(2,1)S(1)}, bf16[152,384]{1,0:T(8,128)(2,1)S(1)}, u32[]{:S(2)}, u32[]{:S(2)}) collective-permute-start(bf16[152,384]{1,0:T(8,128)(2,1)S(1)} %add_convert_fusion.5), channel_id=1, source_target_pairs={{0,2},{1,3},{2,4},{3,5},{4,6},{5,7},{6,0},{7,1},{8,10},{9,11},{10,... | collective-permute-start | bytes 350216 | tf_op jit(solution)/shard_map/ppermute | solution.py:51
  91.7 7.3 %collective-permute-start.17 = (bf16[152,384]{1,0:T(8,128)(2,1)S(1)}, bf16[152,384]{1,0:T(8,128)(2,1)S(1)}, u32[]{:S(2)}, u32[]{:S(2)}) collective-permute-start(bf16[152,384]{1,0:T(8,128)(2,1)S(1)} %add_convert_fusion.5), channel_id=1, source_target_pairs={{0,4},{1,5},{2,6},{3,7},{4,0},{5,1},{6,2},{7,3},{8,12},{9,13},{10,... | collective-permute-start | bytes 350216 | tf_op jit(solution)/shard_map/ppermute | solution.py:51
  93.6 5.4 %collective-permute-start.18 = (bf16[152,384]{1,0:T(8,128)(2,1)S(1)}, bf16[152,384]{1,0:T(8,128)(2,1)S(1)}, u32[]{:S(2)}, u32[]{:S(2)}) collective-permute-start(bf16[152,384]{1,0:T(8,128)(2,1)S(1)} %add_convert_fusion.5), channel_id=1, source_target_pairs={{0,6},{1,7},{2,0},{3,1},{4,2},{5,3},{6,4},{7,5},{8,14},{9,15},{10,... | collective-permute-start | bytes 350216 | tf_op jit(solution)/shard_map/ppermute | solution.py:51
  95.3 7.0 %collective-permute-start.7 = (bf16[152,1536]{1,0:T(8,128)(2,1)S(1)}, bf16[152,1536]{1,0:T(8,128)(2,1)S(1)}, u32[]{:S(2)}, u32[]{:S(2)}) collective-permute-start(bf16[152,1536]{1,0:T(8,128)(2,1)S(1)} %pad_maximum_fusion.1), channel_id=1, source_target_pairs={{0,1},{1,0},{2,3},{3,2},{4,5},{5,4},{6,7},{7,6},{8,9},{9,8},{10,11... | collective-permute-start | bytes 1400840 | tf_op jit(solution)/shard_map/ppermute | solution.py:56
  100.0 13.1 %collective-permute-start.19 = (bf16[152,1536]{1,0:T(8,128)(2,1)}, bf16[152,1536]{1,0:T(8,128)(2,1)}, u32[]{:S(2)}, u32[]{:S(2)}) collective-permute-start(bf16[152,1536]{1,0:T(8,128)(2,1)} %pad_maximum_fusion.7), channel_id=1, source_target_pairs={{0,1},{1,0},{2,3},{3,2},{4,5},{5,4},{6,7},{7,6},{8,9},{9,8},{10,11... | collective-permute-start | bytes 1400840 | tf_op jit(solution)/shard_map/ppermute | solution.py:56
  112.1 16.5 %collective-permute-start.8 = (bf16[152,1536]{1,0:T(8,128)(2,1)}, bf16[152,1536]{1,0:T(8,128)(2,1)}, u32[]{:S(2)}, u32[]{:S(2)}) collective-permute-start(bf16[152,1536]{1,0:T(8,128)(2,1)} %broadcast_select_fusion.3), channel_id=1, source_target_pairs={{0,1},{1,0},{2,3},{3,2},{4,5},{5,4},{6,7},{7,6},{8,9},{9,8},{10,11... | collective-permute-start | bytes 1400840 | tf_op jit(solution)/shard_map/ppermute | solution.py:31
  128.3 5.1 %collective-permute-start.20 = (bf16[152,1536]{1,0:T(8,128)(2,1)S(1)}, bf16[152,1536]{1,0:T(8,128)(2,1)S(1)}, u32[]{:S(2)}, u32[]{:S(2)}) collective-permute-start(bf16[152,1536]{1,0:T(8,128)(2,1)S(1)} %broadcast_select_fusion.1), channel_id=1, source_target_pairs={{0,1},{1,0},{2,3},{3,2},{4,5},{5,4},{6,7},{7,6},{8,9},{9,8},{10,11... | collective-permute-start | bytes 1400840 | tf_op jit(solution)/shard_map/ppermute | solution.py:31
  129.9 13.2 %copy-start.25 = (bf16[152,384]{1,0:T(8,128)(2,1)S(1)}, bf16[152,384]{1,0:T(8,128)(2,1)}, u32[]{:S(2)}) copy-start(bf16[152,384]{1,0:T(8,128)(2,1)} %copy-done.24) | copy-start | bytes 350212
  129.9 7.6 %collective-permute-start.10 = (bf16[152,384]{1,0:T(8,128)(2,1)S(1)}, bf16[152,384]{1,0:T(8,128)(2,1)S(1)}, u32[]{:S(2)}, u32[]{:S(2)}) collective-permute-start(bf16[152,384]{1,0:T(8,128)(2,1)S(1)} %get-tuple-element.47), channel_id=1, source_target_pairs={{0,4},{1,5},{2,6},{3,7},{4,0},{5,1},{6,2},{7,3},{8,12},{9,13},{10,... | collective-permute-start | bytes 350216 | tf_op jit(solution)/shard_map/ppermute | solution.py:37
  132.0 6.0 %collective-permute-start.11 = (bf16[152,384]{1,0:T(8,128)(2,1)S(1)}, bf16[152,384]{1,0:T(8,128)(2,1)S(1)}, u32[]{:S(2)}, u32[]{:S(2)}) collective-permute-start(bf16[152,384]{1,0:T(8,128)(2,1)S(1)} %get-tuple-element.46), channel_id=1, source_target_pairs={{0,6},{1,7},{2,0},{3,1},{4,2},{5,3},{6,4},{7,5},{8,14},{9,15},{10,... | collective-permute-start | bytes 350216 | tf_op jit(solution)/shard_map/ppermute | solution.py:37
  133.4 5.3 %collective-permute-start.9 = (bf16[152,384]{1,0:T(8,128)(2,1)S(1)}, bf16[152,384]{1,0:T(8,128)(2,1)S(1)}, u32[]{:S(2)}, u32[]{:S(2)}) collective-permute-start(bf16[152,384]{1,0:T(8,128)(2,1)S(1)} %get-tuple-element.45), channel_id=1, source_target_pairs={{0,2},{1,3},{2,4},{3,5},{4,6},{5,7},{6,0},{7,1},{8,10},{9,11},{10,... | collective-permute-start | bytes 350216 | tf_op jit(solution)/shard_map/ppermute | solution.py:37
  133.7 8.1 %collective-permute-start.21 = (bf16[152,384]{1,0:T(8,128)(2,1)S(1)}, bf16[152,384]{1,0:T(8,128)(2,1)S(1)}, u32[]{:S(2)}, u32[]{:S(2)}) collective-permute-start(bf16[152,384]{1,0:T(8,128)(2,1)S(1)} %get-tuple-element.55), channel_id=1, source_target_pairs={{0,2},{1,3},{2,4},{3,5},{4,6},{5,7},{6,0},{7,1},{8,10},{9,11},{10,... | collective-permute-start | bytes 350216 | tf_op jit(solution)/shard_map/ppermute | solution.py:37
  134.3 8.7 %collective-permute-start.22 = (bf16[152,384]{1,0:T(8,128)(2,1)S(1)}, bf16[152,384]{1,0:T(8,128)(2,1)S(1)}, u32[]{:S(2)}, u32[]{:S(2)}) collective-permute-start(bf16[152,384]{1,0:T(8,128)(2,1)S(1)} %get-tuple-element.57), channel_id=1, source_target_pairs={{0,4},{1,5},{2,6},{3,7},{4,0},{5,1},{6,2},{7,3},{8,12},{9,13},{10,... | collective-permute-start | bytes 350216 | tf_op jit(solution)/shard_map/ppermute | solution.py:37
  137.6 5.5 %collective-permute-start.23 = (bf16[152,384]{1,0:T(8,128)(2,1)S(1)}, bf16[152,384]{1,0:T(8,128)(2,1)S(1)}, u32[]{:S(2)}, u32[]{:S(2)}) collective-permute-start(bf16[152,384]{1,0:T(8,128)(2,1)S(1)} %get-tuple-element.56), channel_id=1, source_target_pairs={{0,6},{1,7},{2,0},{3,1},{4,2},{5,3},{6,4},{7,5},{8,14},{9,15},{10,... | collective-permute-start | bytes 350216 | tf_op jit(solution)/shard_map/ppermute | solution.py:37
  (35 other events, 101.7 us)

commit v7 on v6

--- a/solution.py
+++ b/solution.py
@@ -208,8 +208,11 @@
         return lax.dynamic_update_slice_in_dim(projected, own_cols, col_start, 1).astype(jnp.bfloat16)
 
     pre_contribution = project(pre_out, hidden_in[per_home:])
-    dec_out, pre_contribution = lax.optimization_barrier((dec_out, pre_contribution))
-    contribution_rows = jnp.concatenate([project(dec_out, hidden_in[:per_home]), pre_contribution], axis=0)
+    row_count = hidden_in.shape[0]
+    half = row_count // 2
+    late_rows, _ = lax.optimization_barrier((pre_contribution[half - per_home :], arrived_q))
+    dec_out, early_rows = lax.optimization_barrier((dec_out, pre_contribution[: half - per_home]))
+    first_rows = jnp.concatenate([project(dec_out, hidden_in[:per_home]), early_rows], axis=0)
 
     def feed_forward(contribution):
         own_residual = pair_then_z_scatter(contribution).astype(jnp.bfloat16)
@@ -224,12 +227,10 @@
         down_cols = pair_then_z_scatter(down_part)
         return (own_residual.astype(jnp.float32) + down_cols).astype(jnp.bfloat16)
 
-    row_count = hidden_in.shape[0]
-    half = row_count // 2
     out_cols = jnp.concatenate(
         [
-            feed_forward(contribution_rows[:half]),
-            feed_forward(contribution_rows[half:]),
+            feed_forward(first_rows),
+            feed_forward(late_rows),
         ],
         axis=0,
     )

time: 173 us -> 184 us (1.064)
  other arithmetic: 29.2 us -> 37.3 us
  starting transfers between devices: 47.7 us -> 41.5 us
  matrix products: 35.7 us -> 39.7 us
  local copies, waits for them, and re-layouts: 10.6 us -> 13.9 us
    all_to_all x1, waiting for transfers between devices: 9.18 us -> 0.01 us  [on_device(): lax.all_to_all(going_back, 'req', split_axis=0, concat_axis=0, tiled=True)]
    ppermute x12, waiting for transfers between devices: 7.1 us -> 14 us  [pair_then_z_scatter(): acc = acc + lax.ppermute(piece, 'head', perm).astype(jnp.float32)]
    ppermute x6, waiting for transfers between devices: 2.16 us -> 6.58 us  [z_then_pair_gather(): parts.append(lax.ppermute(y, 'head', perm))]
    dot_general x2, matrix products: 1.15 us -> 4.36 us  [on_device(): jnp.dot(weights, cache_value[group_pos], preferred_element_type=jnp.float32)]
    all_to_all x1, blocking collectives: 11.8 us -> 14.6 us  [on_device(): lax.all_to_all(outgoing, 'req', split_axis=0, concat_axis=0, tiled=True)]
    unnamed x86 -> x114, local copies, waits for them, and re-layouts: 4.04 us -> 6.52 us
    all_to_all x1, blocking collectives: 15.8 us -> 13.3 us  [on_device(): lax.all_to_all(arrived, 'head', split_axis=0, concat_axis=1, tiled=True)]
    ppermute x12, starting transfers between devices: 16.7 us -> 14.3 us  [pair_then_z_scatter(): acc = acc + lax.ppermute(piece, 'head', perm).astype(jnp.float32)]
  transfers between devices with their start and end apart: 26 -> 26, of which waited for: 11 -> 11; matrix products, arithmetic and copies ran while one was open for 30% -> 37% of each run, Pallas kernels for 0% -> 0%
where the time goes in v7:
time: 184 us; the launch traced here: 183 us
  starting transfers between devices  41.5 us (23%)
  matrix products  39.7 us (22%)
  other arithmetic  37.3 us (20%)
  blocking collectives  27.9 us (15%)
  waiting for transfers between devices  20.9 us (11%)
  local copies, waits for them, and re-layouts  13.9 us (8%)
  between operations  1.91 us (1%)
    all_to_all x1, blocking collectives, on_device(): lax.all_to_all(outgoing, 'req', split_axis=0, concat_axis=0, tiled=True)  14.6 us
    ppermute x12, starting transfers between devices, pair_then_z_scatter(): acc = acc + lax.ppermute(piece, 'head', perm).astype(jnp.float32)  14.3 us
    ppermute x12, waiting for transfers between devices, pair_then_z_scatter(): acc = acc + lax.ppermute(piece, 'head', perm).astype(jnp.float32)  14 us
    all_to_all x1, blocking collectives, on_device(): lax.all_to_all(arrived, 'head', split_axis=0, concat_axis=1, tiled=True)  13.3 us
    dot_general x2, matrix products, feed_forward(): jnp.dot(hidden, down_weight, preferred_element_type=jnp.float32)  8.95 us
    unnamed x17, other arithmetic  7.91 us
    all_to_all x1, starting transfers between devices, on_device(): lax.all_to_all(outgoing_q, 'req', split_axis=0, concat_axis=0, tiled=True)  7.62 us
    all_to_all x1, starting transfers between devices, on_device(): lax.all_to_all(going_back, 'req', split_axis=0, concat_axis=0, tiled=True)  6.92 us
  transfers between devices with their start and end apart: 26, of which 11 were waited for; matrix products, arithmetic and copies ran while one was open for 37% of the time, Pallas kernels for 0%

profile of v7, /device:TPU:1, one launch (start us, length us, event | category | flops | bytes accessed | tf_op | source)
XLA Modules:
  0.0 183.2 jit_solution(8409828535600960036)
XLA Ops:
  2.4 1.9 %convolution_convert_fusion.3 = bf16[768,384]{1,0:T(8,128)(2,1)} fusion(bf16[48,384]{1,0:T(8,128)(2,1)} %param.19, s32[48]{0:T(128)S(1)} %dynamic-slice_add_fusion), kind=kOutput, calls=%fused_computation.55 | convolution fusion | flops 28643328 | bytes 626880 | tf_op jit(solution)/shard_map/dot_general | solution.py:108
  4.3 7.6 %all-to-all-start = ((bf16[16,48,384]{2,1,0:T(8,128)(2,1)}), bf16[16,48,384]{2,1,0:T(8,128)(2,1)}, u32[]{:S(2)}, u32[]{:S(2)}) async-start(bf16[16,48,384]{2,1,0:T(8,128)(2,1)} %bitcast.138), calls=%async_computation | async-start | bytes 1179648 | tf_op jit(solution)/shard_map/all_to_all | solution.py:109
  13.3 4.0 %fusion = (f32[1024]{0:T(1024)S(1)}, f32[1024,2048]{1,0:T(8,128)S(1)}) fusion(pred[2048]{0:T(1024)(128)(4,1)S(1)} %iota_compare_fusion.13, bf16[1024,384]{1,0:T(8,128)(2,1)S(1)} %bitcast.146, bf16[2,2048,384]{2,1,0:T(8,128)(2,1)} %param.25), kind=kOutput, calls=%fused_computation.3 | convolution fusion | flops 1616903168 | bytes 10754048 | tf_op jit(solution)/shard_map/dot_general | solution.py:181
  17.8 2.2 %fusion.1 = f32[1024]{0:T(1024)S(1)} fusion(f32[1024,2048]{1,0:T(8,128)S(1)} %get-tuple-element.77, f32[1024]{0:T(1024)S(1)} %max.12, pred[2048]{0:T(1024)(128)(4,1)S(1)} %iota_compare_fusion.13), kind=kLoop, calls=%fused_computation.4 | loop fusion | flops 8387584 | bytes 8398848 | tf_op jit(solution)/shard_map/reduce_sum | solution.py:193
  20.3 2.4 %fusion.2 = f32[1024,384]{1,0:T(8,128)S(1)} fusion(f32[1024,2048]{1,0:T(8,128)S(1)} %get-tuple-element.77, f32[1024]{0:T(1024)S(1)} %add.298, f32[1024]{0:T(1024)S(1)} %max.12, pred[2048]{0:T(1024)(128)(4,1)S(1)} %iota_compare_fusion.13, bf16[2,2048,384]{2,1,0:T(8,128)(2,1)S(1)} %copy-done.49), kind=kOutput, calls=%fused_computation.5 | convolution fusion | flops 1621098496 | bytes 11544576 | tf_op jit(solution)/shard_map/dot_general | solution.py:194
  23.3 4.3 %fusion.152 = f32[256,3072]{1,0:T(8,128)} fusion(bf16[256,384]{1,0:T(8,128)(2,1)S(1)} %select_reduce_fusion, bf16[384,3072]{1,0:T(8,128)(2,1)} %param.31), kind=kOutput, calls=%fused_computation.301 | convolution fusion | flops 603979776 | bytes 5701632 | tf_op jit(solution)/shard_map/dot_general | solution.py:204
  27.6 1.9 %add_dynamic-update-slice_fusion = f32[256,3072]{1,0:T(8,128)} fusion(f32[256,3072]{1,0:T(8,128)} %fusion.152, s32[]{:T(128)S(6)} %select_n.378, bf16[304,384]{1,0:T(8,128)(2,1)} %param.18), kind=kLoop, calls=%fused_computation.107 | loop fusion | flops 196608 | bytes 983044 | tf_op jit(solution)/shard_map/dynamic_update_slice | solution.py:208
  29.4 2.1 %convert_element_type.250 = bf16[256,3072]{1,0:T(8,128)(2,1)S(1)} convert(f32[256,3072]{1,0:T(8,128)} %add_dynamic-update-slice_fusion) | non-fusion elementwise | flops 786432 | bytes 4718592 | tf_op jit(solution)/shard_map/convert_element_type | solution.py:208
  41.2 2.2 %fusion.149 = (f32[192]{0:T(256)S(1)}, f32[192,2048]{1,0:T(8,128)S(1)}) fusion(bf16[192,384]{1,0:T(8,128)(2,1)S(1)} %bitcast.153, bf16[2,2048,384]{2,1,0:T(8,128)(2,1)} %param.25, pred[2048]{0:T(1024)(128)(4,1)S(1)} %iota_compare_fusion.14), kind=kOutput, calls=%fused_computation.298 | convolution fusion | flops 303169344 | bytes 3296000 | tf_op jit(solution)/shard_map/dot_general | solution.py:135
  52.8 2.3 %fusion.37 = bf16[48,384]{1,0:T(8,128)(2,1)S(1)} fusion(bf16[4,48,2048]{2,1,0:T(8,128)(2,1)} %bitcast.148, bf16[2,2048,384]{2,1,0:T(8,128)(2,1)} %param.26, pred[4,384]{1,0:T(4,128)(4,1)S(1)} %iota_compare_fusion.16), kind=kOutput, calls=%fused_computation.70 | convolution fusion | flops 302118912 | bytes 2397696 | tf_op jit(solution)/shard_map/dot_general | solution.py:144
  55.2 2.1 %fusion.40 = bf16[48,384]{1,0:T(8,128)(2,1)S(1)} fusion(bf16[4,48,2048]{2,1,0:T(8,128)(2,1)S(1)} %bitcast.149, bf16[2,2048,384]{2,1,0:T(8,128)(2,1)} %param.26, pred[4,384]{1,0:T(4,128)(4,1)S(1)} %iota_compare_fusion.16), kind=kOutput, calls=%fused_computation.71 | convolution fusion | flops 302118912 | bytes 2397696 | tf_op jit(solution)/shard_map/dot_general | solution.py:144
  60.0 3.8 %collective-permute-start.15 = (bf16[152,384]{1,0:T(8,128)(2,1)}, bf16[152,384]{1,0:T(8,128)(2,1)}, u32[]{:S(2)}, u32[]{:S(2)}) collective-permute-start(bf16[152,384]{1,0:T(8,128)(2,1)} %get-tuple-element.66), channel_id=1, source_target_pairs={{0,6},{1,7},{2,0},{3,1},{4,2},{5,3},{6,4},{7,5},{8,14},{9,15},{10,... | collective-permute-start | bytes 350216 | tf_op jit(solution)/shard_map/ppermute | solution.py:37
  65.9 6.9 %all-to-all-start.1 = ((bf16[16,48,512]{2,1,0:T(8,128)(2,1)}), bf16[16,48,512]{2,1,0:T(8,128)(2,1)}, u32[]{:S(2)}, u32[]{:S(2)}) async-start(bf16[16,48,512]{2,1,0:T(8,128)(2,1)} %bitcast.145), calls=%async_computation.1 | async-start | bytes 1572864 | tf_op jit(solution)/shard_map/all_to_all | solution.py:159
  74.0 2.1 %collective-permute-start.18 = (bf16[152,384]{1,0:T(8,128)(2,1)S(1)}, bf16[152,384]{1,0:T(8,128)(2,1)S(1)}, u32[]{:S(2)}, u32[]{:S(2)}) collective-permute-start(bf16[152,384]{1,0:T(8,128)(2,1)S(1)} %add_convert_fusion.5), channel_id=1, source_target_pairs={{0,6},{1,7},{2,0},{3,1},{4,2},{5,3},{6,4},{7,5},{8,14},{9,15},{10,... | collective-permute-start | bytes 350216 | tf_op jit(solution)/shard_map/ppermute | solution.py:51
  76.1 1.8 collective-permute-start.17
  78.7 3.0 %collective-permute-done.17 = bf16[152,384]{1,0:T(8,128)(2,1)S(1)} collective-permute-done((bf16[152,384]{1,0:T(8,128)(2,1)S(1)}, bf16[152,384]{1,0:T(8,128)(2,1)S(1)}, u32[]{:S(2)}, u32[]{:S(2)}) %collective-permute-start.17) | collective-permute-done | bytes 116768 | tf_op jit(solution)/shard_map/ppermute | solution.py:51
  81.6 2.8 %collective-permute-done.16 = bf16[152,384]{1,0:T(8,128)(2,1)S(1)} collective-permute-done((bf16[152,384]{1,0:T(8,128)(2,1)S(1)}, bf16[152,384]{1,0:T(8,128)(2,1)S(1)}, u32[]{:S(2)}, u32[]{:S(2)}) %collective-permute-start.16) | collective-permute-done | bytes 116768 | tf_op jit(solution)/shard_map/ppermute | solution.py:51
  92.1 2.3 %fusion.151 = f32[48,3072]{1,0:T(8,128)S(1)} fusion(bf16[48,384]{1,0:T(8,128)(2,1)S(1)} %fusion.114, bf16[384,3072]{1,0:T(8,128)(2,1)} %param.31), kind=kOutput, calls=%fused_computation.300 | convolution fusion | flops 113246208 | bytes 2985984 | tf_op jit(solution)/shard_map/dot_general | solution.py:204
  104.4 2.1 %collective-permute-start.3 = (bf16[152,384]{1,0:T(8,128)(2,1)S(1)}, bf16[152,384]{1,0:T(8,128)(2,1)S(1)}, u32[]{:S(2)}, u32[]{:S(2)}) collective-permute-start(bf16[152,384]{1,0:T(8,128)(2,1)S(1)} %get-tuple-element.56), channel_id=1, source_target_pairs={{0,6},{1,7},{2,0},{3,1},{4,2},{5,3},{6,4},{7,5},{8,14},{9,15},{10,... | collective-permute-start | bytes 350216 | tf_op jit(solution)/shard_map/ppermute | solution.py:37
  106.5 1.7 collective-permute-start.2
  108.3 1.5 fusion.71
  109.7 2.0 %collective-permute-done.2 = bf16[152,384]{1,0:T(8,128)(2,1)S(1)} collective-permute-done((bf16[152,384]{1,0:T(8,128)(2,1)S(1)}, bf16[152,384]{1,0:T(8,128)(2,1)S(1)}, u32[]{:S(2)}, u32[]{:S(2)}) %collective-permute-start.2) | collective-permute-done | bytes 116768 | tf_op jit(solution)/shard_map/ppermute | solution.py:37
  111.7 3.4 %collective-permute-done.1 = bf16[152,384]{1,0:T(8,128)(2,1)S(1)} collective-permute-done((bf16[152,384]{1,0:T(8,128)(2,1)S(1)}, bf16[152,384]{1,0:T(8,128)(2,1)S(1)}, u32[]{:S(2)}, u32[]{:S(2)}) %collective-permute-start.1) | collective-permute-done | bytes 116768 | tf_op jit(solution)/shard_map/ppermute | solution.py:37
  115.2 1.9 %collective-permute-start.5 = (bf16[152,384]{1,0:T(8,128)(2,1)S(1)}, bf16[152,384]{1,0:T(8,128)(2,1)S(1)}, u32[]{:S(2)}, u32[]{:S(2)}) collective-permute-start(bf16[152,384]{1,0:T(8,128)(2,1)S(1)} %add_convert_fusion.7), channel_id=1, source_target_pairs={{0,4},{1,5},{2,6},{3,7},{4,0},{5,1},{6,2},{7,3},{8,12},{9,13},{10,... | collective-permute-start | bytes 350216 | tf_op jit(solution)/shard_map/ppermute | solution.py:51
  117.9 4.5 %convolution_convert_fusion = bf16[152,3072]{1,0:T(8,128)(2,1)} fusion(bf16[512,3072]{1,0:T(8,128)(2,1)S(1)} %copy-done, bf16[3072,512]{1,0:T(8,128)(2,1)} %param.34, f32[152,512]{1,0:T(8,128)} %fusion.71, bf16[152,3072]{1,0:T(8,128)(2,1)} %copy-done.6, f32[152]{0:T(256)S(1)} %add_rsqrt_fusion, f32[3072]{0:T(1024)S(1)} %copy-done.54), kind=kOutput, calls=%fused_computation.6 | convolution fusion | flops 959102976 | bytes 8483424 | tf_op jit(solution)/shard_map/dot_general | solution.py:226
  124.1 2.5 %collective-permute-start.7 = (bf16[152,1536]{1,0:T(8,128)(2,1)S(1)}, bf16[152,1536]{1,0:T(8,128)(2,1)S(1)}, u32[]{:S(2)}, u32[]{:S(2)}) collective-permute-start(bf16[152,1536]{1,0:T(8,128)(2,1)S(1)} %pad_maximum_fusion.2), channel_id=1, source_target_pairs={{0,1},{1,0},{2,3},{3,2},{4,5},{5,4},{6,7},{7,6},{8,9},{9,8},{10,11... | collective-permute-start | bytes 1400840 | tf_op jit(solution)/shard_map/ppermute | solution.py:56
  131.3 4.5 %convolution_convert_fusion.1 = bf16[152,3072]{1,0:T(8,128)(2,1)} fusion(bf16[512,3072]{1,0:T(8,128)(2,1)S(1)} %copy-done, bf16[3072,512]{1,0:T(8,128)(2,1)} %param.34, f32[152,512]{1,0:T(8,128)} %fusion.75, bf16[152,3072]{1,0:T(8,128)(2,1)} %copy-done.7, f32[3072]{0:T(1024)S(1)} %copy-done.54, f32[152]{0:T(256)S(1)} %add_rsqrt_fusion.1), kind=kOutput, calls=%fused_computation.7 | convolution fusion | flops 959102976 | bytes 8483424 | tf_op jit(solution)/shard_map/dot_general | solution.py:226
  141.5 2.1 %collective-permute-start.11 = (bf16[152,384]{1,0:T(8,128)(2,1)S(1)}, bf16[152,384]{1,0:T(8,128)(2,1)S(1)}, u32[]{:S(2)}, u32[]{:S(2)}) collective-permute-start(bf16[152,384]{1,0:T(8,128)(2,1)S(1)} %get-tuple-element.49), channel_id=1, source_target_pairs={{0,6},{1,7},{2,0},{3,1},{4,2},{5,3},{6,4},{7,5},{8,14},{9,15},{10,... | collective-permute-start | bytes 350216 | tf_op jit(solution)/shard_map/ppermute | solution.py:37
  145.4 4.3 %collective-permute-done.21 = bf16[152,384]{1,0:T(8,128)(2,1)S(1)} collective-permute-done((bf16[152,384]{1,0:T(8,128)(2,1)S(1)}, bf16[152,384]{1,0:T(8,128)(2,1)S(1)}, u32[]{:S(2)}, u32[]{:S(2)}) %collective-permute-start.21) | collective-permute-done | bytes 116768 | tf_op jit(solution)/shard_map/ppermute | solution.py:37
  150.4 3.4 %collective-permute-done.9 = bf16[152,384]{1,0:T(8,128)(2,1)S(1)} collective-permute-done((bf16[152,384]{1,0:T(8,128)(2,1)S(1)}, bf16[152,384]{1,0:T(8,128)(2,1)S(1)}, u32[]{:S(2)}, u32[]{:S(2)}) %collective-permute-start.9) | collective-permute-done | bytes 116768 | tf_op jit(solution)/shard_map/ppermute | solution.py:37
  154.4 14.6 %all_to_all.52 = bf16[16,40,384]{2,1,0:T(8,128)(2,1)S(1)} all-to-all(bf16[16,40,384]{2,1,0:T(8,128)(2,1)S(1)} %bitcast.150), channel_id=1, replica_groups=mesh['req'=16,'head'=8] {'req'}, dimensions={0} | all-to-all | bytes 983040 | tf_op jit(solution)/shard_map/all_to_all | solution.py:249
  169.0 13.3 %all_to_all.53 = bf16[8,80,384]{2,1,0:T(8,128)(2,1)S(1)} all-to-all(bf16[8,80,384]{2,1,0:T(8,128)(2,1)S(1)} %bitcast.139), channel_id=1, replica_groups=mesh['req'=16,'head'=8] {'head'}, dimensions={0} | all-to-all | bytes 983040 | tf_op jit(solution)/shard_map/all_to_all | solution.py:250
  (274 shorter events, 63.9 us)
Async XLA Ops:
  0.0 117.9 %copy-start = (bf16[512,3072]{1,0:T(8,128)(2,1)S(1)}, bf16[512,3072]{1,0:T(8,128)(2,1)}, u32[]{:S(2)}) copy-start(bf16[512,3072]{1,0:T(8,128)(2,1)} %param.35) | copy-start | bytes 9437188
  0.0 13.2 %copy-start.36 = (bf16[256,384]{1,0:T(8,128)(2,1)S(1)}, bf16[256,384]{1,0:T(8,128)(2,1)}, u32[]{:S(2)}) copy-start(bf16[256,384]{1,0:T(8,128)(2,1)} %param.22) | copy-start | bytes 589828
  4.3 35.5 %all-to-all-start = ((bf16[16,48,384]{2,1,0:T(8,128)(2,1)}), bf16[16,48,384]{2,1,0:T(8,128)(2,1)}, u32[]{:S(2)}, u32[]{:S(2)}) async-start(bf16[16,48,384]{2,1,0:T(8,128)(2,1)} %bitcast.138), calls=%async_computation | async-start | bytes 1179648 | tf_op jit(solution)/shard_map/all_to_all | solution.py:109
  49.7 7.5 %collective-permute-start.12 = (bf16[152,1536]{1,0:T(8,128)(2,1)}, bf16[152,1536]{1,0:T(8,128)(2,1)}, u32[]{:S(2)}, u32[]{:S(2)}) collective-permute-start(bf16[152,1536]{1,0:T(8,128)(2,1)} %broadcast_select_fusion.2), channel_id=1, source_target_pairs={{0,1},{1,0},{2,3},{3,2},{4,5},{5,4},{6,7},{7,6},{8,9},{9,8},{10,11... | collective-permute-start | bytes 1400840 | tf_op jit(solution)/shard_map/ppermute | solution.py:31
  59.3 18.5 %copy-start.35 = (f32[48,384]{1,0:T(8,128)S(1)}, f32[48,384]{1,0:T(8,128)}, u32[]{:S(2)}) copy-start(f32[48,384]{1,0:T(8,128)} %convert_multiply_fusion.4) | copy-start | bytes 221188
  60.0 12.8 %collective-permute-start.15 = (bf16[152,384]{1,0:T(8,128)(2,1)}, bf16[152,384]{1,0:T(8,128)(2,1)}, u32[]{:S(2)}, u32[]{:S(2)}) collective-permute-start(bf16[152,384]{1,0:T(8,128)(2,1)} %get-tuple-element.66), channel_id=1, source_target_pairs={{0,6},{1,7},{2,0},{3,1},{4,2},{5,3},{6,4},{7,5},{8,14},{9,15},{10,... | collective-permute-start | bytes 350216 | tf_op jit(solution)/shard_map/ppermute | solution.py:37
  63.8 9.0 %collective-permute-start.14 = (bf16[152,384]{1,0:T(8,128)(2,1)S(1)}, bf16[152,384]{1,0:T(8,128)(2,1)}, u32[]{:S(2)}, u32[]{:S(2)}) collective-permute-start(bf16[152,384]{1,0:T(8,128)(2,1)S(1)} %get-tuple-element.67), channel_id=1, source_target_pairs={{0,4},{1,5},{2,6},{3,7},{4,0},{5,1},{6,2},{7,3},{8,12},{9,13},{10,... | collective-permute-start | bytes 350216 | tf_op jit(solution)/shard_map/ppermute | solution.py:37
  63.8 9.0 %collective-permute-start.13 = (bf16[152,384]{1,0:T(8,128)(2,1)S(1)}, bf16[152,384]{1,0:T(8,128)(2,1)}, u32[]{:S(2)}, u32[]{:S(2)}) collective-permute-start(bf16[152,384]{1,0:T(8,128)(2,1)S(1)} %get-tuple-element.65), channel_id=1, source_target_pairs={{0,2},{1,3},{2,4},{3,5},{4,6},{5,7},{6,0},{7,1},{8,10},{9,11},{10,... | collective-permute-start | bytes 350216 | tf_op jit(solution)/shard_map/ppermute | solution.py:37
  65.9 21.7 %all-to-all-start.1 = ((bf16[16,48,512]{2,1,0:T(8,128)(2,1)}), bf16[16,48,512]{2,1,0:T(8,128)(2,1)}, u32[]{:S(2)}, u32[]{:S(2)}) async-start(bf16[16,48,512]{2,1,0:T(8,128)(2,1)} %bitcast.145), calls=%async_computation.1 | async-start | bytes 1572864 | tf_op jit(solution)/shard_map/all_to_all | solution.py:159
  72.8 14.7 %copy-start.40 = (s32[48]{0:T(128)S(1)}, s32[48]{0:T(128)}, u32[]{:S(2)}) copy-start(s32[48]{0:T(128)} %copy-done.39) | copy-start | bytes 580
  74.0 4.7 %collective-permute-start.18 = (bf16[152,384]{1,0:T(8,128)(2,1)S(1)}, bf16[152,384]{1,0:T(8,128)(2,1)S(1)}, u32[]{:S(2)}, u32[]{:S(2)}) collective-permute-start(bf16[152,384]{1,0:T(8,128)(2,1)S(1)} %add_convert_fusion.5), channel_id=1, source_target_pairs={{0,6},{1,7},{2,0},{3,1},{4,2},{5,3},{6,4},{7,5},{8,14},{9,15},{10,... | collective-permute-start | bytes 350216 | tf_op jit(solution)/shard_map/ppermute | solution.py:51
  76.1 5.6 %collective-permute-start.17 = (bf16[152,384]{1,0:T(8,128)(2,1)S(1)}, bf16[152,384]{1,0:T(8,128)(2,1)S(1)}, u32[]{:S(2)}, u32[]{:S(2)}) collective-permute-start(bf16[152,384]{1,0:T(8,128)(2,1)S(1)} %add_convert_fusion.5), channel_id=1, source_target_pairs={{0,4},{1,5},{2,6},{3,7},{4,0},{5,1},{6,2},{7,3},{8,12},{9,13},{10,... | collective-permute-start | bytes 350216 | tf_op jit(solution)/shard_map/ppermute | solution.py:51
  77.8 6.6 %collective-permute-start.16 = (bf16[152,384]{1,0:T(8,128)(2,1)S(1)}, bf16[152,384]{1,0:T(8,128)(2,1)S(1)}, u32[]{:S(2)}, u32[]{:S(2)}) collective-permute-start(bf16[152,384]{1,0:T(8,128)(2,1)S(1)} %add_convert_fusion.5), channel_id=1, source_target_pairs={{0,2},{1,3},{2,4},{3,5},{4,6},{5,7},{6,0},{7,1},{8,10},{9,11},{10,... | collective-permute-start | bytes 350216 | tf_op jit(solution)/shard_map/ppermute | solution.py:51
  86.1 10.2 %collective-permute-start.19 = (bf16[152,1536]{1,0:T(8,128)(2,1)}, bf16[152,1536]{1,0:T(8,128)(2,1)}, u32[]{:S(2)}, u32[]{:S(2)}) collective-permute-start(bf16[152,1536]{1,0:T(8,128)(2,1)} %pad_maximum_fusion.8), channel_id=1, source_target_pairs={{0,1},{1,0},{2,3},{3,2},{4,5},{5,4},{6,7},{7,6},{8,9},{9,8},{10,11... | collective-permute-start | bytes 1400840 | tf_op jit(solution)/shard_map/ppermute | solution.py:56
  95.4 8.7 %collective-permute-start = (bf16[152,1536]{1,0:T(8,128)(2,1)S(1)}, bf16[152,1536]{1,0:T(8,128)(2,1)S(1)}, u32[]{:S(2)}, u32[]{:S(2)}) collective-permute-start(bf16[152,1536]{1,0:T(8,128)(2,1)S(1)} %broadcast_select_fusion.4), channel_id=1, source_target_pairs={{0,1},{1,0},{2,3},{3,2},{4,5},{5,4},{6,7},{7,6},{8,9},{9,8},{10,11... | collective-permute-start | bytes 1400840 | tf_op jit(solution)/shard_map/ppermute | solution.py:31
  104.4 5.3 %collective-permute-start.3 = (bf16[152,384]{1,0:T(8,128)(2,1)S(1)}, bf16[152,384]{1,0:T(8,128)(2,1)S(1)}, u32[]{:S(2)}, u32[]{:S(2)}) collective-permute-start(bf16[152,384]{1,0:T(8,128)(2,1)S(1)} %get-tuple-element.56), channel_id=1, source_target_pairs={{0,6},{1,7},{2,0},{3,1},{4,2},{5,3},{6,4},{7,5},{8,14},{9,15},{10,... | collective-permute-start | bytes 350216 | tf_op jit(solution)/shard_map/ppermute | solution.py:37
  106.5 5.2 %collective-permute-start.2 = (bf16[152,384]{1,0:T(8,128)(2,1)S(1)}, bf16[152,384]{1,0:T(8,128)(2,1)S(1)}, u32[]{:S(2)}, u32[]{:S(2)}) collective-permute-start(bf16[152,384]{1,0:T(8,128)(2,1)S(1)} %get-tuple-element.57), channel_id=1, source_target_pairs={{0,4},{1,5},{2,6},{3,7},{4,0},{5,1},{6,2},{7,3},{8,12},{9,13},{10,... | collective-permute-start | bytes 350216 | tf_op jit(solution)/shard_map/ppermute | solution.py:37
  108.3 6.8 %collective-permute-start.1 = (bf16[152,384]{1,0:T(8,128)(2,1)S(1)}, bf16[152,384]{1,0:T(8,128)(2,1)S(1)}, u32[]{:S(2)}, u32[]{:S(2)}) collective-permute-start(bf16[152,384]{1,0:T(8,128)(2,1)S(1)} %get-tuple-element.55), channel_id=1, source_target_pairs={{0,2},{1,3},{2,4},{3,5},{4,6},{5,7},{6,0},{7,1},{8,10},{9,11},{10,... | collective-permute-start | bytes 350216 | tf_op jit(solution)/shard_map/ppermute | solution.py:37
  115.2 7.2 %collective-permute-start.6 = (bf16[152,384]{1,0:T(8,128)(2,1)S(1)}, bf16[152,384]{1,0:T(8,128)(2,1)S(1)}, u32[]{:S(2)}, u32[]{:S(2)}) collective-permute-start(bf16[152,384]{1,0:T(8,128)(2,1)S(1)} %add_convert_fusion.7), channel_id=1, source_target_pairs={{0,6},{1,7},{2,0},{3,1},{4,2},{5,3},{6,4},{7,5},{8,14},{9,15},{10,... | collective-permute-start | bytes 350216 | tf_op jit(solution)/shard_map/ppermute | solution.py:51
  115.2 7.1 %collective-permute-start.5 = (bf16[152,384]{1,0:T(8,128)(2,1)S(1)}, bf16[152,384]{1,0:T(8,128)(2,1)S(1)}, u32[]{:S(2)}, u32[]{:S(2)}) collective-permute-start(bf16[152,384]{1,0:T(8,128)(2,1)S(1)} %add_convert_fusion.7), channel_id=1, source_target_pairs={{0,4},{1,5},{2,6},{3,7},{4,0},{5,1},{6,2},{7,3},{8,12},{9,13},{10,... | collective-permute-start | bytes 350216 | tf_op jit(solution)/shard_map/ppermute | solution.py:51
  117.1 5.9 %collective-permute-start.4 = (bf16[152,384]{1,0:T(8,128)(2,1)S(1)}, bf16[152,384]{1,0:T(8,128)(2,1)}, u32[]{:S(2)}, u32[]{:S(2)}) collective-permute-start(bf16[152,384]{1,0:T(8,128)(2,1)S(1)} %add_convert_fusion.7), channel_id=1, source_target_pairs={{0,2},{1,3},{2,4},{3,5},{4,6},{5,7},{6,0},{7,1},{8,10},{9,11},{10,... | collective-permute-start | bytes 350216 | tf_op jit(solution)/shard_map/ppermute | solution.py:51
  124.1 4.0 %collective-permute-start.7 = (bf16[152,1536]{1,0:T(8,128)(2,1)S(1)}, bf16[152,1536]{1,0:T(8,128)(2,1)S(1)}, u32[]{:S(2)}, u32[]{:S(2)}) collective-permute-start(bf16[152,1536]{1,0:T(8,128)(2,1)S(1)} %pad_maximum_fusion.2), channel_id=1, source_target_pairs={{0,1},{1,0},{2,3},{3,2},{4,5},{5,4},{6,7},{7,6},{8,9},{9,8},{10,11... | collective-permute-start | bytes 1400840 | tf_op jit(solution)/shard_map/ppermute | solution.py:56
  127.7 9.8 %collective-permute-start.20 = (bf16[152,1536]{1,0:T(8,128)(2,1)}, bf16[152,1536]{1,0:T(8,128)(2,1)}, u32[]{:S(2)}, u32[]{:S(2)}) collective-permute-start(bf16[152,1536]{1,0:T(8,128)(2,1)} %broadcast_select_fusion.1), channel_id=1, source_target_pairs={{0,1},{1,0},{2,3},{3,2},{4,5},{5,4},{6,7},{7,6},{8,9},{9,8},{10,11... | collective-permute-start | bytes 1400840 | tf_op jit(solution)/shard_map/ppermute | solution.py:31
  137.4 3.9 %collective-permute-start.8 = (bf16[152,1536]{1,0:T(8,128)(2,1)S(1)}, bf16[152,1536]{1,0:T(8,128)(2,1)S(1)}, u32[]{:S(2)}, u32[]{:S(2)}) collective-permute-start(bf16[152,1536]{1,0:T(8,128)(2,1)S(1)} %broadcast_select_fusion.3), channel_id=1, source_target_pairs={{0,1},{1,0},{2,3},{3,2},{4,5},{5,4},{6,7},{7,6},{8,9},{9,8},{10,11... | collective-permute-start | bytes 1400840 | tf_op jit(solution)/shard_map/ppermute | solution.py:31
  138.8 15.1 %copy-start.31 = (bf16[152,384]{1,0:T(8,128)(2,1)S(1)}, bf16[152,384]{1,0:T(8,128)(2,1)}, u32[]{:S(2)}) copy-start(bf16[152,384]{1,0:T(8,128)(2,1)} %copy-done.30) | copy-start | bytes 350212
  138.8 5.9 %collective-permute-start.23 = (bf16[152,384]{1,0:T(8,128)(2,1)S(1)}, bf16[152,384]{1,0:T(8,128)(2,1)S(1)}, u32[]{:S(2)}, u32[]{:S(2)}) collective-permute-start(bf16[152,384]{1,0:T(8,128)(2,1)S(1)} %get-tuple-element.59), channel_id=1, source_target_pairs={{0,6},{1,7},{2,0},{3,1},{4,2},{5,3},{6,4},{7,5},{8,14},{9,15},{10,... | collective-permute-start | bytes 350216 | tf_op jit(solution)/shard_map/ppermute | solution.py:37
  139.9 5.5 %collective-permute-start.22 = (bf16[152,384]{1,0:T(8,128)(2,1)S(1)}, bf16[152,384]{1,0:T(8,128)(2,1)S(1)}, u32[]{:S(2)}, u32[]{:S(2)}) collective-permute-start(bf16[152,384]{1,0:T(8,128)(2,1)S(1)} %get-tuple-element.60), channel_id=1, source_target_pairs={{0,4},{1,5},{2,6},{3,7},{4,0},{5,1},{6,2},{7,3},{8,12},{9,13},{10,... | collective-permute-start | bytes 350216 | tf_op jit(solution)/shard_map/ppermute | solution.py:37
  140.6 13.3 %copy-start.41 = (s32[304]{0:T(512)S(1)}, s32[304]{0:T(512)}, u32[]{:S(2)}) copy-start(s32[304]{0:T(512)} %multiply_add_fusion) | copy-start | bytes 3652
  140.6 9.1 %collective-permute-start.21 = (bf16[152,384]{1,0:T(8,128)(2,1)S(1)}, bf16[152,384]{1,0:T(8,128)(2,1)S(1)}, u32[]{:S(2)}, u32[]{:S(2)}) collective-permute-start(bf16[152,384]{1,0:T(8,128)(2,1)S(1)} %get-tuple-element.58), channel_id=1, source_target_pairs={{0,2},{1,3},{2,4},{3,5},{4,6},{5,7},{6,0},{7,1},{8,10},{9,11},{10,... | collective-permute-start | bytes 350216 | tf_op jit(solution)/shard_map/ppermute | solution.py:37
  141.5 8.4 %collective-permute-start.11 = (bf16[152,384]{1,0:T(8,128)(2,1)S(1)}, bf16[152,384]{1,0:T(8,128)(2,1)S(1)}, u32[]{:S(2)}, u32[]{:S(2)}) collective-permute-start(bf16[152,384]{1,0:T(8,128)(2,1)S(1)} %get-tuple-element.49), channel_id=1, source_target_pairs={{0,6},{1,7},{2,0},{3,1},{4,2},{5,3},{6,4},{7,5},{8,14},{9,15},{10,... | collective-permute-start | bytes 350216 | tf_op jit(solution)/shard_map/ppermute | solution.py:37
  143.6 6.8 %collective-permute-start.10 = (bf16[152,384]{1,0:T(8,128)(2,1)S(1)}, bf16[152,384]{1,0:T(8,128)(2,1)S(1)}, u32[]{:S(2)}, u32[]{:S(2)}) collective-permute-start(bf16[152,384]{1,0:T(8,128)(2,1)S(1)} %get-tuple-element.50), channel_id=1, source_target_pairs={{0,4},{1,5},{2,6},{3,7},{4,0},{5,1},{6,2},{7,3},{8,12},{9,13},{10,... | collective-permute-start | bytes 350216 | tf_op jit(solution)/shard_map/ppermute | solution.py:37
  144.7 9.2 %collective-permute-start.9 = (bf16[152,384]{1,0:T(8,128)(2,1)S(1)}, bf16[152,384]{1,0:T(8,128)(2,1)S(1)}, u32[]{:S(2)}, u32[]{:S(2)}) collective-permute-start(bf16[152,384]{1,0:T(8,128)(2,1)S(1)} %get-tuple-element.48), channel_id=1, source_target_pairs={{0,2},{1,3},{2,4},{3,5},{4,6},{5,7},{6,0},{7,1},{8,10},{9,11},{10,... | collective-permute-start | bytes 350216 | tf_op jit(solution)/shard_map/ppermute | solution.py:37
  (50 other events, 162.8 us)

commit v8 on v5

--- a/solution.py
+++ b/solution.py
@@ -21,13 +21,12 @@
     n = lax.axis_size("head")
     ring = n // 2
     width = cols // n
+    half = cols // 2
     h = lax.axis_index("head")
     zc = h // 2
     on_first = h % 2 == 0
-    even = jnp.concatenate([x[:, (2 * z) * width : (2 * z + 1) * width] for z in range(ring)], 1)
-    odd = jnp.concatenate([x[:, (2 * z + 1) * width : (2 * z + 2) * width] for z in range(ring)], 1)
-    mine = jnp.where(on_first, even, odd)
-    other = jnp.where(on_first, odd, even)
+    mine = jnp.where(on_first, x[:, :half], x[:, half:])
+    other = jnp.where(on_first, x[:, half:], x[:, :half])
     got = lax.ppermute(other, "head", [(i, i ^ 1) for i in range(n)])
     pair_sum = (mine.astype(jnp.float32) + got.astype(jnp.float32)).astype(jnp.bfloat16)
     acc = lax.dynamic_slice_in_dim(pair_sum, zc * width, width, 1).astype(jnp.float32)
@@ -54,13 +53,9 @@
         [lax.dynamic_index_in_dim(stacked, (zc - zz) % ring, 0, keepdims=False) for zz in range(ring)], 1
     )
     got = lax.ppermute(in_order, "head", [(i, i ^ 1) for i in range(n)])
-    pieces = []
-    for z in range(ring):
-        mine_z = in_order[:, z * width : (z + 1) * width]
-        got_z = got[:, z * width : (z + 1) * width]
-        pieces.append(jnp.where(on_first, mine_z, got_z))
-        pieces.append(jnp.where(on_first, got_z, mine_z))
-    return jnp.concatenate(pieces, 1)
+    return jnp.where(
+        on_first, jnp.concatenate([in_order, got], 1), jnp.concatenate([got, in_order], 1)
+    )
 
 
 def on_device(
@@ -242,7 +237,15 @@
     ).astype(jnp.bfloat16)
     outgoing = jnp.dot(placing, out_cols, preferred_element_type=jnp.float32).astype(jnp.bfloat16)
     arrived = lax.all_to_all(outgoing, "req", split_axis=0, concat_axis=0, tiled=True)
-    return lax.all_to_all(arrived, "head", split_axis=0, concat_axis=1, tiled=True)
+    routed = lax.all_to_all(arrived, "head", split_axis=0, concat_axis=1, tiled=True)
+    ring = head_count // 2
+    return jnp.concatenate(
+        [
+            routed[:, ((b % ring) * 2 + b // ring) * width_here : ((b % ring) * 2 + b // ring + 1) * width_here]
+            for b in range(head_count)
+        ],
+        axis=1,
+    )
 
 
 def solution(mesh):

time: 173 us -> 173 us (level)
  other arithmetic: 23.4 us -> 18.7 us
  matrix products: 39 us -> 41.5 us
  local copies, waits for them, and re-layouts: 11.7 us -> 13.7 us
    unnamed x17 -> x3, other arithmetic: 7.9 us -> 0.96 us
    unnamed x86 -> x89, local copies, waits for them, and re-layouts: 5.09 us -> 10.4 us
    slice x5 -> x1, local copies, waits for them, and re-layouts: 3.24 us -> 0.22 us  [the longest x4 3.03 us: pair_then_z_scatter(): x[:, 2 * z * width:(2 * z + 1) * width]]
    select_n x4, other arithmetic: 1.37 us -> 3.49 us  [pair_then_z_scatter(): other = jnp.where(on_first, x[:, half:], x[:, :half])]
  transfers between devices with their start and end apart: 26 -> 26, of which waited for: 11 -> 11; matrix products, arithmetic and copies ran while one was open for 29% -> 26% of each run, Pallas kernels for 0% -> 0%
where the time goes in v8:
time: 173 us; the launch traced here: 172 us
  starting transfers between devices  48.2 us (28%)
  matrix products  41.5 us (24%)
  blocking collectives  27.6 us (16%)
  waiting for transfers between devices  20.7 us (12%)
  other arithmetic  18.7 us (11%)
  local copies, waits for them, and re-layouts  13.7 us (8%)
    ppermute x12, starting transfers between devices, pair_then_z_scatter(): acc = acc + lax.ppermute(piece, 'head', perm).astype(jnp.float32)  17 us
    all_to_all x1, blocking collectives, on_device(): lax.all_to_all(arrived, 'head', split_axis=0, concat_axis=1, tiled=True)  15.6 us
    all_to_all x1, blocking collectives, on_device(): lax.all_to_all(outgoing, 'req', split_axis=0, concat_axis=0, tiled=True)  12 us
    all_to_all x1, waiting for transfers between devices, on_device(): lax.all_to_all(going_back, 'req', split_axis=0, concat_axis=0, tiled=True)  10.4 us
    unnamed x89, local copies, waits for them, and re-layouts  10.4 us
    dot_general x2, matrix products, feed_forward(): jnp.dot(hidden, down_weight, preferred_element_type=jnp.float32)  8.96 us
    ppermute x6, starting transfers between devices, z_then_pair_gather(): parts.append(lax.ppermute(y, 'head', perm))  8.22 us
    all_to_all x1, starting transfers between devices, on_device(): lax.all_to_all(outgoing_q, 'req', split_axis=0, concat_axis=0, tiled=True)  7.62 us
  transfers between devices with their start and end apart: 26, of which 11 were waited for; matrix products, arithmetic and copies ran while one was open for 26% of the time, Pallas kernels for 0%

profile of v8, /device:TPU:1, one launch (start us, length us, event | category | flops | bytes accessed | tf_op | source)
XLA Modules:
  0.0 172.1 jit_solution(7216992670828200724)
XLA Ops:
  2.4 1.9 %convolution_convert_fusion.3 = bf16[768,384]{1,0:T(8,128)(2,1)} fusion(bf16[48,384]{1,0:T(8,128)(2,1)} %param.19, s32[48]{0:T(128)S(1)} %dynamic-slice_add_fusion), kind=kOutput, calls=%fused_computation.48 | convolution fusion | flops 28643328 | bytes 626880 | tf_op jit(solution)/shard_map/dot_general | solution.py:103
  4.3 7.6 %all-to-all-start = ((bf16[16,48,384]{2,1,0:T(8,128)(2,1)}), bf16[16,48,384]{2,1,0:T(8,128)(2,1)}, u32[]{:S(2)}, u32[]{:S(2)}) async-start(bf16[16,48,384]{2,1,0:T(8,128)(2,1)} %bitcast.144), calls=%async_computation | async-start | bytes 1179648 | tf_op jit(solution)/shard_map/all_to_all | solution.py:104
  16.2 4.0 %fusion = (f32[1024]{0:T(1024)S(1)}, f32[1024,2048]{1,0:T(8,128)S(1)}) fusion(pred[2048]{0:T(1024)(128)(4,1)S(1)} %iota_compare_fusion.12, bf16[1024,384]{1,0:T(8,128)(2,1)S(1)} %bitcast.160, bf16[2,2048,384]{2,1,0:T(8,128)(2,1)} %param.25), kind=kOutput, calls=%fused_computation.3 | convolution fusion | flops 1616903168 | bytes 10754048 | tf_op jit(solution)/shard_map/dot_general | solution.py:176
  20.8 2.2 %fusion.1 = f32[1024]{0:T(1024)S(1)} fusion(f32[1024,2048]{1,0:T(8,128)S(1)} %get-tuple-element.62, f32[1024]{0:T(1024)S(1)} %max.12, pred[2048]{0:T(1024)(128)(4,1)S(1)} %iota_compare_fusion.12), kind=kLoop, calls=%fused_computation.4 | loop fusion | flops 8387584 | bytes 8398848 | tf_op jit(solution)/shard_map/reduce_sum | solution.py:188
  25.3 7.5 %fusion.2 = f32[1024,384]{1,0:T(8,128)} fusion(f32[1024,2048]{1,0:T(8,128)} %copy-done.2, f32[1024]{0:T(1024)S(1)} %add.298, f32[1024]{0:T(1024)S(1)} %max.12, pred[2048]{0:T(1024)(128)(4,1)S(1)} %iota_compare_fusion.12, bf16[2,2048,384]{2,1,0:T(8,128)(2,1)} %param.26), kind=kOutput, calls=%fused_computation.5 | convolution fusion | flops 1621098496 | bytes 11544576 | tf_op jit(solution)/shard_map/dot_general | solution.py:189
  35.0 2.2 %fusion.130 = (f32[192]{0:T(256)S(1)}, f32[192,2048]{1,0:T(8,128)S(1)}) fusion(bf16[192,384]{1,0:T(8,128)(2,1)S(1)} %bitcast.167, bf16[2,2048,384]{2,1,0:T(8,128)(2,1)} %param.25, pred[2048]{0:T(1024)(128)(4,1)S(1)} %iota_compare_fusion.14), kind=kOutput, calls=%fused_computation.270 | convolution fusion | flops 303169344 | bytes 3296000 | tf_op jit(solution)/shard_map/dot_general | solution.py:130
  43.0 2.2 %fusion.35 = bf16[48,384]{1,0:T(8,128)(2,1)S(1)} fusion(bf16[4,48,2048]{2,1,0:T(8,128)(2,1)} %bitcast.163, bf16[2,2048,384]{2,1,0:T(8,128)(2,1)} %param.26, pred[4,384]{1,0:T(4,128)(4,1)S(1)} %iota_compare_fusion.15), kind=kOutput, calls=%fused_computation.52 | convolution fusion | flops 302118912 | bytes 2397696 | tf_op jit(solution)/shard_map/dot_general | solution.py:139
  47.0 6.7 %all-to-all-start.1 = ((bf16[16,48,512]{2,1,0:T(8,128)(2,1)}), bf16[16,48,512]{2,1,0:T(8,128)(2,1)}, u32[]{:S(2)}, u32[]{:S(2)}) async-start(bf16[16,48,512]{2,1,0:T(8,128)(2,1)} %bitcast.159), calls=%async_computation.1 | async-start | bytes 1572864 | tf_op jit(solution)/shard_map/all_to_all | solution.py:154
  53.6 2.3 %convolution_add_fusion = f32[1024,384]{1,0:T(8,128)S(1)} fusion(f32[1024,384]{1,0:T(8,128)} %fusion.2, bf16[256,384]{1,0:T(8,128)(2,1)} %param.24, f32[1024,256]{0,1:T(8,128)} %copy-done.16, f32[1024]{0:T(1024)S(1)} %add.298, f32[1024]{0:T(1024)S(1)} %max.12), kind=kOutput, calls=%fused_computation.38 | convolution fusion | flops 202506240 | bytes 4399104 | tf_op jit(solution)/shard_map/dot_general | solution.py:191
  56.1 10.4 %all-to-all-done.1 = bf16[16,48,512]{2,1,0:T(8,128)(2,1)} async-done(((bf16[16,48,512]{2,1,0:T(8,128)(2,1)}), bf16[16,48,512]{2,1,0:T(8,128)(2,1)}, u32[]{:S(2)}, u32[]{:S(2)}) %all-to-all-start.1) | async-done | bytes 786464 | tf_op jit(solution)/shard_map/all_to_all | solution.py:154
  68.3 2.5 %fusion.71 = f32[152,3072]{1,0:T(8,128)S(1)} fusion(bf16[384,3072]{1,0:T(8,128)(2,1)} %param.31, bf16[256,384]{1,0:T(8,128)(2,1)S(1)} %select_reduce_fusion), kind=kOutput, calls=%fused_computation.123 | convolution fusion | flops 358612992 | bytes 4343808 | tf_op jit(solution)/shard_map/dot_general | solution.py:201
  72.0 2.5 %collective-permute-start = (bf16[152,1536]{1,0:T(8,128)(2,1)S(1)}, bf16[152,1536]{1,0:T(8,128)(2,1)S(1)}, u32[]{:S(2)}, u32[]{:S(2)}) collective-permute-start(bf16[152,1536]{1,0:T(8,128)(2,1)S(1)} %broadcast_select_fusion.6), channel_id=1, source_target_pairs={{0,1},{1,0},{2,3},{3,2},{4,5},{5,4},{6,7},{7,6},{8,9},{9,8},{10,11... | collective-permute-start | bytes 1400840 | tf_op jit(solution)/shard_map/ppermute | solution.py:30
  76.3 1.7 collective-permute-start.1
  78.0 3.3 %collective-permute-start.2 = (bf16[152,384]{1,0:T(8,128)(2,1)S(1)}, bf16[152,384]{1,0:T(8,128)(2,1)S(1)}, u32[]{:S(2)}, u32[]{:S(2)}) collective-permute-start(bf16[152,384]{1,0:T(8,128)(2,1)S(1)} %get-tuple-element.38), channel_id=1, source_target_pairs={{0,4},{1,5},{2,6},{3,7},{4,0},{5,1},{6,2},{7,3},{8,12},{9,13},{10,... | collective-permute-start | bytes 350216 | tf_op jit(solution)/shard_map/ppermute | solution.py:36
  83.5 2.1 %collective-permute-start.15 = (bf16[152,384]{1,0:T(8,128)(2,1)S(1)}, bf16[152,384]{1,0:T(8,128)(2,1)S(1)}, u32[]{:S(2)}, u32[]{:S(2)}) collective-permute-start(bf16[152,384]{1,0:T(8,128)(2,1)S(1)} %get-tuple-element.45), channel_id=1, source_target_pairs={{0,6},{1,7},{2,0},{3,1},{4,2},{5,3},{6,4},{7,5},{8,14},{9,15},{10,... | collective-permute-start | bytes 350216 | tf_op jit(solution)/shard_map/ppermute | solution.py:36
  86.8 1.7 collective-permute-start.4
  88.5 1.8 %collective-permute-start.5 = (bf16[152,384]{1,0:T(8,128)(2,1)S(1)}, bf16[152,384]{1,0:T(8,128)(2,1)S(1)}, u32[]{:S(2)}, u32[]{:S(2)}) collective-permute-start(bf16[152,384]{1,0:T(8,128)(2,1)S(1)} %add_convert_fusion.7), channel_id=1, source_target_pairs={{0,4},{1,5},{2,6},{3,7},{4,0},{5,1},{6,2},{7,3},{8,12},{9,13},{10,... | collective-permute-start | bytes 350216 | tf_op jit(solution)/shard_map/ppermute | solution.py:50
  91.8 1.6 collective-permute-start.16
  93.4 1.8 %collective-permute-start.17 = (bf16[152,384]{1,0:T(8,128)(2,1)S(1)}, bf16[152,384]{1,0:T(8,128)(2,1)S(1)}, u32[]{:S(2)}, u32[]{:S(2)}) collective-permute-start(bf16[152,384]{1,0:T(8,128)(2,1)S(1)} %add_convert_fusion.5), channel_id=1, source_target_pairs={{0,4},{1,5},{2,6},{3,7},{4,0},{5,1},{6,2},{7,3},{8,12},{9,13},{10,... | collective-permute-start | bytes 350216 | tf_op jit(solution)/shard_map/ppermute | solution.py:50
  97.0 2.4 %collective-permute-start.7 = (bf16[152,1536]{1,0:T(8,128)(2,1)S(1)}, bf16[152,1536]{1,0:T(8,128)(2,1)S(1)}, u32[]{:S(2)}, u32[]{:S(2)}) collective-permute-start(bf16[152,1536]{1,0:T(8,128)(2,1)S(1)} %pad_maximum_fusion.1), channel_id=1, source_target_pairs={{0,1},{1,0},{2,3},{3,2},{4,5},{5,4},{6,7},{7,6},{8,9},{9,8},{10,11... | collective-permute-start | bytes 1400840 | tf_op jit(solution)/shard_map/ppermute | solution.py:55
  102.7 2.4 %collective-permute-start.19 = (bf16[152,1536]{1,0:T(8,128)(2,1)}, bf16[152,1536]{1,0:T(8,128)(2,1)}, u32[]{:S(2)}, u32[]{:S(2)}) collective-permute-start(bf16[152,1536]{1,0:T(8,128)(2,1)} %pad_maximum_fusion.3), channel_id=1, source_target_pairs={{0,1},{1,0},{2,3},{3,2},{4,5},{5,4},{6,7},{7,6},{8,9},{9,8},{10,11... | collective-permute-start | bytes 1400840 | tf_op jit(solution)/shard_map/ppermute | solution.py:55
  109.0 4.5 %convolution_convert_fusion.1 = bf16[152,3072]{1,0:T(8,128)(2,1)} fusion(bf16[512,3072]{1,0:T(8,128)(2,1)S(1)} %copy-done, f32[152,512]{1,0:T(8,128)} %fusion.122, bf16[3072,512]{1,0:T(8,128)(2,1)} %param.34, f32[3072]{0:T(1024)S(1)} %copy-done.30, f32[152]{0:T(256)S(1)} %add_rsqrt_fusion.1, bf16[152,3072]{1,0:T(8,128)(2,1)} %copy-done.9, ...), kind=kOutput, calls=%fused_computation.7 | convolution fusion | flops 959569920 | bytes 9417313 | tf_op jit(solution)/shard_map/dot_general | solution.py:214
  113.5 2.0 %broadcast_select_fusion.5 = bf16[152,1536]{1,0:T(8,128)(2,1)} fusion(pred[]{:T(512)S(6)} %eq.233, bf16[152,3072]{1,0:T(8,128)(2,1)} %convolution_convert_fusion.1), kind=kLoop, calls=%fused_computation.77 | loop fusion | flops 233472 | bytes 1400833 | tf_op jit(solution)/shard_map/jit(_where)/select_n | solution.py:29
  115.6 2.1 %constant_dynamic-update-slice_fusion.19 = (bf16[152,3072]{1,0:T(8,128)(2,1)S(1)}, bf16[152,3072]{1,0:T(8,128)(2,1)}) fusion(bf16[152,1536]{1,0:T(8,128)(2,1)} %collective-permute-done.19, bf16[152,3072]{1,0:T(8,128)(2,1)} %copy-done.7), kind=kLoop, calls=%fused_computation.175 | loop fusion | bytes 1400832
  119.1 1.4 fusion.118
  120.5 4.5 %convolution_convert_fusion = bf16[152,3072]{1,0:T(8,128)(2,1)} fusion(bf16[512,3072]{1,0:T(8,128)(2,1)S(1)} %copy-done, f32[152,512]{1,0:T(8,128)} %fusion.118, bf16[3072,512]{1,0:T(8,128)(2,1)} %param.34, f32[152]{0:T(256)S(1)} %add_rsqrt_fusion, f32[3072]{0:T(1024)S(1)} %copy-done.30, bf16[152,3072]{1,0:T(8,128)(2,1)} %get-tuple-element.43, ...), kind=kOutput, calls=%fused_computation.6 | convolution fusion | flops 959569920 | bytes 9417313 | tf_op jit(solution)/shard_map/dot_general | solution.py:214
  128.9 2.0 %collective-permute-start.10 = (bf16[152,384]{1,0:T(8,128)(2,1)S(1)}, bf16[152,384]{1,0:T(8,128)(2,1)S(1)}, u32[]{:S(2)}, u32[]{:S(2)}) collective-permute-start(bf16[152,384]{1,0:T(8,128)(2,1)S(1)} %get-tuple-element.33), channel_id=1, source_target_pairs={{0,4},{1,5},{2,6},{3,7},{4,0},{5,1},{6,2},{7,3},{8,12},{9,13},{10,... | collective-permute-start | bytes 350216 | tf_op jit(solution)/shard_map/ppermute | solution.py:36
  133.2 3.2 %collective-permute-start.22 = (bf16[152,384]{1,0:T(8,128)(2,1)S(1)}, bf16[152,384]{1,0:T(8,128)(2,1)S(1)}, u32[]{:S(2)}, u32[]{:S(2)}) collective-permute-start(bf16[152,384]{1,0:T(8,128)(2,1)S(1)} %get-tuple-element.41), channel_id=1, source_target_pairs={{0,4},{1,5},{2,6},{3,7},{4,0},{5,1},{6,2},{7,3},{8,12},{9,13},{10,... | collective-permute-start | bytes 350216 | tf_op jit(solution)/shard_map/ppermute | solution.py:36
  137.8 2.8 %collective-permute-done.21 = bf16[152,384]{1,0:T(8,128)(2,1)S(1)} collective-permute-done((bf16[152,384]{1,0:T(8,128)(2,1)S(1)}, bf16[152,384]{1,0:T(8,128)(2,1)S(1)}, u32[]{:S(2)}, u32[]{:S(2)}) %collective-permute-start.21) | collective-permute-done | bytes 116768 | tf_op jit(solution)/shard_map/ppermute | solution.py:36
  140.5 1.8 %collective-permute-done.22 = bf16[152,384]{1,0:T(8,128)(2,1)S(1)} collective-permute-done((bf16[152,384]{1,0:T(8,128)(2,1)S(1)}, bf16[152,384]{1,0:T(8,128)(2,1)S(1)}, u32[]{:S(2)}, u32[]{:S(2)}) %collective-permute-start.22) | collective-permute-done | bytes 116768 | tf_op jit(solution)/shard_map/ppermute | solution.py:36
  142.9 12.0 %all_to_all.52 = bf16[16,40,384]{2,1,0:T(8,128)(2,1)S(1)} all-to-all(bf16[16,40,384]{2,1,0:T(8,128)(2,1)S(1)} %bitcast.164), channel_id=1, replica_groups=mesh['req'=16,'head'=8] {'req'}, dimensions={0} | all-to-all | bytes 983040 | tf_op jit(solution)/shard_map/all_to_all | solution.py:239
  154.9 15.6 %all_to_all.53 = bf16[8,80,384]{2,1,0:T(8,128)(2,1)S(1)} all-to-all(bf16[8,80,384]{2,1,0:T(8,128)(2,1)S(1)} %bitcast.153), channel_id=1, replica_groups=mesh['req'=16,'head'=8] {'head'}, dimensions={0} | all-to-all | bytes 983040 | tf_op jit(solution)/shard_map/all_to_all | solution.py:240
  (226 shorter events, 47.8 us)
Async XLA Ops:
  0.0 109.0 %copy-start = (bf16[512,3072]{1,0:T(8,128)(2,1)S(1)}, bf16[512,3072]{1,0:T(8,128)(2,1)}, u32[]{:S(2)}) copy-start(bf16[512,3072]{1,0:T(8,128)(2,1)} %param.35) | copy-start | bytes 9437188
  0.0 13.8 %copy-start.23 = (s32[2]{0:T(128)S(1)}, s32[2]{0:T(128)}, u32[]{:S(2)}) copy-start(s32[2]{0:T(128)} %param.28) | copy-start | bytes 28
  0.0 16.1 %copy-start.18 = (bf16[256,384]{1,0:T(8,128)(2,1)S(1)}, bf16[256,384]{1,0:T(8,128)(2,1)}, u32[]{:S(2)}) copy-start(bf16[256,384]{1,0:T(8,128)(2,1)} %param.22) | copy-start | bytes 589828
  4.3 29.3 %all-to-all-start = ((bf16[16,48,384]{2,1,0:T(8,128)(2,1)}), bf16[16,48,384]{2,1,0:T(8,128)(2,1)}, u32[]{:S(2)}, u32[]{:S(2)}) async-start(bf16[16,48,384]{2,1,0:T(8,128)(2,1)} %bitcast.144), calls=%async_computation | async-start | bytes 1179648 | tf_op jit(solution)/shard_map/all_to_all | solution.py:104
  25.3 8.1 %copy-start.19 = (bf16[48,384]{1,0:T(8,128)(2,1)S(1)}, bf16[48,384]{1,0:T(8,128)(2,1)}, u32[]{:S(2)}) copy-start(bf16[48,384]{1,0:T(8,128)(2,1)} %param.19) | copy-start | bytes 110596
  25.3 8.1 %copy-start.21 = (bf16[48,384]{1,0:T(8,128)(2,1)S(1)}, bf16[48,384]{1,0:T(8,128)(2,1)}, u32[]{:S(2)}) copy-start(bf16[48,384]{1,0:T(8,128)(2,1)} %param.20) | copy-start | bytes 110596
  47.0 19.5 %all-to-all-start.1 = ((bf16[16,48,512]{2,1,0:T(8,128)(2,1)}), bf16[16,48,512]{2,1,0:T(8,128)(2,1)}, u32[]{:S(2)}, u32[]{:S(2)}) async-start(bf16[16,48,512]{2,1,0:T(8,128)(2,1)} %bitcast.159), calls=%async_computation.1 | async-start | bytes 1572864 | tf_op jit(solution)/shard_map/all_to_all | solution.py:154
  56.0 12.3 %copy-start.20 = (bf16[48,384]{1,0:T(8,128)(2,1)S(1)}, bf16[48,384]{1,0:T(8,128)(2,1)}, u32[]{:S(2)}) copy-start(bf16[48,384]{1,0:T(8,128)(2,1)} %param.21) | copy-start | bytes 110596
  72.0 4.0 %collective-permute-start = (bf16[152,1536]{1,0:T(8,128)(2,1)S(1)}, bf16[152,1536]{1,0:T(8,128)(2,1)S(1)}, u32[]{:S(2)}, u32[]{:S(2)}) collective-permute-start(bf16[152,1536]{1,0:T(8,128)(2,1)S(1)} %broadcast_select_fusion.6), channel_id=1, source_target_pairs={{0,1},{1,0},{2,3},{3,2},{4,5},{5,4},{6,7},{7,6},{8,9},{9,8},{10,11... | collective-permute-start | bytes 1400840 | tf_op jit(solution)/shard_map/ppermute | solution.py:30
  74.8 7.3 %collective-permute-start.12 = (bf16[152,1536]{1,0:T(8,128)(2,1)S(1)}, bf16[152,1536]{1,0:T(8,128)(2,1)S(1)}, u32[]{:S(2)}, u32[]{:S(2)}) collective-permute-start(bf16[152,1536]{1,0:T(8,128)(2,1)S(1)} %broadcast_select_fusion.4), channel_id=1, source_target_pairs={{0,1},{1,0},{2,3},{3,2},{4,5},{5,4},{6,7},{7,6},{8,9},{9,8},{10,11... | collective-permute-start | bytes 1400840 | tf_op jit(solution)/shard_map/ppermute | solution.py:30
  76.3 7.2 %collective-permute-start.1 = (bf16[152,384]{1,0:T(8,128)(2,1)S(1)}, bf16[152,384]{1,0:T(8,128)(2,1)S(1)}, u32[]{:S(2)}, u32[]{:S(2)}) collective-permute-start(bf16[152,384]{1,0:T(8,128)(2,1)S(1)} %get-tuple-element.36), channel_id=1, source_target_pairs={{0,2},{1,3},{2,4},{3,5},{4,6},{5,7},{6,0},{7,1},{8,10},{9,11},{10,... | collective-permute-start | bytes 350216 | tf_op jit(solution)/shard_map/ppermute | solution.py:36
  78.0 8.7 %collective-permute-start.2 = (bf16[152,384]{1,0:T(8,128)(2,1)S(1)}, bf16[152,384]{1,0:T(8,128)(2,1)S(1)}, u32[]{:S(2)}, u32[]{:S(2)}) collective-permute-start(bf16[152,384]{1,0:T(8,128)(2,1)S(1)} %get-tuple-element.38), channel_id=1, source_target_pairs={{0,4},{1,5},{2,6},{3,7},{4,0},{5,1},{6,2},{7,3},{8,12},{9,13},{10,... | collective-permute-start | bytes 350216 | tf_op jit(solution)/shard_map/ppermute | solution.py:36
  81.3 5.4 %collective-permute-start.3 = (bf16[152,384]{1,0:T(8,128)(2,1)S(1)}, bf16[152,384]{1,0:T(8,128)(2,1)S(1)}, u32[]{:S(2)}, u32[]{:S(2)}) collective-permute-start(bf16[152,384]{1,0:T(8,128)(2,1)S(1)} %get-tuple-element.37), channel_id=1, source_target_pairs={{0,6},{1,7},{2,0},{3,1},{4,2},{5,3},{6,4},{7,5},{8,14},{9,15},{10,... | collective-permute-start | bytes 350216 | tf_op jit(solution)/shard_map/ppermute | solution.py:36
  82.3 8.1 %collective-permute-start.13 = (bf16[152,384]{1,0:T(8,128)(2,1)S(1)}, bf16[152,384]{1,0:T(8,128)(2,1)S(1)}, u32[]{:S(2)}, u32[]{:S(2)}) collective-permute-start(bf16[152,384]{1,0:T(8,128)(2,1)S(1)} %get-tuple-element.44), channel_id=1, source_target_pairs={{0,2},{1,3},{2,4},{3,5},{4,6},{5,7},{6,0},{7,1},{8,10},{9,11},{10,... | collective-permute-start | bytes 350216 | tf_op jit(solution)/shard_map/ppermute | solution.py:36
  83.1 8.6 %collective-permute-start.14 = (bf16[152,384]{1,0:T(8,128)(2,1)S(1)}, bf16[152,384]{1,0:T(8,128)(2,1)S(1)}, u32[]{:S(2)}, u32[]{:S(2)}) collective-permute-start(bf16[152,384]{1,0:T(8,128)(2,1)S(1)} %get-tuple-element.46), channel_id=1, source_target_pairs={{0,4},{1,5},{2,6},{3,7},{4,0},{5,1},{6,2},{7,3},{8,12},{9,13},{10,... | collective-permute-start | bytes 350216 | tf_op jit(solution)/shard_map/ppermute | solution.py:36
  83.5 8.2 %collective-permute-start.15 = (bf16[152,384]{1,0:T(8,128)(2,1)S(1)}, bf16[152,384]{1,0:T(8,128)(2,1)S(1)}, u32[]{:S(2)}, u32[]{:S(2)}) collective-permute-start(bf16[152,384]{1,0:T(8,128)(2,1)S(1)} %get-tuple-element.45), channel_id=1, source_target_pairs={{0,6},{1,7},{2,0},{3,1},{4,2},{5,3},{6,4},{7,5},{8,14},{9,15},{10,... | collective-permute-start | bytes 350216 | tf_op jit(solution)/shard_map/ppermute | solution.py:36
  86.8 8.4 %collective-permute-start.4 = (bf16[152,384]{1,0:T(8,128)(2,1)S(1)}, bf16[152,384]{1,0:T(8,128)(2,1)S(1)}, u32[]{:S(2)}, u32[]{:S(2)}) collective-permute-start(bf16[152,384]{1,0:T(8,128)(2,1)S(1)} %add_convert_fusion.7), channel_id=1, source_target_pairs={{0,2},{1,3},{2,4},{3,5},{4,6},{5,7},{6,0},{7,1},{8,10},{9,11},{10,... | collective-permute-start | bytes 350216 | tf_op jit(solution)/shard_map/ppermute | solution.py:50
  88.5 8.2 %collective-permute-start.5 = (bf16[152,384]{1,0:T(8,128)(2,1)S(1)}, bf16[152,384]{1,0:T(8,128)(2,1)S(1)}, u32[]{:S(2)}, u32[]{:S(2)}) collective-permute-start(bf16[152,384]{1,0:T(8,128)(2,1)S(1)} %add_convert_fusion.7), channel_id=1, source_target_pairs={{0,4},{1,5},{2,6},{3,7},{4,0},{5,1},{6,2},{7,3},{8,12},{9,13},{10,... | collective-permute-start | bytes 350216 | tf_op jit(solution)/shard_map/ppermute | solution.py:50
  90.3 6.4 %collective-permute-start.6 = (bf16[152,384]{1,0:T(8,128)(2,1)S(1)}, bf16[152,384]{1,0:T(8,128)(2,1)S(1)}, u32[]{:S(2)}, u32[]{:S(2)}) collective-permute-start(bf16[152,384]{1,0:T(8,128)(2,1)S(1)} %add_convert_fusion.7), channel_id=1, source_target_pairs={{0,6},{1,7},{2,0},{3,1},{4,2},{5,3},{6,4},{7,5},{8,14},{9,15},{10,... | collective-permute-start | bytes 350216 | tf_op jit(solution)/shard_map/ppermute | solution.py:50
  91.8 8.0 %collective-permute-start.16 = (bf16[152,384]{1,0:T(8,128)(2,1)S(1)}, bf16[152,384]{1,0:T(8,128)(2,1)S(1)}, u32[]{:S(2)}, u32[]{:S(2)}) collective-permute-start(bf16[152,384]{1,0:T(8,128)(2,1)S(1)} %add_convert_fusion.5), channel_id=1, source_target_pairs={{0,2},{1,3},{2,4},{3,5},{4,6},{5,7},{6,0},{7,1},{8,10},{9,11},{10,... | collective-permute-start | bytes 350216 | tf_op jit(solution)/shard_map/ppermute | solution.py:50
  93.4 7.2 %collective-permute-start.17 = (bf16[152,384]{1,0:T(8,128)(2,1)S(1)}, bf16[152,384]{1,0:T(8,128)(2,1)S(1)}, u32[]{:S(2)}, u32[]{:S(2)}) collective-permute-start(bf16[152,384]{1,0:T(8,128)(2,1)S(1)} %add_convert_fusion.5), channel_id=1, source_target_pairs={{0,4},{1,5},{2,6},{3,7},{4,0},{5,1},{6,2},{7,3},{8,12},{9,13},{10,... | collective-permute-start | bytes 350216 | tf_op jit(solution)/shard_map/ppermute | solution.py:50
  95.2 5.4 %collective-permute-start.18 = (bf16[152,384]{1,0:T(8,128)(2,1)S(1)}, bf16[152,384]{1,0:T(8,128)(2,1)S(1)}, u32[]{:S(2)}, u32[]{:S(2)}) collective-permute-start(bf16[152,384]{1,0:T(8,128)(2,1)S(1)} %add_convert_fusion.5), channel_id=1, source_target_pairs={{0,6},{1,7},{2,0},{3,1},{4,2},{5,3},{6,4},{7,5},{8,14},{9,15},{10,... | collective-permute-start | bytes 350216 | tf_op jit(solution)/shard_map/ppermute | solution.py:50
  97.0 8.0 %collective-permute-start.7 = (bf16[152,1536]{1,0:T(8,128)(2,1)S(1)}, bf16[152,1536]{1,0:T(8,128)(2,1)S(1)}, u32[]{:S(2)}, u32[]{:S(2)}) collective-permute-start(bf16[152,1536]{1,0:T(8,128)(2,1)S(1)} %pad_maximum_fusion.1), channel_id=1, source_target_pairs={{0,1},{1,0},{2,3},{3,2},{4,5},{5,4},{6,7},{7,6},{8,9},{9,8},{10,11... | collective-permute-start | bytes 1400840 | tf_op jit(solution)/shard_map/ppermute | solution.py:55
  102.7 12.9 %collective-permute-start.19 = (bf16[152,1536]{1,0:T(8,128)(2,1)}, bf16[152,1536]{1,0:T(8,128)(2,1)}, u32[]{:S(2)}, u32[]{:S(2)}) collective-permute-start(bf16[152,1536]{1,0:T(8,128)(2,1)} %pad_maximum_fusion.3), channel_id=1, source_target_pairs={{0,1},{1,0},{2,3},{3,2},{4,5},{5,4},{6,7},{7,6},{8,9},{9,8},{10,11... | collective-permute-start | bytes 1400840 | tf_op jit(solution)/shard_map/ppermute | solution.py:55
  115.6 12.1 %collective-permute-start.8 = (bf16[152,1536]{1,0:T(8,128)(2,1)}, bf16[152,1536]{1,0:T(8,128)(2,1)}, u32[]{:S(2)}, u32[]{:S(2)}) collective-permute-start(bf16[152,1536]{1,0:T(8,128)(2,1)} %broadcast_select_fusion.5), channel_id=1, source_target_pairs={{0,1},{1,0},{2,3},{3,2},{4,5},{5,4},{6,7},{7,6},{8,9},{9,8},{10,11... | collective-permute-start | bytes 1400840 | tf_op jit(solution)/shard_map/ppermute | solution.py:30
  126.4 6.0 %collective-permute-start.20 = (bf16[152,1536]{1,0:T(8,128)(2,1)S(1)}, bf16[152,1536]{1,0:T(8,128)(2,1)S(1)}, u32[]{:S(2)}, u32[]{:S(2)}) collective-permute-start(bf16[152,1536]{1,0:T(8,128)(2,1)S(1)} %broadcast_select_fusion.3), channel_id=1, source_target_pairs={{0,1},{1,0},{2,3},{3,2},{4,5},{5,4},{6,7},{7,6},{8,9},{9,8},{10,11... | collective-permute-start | bytes 1400840 | tf_op jit(solution)/shard_map/ppermute | solution.py:30
  128.9 7.6 %collective-permute-start.10 = (bf16[152,384]{1,0:T(8,128)(2,1)S(1)}, bf16[152,384]{1,0:T(8,128)(2,1)S(1)}, u32[]{:S(2)}, u32[]{:S(2)}) collective-permute-start(bf16[152,384]{1,0:T(8,128)(2,1)S(1)} %get-tuple-element.33), channel_id=1, source_target_pairs={{0,4},{1,5},{2,6},{3,7},{4,0},{5,1},{6,2},{7,3},{8,12},{9,13},{10,... | collective-permute-start | bytes 350216 | tf_op jit(solution)/shard_map/ppermute | solution.py:36
  130.9 6.3 %collective-permute-start.11 = (bf16[152,384]{1,0:T(8,128)(2,1)S(1)}, bf16[152,384]{1,0:T(8,128)(2,1)S(1)}, u32[]{:S(2)}, u32[]{:S(2)}) collective-permute-start(bf16[152,384]{1,0:T(8,128)(2,1)S(1)} %get-tuple-element.32), channel_id=1, source_target_pairs={{0,6},{1,7},{2,0},{3,1},{4,2},{5,3},{6,4},{7,5},{8,14},{9,15},{10,... | collective-permute-start | bytes 350216 | tf_op jit(solution)/shard_map/ppermute | solution.py:36
  132.3 5.4 %collective-permute-start.9 = (bf16[152,384]{1,0:T(8,128)(2,1)S(1)}, bf16[152,384]{1,0:T(8,128)(2,1)S(1)}, u32[]{:S(2)}, u32[]{:S(2)}) collective-permute-start(bf16[152,384]{1,0:T(8,128)(2,1)S(1)} %get-tuple-element.31), channel_id=1, source_target_pairs={{0,2},{1,3},{2,4},{3,5},{4,6},{5,7},{6,0},{7,1},{8,10},{9,11},{10,... | collective-permute-start | bytes 350216 | tf_op jit(solution)/shard_map/ppermute | solution.py:36
  132.6 7.9 %collective-permute-start.21 = (bf16[152,384]{1,0:T(8,128)(2,1)S(1)}, bf16[152,384]{1,0:T(8,128)(2,1)S(1)}, u32[]{:S(2)}, u32[]{:S(2)}) collective-permute-start(bf16[152,384]{1,0:T(8,128)(2,1)S(1)} %get-tuple-element.39), channel_id=1, source_target_pairs={{0,2},{1,3},{2,4},{3,5},{4,6},{5,7},{6,0},{7,1},{8,10},{9,11},{10,... | collective-permute-start | bytes 350216 | tf_op jit(solution)/shard_map/ppermute | solution.py:36
  133.2 9.1 %collective-permute-start.22 = (bf16[152,384]{1,0:T(8,128)(2,1)S(1)}, bf16[152,384]{1,0:T(8,128)(2,1)S(1)}, u32[]{:S(2)}, u32[]{:S(2)}) collective-permute-start(bf16[152,384]{1,0:T(8,128)(2,1)S(1)} %get-tuple-element.41), channel_id=1, source_target_pairs={{0,4},{1,5},{2,6},{3,7},{4,0},{5,1},{6,2},{7,3},{8,12},{9,13},{10,... | collective-permute-start | bytes 350216 | tf_op jit(solution)/shard_map/ppermute | solution.py:36
  136.5 5.8 %collective-permute-start.23 = (bf16[152,384]{1,0:T(8,128)(2,1)S(1)}, bf16[152,384]{1,0:T(8,128)(2,1)S(1)}, u32[]{:S(2)}, u32[]{:S(2)}) collective-permute-start(bf16[152,384]{1,0:T(8,128)(2,1)S(1)} %get-tuple-element.40), channel_id=1, source_target_pairs={{0,6},{1,7},{2,0},{3,1},{4,2},{5,3},{6,4},{7,5},{8,14},{9,15},{10,... | collective-permute-start | bytes 350216 | tf_op jit(solution)/shard_map/ppermute | solution.py:36
  (25 other events, 70.4 us)

commit v9 on v5

--- a/solution.py
+++ b/solution.py
@@ -197,8 +197,11 @@
     pre_out = jnp.sum(
         jnp.where(head_mask[:, None, :], pre_mixed.reshape(heads_here, stretch_len, width_here), 0.0), axis=0
     ).astype(jnp.bfloat16)
-    dec_out, pre_out = lax.optimization_barrier((dec_out, pre_out))
-    attn_rows = jnp.concatenate([dec_out, pre_out], axis=0)
+    row_count = hidden_in.shape[0]
+    half = row_count // 2
+    late_attn, _ = lax.optimization_barrier((pre_out[half - per_home :], going_back))
+    dec_out, early_pre = lax.optimization_barrier((dec_out, pre_out[: half - per_home]))
+    early_attn = jnp.concatenate([dec_out, early_pre], axis=0)
     head_me = lax.axis_index("head")
     col_start = head_me * width_here
 
@@ -220,12 +223,10 @@
         down_cols = pair_then_z_scatter(down_part)
         return (own_residual.astype(jnp.float32) + down_cols).astype(jnp.bfloat16)
 
-    row_count = hidden_in.shape[0]
-    half = row_count // 2
     out_cols = jnp.concatenate(
         [
-            feed_forward(attn_rows[:half], hidden_in[:half]),
-            feed_forward(attn_rows[half:], hidden_in[half:]),
+            feed_forward(early_attn, hidden_in[:half]),
+            feed_forward(late_attn, hidden_in[half:]),
         ],
         axis=0,
     )

time: 173 us -> 167 us (0.965)
  matrix products: 39 us -> 35.1 us
    dot_general x1, matrix products: 7.43 us -> 2.38 us  [on_device(): jnp.dot((raised_cache / total).astype(jnp.bfloat16), cache_value[0], pref...]
    dot_general x2, matrix products: 3.13 us -> 6.08 us  [feed_forward(): jnp.dot(attn_chunk, out_weight, preferred_element_type=jnp.float32)]
    dot_general x1, matrix products: 2.33 us -> 0.49 us  [on_device(): jnp.dot((raised_self / total).astype(jnp.bfloat16), pre_value, preferred_...]
    unnamed x86 -> x88, local copies, waits for them, and re-layouts: 5.09 us -> 3.95 us
  transfers between devices with their start and end apart: 26 -> 26, of which waited for: 11 -> 11; matrix products, arithmetic and copies ran while one was open for 29% -> 28% of each run, Pallas kernels for 0% -> 0%
where the time goes in v9:
time: 167 us; the launch traced here: 166 us
  starting transfers between devices  47.7 us (29%)
  matrix products  35.1 us (21%)
  blocking collectives  27.6 us (17%)
  other arithmetic  23.6 us (14%)
  waiting for transfers between devices  19.3 us (12%)
  local copies, waits for them, and re-layouts  10.6 us (6%)
  between operations  1.87 us (1%)
    ppermute x12, starting transfers between devices, pair_then_z_scatter(): acc = acc + lax.ppermute(piece, 'head', perm).astype(jnp.float32)  16.7 us
    all_to_all x1, blocking collectives, on_device(): lax.all_to_all(arrived, 'head', split_axis=0, concat_axis=1, tiled=True)  15.8 us
    all_to_all x1, blocking collectives, on_device(): lax.all_to_all(outgoing, 'req', split_axis=0, concat_axis=0, tiled=True)  11.8 us
    all_to_all x1, waiting for transfers between devices, on_device(): lax.all_to_all(going_back, 'req', split_axis=0, concat_axis=0, tiled=True)  9.09 us
    dot_general x2, matrix products, feed_forward(): jnp.dot(hidden, down_weight, preferred_element_type=jnp.float32)  8.92 us
    ppermute x6, starting transfers between devices, z_then_pair_gather(): parts.append(lax.ppermute(y, 'head', perm))  8.12 us
    unnamed x17, other arithmetic  7.91 us
    all_to_all x1, starting transfers between devices, on_device(): lax.all_to_all(outgoing_q, 'req', split_axis=0, concat_axis=0, tiled=True)  7.62 us
  transfers between devices with their start and end apart: 26, of which 11 were waited for; matrix products, arithmetic and copies ran while one was open for 28% of the time, Pallas kernels for 0%

profile of v9, /device:TPU:1, one launch (start us, length us, event | category | flops | bytes accessed | tf_op | source)
XLA Modules:
  0.0 165.8 jit_solution(17346982488604610030)
XLA Ops:
  2.4 1.9 %convolution_convert_fusion.3 = bf16[768,384]{1,0:T(8,128)(2,1)} fusion(bf16[48,384]{1,0:T(8,128)(2,1)} %param.19, s32[48]{0:T(128)S(1)} %dynamic-slice_add_fusion), kind=kOutput, calls=%fused_computation.48 | convolution fusion | flops 28643328 | bytes 626880 | tf_op jit(solution)/shard_map/dot_general | solution.py:108
  4.3 7.6 %all-to-all-start = ((bf16[16,48,384]{2,1,0:T(8,128)(2,1)}), bf16[16,48,384]{2,1,0:T(8,128)(2,1)}, u32[]{:S(2)}, u32[]{:S(2)}) async-start(bf16[16,48,384]{2,1,0:T(8,128)(2,1)} %bitcast.137), calls=%async_computation | async-start | bytes 1179648 | tf_op jit(solution)/shard_map/all_to_all | solution.py:109
  13.1 4.0 %fusion = (f32[1024]{0:T(1024)S(1)}, f32[1024,2048]{1,0:T(8,128)S(1)}) fusion(pred[2048]{0:T(1024)(128)(4,1)S(1)} %iota_compare_fusion.12, bf16[1024,384]{1,0:T(8,128)(2,1)S(1)} %bitcast.145, bf16[2,2048,384]{2,1,0:T(8,128)(2,1)} %param.25), kind=kOutput, calls=%fused_computation.3 | convolution fusion | flops 1616903168 | bytes 10754048 | tf_op jit(solution)/shard_map/dot_general | solution.py:181
  17.7 2.2 %fusion.1 = f32[1024]{0:T(1024)S(1)} fusion(f32[1024,2048]{1,0:T(8,128)S(1)} %get-tuple-element.84, f32[1024]{0:T(1024)S(1)} %max.12, pred[2048]{0:T(1024)(128)(4,1)S(1)} %iota_compare_fusion.12), kind=kLoop, calls=%fused_computation.4 | loop fusion | flops 8387584 | bytes 8398848 | tf_op jit(solution)/shard_map/reduce_sum | solution.py:193
  20.1 2.4 %fusion.2 = f32[1024,384]{1,0:T(8,128)S(1)} fusion(f32[1024,2048]{1,0:T(8,128)S(1)} %get-tuple-element.84, f32[1024]{0:T(1024)S(1)} %add.298, f32[1024]{0:T(1024)S(1)} %max.12, pred[2048]{0:T(1024)(128)(4,1)S(1)} %iota_compare_fusion.12, bf16[2,2048,384]{2,1,0:T(8,128)(2,1)S(1)} %copy-done.35), kind=kOutput, calls=%fused_computation.5 | convolution fusion | flops 1621098496 | bytes 11544576 | tf_op jit(solution)/shard_map/dot_general | solution.py:194
  29.8 2.2 %fusion.142 = (f32[192]{0:T(256)S(1)}, f32[192,2048]{1,0:T(8,128)S(1)}) fusion(bf16[192,384]{1,0:T(8,128)(2,1)S(1)} %bitcast.152, bf16[2,2048,384]{2,1,0:T(8,128)(2,1)} %param.25, pred[2048]{0:T(1024)(128)(4,1)S(1)} %iota_compare_fusion.14), kind=kOutput, calls=%fused_computation.277 | convolution fusion | flops 303169344 | bytes 3296000 | tf_op jit(solution)/shard_map/dot_general | solution.py:135
  39.8 6.7 %all-to-all-start.1 = ((bf16[16,48,512]{2,1,0:T(8,128)(2,1)}), bf16[16,48,512]{2,1,0:T(8,128)(2,1)}, u32[]{:S(2)}, u32[]{:S(2)}) async-start(bf16[16,48,512]{2,1,0:T(8,128)(2,1)} %bitcast.144), calls=%async_computation.1 | async-start | bytes 1572864 | tf_op jit(solution)/shard_map/all_to_all | solution.py:159
  46.6 3.6 %fusion.144 = f32[152,3072]{1,0:T(8,128)} fusion(bf16[152,384]{1,0:T(8,128)(2,1)S(1)} %slice-done, bf16[384,3072]{1,0:T(8,128)(2,1)} %param.31), kind=kOutput, calls=%fused_computation.279 | convolution fusion | flops 358612992 | bytes 4343808 | tf_op jit(solution)/shard_map/dot_general | solution.py:209
  50.2 9.1 %all-to-all-done.1 = bf16[16,48,512]{2,1,0:T(8,128)(2,1)} async-done(((bf16[16,48,512]{2,1,0:T(8,128)(2,1)}), bf16[16,48,512]{2,1,0:T(8,128)(2,1)}, u32[]{:S(2)}, u32[]{:S(2)}) %all-to-all-start.1) | async-done | bytes 786464 | tf_op jit(solution)/shard_map/all_to_all | solution.py:159
  59.3 1.4 fusion.48
  61.2 2.5 %fusion.85 = f32[152,3072]{1,0:T(8,128)S(1)} fusion(bf16[384,3072]{1,0:T(8,128)(2,1)} %param.31, bf16[104,384]{1,0:T(8,128)(2,1)S(1)} %slice-done.1, bf16[48,384]{1,0:T(8,128)(2,1)S(1)} %fusion.105), kind=kOutput, calls=%fused_computation.134 | convolution fusion | flops 358846464 | bytes 4343808 | tf_op jit(solution)/shard_map/dot_general | solution.py:209
  64.1 2.5 %collective-permute-start = (bf16[152,1536]{1,0:T(8,128)(2,1)S(1)}, bf16[152,1536]{1,0:T(8,128)(2,1)S(1)}, u32[]{:S(2)}, u32[]{:S(2)}) collective-permute-start(bf16[152,1536]{1,0:T(8,128)(2,1)S(1)} %broadcast_select_fusion.4), channel_id=1, source_target_pairs={{0,1},{1,0},{2,3},{3,2},{4,5},{5,4},{6,7},{7,6},{8,9},{9,8},{10,11... | collective-permute-start | bytes 1400840 | tf_op jit(solution)/shard_map/ppermute | solution.py:31
  68.4 1.7 %collective-permute-start.1 = (bf16[152,384]{1,0:T(8,128)(2,1)S(1)}, bf16[152,384]{1,0:T(8,128)(2,1)S(1)}, u32[]{:S(2)}, u32[]{:S(2)}) collective-permute-start(bf16[152,384]{1,0:T(8,128)(2,1)S(1)} %get-tuple-element.56), channel_id=1, source_target_pairs={{0,2},{1,3},{2,4},{3,5},{4,6},{5,7},{6,0},{7,1},{8,10},{9,11},{10,... | collective-permute-start | bytes 350216 | tf_op jit(solution)/shard_map/ppermute | solution.py:37
  70.1 3.3 %collective-permute-start.2 = (bf16[152,384]{1,0:T(8,128)(2,1)S(1)}, bf16[152,384]{1,0:T(8,128)(2,1)S(1)}, u32[]{:S(2)}, u32[]{:S(2)}) collective-permute-start(bf16[152,384]{1,0:T(8,128)(2,1)S(1)} %get-tuple-element.58), channel_id=1, source_target_pairs={{0,4},{1,5},{2,6},{3,7},{4,0},{5,1},{6,2},{7,3},{8,12},{9,13},{10,... | collective-permute-start | bytes 350216 | tf_op jit(solution)/shard_map/ppermute | solution.py:37
  75.6 2.0 %collective-permute-start.15 = (bf16[152,384]{1,0:T(8,128)(2,1)S(1)}, bf16[152,384]{1,0:T(8,128)(2,1)S(1)}, u32[]{:S(2)}, u32[]{:S(2)}) collective-permute-start(bf16[152,384]{1,0:T(8,128)(2,1)S(1)} %get-tuple-element.67), channel_id=1, source_target_pairs={{0,6},{1,7},{2,0},{3,1},{4,2},{5,3},{6,4},{7,5},{8,14},{9,15},{10,... | collective-permute-start | bytes 350216 | tf_op jit(solution)/shard_map/ppermute | solution.py:37
  78.9 1.6 collective-permute-start.4
  80.5 1.9 %collective-permute-start.5 = (bf16[152,384]{1,0:T(8,128)(2,1)S(1)}, bf16[152,384]{1,0:T(8,128)(2,1)S(1)}, u32[]{:S(2)}, u32[]{:S(2)}) collective-permute-start(bf16[152,384]{1,0:T(8,128)(2,1)S(1)} %add_convert_fusion.7), channel_id=1, source_target_pairs={{0,4},{1,5},{2,6},{3,7},{4,0},{5,1},{6,2},{7,3},{8,12},{9,13},{10,... | collective-permute-start | bytes 350216 | tf_op jit(solution)/shard_map/ppermute | solution.py:51
  83.9 1.5 collective-permute-start.16
  85.4 1.8 %collective-permute-start.17 = (bf16[152,384]{1,0:T(8,128)(2,1)S(1)}, bf16[152,384]{1,0:T(8,128)(2,1)S(1)}, u32[]{:S(2)}, u32[]{:S(2)}) collective-permute-start(bf16[152,384]{1,0:T(8,128)(2,1)S(1)} %add_convert_fusion.5), channel_id=1, source_target_pairs={{0,4},{1,5},{2,6},{3,7},{4,0},{5,1},{6,2},{7,3},{8,12},{9,13},{10,... | collective-permute-start | bytes 350216 | tf_op jit(solution)/shard_map/ppermute | solution.py:51
  89.0 2.4 %collective-permute-start.7 = (bf16[152,1536]{1,0:T(8,128)(2,1)S(1)}, bf16[152,1536]{1,0:T(8,128)(2,1)S(1)}, u32[]{:S(2)}, u32[]{:S(2)}) collective-permute-start(bf16[152,1536]{1,0:T(8,128)(2,1)S(1)} %pad_maximum_fusion.3), channel_id=1, source_target_pairs={{0,1},{1,0},{2,3},{3,2},{4,5},{5,4},{6,7},{7,6},{8,9},{9,8},{10,11... | collective-permute-start | bytes 1400840 | tf_op jit(solution)/shard_map/ppermute | solution.py:56
  93.6 2.4 %collective-permute-start.19 = (bf16[152,1536]{1,0:T(8,128)(2,1)}, bf16[152,1536]{1,0:T(8,128)(2,1)}, u32[]{:S(2)}, u32[]{:S(2)}) collective-permute-start(bf16[152,1536]{1,0:T(8,128)(2,1)} %pad_maximum_fusion.9), channel_id=1, source_target_pairs={{0,1},{1,0},{2,3},{3,2},{4,5},{5,4},{6,7},{7,6},{8,9},{9,8},{10,11... | collective-permute-start | bytes 1400840 | tf_op jit(solution)/shard_map/ppermute | solution.py:56
  97.3 1.4 fusion.71
  98.8 4.5 %convolution_convert_fusion.1 = bf16[152,3072]{1,0:T(8,128)(2,1)} fusion(bf16[512,3072]{1,0:T(8,128)(2,1)S(1)} %copy-done, bf16[3072,512]{1,0:T(8,128)(2,1)} %param.34, f32[152,512]{1,0:T(8,128)} %fusion.71, bf16[152,3072]{1,0:T(8,128)(2,1)} %copy-done.4, f32[3072]{0:T(1024)S(1)} %copy-done.41, f32[152]{0:T(256)S(1)} %add_rsqrt_fusion.1), kind=kOutput, calls=%fused_computation.7 | convolution fusion | flops 959102976 | bytes 8483424 | tf_op jit(solution)/shard_map/dot_general | solution.py:222
  103.2 1.4 fusion.133
  116.0 4.5 %convolution_convert_fusion = bf16[152,3072]{1,0:T(8,128)(2,1)} fusion(bf16[512,3072]{1,0:T(8,128)(2,1)S(1)} %copy-done, bf16[3072,512]{1,0:T(8,128)(2,1)} %param.34, f32[152,512]{1,0:T(8,128)S(1)} %fusion.67, bf16[152,3072]{1,0:T(8,128)(2,1)} %copy-done.5, f32[152]{0:T(256)S(1)} %add_rsqrt_fusion, f32[3072]{0:T(1024)S(1)} %copy-done.41), kind=kOutput, calls=%fused_computation.6 | convolution fusion | flops 959102976 | bytes 8483424 | tf_op jit(solution)/shard_map/dot_general | solution.py:222
  120.5 1.4 fusion.135
  123.6 2.0 %collective-permute-start.10 = (bf16[152,384]{1,0:T(8,128)(2,1)S(1)}, bf16[152,384]{1,0:T(8,128)(2,1)S(1)}, u32[]{:S(2)}, u32[]{:S(2)}) collective-permute-start(bf16[152,384]{1,0:T(8,128)(2,1)S(1)} %get-tuple-element.51), channel_id=1, source_target_pairs={{0,4},{1,5},{2,6},{3,7},{4,0},{5,1},{6,2},{7,3},{8,12},{9,13},{10,... | collective-permute-start | bytes 350216 | tf_op jit(solution)/shard_map/ppermute | solution.py:37
  125.7 1.4 collective-permute-start.11
  128.0 3.2 %collective-permute-start.22 = (bf16[152,384]{1,0:T(8,128)(2,1)S(1)}, bf16[152,384]{1,0:T(8,128)(2,1)S(1)}, u32[]{:S(2)}, u32[]{:S(2)}) collective-permute-start(bf16[152,384]{1,0:T(8,128)(2,1)S(1)} %get-tuple-element.61), channel_id=1, source_target_pairs={{0,4},{1,5},{2,6},{3,7},{4,0},{5,1},{6,2},{7,3},{8,12},{9,13},{10,... | collective-permute-start | bytes 350216 | tf_op jit(solution)/shard_map/ppermute | solution.py:37
  132.5 3.0 %collective-permute-done.21 = bf16[152,384]{1,0:T(8,128)(2,1)S(1)} collective-permute-done((bf16[152,384]{1,0:T(8,128)(2,1)S(1)}, bf16[152,384]{1,0:T(8,128)(2,1)S(1)}, u32[]{:S(2)}, u32[]{:S(2)}) %collective-permute-start.21) | collective-permute-done | bytes 116768 | tf_op jit(solution)/shard_map/ppermute | solution.py:37
  137.3 11.8 %all_to_all.52 = bf16[16,40,384]{2,1,0:T(8,128)(2,1)S(1)} all-to-all(bf16[16,40,384]{2,1,0:T(8,128)(2,1)S(1)} %bitcast.149), channel_id=1, replica_groups=mesh['req'=16,'head'=8] {'req'}, dimensions={0} | all-to-all | bytes 983040 | tf_op jit(solution)/shard_map/all_to_all | solution.py:245
  149.1 15.8 %all_to_all.53 = bf16[8,80,384]{2,1,0:T(8,128)(2,1)S(1)} all-to-all(bf16[8,80,384]{2,1,0:T(8,128)(2,1)S(1)} %bitcast.138), channel_id=1, replica_groups=mesh['req'=16,'head'=8] {'head'}, dimensions={0} | all-to-all | bytes 983040 | tf_op jit(solution)/shard_map/all_to_all | solution.py:246
  (248 shorter events, 48.6 us)
Async XLA Ops:
  0.0 98.8 %copy-start = (bf16[512,3072]{1,0:T(8,128)(2,1)S(1)}, bf16[512,3072]{1,0:T(8,128)(2,1)}, u32[]{:S(2)}) copy-start(bf16[512,3072]{1,0:T(8,128)(2,1)} %param.35) | copy-start | bytes 9437188
  0.0 13.0 %copy-start.28 = (bf16[256,384]{1,0:T(8,128)(2,1)S(1)}, bf16[256,384]{1,0:T(8,128)(2,1)}, u32[]{:S(2)}) copy-start(bf16[256,384]{1,0:T(8,128)(2,1)} %param.22) | copy-start | bytes 589828
  4.3 24.0 %all-to-all-start = ((bf16[16,48,384]{2,1,0:T(8,128)(2,1)}), bf16[16,48,384]{2,1,0:T(8,128)(2,1)}, u32[]{:S(2)}, u32[]{:S(2)}) async-start(bf16[16,48,384]{2,1,0:T(8,128)(2,1)} %bitcast.137), calls=%async_computation | async-start | bytes 1179648 | tf_op jit(solution)/shard_map/all_to_all | solution.py:109
  39.8 19.5 %all-to-all-start.1 = ((bf16[16,48,512]{2,1,0:T(8,128)(2,1)}), bf16[16,48,512]{2,1,0:T(8,128)(2,1)}, u32[]{:S(2)}, u32[]{:S(2)}) async-start(bf16[16,48,512]{2,1,0:T(8,128)(2,1)} %bitcast.144), calls=%async_computation.1 | async-start | bytes 1572864 | tf_op jit(solution)/shard_map/all_to_all | solution.py:159
  46.6 14.5 %copy-start.30 = (bf16[48,384]{1,0:T(8,128)(2,1)S(1)}, bf16[48,384]{1,0:T(8,128)(2,1)}, u32[]{:S(2)}) copy-start(bf16[48,384]{1,0:T(8,128)(2,1)} %param.21) | copy-start | bytes 110596
  46.6 14.5 %slice-start.1 = ((bf16[256,384]{1,0:T(8,128)(2,1)}), bf16[104,384]{1,0:T(8,128)(2,1)S(1)}, s32[]{:S(2)}) async-start(bf16[256,384]{1,0:T(8,128)(2,1)} %copy-done.26), calls=%async_computation.5 | async-start | bytes 159744 | tf_op jit(solution)/shard_map/slice | solution.py:203
  64.1 4.0 %collective-permute-start = (bf16[152,1536]{1,0:T(8,128)(2,1)S(1)}, bf16[152,1536]{1,0:T(8,128)(2,1)S(1)}, u32[]{:S(2)}, u32[]{:S(2)}) collective-permute-start(bf16[152,1536]{1,0:T(8,128)(2,1)S(1)} %broadcast_select_fusion.4), channel_id=1, source_target_pairs={{0,1},{1,0},{2,3},{3,2},{4,5},{5,4},{6,7},{7,6},{8,9},{9,8},{10,11... | collective-permute-start | bytes 1400840 | tf_op jit(solution)/shard_map/ppermute | solution.py:31
  67.0 7.1 %collective-permute-start.12 = (bf16[152,1536]{1,0:T(8,128)(2,1)S(1)}, bf16[152,1536]{1,0:T(8,128)(2,1)S(1)}, u32[]{:S(2)}, u32[]{:S(2)}) collective-permute-start(bf16[152,1536]{1,0:T(8,128)(2,1)S(1)} %broadcast_select_fusion.2), channel_id=1, source_target_pairs={{0,1},{1,0},{2,3},{3,2},{4,5},{5,4},{6,7},{7,6},{8,9},{9,8},{10,11... | collective-permute-start | bytes 1400840 | tf_op jit(solution)/shard_map/ppermute | solution.py:31
  68.4 7.2 %collective-permute-start.1 = (bf16[152,384]{1,0:T(8,128)(2,1)S(1)}, bf16[152,384]{1,0:T(8,128)(2,1)S(1)}, u32[]{:S(2)}, u32[]{:S(2)}) collective-permute-start(bf16[152,384]{1,0:T(8,128)(2,1)S(1)} %get-tuple-element.56), channel_id=1, source_target_pairs={{0,2},{1,3},{2,4},{3,5},{4,6},{5,7},{6,0},{7,1},{8,10},{9,11},{10,... | collective-permute-start | bytes 350216 | tf_op jit(solution)/shard_map/ppermute | solution.py:37
  70.1 8.7 %collective-permute-start.2 = (bf16[152,384]{1,0:T(8,128)(2,1)S(1)}, bf16[152,384]{1,0:T(8,128)(2,1)S(1)}, u32[]{:S(2)}, u32[]{:S(2)}) collective-permute-start(bf16[152,384]{1,0:T(8,128)(2,1)S(1)} %get-tuple-element.58), channel_id=1, source_target_pairs={{0,4},{1,5},{2,6},{3,7},{4,0},{5,1},{6,2},{7,3},{8,12},{9,13},{10,... | collective-permute-start | bytes 350216 | tf_op jit(solution)/shard_map/ppermute | solution.py:37
  73.4 5.4 %collective-permute-start.3 = (bf16[152,384]{1,0:T(8,128)(2,1)S(1)}, bf16[152,384]{1,0:T(8,128)(2,1)S(1)}, u32[]{:S(2)}, u32[]{:S(2)}) collective-permute-start(bf16[152,384]{1,0:T(8,128)(2,1)S(1)} %get-tuple-element.57), channel_id=1, source_target_pairs={{0,6},{1,7},{2,0},{3,1},{4,2},{5,3},{6,4},{7,5},{8,14},{9,15},{10,... | collective-permute-start | bytes 350216 | tf_op jit(solution)/shard_map/ppermute | solution.py:37
  74.4 8.0 %collective-permute-start.13 = (bf16[152,384]{1,0:T(8,128)(2,1)S(1)}, bf16[152,384]{1,0:T(8,128)(2,1)S(1)}, u32[]{:S(2)}, u32[]{:S(2)}) collective-permute-start(bf16[152,384]{1,0:T(8,128)(2,1)S(1)} %get-tuple-element.66), channel_id=1, source_target_pairs={{0,2},{1,3},{2,4},{3,5},{4,6},{5,7},{6,0},{7,1},{8,10},{9,11},{10,... | collective-permute-start | bytes 350216 | tf_op jit(solution)/shard_map/ppermute | solution.py:37
  75.2 8.6 %collective-permute-start.14 = (bf16[152,384]{1,0:T(8,128)(2,1)S(1)}, bf16[152,384]{1,0:T(8,128)(2,1)S(1)}, u32[]{:S(2)}, u32[]{:S(2)}) collective-permute-start(bf16[152,384]{1,0:T(8,128)(2,1)S(1)} %get-tuple-element.68), channel_id=1, source_target_pairs={{0,4},{1,5},{2,6},{3,7},{4,0},{5,1},{6,2},{7,3},{8,12},{9,13},{10,... | collective-permute-start | bytes 350216 | tf_op jit(solution)/shard_map/ppermute | solution.py:37
  75.6 8.2 %collective-permute-start.15 = (bf16[152,384]{1,0:T(8,128)(2,1)S(1)}, bf16[152,384]{1,0:T(8,128)(2,1)S(1)}, u32[]{:S(2)}, u32[]{:S(2)}) collective-permute-start(bf16[152,384]{1,0:T(8,128)(2,1)S(1)} %get-tuple-element.67), channel_id=1, source_target_pairs={{0,6},{1,7},{2,0},{3,1},{4,2},{5,3},{6,4},{7,5},{8,14},{9,15},{10,... | collective-permute-start | bytes 350216 | tf_op jit(solution)/shard_map/ppermute | solution.py:37
  78.9 10.1 %copy-start.22 = (bf16[152,384]{1,0:T(8,128)(2,1)}, bf16[152,384]{1,0:T(8,128)(2,1)S(1)}, u32[]{:S(2)}) copy-start(bf16[152,384]{1,0:T(8,128)(2,1)S(1)} %add_convert_fusion.7) | copy-start | bytes 350212
  78.9 8.4 %collective-permute-start.4 = (bf16[152,384]{1,0:T(8,128)(2,1)S(1)}, bf16[152,384]{1,0:T(8,128)(2,1)S(1)}, u32[]{:S(2)}, u32[]{:S(2)}) collective-permute-start(bf16[152,384]{1,0:T(8,128)(2,1)S(1)} %add_convert_fusion.7), channel_id=1, source_target_pairs={{0,2},{1,3},{2,4},{3,5},{4,6},{5,7},{6,0},{7,1},{8,10},{9,11},{10,... | collective-permute-start | bytes 350216 | tf_op jit(solution)/shard_map/ppermute | solution.py:51
  80.5 8.3 %collective-permute-start.5 = (bf16[152,384]{1,0:T(8,128)(2,1)S(1)}, bf16[152,384]{1,0:T(8,128)(2,1)S(1)}, u32[]{:S(2)}, u32[]{:S(2)}) collective-permute-start(bf16[152,384]{1,0:T(8,128)(2,1)S(1)} %add_convert_fusion.7), channel_id=1, source_target_pairs={{0,4},{1,5},{2,6},{3,7},{4,0},{5,1},{6,2},{7,3},{8,12},{9,13},{10,... | collective-permute-start | bytes 350216 | tf_op jit(solution)/shard_map/ppermute | solution.py:51
  82.4 6.4 %collective-permute-start.6 = (bf16[152,384]{1,0:T(8,128)(2,1)S(1)}, bf16[152,384]{1,0:T(8,128)(2,1)S(1)}, u32[]{:S(2)}, u32[]{:S(2)}) collective-permute-start(bf16[152,384]{1,0:T(8,128)(2,1)S(1)} %add_convert_fusion.7), channel_id=1, source_target_pairs={{0,6},{1,7},{2,0},{3,1},{4,2},{5,3},{6,4},{7,5},{8,14},{9,15},{10,... | collective-permute-start | bytes 350216 | tf_op jit(solution)/shard_map/ppermute | solution.py:51
  83.9 7.9 %collective-permute-start.16 = (bf16[152,384]{1,0:T(8,128)(2,1)S(1)}, bf16[152,384]{1,0:T(8,128)(2,1)S(1)}, u32[]{:S(2)}, u32[]{:S(2)}) collective-permute-start(bf16[152,384]{1,0:T(8,128)(2,1)S(1)} %add_convert_fusion.5), channel_id=1, source_target_pairs={{0,2},{1,3},{2,4},{3,5},{4,6},{5,7},{6,0},{7,1},{8,10},{9,11},{10,... | collective-permute-start | bytes 350216 | tf_op jit(solution)/shard_map/ppermute | solution.py:51
  85.4 7.2 %collective-permute-start.17 = (bf16[152,384]{1,0:T(8,128)(2,1)S(1)}, bf16[152,384]{1,0:T(8,128)(2,1)S(1)}, u32[]{:S(2)}, u32[]{:S(2)}) collective-permute-start(bf16[152,384]{1,0:T(8,128)(2,1)S(1)} %add_convert_fusion.5), channel_id=1, source_target_pairs={{0,4},{1,5},{2,6},{3,7},{4,0},{5,1},{6,2},{7,3},{8,12},{9,13},{10,... | collective-permute-start | bytes 350216 | tf_op jit(solution)/shard_map/ppermute | solution.py:51
  87.2 5.4 %collective-permute-start.18 = (bf16[152,384]{1,0:T(8,128)(2,1)S(1)}, bf16[152,384]{1,0:T(8,128)(2,1)S(1)}, u32[]{:S(2)}, u32[]{:S(2)}) collective-permute-start(bf16[152,384]{1,0:T(8,128)(2,1)S(1)} %add_convert_fusion.5), channel_id=1, source_target_pairs={{0,6},{1,7},{2,0},{3,1},{4,2},{5,3},{6,4},{7,5},{8,14},{9,15},{10,... | collective-permute-start | bytes 350216 | tf_op jit(solution)/shard_map/ppermute | solution.py:51
  89.0 7.0 %collective-permute-start.7 = (bf16[152,1536]{1,0:T(8,128)(2,1)S(1)}, bf16[152,1536]{1,0:T(8,128)(2,1)S(1)}, u32[]{:S(2)}, u32[]{:S(2)}) collective-permute-start(bf16[152,1536]{1,0:T(8,128)(2,1)S(1)} %pad_maximum_fusion.3), channel_id=1, source_target_pairs={{0,1},{1,0},{2,3},{3,2},{4,5},{5,4},{6,7},{7,6},{8,9},{9,8},{10,11... | collective-permute-start | bytes 1400840 | tf_op jit(solution)/shard_map/ppermute | solution.py:56
  93.6 13.1 %collective-permute-start.19 = (bf16[152,1536]{1,0:T(8,128)(2,1)}, bf16[152,1536]{1,0:T(8,128)(2,1)}, u32[]{:S(2)}, u32[]{:S(2)}) collective-permute-start(bf16[152,1536]{1,0:T(8,128)(2,1)} %pad_maximum_fusion.9), channel_id=1, source_target_pairs={{0,1},{1,0},{2,3},{3,2},{4,5},{5,4},{6,7},{7,6},{8,9},{9,8},{10,11... | collective-permute-start | bytes 1400840 | tf_op jit(solution)/shard_map/ppermute | solution.py:56
  105.8 16.5 %collective-permute-start.8 = (bf16[152,1536]{1,0:T(8,128)(2,1)}, bf16[152,1536]{1,0:T(8,128)(2,1)}, u32[]{:S(2)}, u32[]{:S(2)}) collective-permute-start(bf16[152,1536]{1,0:T(8,128)(2,1)} %broadcast_select_fusion.3), channel_id=1, source_target_pairs={{0,1},{1,0},{2,3},{3,2},{4,5},{5,4},{6,7},{7,6},{8,9},{9,8},{10,11... | collective-permute-start | bytes 1400840 | tf_op jit(solution)/shard_map/ppermute | solution.py:31
  122.0 5.1 %collective-permute-start.20 = (bf16[152,1536]{1,0:T(8,128)(2,1)S(1)}, bf16[152,1536]{1,0:T(8,128)(2,1)S(1)}, u32[]{:S(2)}, u32[]{:S(2)}) collective-permute-start(bf16[152,1536]{1,0:T(8,128)(2,1)S(1)} %broadcast_select_fusion.1), channel_id=1, source_target_pairs={{0,1},{1,0},{2,3},{3,2},{4,5},{5,4},{6,7},{7,6},{8,9},{9,8},{10,11... | collective-permute-start | bytes 1400840 | tf_op jit(solution)/shard_map/ppermute | solution.py:31
  123.6 13.2 %copy-start.25 = (bf16[152,384]{1,0:T(8,128)(2,1)S(1)}, bf16[152,384]{1,0:T(8,128)(2,1)}, u32[]{:S(2)}) copy-start(bf16[152,384]{1,0:T(8,128)(2,1)} %copy-done.24) | copy-start | bytes 350212
  123.6 7.6 %collective-permute-start.10 = (bf16[152,384]{1,0:T(8,128)(2,1)S(1)}, bf16[152,384]{1,0:T(8,128)(2,1)S(1)}, u32[]{:S(2)}, u32[]{:S(2)}) collective-permute-start(bf16[152,384]{1,0:T(8,128)(2,1)S(1)} %get-tuple-element.51), channel_id=1, source_target_pairs={{0,4},{1,5},{2,6},{3,7},{4,0},{5,1},{6,2},{7,3},{8,12},{9,13},{10,... | collective-permute-start | bytes 350216 | tf_op jit(solution)/shard_map/ppermute | solution.py:37
  125.7 6.0 %collective-permute-start.11 = (bf16[152,384]{1,0:T(8,128)(2,1)S(1)}, bf16[152,384]{1,0:T(8,128)(2,1)S(1)}, u32[]{:S(2)}, u32[]{:S(2)}) collective-permute-start(bf16[152,384]{1,0:T(8,128)(2,1)S(1)} %get-tuple-element.50), channel_id=1, source_target_pairs={{0,6},{1,7},{2,0},{3,1},{4,2},{5,3},{6,4},{7,5},{8,14},{9,15},{10,... | collective-permute-start | bytes 350216 | tf_op jit(solution)/shard_map/ppermute | solution.py:37
  127.1 5.3 %collective-permute-start.9 = (bf16[152,384]{1,0:T(8,128)(2,1)S(1)}, bf16[152,384]{1,0:T(8,128)(2,1)S(1)}, u32[]{:S(2)}, u32[]{:S(2)}) collective-permute-start(bf16[152,384]{1,0:T(8,128)(2,1)S(1)} %get-tuple-element.49), channel_id=1, source_target_pairs={{0,2},{1,3},{2,4},{3,5},{4,6},{5,7},{6,0},{7,1},{8,10},{9,11},{10,... | collective-permute-start | bytes 350216 | tf_op jit(solution)/shard_map/ppermute | solution.py:37
  127.4 8.1 %collective-permute-start.21 = (bf16[152,384]{1,0:T(8,128)(2,1)S(1)}, bf16[152,384]{1,0:T(8,128)(2,1)S(1)}, u32[]{:S(2)}, u32[]{:S(2)}) collective-permute-start(bf16[152,384]{1,0:T(8,128)(2,1)S(1)} %get-tuple-element.59), channel_id=1, source_target_pairs={{0,2},{1,3},{2,4},{3,5},{4,6},{5,7},{6,0},{7,1},{8,10},{9,11},{10,... | collective-permute-start | bytes 350216 | tf_op jit(solution)/shard_map/ppermute | solution.py:37
  128.0 8.8 %collective-permute-start.22 = (bf16[152,384]{1,0:T(8,128)(2,1)S(1)}, bf16[152,384]{1,0:T(8,128)(2,1)S(1)}, u32[]{:S(2)}, u32[]{:S(2)}) collective-permute-start(bf16[152,384]{1,0:T(8,128)(2,1)S(1)} %get-tuple-element.61), channel_id=1, source_target_pairs={{0,4},{1,5},{2,6},{3,7},{4,0},{5,1},{6,2},{7,3},{8,12},{9,13},{10,... | collective-permute-start | bytes 350216 | tf_op jit(solution)/shard_map/ppermute | solution.py:37
  131.2 5.5 %collective-permute-start.23 = (bf16[152,384]{1,0:T(8,128)(2,1)S(1)}, bf16[152,384]{1,0:T(8,128)(2,1)S(1)}, u32[]{:S(2)}, u32[]{:S(2)}) collective-permute-start(bf16[152,384]{1,0:T(8,128)(2,1)S(1)} %get-tuple-element.60), channel_id=1, source_target_pairs={{0,6},{1,7},{2,0},{3,1},{4,2},{5,3},{6,4},{7,5},{8,14},{9,15},{10,... | collective-permute-start | bytes 350216 | tf_op jit(solution)/shard_map/ppermute | solution.py:37
  (38 other events, 125.8 us)

commit v10 on v9

--- a/solution.py
+++ b/solution.py
@@ -198,7 +198,7 @@
         jnp.where(head_mask[:, None, :], pre_mixed.reshape(heads_here, stretch_len, width_here), 0.0), axis=0
     ).astype(jnp.bfloat16)
     row_count = hidden_in.shape[0]
-    half = row_count // 2
+    half = 8 * ((row_count // 3 + 7) // 8)
     late_attn, _ = lax.optimization_barrier((pre_out[half - per_home :], going_back))
     dec_out, early_pre = lax.optimization_barrier((dec_out, pre_out[: half - per_home]))
     early_attn = jnp.concatenate([dec_out, early_pre], axis=0)

time: 167 us -> 185 us (1.11)
  other arithmetic: 23.6 us -> 34.7 us
  waiting for transfers between devices: 19.3 us -> 27.5 us
  starting transfers between devices: 47.7 us -> 42 us
  local copies, waits for them, and re-layouts: 10.6 us -> 13.8 us
    ppermute x6, waiting for transfers between devices: 2.13 us -> 13 us  [z_then_pair_gather(): parts.append(lax.ppermute(y, 'head', perm))]
    all_to_all x1, waiting for transfers between devices: 9.09 us -> 2.83 us  [on_device(): lax.all_to_all(going_back, 'req', split_axis=0, concat_axis=0, tiled=True)]
    ppermute x12, starting transfers between devices: 16.7 us -> 12.1 us  [pair_then_z_scatter(): acc = acc + lax.ppermute(piece, 'head', perm).astype(jnp.float32)]
    ppermute x12, waiting for transfers between devices: 7.06 us -> 10.8 us  [pair_then_z_scatter(): acc = acc + lax.ppermute(piece, 'head', perm).astype(jnp.float32)]
    dot_general x2, matrix products: 1.14 us -> 4.6 us  [on_device(): jnp.dot(weights, cache_value[group_pos], preferred_element_type=jnp.float32)]
    dot_general x2, matrix products: 6.08 us -> 3 us  [feed_forward(): jnp.dot(attn_chunk, out_weight, preferred_element_type=jnp.float32)]
    unnamed x88 -> x122, local copies, waits for them, and re-layouts: 3.95 us -> 4.85 us
  transfers between devices with their start and end apart: 26 -> 26, of which waited for: 11 -> 15; matrix products, arithmetic and copies ran while one was open for 28% -> 23% of each run, Pallas kernels for 0% -> 0%
where the time goes in v10:
time: 185 us; the launch traced here: 183 us
  starting transfers between devices  42 us (23%)
  matrix products  36.6 us (20%)
  other arithmetic  34.7 us (19%)
  waiting for transfers between devices  27.5 us (15%)
  blocking collectives  27 us (15%)
  local copies, waits for them, and re-layouts  13.8 us (7%)
    all_to_all x1, blocking collectives, on_device(): lax.all_to_all(arrived, 'head', split_axis=0, concat_axis=1, tiled=True)  14.1 us
    ppermute x6, waiting for transfers between devices, z_then_pair_gather(): parts.append(lax.ppermute(y, 'head', perm))  13 us
    all_to_all x1, blocking collectives, on_device(): lax.all_to_all(outgoing, 'req', split_axis=0, concat_axis=0, tiled=True)  12.9 us
    ppermute x12, starting transfers between devices, pair_then_z_scatter(): acc = acc + lax.ppermute(piece, 'head', perm).astype(jnp.float32)  12.1 us
    ppermute x12, waiting for transfers between devices, pair_then_z_scatter(): acc = acc + lax.ppermute(piece, 'head', perm).astype(jnp.float32)  10.8 us
    dot_general x2, matrix products, feed_forward(): jnp.dot(hidden, down_weight, preferred_element_type=jnp.float32)  9.11 us
    unnamed x17, other arithmetic  7.9 us
    ppermute x6, starting transfers between devices, z_then_pair_gather(): parts.append(lax.ppermute(y, 'head', perm))  7.75 us
  transfers between devices with their start and end apart: 26, of which 15 were waited for; matrix products, arithmetic and copies ran while one was open for 23% of the time, Pallas kernels for 0%

profile of v10, /device:TPU:1, one launch (start us, length us, event | category | flops | bytes accessed | tf_op | source)
XLA Modules:
  0.0 183.3 jit_solution(7312623335847802688)
XLA Ops:
  2.4 1.9 %convolution_convert_fusion.3 = bf16[768,384]{1,0:T(8,128)(2,1)} fusion(bf16[48,384]{1,0:T(8,128)(2,1)} %param.19, s32[48]{0:T(128)S(1)} %dynamic-slice_add_fusion), kind=kOutput, calls=%fused_computation.45 | convolution fusion | flops 28643328 | bytes 626880 | tf_op jit(solution)/shard_map/dot_general | solution.py:108
  4.3 7.6 %all-to-all-start = ((bf16[16,48,384]{2,1,0:T(8,128)(2,1)}), bf16[16,48,384]{2,1,0:T(8,128)(2,1)}, u32[]{:S(2)}, u32[]{:S(2)}) async-start(bf16[16,48,384]{2,1,0:T(8,128)(2,1)} %bitcast.137), calls=%async_computation | async-start | bytes 1179648 | tf_op jit(solution)/shard_map/all_to_all | solution.py:109
  13.2 4.0 %fusion = (f32[1024]{0:T(1024)S(1)}, f32[1024,2048]{1,0:T(8,128)S(1)}) fusion(pred[2048]{0:T(1024)(128)(4,1)S(1)} %iota_compare_fusion.12, bf16[1024,384]{1,0:T(8,128)(2,1)S(1)} %bitcast.144, bf16[2,2048,384]{2,1,0:T(8,128)(2,1)} %param.25), kind=kOutput, calls=%fused_computation.3 | convolution fusion | flops 1616903168 | bytes 10754048 | tf_op jit(solution)/shard_map/dot_general | solution.py:181
  17.7 2.2 %fusion.1 = f32[1024]{0:T(1024)S(1)} fusion(f32[1024,2048]{1,0:T(8,128)S(1)} %get-tuple-element.82, f32[1024]{0:T(1024)S(1)} %max.12, pred[2048]{0:T(1024)(128)(4,1)S(1)} %iota_compare_fusion.12), kind=kLoop, calls=%fused_computation.4 | loop fusion | flops 8387584 | bytes 8398848 | tf_op jit(solution)/shard_map/reduce_sum | solution.py:193
  20.2 2.4 %fusion.2 = f32[1024,384]{1,0:T(8,128)S(1)} fusion(f32[1024,2048]{1,0:T(8,128)S(1)} %get-tuple-element.82, f32[1024]{0:T(1024)S(1)} %add.306, f32[1024]{0:T(1024)S(1)} %max.12, pred[2048]{0:T(1024)(128)(4,1)S(1)} %iota_compare_fusion.12, bf16[2,2048,384]{2,1,0:T(8,128)(2,1)S(1)} %copy-done.56), kind=kOutput, calls=%fused_computation.5 | convolution fusion | flops 1621098496 | bytes 11544576 | tf_op jit(solution)/shard_map/dot_general | solution.py:194
  28.4 2.2 %fusion.141 = (f32[192]{0:T(256)S(1)}, f32[192,2048]{1,0:T(8,128)S(1)}) fusion(bf16[192,384]{1,0:T(8,128)(2,1)S(1)} %bitcast.152, bf16[2,2048,384]{2,1,0:T(8,128)(2,1)} %param.25, pred[2048]{0:T(1024)(128)(4,1)S(1)} %iota_compare_fusion.13), kind=kOutput, calls=%fused_computation.276 | convolution fusion | flops 303169344 | bytes 3296000 | tf_op jit(solution)/shard_map/dot_general | solution.py:135
  35.6 2.2 %fusion.36 = bf16[48,384]{1,0:T(8,128)(2,1)S(1)} fusion(bf16[4,48,2048]{2,1,0:T(8,128)(2,1)} %bitcast.146, bf16[2,2048,384]{2,1,0:T(8,128)(2,1)} %param.26, pred[4,384]{1,0:T(4,128)(4,1)S(1)} %iota_compare_fusion.15), kind=kOutput, calls=%fused_computation.57 | convolution fusion | flops 302118912 | bytes 2397696 | tf_op jit(solution)/shard_map/dot_general | solution.py:144
  38.2 2.4 %fusion.39 = bf16[48,384]{1,0:T(8,128)(2,1)S(1)} fusion(bf16[4,48,2048]{2,1,0:T(8,128)(2,1)} %bitcast.147, bf16[2,2048,384]{2,1,0:T(8,128)(2,1)} %param.26, pred[4,384]{1,0:T(4,128)(4,1)S(1)} %iota_compare_fusion.15), kind=kOutput, calls=%fused_computation.58 | convolution fusion | flops 302118912 | bytes 2397696 | tf_op jit(solution)/shard_map/dot_general | solution.py:144
  47.6 6.9 %all-to-all-start.1 = ((bf16[16,48,512]{2,1,0:T(8,128)(2,1)}), bf16[16,48,512]{2,1,0:T(8,128)(2,1)}, u32[]{:S(2)}, u32[]{:S(2)}) async-start(bf16[16,48,512]{2,1,0:T(8,128)(2,1)} %bitcast.143), calls=%async_computation.1 | async-start | bytes 1572864 | tf_op jit(solution)/shard_map/all_to_all | solution.py:159
  58.0 1.6 add_convert_fusion.1
  61.2 3.8 %collective-permute-start.15 = (bf16[200,384]{1,0:T(8,128)(2,1)}, bf16[200,384]{1,0:T(8,128)(2,1)}, u32[]{:S(2)}, u32[]{:S(2)}) collective-permute-start(bf16[200,384]{1,0:T(8,128)(2,1)} %get-tuple-element.57), channel_id=1, source_target_pairs={{0,6},{1,7},{2,0},{3,1},{4,2},{5,3},{6,4},{7,5},{8,14},{9,15},{10,... | collective-permute-start | bytes 460808 | tf_op jit(solution)/shard_map/ppermute | solution.py:37
  65.6 2.8 %all-to-all-done.1 = bf16[16,48,512]{2,1,0:T(8,128)(2,1)} async-done(((bf16[16,48,512]{2,1,0:T(8,128)(2,1)}), bf16[16,48,512]{2,1,0:T(8,128)(2,1)}, u32[]{:S(2)}, u32[]{:S(2)}) %all-to-all-start.1) | async-done | bytes 786464 | tf_op jit(solution)/shard_map/all_to_all | solution.py:159
  68.5 1.4 fusion.53
  70.3 2.2 %fusion.100 = f32[104,3072]{1,0:T(8,128)S(1)} fusion(bf16[384,3072]{1,0:T(8,128)(2,1)} %param.31, bf16[56,384]{1,0:T(8,128)(2,1)S(1)} %slice-done.1, bf16[48,384]{1,0:T(8,128)(2,1)S(1)} %fusion.105), kind=kOutput, calls=%fused_computation.161 | convolution fusion | flops 245526528 | bytes 3717120 | tf_op jit(solution)/shard_map/dot_general | solution.py:209
  74.5 1.4 collective-permute-start
  77.1 3.8 %collective-permute-start.18 = (bf16[200,384]{1,0:T(8,128)(2,1)S(1)}, bf16[200,384]{1,0:T(8,128)(2,1)}, u32[]{:S(2)}, u32[]{:S(2)}) collective-permute-start(bf16[200,384]{1,0:T(8,128)(2,1)S(1)} %add_convert_fusion.5), channel_id=1, source_target_pairs={{0,6},{1,7},{2,0},{3,1},{4,2},{5,3},{6,4},{7,5},{8,14},{9,15},{10,... | collective-permute-start | bytes 460808 | tf_op jit(solution)/shard_map/ppermute | solution.py:51
  82.4 5.2 %collective-permute-done.18 = bf16[200,384]{1,0:T(8,128)(2,1)} collective-permute-done((bf16[200,384]{1,0:T(8,128)(2,1)S(1)}, bf16[200,384]{1,0:T(8,128)(2,1)}, u32[]{:S(2)}, u32[]{:S(2)}) %collective-permute-start.18) | collective-permute-done | bytes 153632 | tf_op jit(solution)/shard_map/ppermute | solution.py:51
  87.9 3.5 %collective-permute-done.16 = bf16[200,384]{1,0:T(8,128)(2,1)} collective-permute-done((bf16[200,384]{1,0:T(8,128)(2,1)S(1)}, bf16[200,384]{1,0:T(8,128)(2,1)}, u32[]{:S(2)}, u32[]{:S(2)}) %collective-permute-start.16) | collective-permute-done | bytes 153632 | tf_op jit(solution)/shard_map/ppermute | solution.py:51
  95.4 1.6 collective-permute-start.19
  97.2 1.6 collective-permute-done.2
  99.7 2.5 %collective-permute-start.6 = (bf16[104,384]{1,0:T(8,128)(2,1)S(1)}, bf16[104,384]{1,0:T(8,128)(2,1)S(1)}, u32[]{:S(2)}, u32[]{:S(2)}) collective-permute-start(bf16[104,384]{1,0:T(8,128)(2,1)S(1)} %add_convert_fusion.7), channel_id=1, source_target_pairs={{0,6},{1,7},{2,0},{3,1},{4,2},{5,3},{6,4},{7,5},{8,14},{9,15},{10,... | collective-permute-start | bytes 239624 | tf_op jit(solution)/shard_map/ppermute | solution.py:51
  104.5 2.7 %collective-permute-done.5 = bf16[104,384]{1,0:T(8,128)(2,1)S(1)} collective-permute-done((bf16[104,384]{1,0:T(8,128)(2,1)S(1)}, bf16[104,384]{1,0:T(8,128)(2,1)S(1)}, u32[]{:S(2)}, u32[]{:S(2)}) %collective-permute-start.5) | collective-permute-done | bytes 79904 | tf_op jit(solution)/shard_map/ppermute | solution.py:51
  108.5 3.1 %collective-permute-start.7 = (bf16[104,1536]{1,0:T(8,128)(2,1)}, bf16[104,1536]{1,0:T(8,128)(2,1)}, u32[]{:S(2)}, u32[]{:S(2)}) collective-permute-start(bf16[104,1536]{1,0:T(8,128)(2,1)} %pad_maximum_fusion.9), channel_id=1, source_target_pairs={{0,1},{1,0},{2,3},{3,2},{4,5},{5,4},{6,7},{7,6},{8,9},{9,8},{10,11... | collective-permute-start | bytes 958472 | tf_op jit(solution)/shard_map/ppermute | solution.py:56
  114.1 1.6 fusion.57
  115.7 5.0 %convolution_convert_fusion = bf16[200,3072]{1,0:T(8,128)(2,1)} fusion(bf16[512,3072]{1,0:T(8,128)(2,1)S(1)} %copy-done, bf16[3072,512]{1,0:T(8,128)(2,1)} %param.34, f32[200,512]{1,0:T(8,128)} %fusion.57, bf16[200,3072]{1,0:T(8,128)(2,1)} %copy-done.6, f32[3072]{0:T(1024)S(1)} %copy-done.44, f32[200]{0:T(256)S(1)} %add_rsqrt_fusion), kind=kOutput, calls=%fused_computation.6 | convolution fusion | flops 1261977600 | bytes 9171744 | tf_op jit(solution)/shard_map/dot_general | solution.py:222
  120.7 2.5 %fusion.133 = (bf16[200,384]{1,0:T(8,128)(2,1)S(1)}, bf16[200,384]{1,0:T(8,128)(2,1)}, bf16[200,384]{1,0:T(8,128)(2,1)}, bf16[200,384]{1,0:T(8,128)(2,1)}, bf16[...) fusion(bf16[200,3072]{1,0:T(8,128)(2,1)} %convolution_convert_fusion), kind=kLoop, calls=%fused_computation.268 | loop fusion | bytes 2457600 | tf_op jit(solution)/shard_map/slice | solution.py:27
  132.9 4.1 %convolution_convert_fusion.1 = bf16[104,3072]{1,0:T(8,128)(2,1)} fusion(bf16[512,3072]{1,0:T(8,128)(2,1)S(1)} %copy-done, bf16[3072,512]{1,0:T(8,128)(2,1)} %param.34, f32[104,512]{1,0:T(8,128)} %fusion.78, bf16[104,3072]{1,0:T(8,128)(2,1)} %copy-done.2, f32[3072]{0:T(1024)S(1)} %copy-done.44, f32[104]{0:T(128)S(1)} %add_rsqrt_fusion.1), kind=kOutput, calls=%fused_computation.7 | convolution fusion | flops 656228352 | bytes 7795104 | tf_op jit(solution)/shard_map/dot_general | solution.py:222
  142.5 2.3 %collective-permute-start.23 = (bf16[200,384]{1,0:T(8,128)(2,1)S(1)}, bf16[200,384]{1,0:T(8,128)(2,1)S(1)}, u32[]{:S(2)}, u32[]{:S(2)}) collective-permute-start(bf16[200,384]{1,0:T(8,128)(2,1)S(1)} %get-tuple-element.50), channel_id=1, source_target_pairs={{0,6},{1,7},{2,0},{3,1},{4,2},{5,3},{6,4},{7,5},{8,14},{9,15},{10,... | collective-permute-start | bytes 460808 | tf_op jit(solution)/shard_map/ppermute | solution.py:37
  146.7 1.9 %collective-permute-done.9 = bf16[104,384]{1,0:T(8,128)(2,1)S(1)} collective-permute-done((bf16[104,384]{1,0:T(8,128)(2,1)S(1)}, bf16[104,384]{1,0:T(8,128)(2,1)S(1)}, u32[]{:S(2)}, u32[]{:S(2)}) %collective-permute-start.9) | collective-permute-done | bytes 79904 | tf_op jit(solution)/shard_map/ppermute | solution.py:37
  150.4 4.5 %collective-permute-done.21 = bf16[200,384]{1,0:T(8,128)(2,1)S(1)} collective-permute-done((bf16[200,384]{1,0:T(8,128)(2,1)S(1)}, bf16[200,384]{1,0:T(8,128)(2,1)S(1)}, u32[]{:S(2)}, u32[]{:S(2)}) %collective-permute-start.21) | collective-permute-done | bytes 153632 | tf_op jit(solution)/shard_map/ppermute | solution.py:37
  155.5 12.9 %all_to_all.52 = bf16[16,40,384]{2,1,0:T(8,128)(2,1)S(1)} all-to-all(bf16[16,40,384]{2,1,0:T(8,128)(2,1)S(1)} %bitcast.149), channel_id=1, replica_groups=mesh['req'=16,'head'=8] {'req'}, dimensions={0} | all-to-all | bytes 983040 | tf_op jit(solution)/shard_map/all_to_all | solution.py:245
  168.4 14.1 %all_to_all.53 = bf16[8,80,384]{2,1,0:T(8,128)(2,1)S(1)} all-to-all(bf16[8,80,384]{2,1,0:T(8,128)(2,1)S(1)} %bitcast.138), channel_id=1, replica_groups=mesh['req'=16,'head'=8] {'head'}, dimensions={0} | all-to-all | bytes 983040 | tf_op jit(solution)/shard_map/all_to_all | solution.py:246
  (283 shorter events, 63.6 us)
Async XLA Ops:
  0.0 115.7 %copy-start = (bf16[512,3072]{1,0:T(8,128)(2,1)S(1)}, bf16[512,3072]{1,0:T(8,128)(2,1)}, u32[]{:S(2)}) copy-start(bf16[512,3072]{1,0:T(8,128)(2,1)} %param.35) | copy-start | bytes 9437188
  0.0 12.0 %copy-start.54 = (s32[304,1]{0,1:T(1,128)S(1)}, s32[304,1]{0,1:T(1,128)}, u32[]{:S(2)}) copy-start(s32[304,1]{0,1:T(1,128)} %param.30) | copy-start | bytes 3652
  0.0 13.1 %copy-start.40 = (bf16[256,384]{1,0:T(8,128)(2,1)S(1)}, bf16[256,384]{1,0:T(8,128)(2,1)}, u32[]{:S(2)}) copy-start(bf16[256,384]{1,0:T(8,128)(2,1)} %param.22) | copy-start | bytes 589828
  4.3 22.7 %all-to-all-start = ((bf16[16,48,384]{2,1,0:T(8,128)(2,1)}), bf16[16,48,384]{2,1,0:T(8,128)(2,1)}, u32[]{:S(2)}, u32[]{:S(2)}) async-start(bf16[16,48,384]{2,1,0:T(8,128)(2,1)} %bitcast.137), calls=%async_computation | async-start | bytes 1179648 | tf_op jit(solution)/shard_map/all_to_all | solution.py:109
  12.0 33.9 %copy-start.46 = (s32[304]{0:T(512)}, s32[304]{0:T(512)S(1)}, u32[]{:S(2)}) copy-start(s32[304]{0:T(512)S(1)} %reduce.2) | copy-start | bytes 3652
  12.7 25.5 %copy-start.42 = (pred[4,384]{1,0:T(4,128)(4,1)}, pred[4,384]{1,0:T(4,128)(4,1)S(1)}, u32[]{:S(2)}) copy-start(pred[4,384]{1,0:T(4,128)(4,1)S(1)} %iota_compare_fusion.15) | copy-start | bytes 4612
  45.0 13.0 %collective-permute-start.12 = (bf16[200,1536]{1,0:T(8,128)(2,1)}, bf16[200,1536]{1,0:T(8,128)(2,1)}, u32[]{:S(2)}, u32[]{:S(2)}) collective-permute-start(bf16[200,1536]{1,0:T(8,128)(2,1)} %broadcast_select_fusion.2), channel_id=1, source_target_pairs={{0,1},{1,0},{2,3},{3,2},{4,5},{5,4},{6,7},{7,6},{8,9},{9,8},{10,11... | collective-permute-start | bytes 1843208 | tf_op jit(solution)/shard_map/ppermute | solution.py:31
  46.8 12.7 %copy-start.38 = (s32[16,3,128]{2,0,1:T(8,128)}, s32[16,3,128]{2,0,1:T(8,128)S(1)}, u32[]{:S(2)}) copy-start(s32[16,3,128]{2,0,1:T(8,128)S(1)} %reduce-window.14) | copy-start | bytes 73732
  47.6 20.8 %all-to-all-start.1 = ((bf16[16,48,512]{2,1,0:T(8,128)(2,1)}), bf16[16,48,512]{2,1,0:T(8,128)(2,1)}, u32[]{:S(2)}, u32[]{:S(2)}) async-start(bf16[16,48,512]{2,1,0:T(8,128)(2,1)} %bitcast.143), calls=%async_computation.1 | async-start | bytes 1572864 | tf_op jit(solution)/shard_map/all_to_all | solution.py:159
  61.2 14.7 %collective-permute-start.15 = (bf16[200,384]{1,0:T(8,128)(2,1)}, bf16[200,384]{1,0:T(8,128)(2,1)}, u32[]{:S(2)}, u32[]{:S(2)}) collective-permute-start(bf16[200,384]{1,0:T(8,128)(2,1)} %get-tuple-element.57), channel_id=1, source_target_pairs={{0,6},{1,7},{2,0},{3,1},{4,2},{5,3},{6,4},{7,5},{8,14},{9,15},{10,... | collective-permute-start | bytes 460808 | tf_op jit(solution)/shard_map/ppermute | solution.py:37
  64.9 11.0 %collective-permute-start.14 = (bf16[200,384]{1,0:T(8,128)(2,1)}, bf16[200,384]{1,0:T(8,128)(2,1)}, u32[]{:S(2)}, u32[]{:S(2)}) collective-permute-start(bf16[200,384]{1,0:T(8,128)(2,1)} %get-tuple-element.58), channel_id=1, source_target_pairs={{0,4},{1,5},{2,6},{3,7},{4,0},{5,1},{6,2},{7,3},{8,12},{9,13},{10,... | collective-permute-start | bytes 460808 | tf_op jit(solution)/shard_map/ppermute | solution.py:37
  64.9 11.0 %collective-permute-start.13 = (bf16[200,384]{1,0:T(8,128)(2,1)}, bf16[200,384]{1,0:T(8,128)(2,1)}, u32[]{:S(2)}, u32[]{:S(2)}) collective-permute-start(bf16[200,384]{1,0:T(8,128)(2,1)} %get-tuple-element.56), channel_id=1, source_target_pairs={{0,2},{1,3},{2,4},{3,5},{4,6},{5,7},{6,0},{7,1},{8,10},{9,11},{10,... | collective-permute-start | bytes 460808 | tf_op jit(solution)/shard_map/ppermute | solution.py:37
  74.5 18.1 %collective-permute-start = (bf16[104,1536]{1,0:T(8,128)(2,1)}, bf16[104,1536]{1,0:T(8,128)(2,1)}, u32[]{:S(2)}, u32[]{:S(2)}) collective-permute-start(bf16[104,1536]{1,0:T(8,128)(2,1)} %broadcast_select_fusion.4), channel_id=1, source_target_pairs={{0,1},{1,0},{2,3},{3,2},{4,5},{5,4},{6,7},{7,6},{8,9},{9,8},{10,11... | collective-permute-start | bytes 958472 | tf_op jit(solution)/shard_map/ppermute | solution.py:31
  77.1 10.5 %collective-permute-start.18 = (bf16[200,384]{1,0:T(8,128)(2,1)S(1)}, bf16[200,384]{1,0:T(8,128)(2,1)}, u32[]{:S(2)}, u32[]{:S(2)}) collective-permute-start(bf16[200,384]{1,0:T(8,128)(2,1)S(1)} %add_convert_fusion.5), channel_id=1, source_target_pairs={{0,6},{1,7},{2,0},{3,1},{4,2},{5,3},{6,4},{7,5},{8,14},{9,15},{10,... | collective-permute-start | bytes 460808 | tf_op jit(solution)/shard_map/ppermute | solution.py:51
  81.0 6.9 %collective-permute-start.17 = (bf16[200,384]{1,0:T(8,128)(2,1)S(1)}, bf16[200,384]{1,0:T(8,128)(2,1)}, u32[]{:S(2)}, u32[]{:S(2)}) collective-permute-start(bf16[200,384]{1,0:T(8,128)(2,1)S(1)} %add_convert_fusion.5), channel_id=1, source_target_pairs={{0,4},{1,5},{2,6},{3,7},{4,0},{5,1},{6,2},{7,3},{8,12},{9,13},{10,... | collective-permute-start | bytes 460808 | tf_op jit(solution)/shard_map/ppermute | solution.py:51
  81.0 10.4 %collective-permute-start.16 = (bf16[200,384]{1,0:T(8,128)(2,1)S(1)}, bf16[200,384]{1,0:T(8,128)(2,1)}, u32[]{:S(2)}, u32[]{:S(2)}) collective-permute-start(bf16[200,384]{1,0:T(8,128)(2,1)S(1)} %add_convert_fusion.5), channel_id=1, source_target_pairs={{0,2},{1,3},{2,4},{3,5},{4,6},{5,7},{6,0},{7,1},{8,10},{9,11},{10,... | collective-permute-start | bytes 460808 | tf_op jit(solution)/shard_map/ppermute | solution.py:51
  93.8 3.3 %collective-permute-start.3 = (bf16[104,384]{1,0:T(8,128)(2,1)S(1)}, bf16[104,384]{1,0:T(8,128)(2,1)S(1)}, u32[]{:S(2)}, u32[]{:S(2)}) collective-permute-start(bf16[104,384]{1,0:T(8,128)(2,1)S(1)} %get-tuple-element.67), channel_id=1, source_target_pairs={{0,6},{1,7},{2,0},{3,1},{4,2},{5,3},{6,4},{7,5},{8,14},{9,15},{10,... | collective-permute-start | bytes 239624 | tf_op jit(solution)/shard_map/ppermute | solution.py:37
  94.0 4.8 %collective-permute-start.2 = (bf16[104,384]{1,0:T(8,128)(2,1)S(1)}, bf16[104,384]{1,0:T(8,128)(2,1)S(1)}, u32[]{:S(2)}, u32[]{:S(2)}) collective-permute-start(bf16[104,384]{1,0:T(8,128)(2,1)S(1)} %get-tuple-element.68), channel_id=1, source_target_pairs={{0,4},{1,5},{2,6},{3,7},{4,0},{5,1},{6,2},{7,3},{8,12},{9,13},{10,... | collective-permute-start | bytes 239624 | tf_op jit(solution)/shard_map/ppermute | solution.py:37
  94.4 5.2 %collective-permute-start.1 = (bf16[104,384]{1,0:T(8,128)(2,1)S(1)}, bf16[104,384]{1,0:T(8,128)(2,1)S(1)}, u32[]{:S(2)}, u32[]{:S(2)}) collective-permute-start(bf16[104,384]{1,0:T(8,128)(2,1)S(1)} %get-tuple-element.66), channel_id=1, source_target_pairs={{0,2},{1,3},{2,4},{3,5},{4,6},{5,7},{6,0},{7,1},{8,10},{9,11},{10,... | collective-permute-start | bytes 239624 | tf_op jit(solution)/shard_map/ppermute | solution.py:37
  95.4 16.1 %collective-permute-start.19 = (bf16[200,1536]{1,0:T(8,128)(2,1)S(1)}, bf16[200,1536]{1,0:T(8,128)(2,1)S(1)}, u32[]{:S(2)}, u32[]{:S(2)}) collective-permute-start(bf16[200,1536]{1,0:T(8,128)(2,1)S(1)} %pad_maximum_fusion.3), channel_id=1, source_target_pairs={{0,1},{1,0},{2,3},{3,2},{4,5},{5,4},{6,7},{7,6},{8,9},{9,8},{10,11... | collective-permute-start | bytes 1843208 | tf_op jit(solution)/shard_map/ppermute | solution.py:56
  99.7 4.8 %collective-permute-start.6 = (bf16[104,384]{1,0:T(8,128)(2,1)S(1)}, bf16[104,384]{1,0:T(8,128)(2,1)S(1)}, u32[]{:S(2)}, u32[]{:S(2)}) collective-permute-start(bf16[104,384]{1,0:T(8,128)(2,1)S(1)} %add_convert_fusion.7), channel_id=1, source_target_pairs={{0,6},{1,7},{2,0},{3,1},{4,2},{5,3},{6,4},{7,5},{8,14},{9,15},{10,... | collective-permute-start | bytes 239624 | tf_op jit(solution)/shard_map/ppermute | solution.py:51
  102.2 4.9 %collective-permute-start.5 = (bf16[104,384]{1,0:T(8,128)(2,1)S(1)}, bf16[104,384]{1,0:T(8,128)(2,1)S(1)}, u32[]{:S(2)}, u32[]{:S(2)}) collective-permute-start(bf16[104,384]{1,0:T(8,128)(2,1)S(1)} %add_convert_fusion.7), channel_id=1, source_target_pairs={{0,4},{1,5},{2,6},{3,7},{4,0},{5,1},{6,2},{7,3},{8,12},{9,13},{10,... | collective-permute-start | bytes 239624 | tf_op jit(solution)/shard_map/ppermute | solution.py:51
  102.2 5.3 %collective-permute-start.4 = (bf16[104,384]{1,0:T(8,128)(2,1)S(1)}, bf16[104,384]{1,0:T(8,128)(2,1)S(1)}, u32[]{:S(2)}, u32[]{:S(2)}) collective-permute-start(bf16[104,384]{1,0:T(8,128)(2,1)S(1)} %add_convert_fusion.7), channel_id=1, source_target_pairs={{0,2},{1,3},{2,4},{3,5},{4,6},{5,7},{6,0},{7,1},{8,10},{9,11},{10,... | collective-permute-start | bytes 239624 | tf_op jit(solution)/shard_map/ppermute | solution.py:51
  108.5 14.7 %collective-permute-start.7 = (bf16[104,1536]{1,0:T(8,128)(2,1)}, bf16[104,1536]{1,0:T(8,128)(2,1)}, u32[]{:S(2)}, u32[]{:S(2)}) collective-permute-start(bf16[104,1536]{1,0:T(8,128)(2,1)} %pad_maximum_fusion.9), channel_id=1, source_target_pairs={{0,1},{1,0},{2,3},{3,2},{4,5},{5,4},{6,7},{7,6},{8,9},{9,8},{10,11... | collective-permute-start | bytes 958472 | tf_op jit(solution)/shard_map/ppermute | solution.py:56
  138.5 1.7 collective-permute-start.8
  138.8 3.4 %collective-permute-start.20 = (bf16[200,1536]{1,0:T(8,128)(2,1)S(1)}, bf16[200,1536]{1,0:T(8,128)(2,1)S(1)}, u32[]{:S(2)}, u32[]{:S(2)}) collective-permute-start(bf16[200,1536]{1,0:T(8,128)(2,1)S(1)} %broadcast_select_fusion.1), channel_id=1, source_target_pairs={{0,1},{1,0},{2,3},{3,2},{4,5},{5,4},{6,7},{7,6},{8,9},{9,8},{10,11... | collective-permute-start | bytes 1843208 | tf_op jit(solution)/shard_map/ppermute | solution.py:31
  140.4 5.6 %collective-permute-start.11 = (bf16[104,384]{1,0:T(8,128)(2,1)S(1)}, bf16[104,384]{1,0:T(8,128)(2,1)S(1)}, u32[]{:S(2)}, u32[]{:S(2)}) collective-permute-start(bf16[104,384]{1,0:T(8,128)(2,1)S(1)} %get-tuple-element.60), channel_id=1, source_target_pairs={{0,6},{1,7},{2,0},{3,1},{4,2},{5,3},{6,4},{7,5},{8,14},{9,15},{10,... | collective-permute-start | bytes 239624 | tf_op jit(solution)/shard_map/ppermute | solution.py:37
  141.1 5.6 %collective-permute-start.10 = (bf16[104,384]{1,0:T(8,128)(2,1)S(1)}, bf16[104,384]{1,0:T(8,128)(2,1)S(1)}, u32[]{:S(2)}, u32[]{:S(2)}) collective-permute-start(bf16[104,384]{1,0:T(8,128)(2,1)S(1)} %get-tuple-element.61), channel_id=1, source_target_pairs={{0,4},{1,5},{2,6},{3,7},{4,0},{5,1},{6,2},{7,3},{8,12},{9,13},{10,... | collective-permute-start | bytes 239624 | tf_op jit(solution)/shard_map/ppermute | solution.py:37
  141.7 6.9 %collective-permute-start.9 = (bf16[104,384]{1,0:T(8,128)(2,1)S(1)}, bf16[104,384]{1,0:T(8,128)(2,1)S(1)}, u32[]{:S(2)}, u32[]{:S(2)}) collective-permute-start(bf16[104,384]{1,0:T(8,128)(2,1)S(1)} %get-tuple-element.59), channel_id=1, source_target_pairs={{0,2},{1,3},{2,4},{3,5},{4,6},{5,7},{6,0},{7,1},{8,10},{9,11},{10,... | collective-permute-start | bytes 239624 | tf_op jit(solution)/shard_map/ppermute | solution.py:37
  142.5 6.8 %collective-permute-start.23 = (bf16[200,384]{1,0:T(8,128)(2,1)S(1)}, bf16[200,384]{1,0:T(8,128)(2,1)S(1)}, u32[]{:S(2)}, u32[]{:S(2)}) collective-permute-start(bf16[200,384]{1,0:T(8,128)(2,1)S(1)} %get-tuple-element.50), channel_id=1, source_target_pairs={{0,6},{1,7},{2,0},{3,1},{4,2},{5,3},{6,4},{7,5},{8,14},{9,15},{10,... | collective-permute-start | bytes 460808 | tf_op jit(solution)/shard_map/ppermute | solution.py:37
  144.8 5.6 %collective-permute-start.22 = (bf16[200,384]{1,0:T(8,128)(2,1)S(1)}, bf16[200,384]{1,0:T(8,128)(2,1)S(1)}, u32[]{:S(2)}, u32[]{:S(2)}) collective-permute-start(bf16[200,384]{1,0:T(8,128)(2,1)S(1)} %get-tuple-element.51), channel_id=1, source_target_pairs={{0,4},{1,5},{2,6},{3,7},{4,0},{5,1},{6,2},{7,3},{8,12},{9,13},{10,... | collective-permute-start | bytes 460808 | tf_op jit(solution)/shard_map/ppermute | solution.py:37
  145.9 9.0 %collective-permute-start.21 = (bf16[200,384]{1,0:T(8,128)(2,1)S(1)}, bf16[200,384]{1,0:T(8,128)(2,1)S(1)}, u32[]{:S(2)}, u32[]{:S(2)}) collective-permute-start(bf16[200,384]{1,0:T(8,128)(2,1)S(1)} %get-tuple-element.49), channel_id=1, source_target_pairs={{0,2},{1,3},{2,4},{3,5},{4,6},{5,7},{6,0},{7,1},{8,10},{9,11},{10,... | collective-permute-start | bytes 460808 | tf_op jit(solution)/shard_map/ppermute | solution.py:37
  (55 other events, 293.1 us)

commit v11 on v10

--- a/solution.py
+++ b/solution.py
@@ -198,7 +198,7 @@
         jnp.where(head_mask[:, None, :], pre_mixed.reshape(heads_here, stretch_len, width_here), 0.0), axis=0
     ).astype(jnp.bfloat16)
     row_count = hidden_in.shape[0]
-    half = 8 * ((row_count // 3 + 7) // 8)
+    half = row_count - 8 * ((row_count // 3 + 7) // 8)
     late_attn, _ = lax.optimization_barrier((pre_out[half - per_home :], going_back))
     dec_out, early_pre = lax.optimization_barrier((dec_out, pre_out[: half - per_home]))
     early_attn = jnp.concatenate([dec_out, early_pre], axis=0)

time: 185 us -> 189 us (1.022)
  other arithmetic: 34.7 us -> 40.5 us
  local copies, waits for them, and re-layouts: 13.8 us -> 11.6 us
  waiting for transfers between devices: 27.5 us -> 29.6 us
    ppermute x12, waiting for transfers between devices: 10.8 us -> 17.6 us  [pair_then_z_scatter(): acc = acc + lax.ppermute(piece, 'head', perm).astype(jnp.float32)]
    unnamed x17, other arithmetic: 7.9 us -> 14.3 us
    all_to_all x1, waiting for transfers between devices: 2.83 us -> 0.01 us  [on_device(): lax.all_to_all(going_back, 'req', split_axis=0, concat_axis=0, tiled=True)]
    ppermute x12, starting transfers between devices: 12.1 us -> 14.3 us  [pair_then_z_scatter(): acc = acc + lax.ppermute(piece, 'head', perm).astype(jnp.float32)]
    ppermute x2, starting transfers between devices: 4.64 us -> 2.59 us  [z_then_pair_gather(): got = lax.ppermute(in_order, 'head', [(i, i ^ 1) for i in range(n)])]
    unnamed x122 -> x108, local copies, waits for them, and re-layouts: 4.85 us -> 3.57 us
  transfers between devices with their start and end apart: 26 -> 26, of which waited for: 15 -> 12; matrix products, arithmetic and copies ran while one was open for 23% -> 32% of each run, Pallas kernels for 0% -> 0%
where the time goes in v11:
time: 189 us; the launch traced here: 188 us
  starting transfers between devices  41.4 us (22%)
  other arithmetic  40.5 us (21%)
  matrix products  36.7 us (19%)
  waiting for transfers between devices  29.6 us (16%)
  blocking collectives  26.2 us (14%)
  local copies, waits for them, and re-layouts  11.6 us (6%)
    ppermute x12, waiting for transfers between devices, pair_then_z_scatter(): acc = acc + lax.ppermute(piece, 'head', perm).astype(jnp.float32)  17.6 us
    unnamed x17, other arithmetic  14.3 us
    ppermute x12, starting transfers between devices, pair_then_z_scatter(): acc = acc + lax.ppermute(piece, 'head', perm).astype(jnp.float32)  14.3 us
    all_to_all x1, blocking collectives, on_device(): lax.all_to_all(arrived, 'head', split_axis=0, concat_axis=1, tiled=True)  13.3 us
    all_to_all x1, blocking collectives, on_device(): lax.all_to_all(outgoing, 'req', split_axis=0, concat_axis=0, tiled=True)  12.9 us
    ppermute x6, waiting for transfers between devices, z_then_pair_gather(): parts.append(lax.ppermute(y, 'head', perm))  12 us
    dot_general x2, matrix products, feed_forward(): jnp.dot(hidden, down_weight, preferred_element_type=jnp.float32)  9.12 us
    all_to_all x1, starting transfers between devices, on_device(): lax.all_to_all(outgoing_q, 'req', split_axis=0, concat_axis=0, tiled=True)  7.62 us
  transfers between devices with their start and end apart: 26, of which 12 were waited for; matrix products, arithmetic and copies ran while one was open for 32% of the time, Pallas kernels for 0%

profile of v11, /device:TPU:1, one launch (start us, length us, event | category | flops | bytes accessed | tf_op | source)
XLA Modules:
  0.0 187.7 jit_solution(10098428652703180667)
XLA Ops:
  2.4 1.9 %convolution_convert_fusion.3 = bf16[768,384]{1,0:T(8,128)(2,1)} fusion(bf16[48,384]{1,0:T(8,128)(2,1)} %param.19, s32[48]{0:T(128)S(1)} %dynamic-slice_add_fusion), kind=kOutput, calls=%fused_computation.45 | convolution fusion | flops 28643328 | bytes 626880 | tf_op jit(solution)/shard_map/dot_general | solution.py:108
  4.3 7.6 %all-to-all-start = ((bf16[16,48,384]{2,1,0:T(8,128)(2,1)}), bf16[16,48,384]{2,1,0:T(8,128)(2,1)}, u32[]{:S(2)}, u32[]{:S(2)}) async-start(bf16[16,48,384]{2,1,0:T(8,128)(2,1)} %bitcast.137), calls=%async_computation | async-start | bytes 1179648 | tf_op jit(solution)/shard_map/all_to_all | solution.py:109
  15.0 4.0 %fusion = (f32[1024]{0:T(1024)S(1)}, f32[1024,2048]{1,0:T(8,128)S(1)}) fusion(pred[2048]{0:T(1024)(128)(4,1)S(1)} %iota_compare_fusion.12, bf16[1024,384]{1,0:T(8,128)(2,1)S(1)} %bitcast.144, bf16[2,2048,384]{2,1,0:T(8,128)(2,1)} %param.25), kind=kOutput, calls=%fused_computation.3 | convolution fusion | flops 1616903168 | bytes 10754048 | tf_op jit(solution)/shard_map/dot_general | solution.py:181
  19.5 2.2 %fusion.1 = f32[1024]{0:T(1024)S(1)} fusion(f32[1024,2048]{1,0:T(8,128)S(1)} %get-tuple-element.82, f32[1024]{0:T(1024)S(1)} %max.12, pred[2048]{0:T(1024)(128)(4,1)S(1)} %iota_compare_fusion.12), kind=kLoop, calls=%fused_computation.4 | loop fusion | flops 8387584 | bytes 8398848 | tf_op jit(solution)/shard_map/reduce_sum | solution.py:193
  21.9 2.4 %fusion.2 = f32[1024,384]{1,0:T(8,128)S(1)} fusion(f32[1024,2048]{1,0:T(8,128)S(1)} %get-tuple-element.82, f32[1024]{0:T(1024)S(1)} %add.306, f32[1024]{0:T(1024)S(1)} %max.12, pred[2048]{0:T(1024)(128)(4,1)S(1)} %iota_compare_fusion.12, bf16[2,2048,384]{2,1,0:T(8,128)(2,1)S(1)} %copy-done.49), kind=kOutput, calls=%fused_computation.5 | convolution fusion | flops 1621098496 | bytes 11544576 | tf_op jit(solution)/shard_map/dot_general | solution.py:194
  30.2 2.2 %fusion.141 = (f32[192]{0:T(256)S(1)}, f32[192,2048]{1,0:T(8,128)S(1)}) fusion(bf16[192,384]{1,0:T(8,128)(2,1)S(1)} %bitcast.155, bf16[2,2048,384]{2,1,0:T(8,128)(2,1)} %param.25, pred[2048]{0:T(1024)(128)(4,1)S(1)} %iota_compare_fusion.13), kind=kOutput, calls=%fused_computation.276 | convolution fusion | flops 303169344 | bytes 3296000 | tf_op jit(solution)/shard_map/dot_general | solution.py:135
  37.4 2.2 %fusion.36 = bf16[48,384]{1,0:T(8,128)(2,1)S(1)} fusion(bf16[4,48,2048]{2,1,0:T(8,128)(2,1)} %bitcast.146, bf16[2,2048,384]{2,1,0:T(8,128)(2,1)} %param.26, pred[4,384]{1,0:T(4,128)(4,1)S(1)} %iota_compare_fusion.15), kind=kOutput, calls=%fused_computation.57 | convolution fusion | flops 302118912 | bytes 2397696 | tf_op jit(solution)/shard_map/dot_general | solution.py:144
  40.0 2.4 %fusion.39 = bf16[48,384]{1,0:T(8,128)(2,1)S(1)} fusion(bf16[4,48,2048]{2,1,0:T(8,128)(2,1)} %bitcast.147, bf16[2,2048,384]{2,1,0:T(8,128)(2,1)} %param.26, pred[4,384]{1,0:T(4,128)(4,1)S(1)} %iota_compare_fusion.15), kind=kOutput, calls=%fused_computation.58 | convolution fusion | flops 302118912 | bytes 2397696 | tf_op jit(solution)/shard_map/dot_general | solution.py:144
  52.0 3.8 %collective-permute-start.15 = (bf16[104,384]{1,0:T(8,128)(2,1)}, bf16[104,384]{1,0:T(8,128)(2,1)}, u32[]{:S(2)}, u32[]{:S(2)}) collective-permute-start(bf16[104,384]{1,0:T(8,128)(2,1)} %get-tuple-element.67), channel_id=1, source_target_pairs={{0,6},{1,7},{2,0},{3,1},{4,2},{5,3},{6,4},{7,5},{8,14},{9,15},{10,... | collective-permute-start | bytes 239624 | tf_op jit(solution)/shard_map/ppermute | solution.py:37
  56.6 6.9 %all-to-all-start.1 = ((bf16[16,48,512]{2,1,0:T(8,128)(2,1)}), bf16[16,48,512]{2,1,0:T(8,128)(2,1)}, u32[]{:S(2)}, u32[]{:S(2)}) async-start(bf16[16,48,512]{2,1,0:T(8,128)(2,1)} %bitcast.143), calls=%async_computation.1 | async-start | bytes 1572864 | tf_op jit(solution)/shard_map/all_to_all | solution.py:159
  64.6 2.1 %collective-permute-start.18 = (bf16[104,384]{1,0:T(8,128)(2,1)S(1)}, bf16[104,384]{1,0:T(8,128)(2,1)S(1)}, u32[]{:S(2)}, u32[]{:S(2)}) collective-permute-start(bf16[104,384]{1,0:T(8,128)(2,1)S(1)} %add_convert_fusion.7), channel_id=1, source_target_pairs={{0,6},{1,7},{2,0},{3,1},{4,2},{5,3},{6,4},{7,5},{8,14},{9,15},{10,... | collective-permute-start | bytes 239624 | tf_op jit(solution)/shard_map/ppermute | solution.py:51
  66.6 1.8 collective-permute-start.17
  69.0 2.8 %collective-permute-done.17 = bf16[104,384]{1,0:T(8,128)(2,1)S(1)} collective-permute-done((bf16[104,384]{1,0:T(8,128)(2,1)S(1)}, bf16[104,384]{1,0:T(8,128)(2,1)S(1)}, u32[]{:S(2)}, u32[]{:S(2)}) %collective-permute-start.17) | collective-permute-done | bytes 79904 | tf_op jit(solution)/shard_map/ppermute | solution.py:51
  71.8 2.3 %collective-permute-done.16 = bf16[104,384]{1,0:T(8,128)(2,1)S(1)} collective-permute-done((bf16[104,384]{1,0:T(8,128)(2,1)S(1)}, bf16[104,384]{1,0:T(8,128)(2,1)S(1)}, u32[]{:S(2)}, u32[]{:S(2)}) %collective-permute-start.16) | collective-permute-done | bytes 79904 | tf_op jit(solution)/shard_map/ppermute | solution.py:51
  75.0 1.6 collective-permute-start.19
  80.0 2.6 %fusion.80 = f32[200,3072]{1,0:T(8,128)S(1)} fusion(bf16[384,3072]{1,0:T(8,128)(2,1)} %param.31, bf16[152,384]{1,0:T(8,128)(2,1)} %slice.250, bf16[48,384]{1,0:T(8,128)(2,1)S(1)} %fusion.105), kind=kOutput, calls=%fused_computation.127 | convolution fusion | flops 472166400 | bytes 4970496 | tf_op jit(solution)/shard_map/dot_general | solution.py:209
  83.1 2.5 %collective-permute-start = (bf16[200,1536]{1,0:T(8,128)(2,1)S(1)}, bf16[200,1536]{1,0:T(8,128)(2,1)S(1)}, u32[]{:S(2)}, u32[]{:S(2)}) collective-permute-start(bf16[200,1536]{1,0:T(8,128)(2,1)S(1)} %broadcast_select_fusion.2), channel_id=1, source_target_pairs={{0,1},{1,0},{2,3},{3,2},{4,5},{5,4},{6,7},{7,6},{8,9},{9,8},{10,11... | collective-permute-start | bytes 1843208 | tf_op jit(solution)/shard_map/ppermute | solution.py:31
  93.5 2.1 %collective-permute-start.3 = (bf16[200,384]{1,0:T(8,128)(2,1)S(1)}, bf16[200,384]{1,0:T(8,128)(2,1)S(1)}, u32[]{:S(2)}, u32[]{:S(2)}) collective-permute-start(bf16[200,384]{1,0:T(8,128)(2,1)S(1)} %get-tuple-element.57), channel_id=1, source_target_pairs={{0,6},{1,7},{2,0},{3,1},{4,2},{5,3},{6,4},{7,5},{8,14},{9,15},{10,... | collective-permute-start | bytes 460808 | tf_op jit(solution)/shard_map/ppermute | solution.py:37
  95.6 1.7 collective-permute-start.2
  97.3 2.5 %collective-permute-done.3 = bf16[200,384]{1,0:T(8,128)(2,1)S(1)} collective-permute-done((bf16[200,384]{1,0:T(8,128)(2,1)S(1)}, bf16[200,384]{1,0:T(8,128)(2,1)S(1)}, u32[]{:S(2)}, u32[]{:S(2)}) %collective-permute-start.3) | collective-permute-done | bytes 153632 | tf_op jit(solution)/shard_map/ppermute | solution.py:37
  99.8 2.5 %collective-permute-done.2 = bf16[200,384]{1,0:T(8,128)(2,1)S(1)} collective-permute-done((bf16[200,384]{1,0:T(8,128)(2,1)S(1)}, bf16[200,384]{1,0:T(8,128)(2,1)S(1)}, u32[]{:S(2)}, u32[]{:S(2)}) %collective-permute-start.2) | collective-permute-done | bytes 153632 | tf_op jit(solution)/shard_map/ppermute | solution.py:37
  102.3 4.0 %collective-permute-done.1 = bf16[200,384]{1,0:T(8,128)(2,1)S(1)} collective-permute-done((bf16[200,384]{1,0:T(8,128)(2,1)S(1)}, bf16[200,384]{1,0:T(8,128)(2,1)S(1)}, u32[]{:S(2)}, u32[]{:S(2)}) %collective-permute-start.1) | collective-permute-done | bytes 153632 | tf_op jit(solution)/shard_map/ppermute | solution.py:37
  109.9 1.6 collective-permute-done.6
  112.6 4.1 %collective-permute-done.4 = bf16[200,384]{1,0:T(8,128)(2,1)S(1)} collective-permute-done((bf16[200,384]{1,0:T(8,128)(2,1)S(1)}, bf16[200,384]{1,0:T(8,128)(2,1)S(1)}, u32[]{:S(2)}, u32[]{:S(2)}) %collective-permute-start.4) | collective-permute-done | bytes 153632 | tf_op jit(solution)/shard_map/ppermute | solution.py:51
  119.4 4.2 %convolution_convert_fusion.1 = bf16[104,3072]{1,0:T(8,128)(2,1)} fusion(bf16[512,3072]{1,0:T(8,128)(2,1)S(1)} %copy-done, bf16[3072,512]{1,0:T(8,128)(2,1)} %param.34, f32[104,512]{1,0:T(8,128)} %fusion.78, bf16[104,3072]{1,0:T(8,128)(2,1)} %copy-done.2, f32[3072]{0:T(1024)S(1)} %copy-done.41, f32[104]{0:T(128)S(1)} %add_rsqrt_fusion.1), kind=kOutput, calls=%fused_computation.7 | convolution fusion | flops 656228352 | bytes 7795104 | tf_op jit(solution)/shard_map/dot_general | solution.py:222
  134.9 1.6 fusion.57
  136.6 4.9 %convolution_convert_fusion = bf16[200,3072]{1,0:T(8,128)(2,1)} fusion(bf16[512,3072]{1,0:T(8,128)(2,1)S(1)} %copy-done, bf16[3072,512]{1,0:T(8,128)(2,1)} %param.34, f32[200,512]{1,0:T(8,128)} %fusion.57, bf16[200,3072]{1,0:T(8,128)(2,1)} %copy-done.9, f32[3072]{0:T(1024)S(1)} %copy-done.41, f32[200]{0:T(256)S(1)} %add_rsqrt_fusion), kind=kOutput, calls=%fused_computation.6 | convolution fusion | flops 1261977600 | bytes 9171744 | tf_op jit(solution)/shard_map/dot_general | solution.py:222
  147.6 2.2 %collective-permute-start.11 = (bf16[200,384]{1,0:T(8,128)(2,1)S(1)}, bf16[200,384]{1,0:T(8,128)(2,1)S(1)}, u32[]{:S(2)}, u32[]{:S(2)}) collective-permute-start(bf16[200,384]{1,0:T(8,128)(2,1)S(1)} %get-tuple-element.50), channel_id=1, source_target_pairs={{0,6},{1,7},{2,0},{3,1},{4,2},{5,3},{6,4},{7,5},{8,14},{9,15},{10,... | collective-permute-start | bytes 460808 | tf_op jit(solution)/shard_map/ppermute | solution.py:37
  151.4 2.0 %collective-permute-done.21 = bf16[104,384]{1,0:T(8,128)(2,1)S(1)} collective-permute-done((bf16[104,384]{1,0:T(8,128)(2,1)S(1)}, bf16[104,384]{1,0:T(8,128)(2,1)S(1)}, u32[]{:S(2)}, u32[]{:S(2)}) %collective-permute-start.21) | collective-permute-done | bytes 79904 | tf_op jit(solution)/shard_map/ppermute | solution.py:37
  155.7 4.4 %collective-permute-done.9 = bf16[200,384]{1,0:T(8,128)(2,1)S(1)} collective-permute-done((bf16[200,384]{1,0:T(8,128)(2,1)S(1)}, bf16[200,384]{1,0:T(8,128)(2,1)S(1)}, u32[]{:S(2)}, u32[]{:S(2)}) %collective-permute-start.9) | collective-permute-done | bytes 153632 | tf_op jit(solution)/shard_map/ppermute | solution.py:37
  160.7 12.9 %all_to_all.52 = bf16[16,40,384]{2,1,0:T(8,128)(2,1)S(1)} all-to-all(bf16[16,40,384]{2,1,0:T(8,128)(2,1)S(1)} %bitcast.149), channel_id=1, replica_groups=mesh['req'=16,'head'=8] {'req'}, dimensions={0} | all-to-all | bytes 983040 | tf_op jit(solution)/shard_map/all_to_all | solution.py:245
  173.5 13.3 %all_to_all.53 = bf16[8,80,384]{2,1,0:T(8,128)(2,1)S(1)} all-to-all(bf16[8,80,384]{2,1,0:T(8,128)(2,1)S(1)} %bitcast.138), channel_id=1, replica_groups=mesh['req'=16,'head'=8] {'head'}, dimensions={0} | all-to-all | bytes 983040 | tf_op jit(solution)/shard_map/all_to_all | solution.py:246
  (268 shorter events, 70.7 us)
Async XLA Ops:
  0.0 119.4 %copy-start = (bf16[512,3072]{1,0:T(8,128)(2,1)S(1)}, bf16[512,3072]{1,0:T(8,128)(2,1)}, u32[]{:S(2)}) copy-start(bf16[512,3072]{1,0:T(8,128)(2,1)} %param.35) | copy-start | bytes 9437188
  0.0 14.8 %copy-start.39 = (bf16[256,384]{1,0:T(8,128)(2,1)S(1)}, bf16[256,384]{1,0:T(8,128)(2,1)}, u32[]{:S(2)}) copy-start(bf16[256,384]{1,0:T(8,128)(2,1)} %param.22) | copy-start | bytes 589828
  4.3 24.5 %all-to-all-start = ((bf16[16,48,384]{2,1,0:T(8,128)(2,1)}), bf16[16,48,384]{2,1,0:T(8,128)(2,1)}, u32[]{:S(2)}, u32[]{:S(2)}) async-start(bf16[16,48,384]{2,1,0:T(8,128)(2,1)} %bitcast.137), calls=%async_computation | async-start | bytes 1179648 | tf_op jit(solution)/shard_map/all_to_all | solution.py:109
  46.9 3.1 %collective-permute-start.12 = (bf16[104,1536]{1,0:T(8,128)(2,1)}, bf16[104,1536]{1,0:T(8,128)(2,1)}, u32[]{:S(2)}, u32[]{:S(2)}) collective-permute-start(bf16[104,1536]{1,0:T(8,128)(2,1)} %broadcast_select_fusion.4), channel_id=1, source_target_pairs={{0,1},{1,0},{2,3},{3,2},{4,5},{5,4},{6,7},{7,6},{8,9},{9,8},{10,11... | collective-permute-start | bytes 958472 | tf_op jit(solution)/shard_map/ppermute | solution.py:31
  51.3 17.1 %copy-start.40 = (s32[384,16]{0,1:T(8,128)S(1)}, s32[384,16]{0,1:T(8,128)}, u32[]{:S(2)}) copy-start(s32[384,16]{0,1:T(8,128)} %bitcast_bitcast_fusion) | copy-start | bytes 73732
  52.0 11.5 %collective-permute-start.15 = (bf16[104,384]{1,0:T(8,128)(2,1)}, bf16[104,384]{1,0:T(8,128)(2,1)}, u32[]{:S(2)}, u32[]{:S(2)}) collective-permute-start(bf16[104,384]{1,0:T(8,128)(2,1)} %get-tuple-element.67), channel_id=1, source_target_pairs={{0,6},{1,7},{2,0},{3,1},{4,2},{5,3},{6,4},{7,5},{8,14},{9,15},{10,... | collective-permute-start | bytes 239624 | tf_op jit(solution)/shard_map/ppermute | solution.py:37
  55.8 7.8 %collective-permute-start.14 = (bf16[104,384]{1,0:T(8,128)(2,1)}, bf16[104,384]{1,0:T(8,128)(2,1)}, u32[]{:S(2)}, u32[]{:S(2)}) collective-permute-start(bf16[104,384]{1,0:T(8,128)(2,1)} %get-tuple-element.68), channel_id=1, source_target_pairs={{0,4},{1,5},{2,6},{3,7},{4,0},{5,1},{6,2},{7,3},{8,12},{9,13},{10,... | collective-permute-start | bytes 239624 | tf_op jit(solution)/shard_map/ppermute | solution.py:37
  55.8 7.8 %collective-permute-start.13 = (bf16[104,384]{1,0:T(8,128)(2,1)}, bf16[104,384]{1,0:T(8,128)(2,1)}, u32[]{:S(2)}, u32[]{:S(2)}) collective-permute-start(bf16[104,384]{1,0:T(8,128)(2,1)} %get-tuple-element.66), channel_id=1, source_target_pairs={{0,2},{1,3},{2,4},{3,5},{4,6},{5,7},{6,0},{7,1},{8,10},{9,11},{10,... | collective-permute-start | bytes 239624 | tf_op jit(solution)/shard_map/ppermute | solution.py:37
  56.6 20.0 %all-to-all-start.1 = ((bf16[16,48,512]{2,1,0:T(8,128)(2,1)}), bf16[16,48,512]{2,1,0:T(8,128)(2,1)}, u32[]{:S(2)}, u32[]{:S(2)}) async-start(bf16[16,48,512]{2,1,0:T(8,128)(2,1)} %bitcast.143), calls=%async_computation.1 | async-start | bytes 1572864 | tf_op jit(solution)/shard_map/all_to_all | solution.py:159
  64.6 4.4 %collective-permute-start.18 = (bf16[104,384]{1,0:T(8,128)(2,1)S(1)}, bf16[104,384]{1,0:T(8,128)(2,1)S(1)}, u32[]{:S(2)}, u32[]{:S(2)}) collective-permute-start(bf16[104,384]{1,0:T(8,128)(2,1)S(1)} %add_convert_fusion.7), channel_id=1, source_target_pairs={{0,6},{1,7},{2,0},{3,1},{4,2},{5,3},{6,4},{7,5},{8,14},{9,15},{10,... | collective-permute-start | bytes 239624 | tf_op jit(solution)/shard_map/ppermute | solution.py:51
  66.6 5.2 %collective-permute-start.17 = (bf16[104,384]{1,0:T(8,128)(2,1)S(1)}, bf16[104,384]{1,0:T(8,128)(2,1)S(1)}, u32[]{:S(2)}, u32[]{:S(2)}) collective-permute-start(bf16[104,384]{1,0:T(8,128)(2,1)S(1)} %add_convert_fusion.7), channel_id=1, source_target_pairs={{0,4},{1,5},{2,6},{3,7},{4,0},{5,1},{6,2},{7,3},{8,12},{9,13},{10,... | collective-permute-start | bytes 239624 | tf_op jit(solution)/shard_map/ppermute | solution.py:51
  68.4 5.7 %collective-permute-start.16 = (bf16[104,384]{1,0:T(8,128)(2,1)S(1)}, bf16[104,384]{1,0:T(8,128)(2,1)S(1)}, u32[]{:S(2)}, u32[]{:S(2)}) collective-permute-start(bf16[104,384]{1,0:T(8,128)(2,1)S(1)} %add_convert_fusion.7), channel_id=1, source_target_pairs={{0,2},{1,3},{2,4},{3,5},{4,6},{5,7},{6,0},{7,1},{8,10},{9,11},{10,... | collective-permute-start | bytes 239624 | tf_op jit(solution)/shard_map/ppermute | solution.py:51
  75.0 10.5 %collective-permute-start.19 = (bf16[104,1536]{1,0:T(8,128)(2,1)}, bf16[104,1536]{1,0:T(8,128)(2,1)}, u32[]{:S(2)}, u32[]{:S(2)}) collective-permute-start(bf16[104,1536]{1,0:T(8,128)(2,1)} %pad_maximum_fusion.9), channel_id=1, source_target_pairs={{0,1},{1,0},{2,3},{3,2},{4,5},{5,4},{6,7},{7,6},{8,9},{9,8},{10,11... | collective-permute-start | bytes 958472 | tf_op jit(solution)/shard_map/ppermute | solution.py:56
  83.1 10.1 %collective-permute-start = (bf16[200,1536]{1,0:T(8,128)(2,1)S(1)}, bf16[200,1536]{1,0:T(8,128)(2,1)S(1)}, u32[]{:S(2)}, u32[]{:S(2)}) collective-permute-start(bf16[200,1536]{1,0:T(8,128)(2,1)S(1)} %broadcast_select_fusion.2), channel_id=1, source_target_pairs={{0,1},{1,0},{2,3},{3,2},{4,5},{5,4},{6,7},{7,6},{8,9},{9,8},{10,11... | collective-permute-start | bytes 1843208 | tf_op jit(solution)/shard_map/ppermute | solution.py:31
  92.9 15.6 %copy-start.2 = (bf16[104,3072]{1,0:T(8,128)(2,1)}, bf16[104,3072]{1,0:T(8,128)(2,1)S(1)}, u32[]{:S(2)}) copy-start(bf16[104,3072]{1,0:T(8,128)(2,1)S(1)} %select_dynamic-update-slice_fusion.8) | copy-start | bytes 1916932
  93.1 15.4 %copy-start.3 = (bf16[3072,512]{1,0:T(8,128)(2,1)S(1)}, bf16[3072,512]{1,0:T(8,128)(2,1)}, u32[]{:S(2)}) copy-start(bf16[3072,512]{1,0:T(8,128)(2,1)} %param.33) | copy-start | bytes 9437188
  93.2 15.4 %copy-start.41 = (f32[3072]{0:T(1024)S(1)}, f32[3072]{0:T(1024)}, u32[]{:S(2)}) copy-start(f32[3072]{0:T(1024)} %param.32) | copy-start | bytes 36868
  93.5 6.4 %collective-permute-start.3 = (bf16[200,384]{1,0:T(8,128)(2,1)S(1)}, bf16[200,384]{1,0:T(8,128)(2,1)S(1)}, u32[]{:S(2)}, u32[]{:S(2)}) collective-permute-start(bf16[200,384]{1,0:T(8,128)(2,1)S(1)} %get-tuple-element.57), channel_id=1, source_target_pairs={{0,6},{1,7},{2,0},{3,1},{4,2},{5,3},{6,4},{7,5},{8,14},{9,15},{10,... | collective-permute-start | bytes 460808 | tf_op jit(solution)/shard_map/ppermute | solution.py:37
  95.6 6.7 %collective-permute-start.2 = (bf16[200,384]{1,0:T(8,128)(2,1)S(1)}, bf16[200,384]{1,0:T(8,128)(2,1)S(1)}, u32[]{:S(2)}, u32[]{:S(2)}) collective-permute-start(bf16[200,384]{1,0:T(8,128)(2,1)S(1)} %get-tuple-element.58), channel_id=1, source_target_pairs={{0,4},{1,5},{2,6},{3,7},{4,0},{5,1},{6,2},{7,3},{8,12},{9,13},{10,... | collective-permute-start | bytes 460808 | tf_op jit(solution)/shard_map/ppermute | solution.py:37
  97.3 9.0 %collective-permute-start.1 = (bf16[200,384]{1,0:T(8,128)(2,1)S(1)}, bf16[200,384]{1,0:T(8,128)(2,1)S(1)}, u32[]{:S(2)}, u32[]{:S(2)}) collective-permute-start(bf16[200,384]{1,0:T(8,128)(2,1)S(1)} %get-tuple-element.56), channel_id=1, source_target_pairs={{0,2},{1,3},{2,4},{3,5},{4,6},{5,7},{6,0},{7,1},{8,10},{9,11},{10,... | collective-permute-start | bytes 460808 | tf_op jit(solution)/shard_map/ppermute | solution.py:37
  106.4 5.1 %collective-permute-start.6 = (bf16[200,384]{1,0:T(8,128)(2,1)S(1)}, bf16[200,384]{1,0:T(8,128)(2,1)S(1)}, u32[]{:S(2)}, u32[]{:S(2)}) collective-permute-start(bf16[200,384]{1,0:T(8,128)(2,1)S(1)} %add_convert_fusion.5), channel_id=1, source_target_pairs={{0,6},{1,7},{2,0},{3,1},{4,2},{5,3},{6,4},{7,5},{8,14},{9,15},{10,... | collective-permute-start | bytes 460808 | tf_op jit(solution)/shard_map/ppermute | solution.py:51
  106.4 6.2 %collective-permute-start.5 = (bf16[200,384]{1,0:T(8,128)(2,1)S(1)}, bf16[200,384]{1,0:T(8,128)(2,1)S(1)}, u32[]{:S(2)}, u32[]{:S(2)}) collective-permute-start(bf16[200,384]{1,0:T(8,128)(2,1)S(1)} %add_convert_fusion.5), channel_id=1, source_target_pairs={{0,4},{1,5},{2,6},{3,7},{4,0},{5,1},{6,2},{7,3},{8,12},{9,13},{10,... | collective-permute-start | bytes 460808 | tf_op jit(solution)/shard_map/ppermute | solution.py:51
  107.8 8.9 %collective-permute-start.4 = (bf16[200,384]{1,0:T(8,128)(2,1)S(1)}, bf16[200,384]{1,0:T(8,128)(2,1)S(1)}, u32[]{:S(2)}, u32[]{:S(2)}) collective-permute-start(bf16[200,384]{1,0:T(8,128)(2,1)S(1)} %add_convert_fusion.5), channel_id=1, source_target_pairs={{0,2},{1,3},{2,4},{3,5},{4,6},{5,7},{6,0},{7,1},{8,10},{9,11},{10,... | collective-permute-start | bytes 460808 | tf_op jit(solution)/shard_map/ppermute | solution.py:51
  118.4 7.4 %collective-permute-start.7 = (bf16[200,1536]{1,0:T(8,128)(2,1)}, bf16[200,1536]{1,0:T(8,128)(2,1)}, u32[]{:S(2)}, u32[]{:S(2)}) collective-permute-start(bf16[200,1536]{1,0:T(8,128)(2,1)} %pad_maximum_fusion.3), channel_id=1, source_target_pairs={{0,1},{1,0},{2,3},{3,2},{4,5},{5,4},{6,7},{7,6},{8,9},{9,8},{10,11... | collective-permute-start | bytes 1843208 | tf_op jit(solution)/shard_map/ppermute | solution.py:56
  125.8 18.0 %collective-permute-start.20 = (bf16[104,1536]{1,0:T(8,128)(2,1)}, bf16[104,1536]{1,0:T(8,128)(2,1)}, u32[]{:S(2)}, u32[]{:S(2)}) collective-permute-start(bf16[104,1536]{1,0:T(8,128)(2,1)} %broadcast_select_fusion.3), channel_id=1, source_target_pairs={{0,1},{1,0},{2,3},{3,2},{4,5},{5,4},{6,7},{7,6},{8,9},{9,8},{10,11... | collective-permute-start | bytes 958472 | tf_op jit(solution)/shard_map/ppermute | solution.py:31
  143.3 4.0 %collective-permute-start.8 = (bf16[200,1536]{1,0:T(8,128)(2,1)S(1)}, bf16[200,1536]{1,0:T(8,128)(2,1)S(1)}, u32[]{:S(2)}, u32[]{:S(2)}) collective-permute-start(bf16[200,1536]{1,0:T(8,128)(2,1)S(1)} %broadcast_select_fusion.1), channel_id=1, source_target_pairs={{0,1},{1,0},{2,3},{3,2},{4,5},{5,4},{6,7},{7,6},{8,9},{9,8},{10,11... | collective-permute-start | bytes 1843208 | tf_op jit(solution)/shard_map/ppermute | solution.py:31
  145.1 5.7 %collective-permute-start.23 = (bf16[104,384]{1,0:T(8,128)(2,1)S(1)}, bf16[104,384]{1,0:T(8,128)(2,1)S(1)}, u32[]{:S(2)}, u32[]{:S(2)}) collective-permute-start(bf16[104,384]{1,0:T(8,128)(2,1)S(1)} %get-tuple-element.60), channel_id=1, source_target_pairs={{0,6},{1,7},{2,0},{3,1},{4,2},{5,3},{6,4},{7,5},{8,14},{9,15},{10,... | collective-permute-start | bytes 239624 | tf_op jit(solution)/shard_map/ppermute | solution.py:37
  146.0 5.5 %collective-permute-start.22 = (bf16[104,384]{1,0:T(8,128)(2,1)S(1)}, bf16[104,384]{1,0:T(8,128)(2,1)S(1)}, u32[]{:S(2)}, u32[]{:S(2)}) collective-permute-start(bf16[104,384]{1,0:T(8,128)(2,1)S(1)} %get-tuple-element.61), channel_id=1, source_target_pairs={{0,4},{1,5},{2,6},{3,7},{4,0},{5,1},{6,2},{7,3},{8,12},{9,13},{10,... | collective-permute-start | bytes 239624 | tf_op jit(solution)/shard_map/ppermute | solution.py:37
  146.7 6.8 %collective-permute-start.21 = (bf16[104,384]{1,0:T(8,128)(2,1)S(1)}, bf16[104,384]{1,0:T(8,128)(2,1)S(1)}, u32[]{:S(2)}, u32[]{:S(2)}) collective-permute-start(bf16[104,384]{1,0:T(8,128)(2,1)S(1)} %get-tuple-element.59), channel_id=1, source_target_pairs={{0,2},{1,3},{2,4},{3,5},{4,6},{5,7},{6,0},{7,1},{8,10},{9,11},{10,... | collective-permute-start | bytes 239624 | tf_op jit(solution)/shard_map/ppermute | solution.py:37
  147.6 6.5 %collective-permute-start.11 = (bf16[200,384]{1,0:T(8,128)(2,1)S(1)}, bf16[200,384]{1,0:T(8,128)(2,1)S(1)}, u32[]{:S(2)}, u32[]{:S(2)}) collective-permute-start(bf16[200,384]{1,0:T(8,128)(2,1)S(1)} %get-tuple-element.50), channel_id=1, source_target_pairs={{0,6},{1,7},{2,0},{3,1},{4,2},{5,3},{6,4},{7,5},{8,14},{9,15},{10,... | collective-permute-start | bytes 460808 | tf_op jit(solution)/shard_map/ppermute | solution.py:37
  149.8 5.9 %collective-permute-start.10 = (bf16[200,384]{1,0:T(8,128)(2,1)S(1)}, bf16[200,384]{1,0:T(8,128)(2,1)S(1)}, u32[]{:S(2)}, u32[]{:S(2)}) collective-permute-start(bf16[200,384]{1,0:T(8,128)(2,1)S(1)} %get-tuple-element.51), channel_id=1, source_target_pairs={{0,4},{1,5},{2,6},{3,7},{4,0},{5,1},{6,2},{7,3},{8,12},{9,13},{10,... | collective-permute-start | bytes 460808 | tf_op jit(solution)/shard_map/ppermute | solution.py:37
  150.8 9.3 %collective-permute-start.9 = (bf16[200,384]{1,0:T(8,128)(2,1)S(1)}, bf16[200,384]{1,0:T(8,128)(2,1)S(1)}, u32[]{:S(2)}, u32[]{:S(2)}) collective-permute-start(bf16[200,384]{1,0:T(8,128)(2,1)S(1)} %get-tuple-element.49), channel_id=1, source_target_pairs={{0,2},{1,3},{2,4},{3,5},{4,6},{5,7},{6,0},{7,1},{8,10},{9,11},{10,... | collective-permute-start | bytes 460808 | tf_op jit(solution)/shard_map/ppermute | solution.py:37
  (47 other events, 204.6 us)
